TPU v7x, 32 devices: a whole 2x2x4 slice. The times are simulated.
32 devices in a mesh: ctx: 16 (over z, y, x), dp: 2 (over core).
Axes of the slice: x: 2, y: 2, z: 4, core: 2. Of those that a mesh axis runs over, the one named last changes fastest.
Arguments:
- queries: bfloat16 [2, 16, 2, 64, 4096], P('dp', 'ctx'), may hold values from -12 to 12
- keys: bfloat16 [2, 16, 2, 64, 512], P('dp', 'ctx'), may hold values from -12 to 12
- values: bfloat16 [2, 16, 2, 64, 512], P('dp', 'ctx'), may hold values from -6 to 6
- doc_bounds: int32 [2, 16, 2, 2, 64], P('dp', 'ctx'), may hold values from 0 to 2047, as said below
- sink_logit: float32 [32], replicated, may hold values from 0 to 3
- out_grad: bfloat16 [2, 16, 2, 64, 4096], P('dp', 'ctx'), may hold values from -9 to 9
Outputs:
- attn_out: bfloat16 [2, 16, 2, 64, 4096], P('dp', 'ctx')
- query_grad: bfloat16 [2, 16, 2, 64, 4096], P('dp', 'ctx')
- key_grad: bfloat16 [2, 16, 2, 64, 512], P('dp', 'ctx')
- value_grad: bfloat16 [2, 16, 2, 64, 512], P('dp', 'ctx')
- sink_grad: float32 [32], replicated
Inputs may be any that keep to these rules, and one draw needn't show every extreme that they name: `doc_bounds`: documents are contiguous runs that tile each pack in position order, each of 1 to 64 tokens; every pack has one of exactly 64 tokens; both entries of a token name its own document's first and last position.
All inputs are finite; a program needn't handle non-finite values.
Results may differ from a plain program's by a relative error of at most 0.025.
Values may be sent and summed in bfloat16 or wider, within the bound.
No kernel may reach another device: no remote copies, remote signals or barrier semaphores. Data moves between devices by JAX's collectives and lax.ppermute only.
A program may use at most 64 MiB of HBM per device.

v0:
```python
import math

import jax
import jax.numpy as jnp
from jax import lax
from jax.sharding import PartitionSpec as P

HEADS = 32
KV_HEADS = 4
HEAD_DIM = 128
GROUP = 8
REACH = 1


def with_halo(shard, sides, width):
    for axis, dim in sides:
        size, length = (lax.axis_size(axis), shard.shape[dim])
        up = [(i, (i + 1) % size) for i in range(size - 1)]
        down = [(j, i) for i, j in up]
        last = lax.slice_in_dim(shard, length - width, length, axis=dim)
        initial = lax.slice_in_dim(shard, 0, width, axis=dim)
        before = lax.ppermute(last, axis, up)
        after = lax.ppermute(initial, axis, down)
        shard = jnp.concatenate([before, shard, after], axis=dim)
    return shard


def pick_lanes(widened, kept, at_fold):
    later = jnp.where(at_fold, kept, widened[3])
    return jnp.stack([later, widened[0]])


def block_scores(query_rows, key_rows, score_scale):
    grouped = query_rows.reshape(query_rows.shape[0], KV_HEADS, GROUP, HEAD_DIM)
    keyed_rows = key_rows.reshape(key_rows.shape[0], KV_HEADS, HEAD_DIM)
    return (
        jnp.einsum("tkgd,ukd->kgtu", grouped, keyed_rows, preferred_element_type=jnp.float32)
        * score_scale
    )


def grad_scores(grad_rows, value_rows):
    grouped = grad_rows.reshape(grad_rows.shape[0], KV_HEADS, GROUP, HEAD_DIM)
    valued = value_rows.reshape(value_rows.shape[0], KV_HEADS, HEAD_DIM)
    return jnp.einsum("tkgd,ukd->kgtu", grouped, valued, preferred_element_type=jnp.float32)


def mix_rows(weights, side_rows):
    shaped = side_rows.reshape(side_rows.shape[0], KV_HEADS, HEAD_DIM)
    mixed = jnp.einsum("kgtu,ukd->tkgd", weights, shaped, preferred_element_type=jnp.float32)
    return mixed.reshape(mixed.shape[0], HEADS * HEAD_DIM)


def key_side_sum(weights, query_rows):
    grouped = query_rows.reshape(query_rows.shape[0], KV_HEADS, GROUP, HEAD_DIM)
    summed = jnp.einsum("kgtu,tkgd->ukd", weights, grouped, preferred_element_type=jnp.float32)
    return summed.reshape(summed.shape[0], KV_HEADS * HEAD_DIM)


def per_device(queries, keys, values, doc_bounds, sink_logit, out_grad):
    block_rows = queries.shape[3]
    query_width = queries.shape[4]
    value_width = keys.shape[4]
    pair_count = lax.axis_size("ctx")
    my_index = lax.axis_index("ctx")
    score_scale = 1.0 / math.sqrt(HEAD_DIM)
    at_fold = my_index == pair_count - 1
    last_block = 2 * pair_count - 1
    span = (REACH + 1) * block_rows
    query_lanes = queries.reshape(2, block_rows, query_width)
    grad_lanes = out_grad.reshape(2, block_rows, query_width)
    key_lanes = keys.reshape(2, block_rows, value_width)
    value_lanes = values.reshape(2, block_rows, value_width)
    bound_lanes = doc_bounds.reshape(2, 2, block_rows)
    row_offsets = jnp.arange(block_rows, dtype=jnp.int32)
    window_offsets = jnp.arange(span, dtype=jnp.int32)
    lane_block = [my_index, last_block - my_index]
    sink_col = sink_logit.reshape(KV_HEADS, GROUP, 1)
    own_pair = jnp.concatenate([key_lanes, value_lanes], axis=2)
    relay_state = own_pair[::-1]
    seen = [own_pair]
    widened = with_halo(relay_state, (("ctx", 0),), 1)
    relay_state = pick_lanes(widened, relay_state[1], at_fold)
    seen.append(relay_state[::-1])
    window_pairs = jnp.concatenate([seen[hop] for hop in range(REACH, -1, -1)], axis=1)
    attended_lanes = []
    dquery_lanes = []
    log_lanes = []
    delta_lanes = []
    partial_lanes = []
    sink_terms = jnp.zeros((KV_HEADS, GROUP), jnp.float32)
    for lane_idx in range(2):
        own_block = lane_block[lane_idx]
        query_pos = own_block * block_rows + row_offsets
        key_pos = (own_block - REACH) * block_rows + window_offsets
        first_pos = bound_lanes[lane_idx, 0]
        query_rows = query_lanes[lane_idx]
        grad_rows = grad_lanes[lane_idx]
        window_keys = window_pairs[lane_idx, :, :value_width]
        window_values = window_pairs[lane_idx, :, value_width:]
        allowed = (key_pos[None, :] <= query_pos[:, None]) & (
            key_pos[None, :] >= first_pos[:, None]
        )
        masked = jnp.where(allowed, block_scores(query_rows, window_keys, score_scale), -jnp.inf)
        row_top = jnp.maximum(sink_col, jnp.max(masked, axis=-1))
        row_total = jnp.exp(sink_col - row_top) + jnp.sum(
            jnp.exp(masked - row_top[..., None]), axis=-1
        )
        log_total = row_top + jnp.log(row_total)
        probs = jnp.exp(masked - log_total[..., None])
        weights = probs.astype(jnp.bfloat16)
        attended = mix_rows(weights, window_values).astype(jnp.bfloat16)
        row_delta = jnp.sum(
            grad_rows.reshape(block_rows, KV_HEADS, GROUP, HEAD_DIM).astype(jnp.float32)
            * attended.reshape(block_rows, KV_HEADS, GROUP, HEAD_DIM).astype(jnp.float32),
            axis=-1,
        )
        delta_cols = jnp.transpose(row_delta, (1, 2, 0))
        sink_terms = sink_terms - jnp.sum(jnp.exp(sink_col - log_total) * delta_cols, axis=-1)
        dprob = grad_scores(grad_rows, window_values)
        dscore = (probs * (dprob - delta_cols[..., None])).astype(jnp.bfloat16)
        dquery = mix_rows(dscore, window_keys)
        key_part = key_side_sum(dscore, query_rows) * score_scale
        value_part = key_side_sum(weights, grad_rows)
        partial_lanes.append(jnp.concatenate([key_part, value_part], axis=1))
        attended_lanes.append(attended)
        dquery_lanes.append((dquery * score_scale).astype(jnp.bfloat16))
        log_lanes.append(log_total.reshape(HEADS, block_rows))
        delta_lanes.append(delta_cols.reshape(HEADS, block_rows))
    partial_all = jnp.stack(partial_lanes)
    gathered = partial_all[:, :block_rows]
    widened = with_halo(gathered, (("ctx", 0),), 1)
    slot = REACH
    gathered = (
        pick_lanes(widened, gathered[1], at_fold)
        + partial_all[:, slot * block_rows : (slot + 1) * block_rows]
    )
    sink_grad = lax.psum(sink_terms.reshape(HEADS), ("ctx", "dp"))
    out_shape = (1, 1, 2, block_rows, query_width)
    pair_out = (1, 1, 2, block_rows, value_width)
    attn_out = jnp.stack(attended_lanes).reshape(out_shape)
    query_grad = jnp.stack(dquery_lanes).reshape(out_shape)
    key_grad = gathered[:, :, :value_width].astype(jnp.bfloat16).reshape(pair_out)
    value_grad = gathered[:, :, value_width:].astype(jnp.bfloat16).reshape(pair_out)
    return (attn_out, query_grad, key_grad, value_grad, sink_grad)


def solution(mesh):
    in_specs = (
        P("dp", "ctx", None, None, None),
        P("dp", "ctx", None, None, None),
        P("dp", "ctx", None, None, None),
        P("dp", "ctx", None, None, None),
        P(),
        P("dp", "ctx", None, None, None),
    )
    out_specs = (
        P("dp", "ctx", None, None, None),
        P("dp", "ctx", None, None, None),
        P("dp", "ctx", None, None, None),
        P("dp", "ctx", None, None, None),
        P(),
    )
    return jax.shard_map(
        per_device, mesh=mesh, in_specs=in_specs, out_specs=out_specs, check_vma=False
    )
```

profile of v0, /device:TPU:8, one launch (start us, length us, event | category | flops | bytes accessed | tf_op | source)
XLA Modules:
  0.0 118.5 jit_solution(2445498028763109154)
XLA Ops:
  0.7 1.2 copy.15
  2.0 0.8 pad_maximum_fusion.2
  2.8 4.2 %collective-permute-start = (bf16[1,64,1024]{1,2,0:T(8,128)(2,1)}, bf16[1,64,1024]{1,2,0:T(8,128)(2,1)S(1)}, u32[]{:S(2)}, u32[]{:S(2)}) collective-permute-start(bf16[1,64,1024]{1,2,0:T(8,128)(2,1)} %pad_maximum_fusion.2), channel_id=1, source_target_pairs={{2,0},{4,2},{6,4},{8,6},{10,8},{12,10},{14,12},{16,14},{18,16},{20... | collective-permute-start | bytes 393224 | tf_op jit(solution)/shard_map/ppermute | solution.py:23
  7.1 0.7 copy-done.10
  7.8 1.1 copy-done.4
  10.2 2.7 %collective-permute-done = bf16[1,64,1024]{1,2,0:T(8,128)(2,1)S(1)} collective-permute-done((bf16[1,64,1024]{1,2,0:T(8,128)(2,1)}, bf16[1,64,1024]{1,2,0:T(8,128)(2,1)S(1)}, u32[]{:S(2)}, u32[]{:S(2)}) %collective-permute-start) | collective-permute-done | bytes 131104 | tf_op jit(solution)/shard_map/ppermute | solution.py:23
  13.0 4.3 %collective-permute-start.1 = (bf16[1,64,1024]{1,2,0:T(8,128)(2,1)S(1)}, bf16[1,64,1024]{1,2,0:T(8,128)(2,1)S(1)}, u32[]{:S(2)}, u32[]{:S(2)}) collective-permute-start(bf16[1,64,1024]{1,2,0:T(8,128)(2,1)S(1)} %get-tuple-element.13), channel_id=1, source_target_pairs={{0,2},{2,4},{4,6},{6,8},{8,10},{10,12},{12,14},{14,16},{16,18},{18... | collective-permute-start | bytes 393224 | tf_op jit(solution)/shard_map/ppermute | solution.py:22
  17.4 7.0 %collective-permute-done.1 = bf16[1,64,1024]{1,2,0:T(8,128)(2,1)S(1)} collective-permute-done((bf16[1,64,1024]{1,2,0:T(8,128)(2,1)S(1)}, bf16[1,64,1024]{1,2,0:T(8,128)(2,1)S(1)}, u32[]{:S(2)}, u32[]{:S(2)}) %collective-permute-start.1) | collective-permute-done | bytes 131104 | tf_op jit(solution)/shard_map/ppermute | solution.py:22
  24.6 0.8 rev.4
  25.4 1.3 %maximum_maximum_fusion = bf16[2,128,1024]{1,2,0:T(8,128)(2,1)S(1)} fusion(bf16[2,64,512]{1,2,0:T(8,128)(2,1)S(1)} %bitcast.167, bf16[2,64,512]{1,2,0:T(8,128)(2,1)S(1)} %bitcast.164, bf16[2,64,1024]{1,2,0:T(8,128)(2,1)} %rev.4), kind=kLoop, calls=%fused_computation.44 | loop fusion | flops 1572864 | bytes 1048576 | tf_op jit(solution)/shard_map/concatenate | solution.py:85
  27.4 0.7 exponential_reduce_fusion.1
  28.7 1.4 %fusion.29 = f32[4,128,128,1]{1,2,3,0:T(8,128)} fusion(bf16[64,4,8,128]{3,2,1,0:T(8,128)(2,1)S(1)} %bitcast.155, f32[4,8,64,128]{3,2,1,0:T(8,128)S(1)} %get-tuple-element.31, f32[4,8,64]{2,1,0:T(8,128)S(1)} %get-tuple-element.26), kind=kOutput, calls=%fused_computation.58 | convolution fusion | flops 67633152 | bytes 1843200 | tf_op jit(solution)/shard_map/kgtu,tkgd->ukd/dot_general | solution.py:56
  30.1 1.3 %multiply_reduce_fusion.1 = (f32[64,4,8]{0,2,1:T(8,128)S(1)}, bf16[64,4,8,128]{3,0,2,1:T(8,128)(2,1)}) fusion(bf16[64,4,8,128]{3,2,1,0:T(8,128)(2,1)S(1)} %bitcast.156, bf16[128,4,128,1]{0,2,3,1:T(8,128)(2,1)S(1)} %bitcast.171, f32[4,8,64,128]{3,2,1,0:T(8,128)S(1)} %get-tuple-element.31, f32[4,8,64]{2,1,0:T(8,128)S(1)} %get-tuple-element.26), kind=kOutput, calls=%fused_computation.34 | convolution fusion | flops 68941824 | bytes 2244608 | tf_op jit(solution)/shard_map/kgtu,ukd->tkgd/dot_general | solution.py:50
  31.4 0.7 fusion.8
  32.1 1.1 fusion.17
  34.3 1.4 %fusion.26 = f32[4,128,128,1]{1,2,3,0:T(8,128)} fusion(bf16[64,4,8,128]{3,2,1,0:T(8,128)(2,1)S(1)} %bitcast.152, f32[4,8,64,128]{3,2,1,0:T(8,128)S(1)} %get-tuple-element.33, f32[4,8,64]{2,1,0:T(8,128)S(1)} %log_add_fusion), kind=kOutput, calls=%fused_computation.55 | convolution fusion | flops 67633152 | bytes 1843200 | tf_op jit(solution)/shard_map/kgtu,tkgd->ukd/dot_general | solution.py:56
  35.6 0.7 multiply_reduce_fusion
  36.3 1.1 copy.24
  37.4 2.1 %convert_element_type.103 = bf16[1,64,4096]{2,1,0:T(8,128)(2,1)} reshape(bf16[64,4,8,128]{3,2,1,0:T(8,128)(2,1)} %copy.24) | data formatting | bytes 1048576 | tf_op jit(solution)/shard_map/convert_element_type | solution.py:112
  39.7 0.7 fusion.9
  41.3 0.8 copy-done
  42.5 1.0 convert_element_type.99
  43.5 39.5 %psum.7 = f32[32]{0:T(128)} all-reduce(f32[32]{0:T(128)S(1)} %sub.122), channel_id=1, replica_groups=mesh['ctx'=16,'dp'=2] {'ctx','dp'}, use_global_device_ids=true, to_apply=%region_8.9 | all-reduce | flops 32 | bytes 256 | tf_op jit(solution)/shard_map/psum | solution.py:138
  83.6 0.7 copy-done.5
  84.4 4.2 %collective-permute-start.2 = (f32[1,64,1024]{1,2,0:T(8,128)S(1)}, f32[1,64,1024]{1,2,0:T(8,128)S(1)}, u32[]{:S(2)}, u32[]{:S(2)}) collective-permute-start(f32[1,64,1024]{1,2,0:T(8,128)S(1)} %bitcast.168), channel_id=1, source_target_pairs={{2,0},{4,2},{6,4},{8,6},{10,8},{12,10},{14,12},{16,14},{18,16},{20... | collective-permute-start | bytes 786440 | tf_op jit(solution)/shard_map/ppermute | solution.py:23
  88.7 1.1 maximum_bitcast_fusion
  90.7 8.8 %collective-permute-done.2 = f32[1,64,1024]{1,2,0:T(8,128)S(1)} collective-permute-done((f32[1,64,1024]{1,2,0:T(8,128)S(1)}, f32[1,64,1024]{1,2,0:T(8,128)S(1)}, u32[]{:S(2)}, u32[]{:S(2)}) %collective-permute-start.2) | collective-permute-done | bytes 262176 | tf_op jit(solution)/shard_map/ppermute | solution.py:23
  99.6 3.7 %collective-permute-start.3 = (f32[1,64,1024]{1,2,0:T(8,128)S(1)}, f32[1,64,1024]{1,2,0:T(8,128)S(1)}, u32[]{:S(2)}, u32[]{:S(2)}) collective-permute-start(f32[1,64,1024]{1,2,0:T(8,128)S(1)} %get-tuple-element.21), channel_id=1, source_target_pairs={{0,2},{2,4},{4,6},{6,8},{8,10},{10,12},{12,14},{14,16},{16,18},{18... | collective-permute-start | bytes 786440 | tf_op jit(solution)/shard_map/ppermute | solution.py:22
  103.3 1.1 maximum_bitcast_fusion.1
  104.4 12.2 %collective-permute-done.3 = f32[1,64,1024]{1,2,0:T(8,128)S(1)} collective-permute-done((f32[1,64,1024]{1,2,0:T(8,128)S(1)}, f32[1,64,1024]{1,2,0:T(8,128)S(1)}, u32[]{:S(2)}, u32[]{:S(2)}) %collective-permute-start.3) | collective-permute-done | bytes 262176 | tf_op jit(solution)/shard_map/ppermute | solution.py:22
  116.9 0.8 copy.40
  117.7 0.8 copy.39
  (57 shorter events, 7.6 us)
Async XLA Ops:
  0.6 1.2 %copy-start.8 = (bf16[1,1,2,64,512]{4,3,2,1,0:T(8,128)(2,1)S(1)}, bf16[1,1,2,64,512]{4,3,2,1,0:T(8,128)(2,1)}, u32[]{:S(2)}) copy-start(bf16[1,1,2,64,512]{4,3,2,1,0:T(8,128)(2,1)} %param.8) | copy-start | bytes 393220
  0.6 7.1 %copy-start.3 = (bf16[1,1,2,64,4096]{4,3,2,1,0:T(8,128)(2,1)S(1)}, bf16[1,1,2,64,4096]{4,3,2,1,0:T(8,128)(2,1)}, u32[]{:S(2)}) copy-start(bf16[1,1,2,64,4096]{4,3,2,1,0:T(8,128)(2,1)} %param.6) | copy-start | bytes 3145732
  2.8 10.1 %collective-permute-start = (bf16[1,64,1024]{1,2,0:T(8,128)(2,1)}, bf16[1,64,1024]{1,2,0:T(8,128)(2,1)S(1)}, u32[]{:S(2)}, u32[]{:S(2)}) collective-permute-start(bf16[1,64,1024]{1,2,0:T(8,128)(2,1)} %pad_maximum_fusion.2), channel_id=1, source_target_pairs={{2,0},{4,2},{6,4},{8,6},{10,8},{12,10},{14,12},{16,14},{18,16},{20... | collective-permute-start | bytes 393224 | tf_op jit(solution)/shard_map/ppermute | solution.py:23
  7.0 0.7 copy-start.10
  7.7 1.2 %copy-start.4 = (bf16[1,1,2,64,4096]{4,3,2,1,0:T(8,128)(2,1)S(1)}, bf16[1,1,2,64,4096]{4,3,2,1,0:T(8,128)(2,1)}, u32[]{:S(2)}) copy-start(bf16[1,1,2,64,4096]{4,3,2,1,0:T(8,128)(2,1)} %param.11) | copy-start | bytes 3145732
  9.1 0.7 copy-start.9
  13.0 11.5 %collective-permute-start.1 = (bf16[1,64,1024]{1,2,0:T(8,128)(2,1)S(1)}, bf16[1,64,1024]{1,2,0:T(8,128)(2,1)S(1)}, u32[]{:S(2)}, u32[]{:S(2)}) collective-permute-start(bf16[1,64,1024]{1,2,0:T(8,128)(2,1)S(1)} %get-tuple-element.13), channel_id=1, source_target_pairs={{0,2},{2,4},{4,6},{6,8},{8,10},{10,12},{12,14},{14,16},{16,18},{18... | collective-permute-start | bytes 393224 | tf_op jit(solution)/shard_map/ppermute | solution.py:22
  41.0 1.0 copy-start
  83.4 1.0 copy-start.5
  83.4 1.0 copy-start.6
  84.4 4.3 %copy-start.1 = (bf16[1,64,4096]{2,1,0:T(8,128)(2,1)S(1)}, bf16[1,64,4096]{2,1,0:T(8,128)(2,1)}, u32[]{:S(2)}) copy-start(bf16[1,64,4096]{2,1,0:T(8,128)(2,1)} %convert_element_type.103) | copy-start | bytes 1572868
  84.4 4.3 %copy-start.2 = (bf16[1,64,4096]{2,1,0:T(8,128)(2,1)S(1)}, bf16[1,64,4096]{2,1,0:T(8,128)(2,1)}, u32[]{:S(2)}) copy-start(bf16[1,64,4096]{2,1,0:T(8,128)(2,1)} %convert_element_type.99) | copy-start | bytes 1572868
  84.4 15.1 %collective-permute-start.2 = (f32[1,64,1024]{1,2,0:T(8,128)S(1)}, f32[1,64,1024]{1,2,0:T(8,128)S(1)}, u32[]{:S(2)}, u32[]{:S(2)}) collective-permute-start(f32[1,64,1024]{1,2,0:T(8,128)S(1)} %bitcast.168), channel_id=1, source_target_pairs={{2,0},{4,2},{6,4},{8,6},{10,8},{12,10},{14,12},{16,14},{18,16},{20... | collective-permute-start | bytes 786440 | tf_op jit(solution)/shard_map/ppermute | solution.py:23
  89.7 0.9 copy-start.7
  99.6 16.9 %collective-permute-start.3 = (f32[1,64,1024]{1,2,0:T(8,128)S(1)}, f32[1,64,1024]{1,2,0:T(8,128)S(1)}, u32[]{:S(2)}, u32[]{:S(2)}) collective-permute-start(f32[1,64,1024]{1,2,0:T(8,128)S(1)} %get-tuple-element.21), channel_id=1, source_target_pairs={{0,2},{2,4},{4,6},{6,8},{8,10},{10,12},{12,14},{14,16},{16,18},{18... | collective-permute-start | bytes 786440 | tf_op jit(solution)/shard_map/ppermute | solution.py:22
where the time goes:
time: 119 us; the launch traced here: 118 us
  blocking collectives  39.5 us (33%)
  waiting for transfers between devices  30.7 us (26%)
  starting transfers between devices  16.4 us (14%)
  local copies, waits for them, and re-layouts  14.8 us (12%)
  matrix products  9.29 us (8%)
  other arithmetic  6.75 us (6%)
    psum x1, blocking collectives, per_device(): sink_grad = lax.psum(sink_terms.reshape(HEADS), ('ctx', 'dp'))  39.5 us
    ppermute x2, waiting for transfers between devices, with_halo(): before = lax.ppermute(last, axis, up)  19.2 us
    ppermute x2, waiting for transfers between devices, with_halo(): after = lax.ppermute(initial, axis, down)  11.5 us
    ppermute x2, starting transfers between devices, with_halo(): after = lax.ppermute(initial, axis, down)  8.44 us
    unnamed x32, local copies, waits for them, and re-layouts  8.03 us
    ppermute x2, starting transfers between devices, with_halo(): before = lax.ppermute(last, axis, up)  7.98 us
    convert_element_type x4, local copies, waits for them, and re-layouts, per_device(): attended = mix_rows(weights, window_values).astype(jnp.bfloat16)  4.55 us
    dot_general x4, matrix products, key_side_sum(): jnp.einsum('kgtu,tkgd->ukd', weights, grouped, preferred_element_type=jnp...  4.3 us
  transfers between devices with their start and end apart: 4, of which 4 were waited for; matrix products, arithmetic and copies ran while one was open for 3% of the time, Pallas kernels for 0%

commit v1 on v0

v1 whole, which is shorter than its diff:
```python
import math

import jax
import jax.numpy as jnp
from jax import lax
from jax.sharding import PartitionSpec as P

HEADS = 32
KV_HEADS = 4
HEAD_DIM = 128
GROUP = 8
REACH = 1


def shift_up(x, axis):
    size = lax.axis_size(axis)
    return lax.ppermute(x, axis, [(i, i + 1) for i in range(size - 1)])


def shift_down(x, axis):
    size = lax.axis_size(axis)
    return lax.ppermute(x, axis, [(i + 1, i) for i in range(size - 1)])


def all_sum(x, axes):
    for axis in axes:
        size = lax.axis_size(axis)
        if size & (size - 1):
            x = lax.psum(x, axis)
            continue
        bit = 1
        while bit < size:
            x = x + lax.ppermute(x, axis, [(i, i ^ bit) for i in range(size)])
            bit *= 2
    return x


def per_device(queries, keys, values, doc_bounds, sink_logit, out_grad):
    block_rows = queries.shape[3]
    query_width = queries.shape[4]
    value_width = keys.shape[4]
    pair_count = lax.axis_size("ctx")
    my_index = lax.axis_index("ctx")
    score_scale = 1.0 / math.sqrt(HEAD_DIM)
    at_fold = my_index == pair_count - 1
    last_block = 2 * pair_count - 1
    span = (REACH + 1) * block_rows

    query_lanes = queries.reshape(2, block_rows, KV_HEADS, GROUP, HEAD_DIM)
    grad_lanes = out_grad.reshape(2, block_rows, KV_HEADS, GROUP, HEAD_DIM)
    own_pair = jnp.concatenate(
        [keys.reshape(2, block_rows, value_width), values.reshape(2, block_rows, value_width)], axis=2
    )
    prev0 = shift_up(own_pair[0], "ctx")
    prev1 = shift_down(own_pair[1], "ctx")
    prev1 = jnp.where(at_fold, own_pair[0], prev1)
    prev_pair = jnp.stack([prev0, prev1])
    window = jnp.concatenate([prev_pair, own_pair], axis=1)
    window_keys = window[:, :, :value_width].reshape(2, span, KV_HEADS, HEAD_DIM)
    window_values = window[:, :, value_width:].reshape(2, span, KV_HEADS, HEAD_DIM)

    lane_block = jnp.stack([my_index, last_block - my_index]).astype(jnp.int32)
    row_offsets = jnp.arange(block_rows, dtype=jnp.int32)
    window_offsets = jnp.arange(span, dtype=jnp.int32)
    query_pos = lane_block[:, None] * block_rows + row_offsets[None, :]
    key_pos = (lane_block[:, None] - REACH) * block_rows + window_offsets[None, :]
    first_pos = doc_bounds.reshape(2, 2, block_rows)[:, 0]
    allowed = (key_pos[:, None, :] <= query_pos[:, :, None]) & (
        key_pos[:, None, :] >= first_pos[:, :, None]
    )
    allowed = allowed[:, None, None]
    sink_col = sink_logit.reshape(1, KV_HEADS, GROUP, 1)

    scores = (
        jnp.einsum(
            "ltkgd,lukd->lkgtu", query_lanes, window_keys, preferred_element_type=jnp.float32
        )
        * score_scale
    )
    masked = jnp.where(allowed, scores, -jnp.inf)
    row_top = jnp.maximum(sink_col, jnp.max(masked, axis=-1))
    row_total = jnp.exp(sink_col - row_top) + jnp.sum(jnp.exp(masked - row_top[..., None]), axis=-1)
    log_total = row_top + jnp.log(row_total)
    probs = jnp.exp(masked - log_total[..., None])
    weights = probs.astype(jnp.bfloat16)
    attended = jnp.einsum(
        "lkgtu,lukd->ltkgd", weights, window_values, preferred_element_type=jnp.float32
    ).astype(jnp.bfloat16)
    row_delta = jnp.sum(grad_lanes.astype(jnp.float32) * attended.astype(jnp.float32), axis=-1)
    delta_cols = jnp.transpose(row_delta, (0, 2, 3, 1))
    sink_terms = -jnp.sum(jnp.exp(sink_col - log_total) * delta_cols, axis=(0, 3))
    sink_grad = all_sum(sink_terms.reshape(HEADS), ("dp", "ctx"))

    dprob = jnp.einsum(
        "ltkgd,lukd->lkgtu", grad_lanes, window_values, preferred_element_type=jnp.float32
    )
    dscore = (probs * (dprob - delta_cols[..., None])).astype(jnp.bfloat16)
    key_part = (
        jnp.einsum("lkgtu,ltkgd->lukd", dscore, query_lanes, preferred_element_type=jnp.float32)
        * score_scale
    )
    value_part = jnp.einsum(
        "lkgtu,ltkgd->lukd", weights, grad_lanes, preferred_element_type=jnp.float32
    )
    partial = jnp.concatenate(
        [key_part.reshape(2, span, value_width), value_part.reshape(2, span, value_width)], axis=2
    )
    dquery = (
        jnp.einsum("lkgtu,lukd->ltkgd", dscore, window_keys, preferred_element_type=jnp.float32)
        * score_scale
    )

    prev_part = partial[:, :block_rows].astype(jnp.bfloat16)
    into0 = shift_down(prev_part[0], "ctx")
    into1 = shift_up(prev_part[1], "ctx")
    into0 = jnp.where(at_fold, prev_part[1], into0)
    own_part = partial[:, block_rows:]
    gathered = own_part + jnp.stack([into0, into1]).astype(jnp.float32)

    out_shape = (1, 1, 2, block_rows, query_width)
    pair_out = (1, 1, 2, block_rows, value_width)
    attn_out = attended.reshape(out_shape)
    query_grad = dquery.astype(jnp.bfloat16).reshape(out_shape)
    key_grad = gathered[:, :, :value_width].astype(jnp.bfloat16).reshape(pair_out)
    value_grad = gathered[:, :, value_width:].astype(jnp.bfloat16).reshape(pair_out)
    return (attn_out, query_grad, key_grad, value_grad, sink_grad)


def solution(mesh):
    in_specs = (
        P("dp", "ctx", None, None, None),
        P("dp", "ctx", None, None, None),
        P("dp", "ctx", None, None, None),
        P("dp", "ctx", None, None, None),
        P(),
        P("dp", "ctx", None, None, None),
    )
    out_specs = (
        P("dp", "ctx", None, None, None),
        P("dp", "ctx", None, None, None),
        P("dp", "ctx", None, None, None),
        P("dp", "ctx", None, None, None),
        P(),
    )
    return jax.shard_map(
        per_device, mesh=mesh, in_specs=in_specs, out_specs=out_specs, check_vma=False
    )
```

time: 119 us -> 65.1 us (0.55)
  the two profiles are of different devices: /device:TPU:8 before, /device:TPU:14 now
where the time goes in v1:
time: 65.1 us; the launch traced here: 64.8 us
  waiting for transfers between devices  24.3 us (37%)
  starting transfers between devices  15.7 us (24%)
  local copies, waits for them, and re-layouts  11.3 us (17%)
  matrix products  7.28 us (11%)
  other arithmetic  5.28 us (8%)
  between operations  0.96 us (1%)
    ppermute x5, waiting for transfers between devices, all_sum(): x = x + lax.ppermute(x, axis, [(i, i ^ bit) for i in range(size)])  10.5 us
    ppermute x2, starting transfers between devices, shift_up(): return lax.ppermute(x, axis, [(i, i + 1) for i in range(size - 1)])  7.43 us
    ppermute x2, waiting for transfers between devices, shift_up(): return lax.ppermute(x, axis, [(i, i + 1) for i in range(size - 1)])  7.03 us
    ppermute x2, waiting for transfers between devices, shift_down(): return lax.ppermute(x, axis, [(i + 1, i) for i in range(size - 1)])  6.83 us
    unnamed x28, local copies, waits for them, and re-layouts  5.63 us
    ppermute x2, starting transfers between devices, shift_down(): return lax.ppermute(x, axis, [(i + 1, i) for i in range(size - 1)])  4.35 us
    ppermute x5, starting transfers between devices, all_sum(): x = x + lax.ppermute(x, axis, [(i, i ^ bit) for i in range(size)])  3.88 us
    dot_general x1, matrix products, per_device(): jnp.einsum('lkgtu,ltkgd->lukd', weights, grad_lanes, preferred_element_ty...  2.03 us
  transfers between devices with their start and end apart: 9, of which 5 were waited for; matrix products, arithmetic and copies ran while one was open for 17% of the time, Pallas kernels for 0%

profile of v1, /device:TPU:14, one launch (start us, length us, event | category | flops | bytes accessed | tf_op | source)
XLA Modules:
  0.0 64.8 jit_solution(7686896844144948364)
XLA Ops:
  0.7 1.2 %copy.15 = bf16[1,1,2,64,512]{3,4,2,1,0:T(8,128)(2,1)S(1)} copy(bf16[1,1,2,64,512]{4,3,2,1,0:T(8,128)(2,1)} %param.7) | data formatting | bytes 262144 | tf_op args[1]
  1.9 1.1 %copy.16 = bf16[1,1,2,64,512]{3,4,2,1,0:T(8,128)(2,1)S(1)} copy(bf16[1,1,2,64,512]{4,3,2,1,0:T(8,128)(2,1)} %param.8) | data formatting | bytes 262144 | tf_op args[2]
  3.0 2.4 %collective-permute-start.1 = (bf16[64,1024]{0,1:T(8,128)(2,1)S(1)}, bf16[64,1024]{0,1:T(8,128)(2,1)S(1)}, u32[]{:S(2)}, u32[]{:S(2)}) collective-permute-start(bf16[64,1024]{0,1:T(8,128)(2,1)S(1)} %fusion.17), channel_id=1, source_target_pairs={{2,0},{4,2},{6,4},{8,6},{10,8},{12,10},{14,12},{16,14},{18,16},{20... | collective-permute-start | bytes 393224 | tf_op jit(solution)/shard_map/ppermute | solution.py:22
  5.6 0.7 %slice.51 = s32[2,1,64]{2,1,0:T(1,128)S(1)} slice(s32[2,2,64]{2,1,0:T(2,128)} %bitcast.111), slice={[0:2], [0:1], [0:64]} | slice | bytes 1024 | tf_op jit(solution)/shard_map/slice | solution.py:67
  6.3 1.2 %copy.44 = bf16[16,8,32,128]{3,2,1,0:T(8,128)(2,1)} copy(bf16[16,8,32,128]{3,1,2,0:T(8,128)(2,1)S(1)} %bitcast.106) | data formatting | bytes 2097152
  7.9 6.8 %collective-permute-done.1 = bf16[64,1024]{0,1:T(8,128)(2,1)S(1)} collective-permute-done((bf16[64,1024]{0,1:T(8,128)(2,1)S(1)}, bf16[64,1024]{0,1:T(8,128)(2,1)S(1)}, u32[]{:S(2)}, u32[]{:S(2)}) %collective-permute-start.1) | collective-permute-done | bytes 131104 | tf_op jit(solution)/shard_map/ppermute | solution.py:22
  14.9 1.9 %collective-permute-start = (bf16[64,1024]{0,1:T(8,128)(2,1)S(1)}, bf16[64,1024]{0,1:T(8,128)(2,1)S(1)}, u32[]{:S(2)}, u32[]{:S(2)}) collective-permute-start(bf16[64,1024]{0,1:T(8,128)(2,1)S(1)} %get-tuple-element.11), channel_id=1, source_target_pairs={{0,2},{2,4},{4,6},{6,8},{8,10},{10,12},{12,14},{14,16},{16,18},{18... | collective-permute-start | bytes 393224 | tf_op jit(solution)/shard_map/ppermute | solution.py:17
  16.9 7.0 %collective-permute-done = bf16[64,1024]{0,1:T(8,128)(2,1)S(1)} collective-permute-done((bf16[64,1024]{0,1:T(8,128)(2,1)S(1)}, bf16[64,1024]{0,1:T(8,128)(2,1)S(1)}, u32[]{:S(2)}, u32[]{:S(2)}) %collective-permute-start) | collective-permute-done | bytes 131104 | tf_op jit(solution)/shard_map/ppermute | solution.py:17
  24.3 0.9 %fusion.22 = (f32[2,4,8,64]{3,2,1,0:T(8,128)S(1)}, f32[2,4,8,64,128]{4,3,2,1,0:T(8,128)S(1)}) fusion(bf16[2,128,4,128,1]{1,3,4,2,0:T(8,128)(2,1)S(1)} %bitcast.104, bf16[2,64,4,8,128]{4,3,2,1,0:T(8,128)(2,1)S(1)} %bitcast.90, pred[2,64,128]{2,1,0:T(8,128)(4,1)S(1)} %compare_and_fusion), kind=kOutput, calls=%fused_computation.49 | convolution fusion | flops 135786496 | bytes 3440640 | tf_op jit(solution)/shard_map/ltkgd,lukd->lkgtu/dot_general | solution.py:75
  25.2 1.3 %exponential_reduce_fusion = f32[2,4,8,64]{3,2,1,0:T(8,128)S(1)} fusion(f32[2,4,8,64,128]{4,3,2,1,0:T(8,128)S(1)} %get-tuple-element.19, f32[2,4,8,64]{3,2,1,0:T(8,128)S(1)} %broadcast_maximum_fusion), kind=kLoop, calls=%fused_computation.7 | loop fusion | flops 1044480 | bytes 2129920 | tf_op jit(solution)/shard_map/reduce_sum | solution.py:82
  26.7 2.0 %fusion.12 = f32[2,4,128,128,1]{2,3,4,1,0:T(8,128)} fusion(bf16[2,64,4,8,128]{4,3,2,1,0:T(8,128)(2,1)S(1)} %bitcast.87, f32[2,4,8,64,128]{4,3,2,1,0:T(8,128)S(1)} %get-tuple-element.19, f32[2,4,8,64]{3,2,1,0:T(8,128)S(1)} %log_add_fusion), kind=kOutput, calls=%fused_computation.23 | convolution fusion | flops 135266304 | bytes 3686400 | tf_op jit(solution)/shard_map/lkgtu,ltkgd->lukd/dot_general | solution.py:102
  28.7 2.0 %multiply_reduce_fusion = (f32[2,64,4,8]{1,3,2,0:T(8,128)S(1)}, bf16[2,64,4,8,128]{4,1,3,2,0:T(8,128)(2,1)}) fusion(bf16[2,64,4,8,128]{4,3,2,1,0:T(8,128)(2,1)S(1)} %bitcast.88, bf16[2,128,4,128,1]{1,3,4,2,0:T(8,128)(2,1)S(1)} %bitcast.102, f32[2,4,8,64,128]{4,3,2,1,0:T(8,128)S(1)} %get-tuple-element.19, f32[2,4,8,64]{3,2,1,0:T(8,128)S(1)} %log_add_fusion), kind=kOutput, calls=%fused_computation.5 | convolution fusion | flops 137883648 | bytes 4489216 | tf_op jit(solution)/shard_map/lkgtu,lukd->ltkgd/dot_general | solution.py:86
  30.9 1.3 %fusion.1 = bf16[2,4,8,64,128]{4,3,2,1,0:T(8,128)(2,1)S(1)} fusion(f32[2,4,8,64,128]{4,3,2,1,0:T(8,128)S(1)} %get-tuple-element.19, bf16[2,128,4,128,1]{1,3,4,2,0:T(8,128)(2,1)S(1)} %bitcast.103, f32[2,4,8,64]{3,2,1,0:T(8,128)S(1)} %bitcast.108, f32[2,4,8,64]{3,2,1,0:T(8,128)S(1)} %log_add_fusion, bf16[2,64,4,8,128]{4,3,2,1,0:T(8,128)(2,1)S(1)} %bitcast.89), kind=kOutput, calls=%fused_computation.2 | convolution fusion | flops 136314880 | bytes 4489216 | tf_op jit(solution)/shard_map/ltkgd,lukd->lkgtu/dot_general | solution.py:94
  32.2 0.7 %fusion.5 = f32[2,4,128,128]{2,3,1,0:T(8,128)S(1)} fusion(bf16[2,4,8,64,128]{4,3,2,1,0:T(8,128)(2,1)S(1)} %fusion.1, bf16[2,64,4,8,128]{4,3,2,1,0:T(8,128)(2,1)S(1)} %bitcast.91), kind=kOutput, calls=%fused_computation.16 | convolution fusion | flops 134348800 | bytes 2621440 | tf_op jit(solution)/shard_map/lkgtu,ltkgd->lukd/dot_general | solution.py:99
  33.3 0.8 %slice_bitcast_fusion.2 = (bf16[64,1024]{0,1:T(8,128)(2,1)}, bf16[64,1024]{0,1:T(8,128)(2,1)S(1)}) fusion(bf16[2,128,1024]{1,2,0:T(8,128)(2,1)S(1)} %fusion.9), kind=kLoop, calls=%fused_computation.33 | loop fusion | bytes 524288 | tf_op jit(solution)/shard_map/squeeze | solution.py:114
  34.1 1.9 %collective-permute-start.2 = (bf16[64,1024]{0,1:T(8,128)(2,1)}, bf16[64,1024]{0,1:T(8,128)(2,1)}, u32[]{:S(2)}, u32[]{:S(2)}) collective-permute-start(bf16[64,1024]{0,1:T(8,128)(2,1)} %get-tuple-element.14), channel_id=1, source_target_pairs={{2,0},{4,2},{6,4},{8,6},{10,8},{12,10},{14,12},{16,14},{18,16},{20... | collective-permute-start | bytes 393224 | tf_op jit(solution)/shard_map/ppermute | solution.py:22
  36.1 1.1 %collective-permute-start.5 = (f32[32]{0:T(128)S(1)}, f32[32]{0:T(128)S(1)}, u32[]{:S(2)}, u32[]{:S(2)}) collective-permute-start(f32[32]{0:T(128)S(1)} %add.81), channel_id=1, source_target_pairs={{0,2},{2,0},{4,6},{6,4},{8,10},{10,8},{12,14},{14,12},{16,18},{18,... | collective-permute-start | bytes 392 | tf_op jit(solution)/shard_map/ppermute | solution.py:33
  37.7 6.3 %collective-permute-done.5 = f32[32]{0:T(128)S(1)} collective-permute-done((f32[32]{0:T(128)S(1)}, f32[32]{0:T(128)S(1)}, u32[]{:S(2)}, u32[]{:S(2)}) %collective-permute-start.5) | collective-permute-done | bytes 160 | tf_op jit(solution)/shard_map/ppermute | solution.py:33
  44.2 5.5 %collective-permute-start.3 = (bf16[64,1024]{0,1:T(8,128)(2,1)S(1)}, bf16[64,1024]{0,1:T(8,128)(2,1)}, u32[]{:S(2)}, u32[]{:S(2)}) collective-permute-start(bf16[64,1024]{0,1:T(8,128)(2,1)S(1)} %get-tuple-element.15), channel_id=1, source_target_pairs={{0,2},{2,4},{4,6},{6,8},{8,10},{10,12},{12,14},{14,16},{16,18},{18... | collective-permute-start | bytes 393224 | tf_op jit(solution)/shard_map/ppermute | solution.py:17
  49.7 0.5 collective-permute-start.7
  50.3 0.7 %copy.25 = bf16[2,64,4,8,128]{4,3,2,1,0:T(8,128)(2,1)S(1)} copy(bf16[2,64,4,8,128]{4,1,3,2,0:T(8,128)(2,1)S(1)} %fusion.4) | data formatting | bytes 2097152 | tf_op jit(solution)/shard_map/convert_element_type | solution.py:123
  50.9 1.3 %reshape.154 = bf16[1,1,2,64,4096]{4,3,2,1,0:T(8,128)(2,1)} reshape(bf16[2,64,4,8,128]{4,3,2,1,0:T(8,128)(2,1)S(1)} %copy.25) | data formatting | bytes 2097152 | tf_op jit(solution)/shard_map/reshape | solution.py:123
  52.2 3.7 %collective-permute-done.7 = f32[32]{0:T(128)S(1)} collective-permute-done((f32[32]{0:T(128)S(1)}, f32[32]{0:T(128)S(1)}, u32[]{:S(2)}, u32[]{:S(2)}) %collective-permute-start.7) | collective-permute-done | bytes 160 | tf_op jit(solution)/shard_map/ppermute | solution.py:33
  55.9 2.0 %collective-permute-start.8 = (f32[32]{0:T(128)S(1)}, f32[32]{0:T(128)S(1)}, u32[]{:S(2)}, u32[]{:S(2)}) collective-permute-start(f32[32]{0:T(128)S(1)} %add.84), channel_id=1, source_target_pairs={{0,16},{2,18},{4,20},{6,22},{8,24},{10,26},{12,28},{14,30},{16,0},... | collective-permute-start | bytes 392 | tf_op jit(solution)/shard_map/ppermute | solution.py:33
  57.9 0.7 %copy.20 = bf16[2,64,4,8,128]{4,3,2,1,0:T(8,128)(2,1)S(1)} copy(bf16[2,64,4,8,128]{4,1,3,2,0:T(8,128)(2,1)S(1)} %copy-done.3) | data formatting | bytes 2097152 | tf_op jit(solution)/shard_map/convert_element_type | solution.py:88
  58.6 1.3 %reshape.152 = bf16[1,1,2,64,4096]{4,3,2,1,0:T(8,128)(2,1)} reshape(bf16[2,64,4,8,128]{4,3,2,1,0:T(8,128)(2,1)S(1)} %copy.20) | data formatting | bytes 2097152 | tf_op jit(solution)/shard_map/reshape | solution.py:122
  59.9 0.5 collective-permute-done.8
  60.4 0.5 add.85
  60.9 1.0 %select_bitcast_fusion = bf16[1,64,1024]{1,2,0:T(8,128)(2,1)S(1)} fusion(bf16[64,1024]{0,1:T(8,128)(2,1)} %collective-permute-done.2, pred[]{:T(512)S(6)} %eq.3, bf16[2,128,1024]{1,2,0:T(8,128)(2,1)S(1)} %copy-done.5), kind=kLoop, calls=%fused_computation.37 | loop fusion | flops 65536 | bytes 393217 | tf_op jit(solution)/shard_map/stack | solution.py:118
  61.9 1.3 %fusion.8 = bf16[2,64,1024]{1,2,0:T(8,128)(2,1)S(1)} fusion(f32[2,128,512]{1,2,0:T(8,128)S(1)} %bitcast.95, f32[2,128,512]{1,2,0:T(8,128)S(1)} %bitcast.93, bf16[1,64,1024]{1,2,0:T(8,128)(2,1)} %bitcast.32, bf16[1,64,1024]{1,2,0:T(8,128)(2,1)S(1)} %select_bitcast_fusion), kind=kLoop, calls=%fused_computation.19 | loop fusion | flops 655360 | bytes 1572864 | tf_op jit(solution)/shard_map/convert.1
  63.2 0.8 %copy.28 = bf16[1,1,2,64,512]{4,3,2,1,0:T(8,128)(2,1)} copy(bf16[1,1,2,64,512]{3,4,2,1,0:T(8,128)(2,1)S(1)} %get-tuple-element.13) | data formatting | bytes 262144
  64.0 0.8 %copy.29 = bf16[1,1,2,64,512]{4,3,2,1,0:T(8,128)(2,1)} copy(bf16[1,1,2,64,512]{3,4,2,1,0:T(8,128)(2,1)S(1)} %get-tuple-element.12) | data formatting | bytes 262144
  (50 shorter events, 2.7 us)
Async XLA Ops:
  0.6 5.7 %copy-start.8 = (bf16[1,1,2,64,4096]{4,3,2,1,0:T(8,128)(2,1)S(1)}, bf16[1,1,2,64,4096]{4,3,2,1,0:T(8,128)(2,1)}, u32[]{:S(2)}) copy-start(bf16[1,1,2,64,4096]{4,3,2,1,0:T(8,128)(2,1)} %param.6) | copy-start | bytes 3145732
  0.6 6.9 %copy-start.10 = (f32[32]{0:T(128)S(1)}, f32[32]{0:T(128)}, u32[]{:S(2)}) copy-start(f32[32]{0:T(128)} %param.10) | copy-start | bytes 388
  0.7 7.0 %copy-start.9 = (bf16[1,1,2,64,4096]{4,3,2,1,0:T(8,128)(2,1)S(1)}, bf16[1,1,2,64,4096]{4,3,2,1,0:T(8,128)(2,1)}, u32[]{:S(2)}) copy-start(bf16[1,1,2,64,4096]{4,3,2,1,0:T(8,128)(2,1)} %param.11) | copy-start | bytes 3145732
  3.0 11.7 %collective-permute-start.1 = (bf16[64,1024]{0,1:T(8,128)(2,1)S(1)}, bf16[64,1024]{0,1:T(8,128)(2,1)S(1)}, u32[]{:S(2)}, u32[]{:S(2)}) collective-permute-start(bf16[64,1024]{0,1:T(8,128)(2,1)S(1)} %fusion.17), channel_id=1, source_target_pairs={{2,0},{4,2},{6,4},{8,6},{10,8},{12,10},{14,12},{16,14},{18,16},{20... | collective-permute-start | bytes 393224 | tf_op jit(solution)/shard_map/ppermute | solution.py:22
  7.9 16.4 %copy-start = (bf16[16,8,32,128]{3,2,1,0:T(8,128)(2,1)S(1)}, bf16[16,8,32,128]{3,2,1,0:T(8,128)(2,1)}, u32[]{:S(2)}) copy-start(bf16[16,8,32,128]{3,2,1,0:T(8,128)(2,1)} %copy.44) | copy-start | bytes 3145732
  14.9 9.1 %collective-permute-start = (bf16[64,1024]{0,1:T(8,128)(2,1)S(1)}, bf16[64,1024]{0,1:T(8,128)(2,1)S(1)}, u32[]{:S(2)}, u32[]{:S(2)}) collective-permute-start(bf16[64,1024]{0,1:T(8,128)(2,1)S(1)} %get-tuple-element.11), channel_id=1, source_target_pairs={{0,2},{2,4},{4,6},{6,8},{8,10},{10,12},{12,14},{14,16},{16,18},{18... | collective-permute-start | bytes 393224 | tf_op jit(solution)/shard_map/ppermute | solution.py:17
  24.3 2.3 %copy-start.6 = (bf16[2,128,512]{1,2,0:T(8,128)(2,1)}, bf16[2,128,512]{1,2,0:T(8,128)(2,1)S(1)}, u32[]{:S(2)}) copy-start(bf16[2,128,512]{1,2,0:T(8,128)(2,1)S(1)} %get-tuple-element.16) | copy-start | bytes 786436
  30.9 5.1 %collective-permute-start.4 = (f32[32]{0:T(128)S(1)}, f32[32]{0:T(128)S(1)}, u32[]{:S(2)}, u32[]{:S(2)}) collective-permute-start(f32[32]{0:T(128)S(1)} %neg.8), channel_id=1, source_target_pairs={{0,1},{1,0},{2,3},{3,2},{4,5},{5,4},{6,7},{7,6},{8,9},{9,8},{10,11... | collective-permute-start | bytes 392 | tf_op jit(solution)/shard_map/ppermute | solution.py:33
  30.9 1.3 %copy-start.1 = (bf16[16,8,32,128]{3,2,1,0:T(8,128)(2,1)S(1)}, bf16[16,8,32,128]{3,2,1,0:T(8,128)(2,1)}, u32[]{:S(2)}) copy-start(bf16[16,8,32,128]{3,2,1,0:T(8,128)(2,1)} %copy.44) | copy-start | bytes 3145732
  32.2 1.0 %copy-start.2 = (f32[2,4,128,128,1]{2,3,4,1,0:T(8,128)S(1)}, f32[2,4,128,128,1]{2,3,4,1,0:T(8,128)}, u32[]{:S(2)}) copy-start(f32[2,4,128,128,1]{2,3,4,1,0:T(8,128)} %fusion.12) | copy-start | bytes 1572868
  32.2 5.0 %copy-start.7 = (bf16[2,128,512]{1,2,0:T(8,128)(2,1)S(1)}, bf16[2,128,512]{1,2,0:T(8,128)(2,1)}, u32[]{:S(2)}) copy-start(bf16[2,128,512]{1,2,0:T(8,128)(2,1)} %copy-done.6) | copy-start | bytes 786436
  33.3 2.8 %copy-start.4 = (bf16[2,128,1024]{1,2,0:T(8,128)(2,1)}, bf16[2,128,1024]{1,2,0:T(8,128)(2,1)S(1)}, u32[]{:S(2)}) copy-start(bf16[2,128,1024]{1,2,0:T(8,128)(2,1)S(1)} %fusion.9) | copy-start | bytes 1572868
  34.1 26.8 %collective-permute-start.2 = (bf16[64,1024]{0,1:T(8,128)(2,1)}, bf16[64,1024]{0,1:T(8,128)(2,1)}, u32[]{:S(2)}, u32[]{:S(2)}) collective-permute-start(bf16[64,1024]{0,1:T(8,128)(2,1)} %get-tuple-element.14), channel_id=1, source_target_pairs={{2,0},{4,2},{6,4},{8,6},{10,8},{12,10},{14,12},{16,14},{18,16},{20... | collective-permute-start | bytes 393224 | tf_op jit(solution)/shard_map/ppermute | solution.py:22
  36.1 7.9 %collective-permute-start.5 = (f32[32]{0:T(128)S(1)}, f32[32]{0:T(128)S(1)}, u32[]{:S(2)}, u32[]{:S(2)}) collective-permute-start(f32[32]{0:T(128)S(1)} %add.81), channel_id=1, source_target_pairs={{0,2},{2,0},{4,6},{6,4},{8,10},{10,8},{12,14},{14,12},{16,18},{18,... | collective-permute-start | bytes 392 | tf_op jit(solution)/shard_map/ppermute | solution.py:33
  44.0 5.8 %collective-permute-start.6 = (f32[32]{0:T(128)S(1)}, f32[32]{0:T(128)S(1)}, u32[]{:S(2)}, u32[]{:S(2)}) collective-permute-start(f32[32]{0:T(128)S(1)} %add.82), channel_id=1, source_target_pairs={{0,4},{2,6},{4,0},{6,2},{8,12},{10,14},{12,8},{14,10},{16,20},{18,... | collective-permute-start | bytes 392 | tf_op jit(solution)/shard_map/ppermute | solution.py:33
  44.2 17.7 %collective-permute-start.3 = (bf16[64,1024]{0,1:T(8,128)(2,1)S(1)}, bf16[64,1024]{0,1:T(8,128)(2,1)}, u32[]{:S(2)}, u32[]{:S(2)}) collective-permute-start(bf16[64,1024]{0,1:T(8,128)(2,1)S(1)} %get-tuple-element.15), channel_id=1, source_target_pairs={{0,2},{2,4},{4,6},{6,8},{8,10},{10,12},{12,14},{14,16},{16,18},{18... | collective-permute-start | bytes 393224 | tf_op jit(solution)/shard_map/ppermute | solution.py:17
  49.7 8.2 %copy-start.3 = (bf16[2,64,4,8,128]{4,1,3,2,0:T(8,128)(2,1)S(1)}, bf16[2,64,4,8,128]{4,1,3,2,0:T(8,128)(2,1)}, u32[]{:S(2)}) copy-start(bf16[2,64,4,8,128]{4,1,3,2,0:T(8,128)(2,1)} %get-tuple-element.21) | copy-start | bytes 3145732
  49.7 6.2 %collective-permute-start.7 = (f32[32]{0:T(128)S(1)}, f32[32]{0:T(128)S(1)}, u32[]{:S(2)}, u32[]{:S(2)}) collective-permute-start(f32[32]{0:T(128)S(1)} %add.83), channel_id=1, source_target_pairs={{0,8},{2,10},{4,12},{6,14},{8,0},{10,2},{12,4},{14,6},{16,24},{18,... | collective-permute-start | bytes 392 | tf_op jit(solution)/shard_map/ppermute | solution.py:33
  55.9 4.4 %collective-permute-start.8 = (f32[32]{0:T(128)S(1)}, f32[32]{0:T(128)S(1)}, u32[]{:S(2)}, u32[]{:S(2)}) collective-permute-start(f32[32]{0:T(128)S(1)} %add.84), channel_id=1, source_target_pairs={{0,16},{2,18},{4,20},{6,22},{8,24},{10,26},{12,28},{14,30},{16,0},... | collective-permute-start | bytes 392 | tf_op jit(solution)/shard_map/ppermute | solution.py:33
  58.6 2.3 %copy-start.5 = (bf16[2,128,1024]{1,2,0:T(8,128)(2,1)S(1)}, bf16[2,128,1024]{1,2,0:T(8,128)(2,1)}, u32[]{:S(2)}) copy-start(bf16[2,128,1024]{1,2,0:T(8,128)(2,1)} %copy-done.4) | copy-start | bytes 1572868

commit v2 on v1

--- a/solution.py
+++ b/solution.py
@@ -23,16 +23,11 @@
 
 
 def all_sum(x, axes):
+    count = 1
     for axis in axes:
-        size = lax.axis_size(axis)
-        if size & (size - 1):
-            x = lax.psum(x, axis)
-            continue
-        bit = 1
-        while bit < size:
-            x = x + lax.ppermute(x, axis, [(i, i ^ bit) for i in range(size)])
-            bit *= 2
-    return x
+        count *= lax.axis_size(axis)
+    spread = jnp.broadcast_to(x[None], (count,) + x.shape)
+    return jnp.sum(lax.all_to_all(spread, axes, 0, 0, tiled=True), axis=0)
 
 
 def per_device(queries, keys, values, doc_bounds, sink_logit, out_grad):
@@ -51,8 +46,9 @@
     own_pair = jnp.concatenate(
         [keys.reshape(2, block_rows, value_width), values.reshape(2, block_rows, value_width)], axis=2
     )
-    prev0 = shift_up(own_pair[0], "ctx")
-    prev1 = shift_down(own_pair[1], "ctx")
+    send0, send1 = lax.optimization_barrier((own_pair[0], own_pair[1]))
+    prev0 = shift_up(send0, "ctx")
+    prev1 = shift_down(send1, "ctx")
     prev1 = jnp.where(at_fold, own_pair[0], prev1)
     prev_pair = jnp.stack([prev0, prev1])
     window = jnp.concatenate([prev_pair, own_pair], axis=1)
@@ -89,7 +85,7 @@
     row_delta = jnp.sum(grad_lanes.astype(jnp.float32) * attended.astype(jnp.float32), axis=-1)
     delta_cols = jnp.transpose(row_delta, (0, 2, 3, 1))
     sink_terms = -jnp.sum(jnp.exp(sink_col - log_total) * delta_cols, axis=(0, 3))
-    sink_grad = all_sum(sink_terms.reshape(HEADS), ("dp", "ctx"))
+    sink_grad = all_sum(sink_terms.reshape(HEADS), ("ctx", "dp"))
 
     dprob = jnp.einsum(
         "ltkgd,lukd->lkgtu", grad_lanes, window_values, preferred_element_type=jnp.float32
@@ -111,8 +107,9 @@
     )
 
     prev_part = partial[:, :block_rows].astype(jnp.bfloat16)
-    into0 = shift_down(prev_part[0], "ctx")
-    into1 = shift_up(prev_part[1], "ctx")
+    send0, send1 = lax.optimization_barrier((prev_part[0], prev_part[1]))
+    into0 = shift_down(send0, "ctx")
+    into1 = shift_up(send1, "ctx")
     into0 = jnp.where(at_fold, prev_part[1], into0)
     own_part = partial[:, block_rows:]
     gathered = own_part + jnp.stack([into0, into1]).astype(jnp.float32)

time: 65.1 us -> 60 us (0.922)
  the two profiles are of different devices: /device:TPU:14 before, /device:TPU:8 now
where the time goes in v2:
time: 60 us; the launch traced here: 59.6 us
  starting transfers between devices  18.9 us (31%)
  waiting for transfers between devices  13.9 us (23%)
  local copies, waits for them, and re-layouts  13.3 us (22%)
  matrix products  7.26 us (12%)
  other arithmetic  5.27 us (9%)
  between operations  0.96 us (2%)
    ppermute x2, starting transfers between devices, shift_down(): return lax.ppermute(x, axis, [(i + 1, i) for i in range(size - 1)])  8.5 us
    ppermute x2, waiting for transfers between devices, shift_up(): return lax.ppermute(x, axis, [(i, i + 1) for i in range(size - 1)])  8.31 us
    unnamed x32, local copies, waits for them, and re-layouts  6.36 us
    ppermute x2, waiting for transfers between devices, shift_down(): return lax.ppermute(x, axis, [(i + 1, i) for i in range(size - 1)])  5.63 us
    ppermute x2, starting transfers between devices, shift_up(): return lax.ppermute(x, axis, [(i, i + 1) for i in range(size - 1)])  5.31 us
    all_to_all x1, starting transfers between devices, all_sum(): return jnp.sum(lax.all_to_all(spread, axes, 0, 0, tiled=True), axis=0)  5.09 us
    dot_general x1, matrix products, per_device(): jnp.einsum('lkgtu,ltkgd->lukd', weights, grad_lanes, preferred_element_ty...  2.02 us
    dot_general x1, matrix products, per_device(): jnp.einsum('lkgtu,lukd->ltkgd', weights, window_values, preferred_element...  1.96 us
  transfers between devices with their start and end apart: 5, of which 2 were waited for; matrix products, arithmetic and copies ran while one was open for 17% of the time, Pallas kernels for 0%

profile of v2, /device:TPU:8, one launch (start us, length us, event | category | flops | bytes accessed | tf_op | source)
XLA Modules:
  0.0 59.6 jit_solution(13441847451417471963)
XLA Ops:
  0.6 1.2 %copy.45 = bf16[1,1,2,64,512]{3,4,2,1,0:T(8,128)(2,1)S(1)} copy(bf16[1,1,2,64,512]{4,3,2,1,0:T(8,128)(2,1)} %param.7) | data formatting | bytes 262144 | tf_op args[1]
  1.8 1.1 %copy.46 = bf16[1,1,2,64,512]{3,4,2,1,0:T(8,128)(2,1)S(1)} copy(bf16[1,1,2,64,512]{4,3,2,1,0:T(8,128)(2,1)} %param.8) | data formatting | bytes 262144 | tf_op args[2]
  3.0 3.4 %collective-permute-start = (bf16[64,1024]{0,1:T(8,128)(2,1)S(1)}, bf16[64,1024]{0,1:T(8,128)(2,1)S(1)}, u32[]{:S(2)}, u32[]{:S(2)}) collective-permute-start(bf16[64,1024]{0,1:T(8,128)(2,1)S(1)} %get-tuple-element.9), channel_id=1, source_target_pairs={{0,2},{2,4},{4,6},{6,8},{8,10},{10,12},{12,14},{14,16},{16,18},{18... | collective-permute-start | bytes 393224 | tf_op jit(solution)/shard_map/ppermute | solution.py:17
  6.4 4.2 %collective-permute-start.1 = (bf16[64,1024]{0,1:T(8,128)(2,1)S(1)}, bf16[64,1024]{0,1:T(8,128)(2,1)}, u32[]{:S(2)}, u32[]{:S(2)}) collective-permute-start(bf16[64,1024]{0,1:T(8,128)(2,1)S(1)} %get-tuple-element.10), channel_id=1, source_target_pairs={{2,0},{4,2},{6,4},{8,6},{10,8},{12,10},{14,12},{16,14},{18,16},{20... | collective-permute-start | bytes 393224 | tf_op jit(solution)/shard_map/ppermute | solution.py:22
  10.9 0.7 %slice.51 = s32[2,1,64]{2,1,0:T(1,128)S(1)} slice(s32[2,2,64]{2,1,0:T(2,128)} %bitcast.111), slice={[0:2], [0:1], [0:64]} | slice | bytes 1024 | tf_op jit(solution)/shard_map/slice | solution.py:63
  11.6 0.7 %max.17 = f32[4,8]{1,0:T(4,128)S(1)} reshape(f32[32]{0:T(128)} %param.10) | data formatting | bytes 256 | tf_op jit(solution)/shard_map/max | solution.py:77
  12.6 1.1 %copy-done.11 = bf16[1,1,2,64,4096]{4,3,2,1,0:T(8,128)(2,1)S(1)} copy-done((bf16[1,1,2,64,4096]{4,3,2,1,0:T(8,128)(2,1)S(1)}, bf16[1,1,2,64,4096]{4,3,2,1,0:T(8,128)(2,1)}, u32[]{:S(2)}) %copy-start.11) | copy-done | bytes 1048600
  14.0 5.6 %collective-permute-done.1 = bf16[64,1024]{0,1:T(8,128)(2,1)} collective-permute-done((bf16[64,1024]{0,1:T(8,128)(2,1)S(1)}, bf16[64,1024]{0,1:T(8,128)(2,1)}, u32[]{:S(2)}, u32[]{:S(2)}) %collective-permute-start.1) | collective-permute-done | bytes 131104 | tf_op jit(solution)/shard_map/ppermute | solution.py:22
  19.6 1.0 %select_bitcast_fusion.1 = bf16[1,64,1024]{1,2,0:T(8,128)(2,1)S(1)} fusion(bf16[64,1024]{0,1:T(8,128)(2,1)S(1)} %get-tuple-element.9, bf16[64,1024]{0,1:T(8,128)(2,1)} %collective-permute-done.1, pred[]{:T(512)S(6)} %eq.3), kind=kLoop, calls=%fused_computation.38 | loop fusion | flops 65536 | bytes 393217 | tf_op jit(solution)/shard_map/stack | solution.py:53
  21.0 0.9 %fusion.21 = (f32[2,4,8,64]{3,2,1,0:T(8,128)S(1)}, f32[2,4,8,64,128]{4,3,2,1,0:T(8,128)S(1)}) fusion(bf16[2,128,4,128,1]{1,3,4,2,0:T(8,128)(2,1)S(1)} %bitcast.102, bf16[2,64,4,8,128]{4,3,2,1,0:T(8,128)(2,1)S(1)} %bitcast.90, pred[2,64,128]{2,1,0:T(8,128)(4,1)S(1)} %compare_and_fusion), kind=kOutput, calls=%fused_computation.49 | convolution fusion | flops 135786496 | bytes 3440640 | tf_op jit(solution)/shard_map/ltkgd,lukd->lkgtu/dot_general | solution.py:71
  21.9 1.3 %exponential_reduce_fusion = f32[2,4,8,64]{3,2,1,0:T(8,128)S(1)} fusion(f32[2,4,8,64,128]{4,3,2,1,0:T(8,128)S(1)} %get-tuple-element.37, f32[2,4,8,64]{3,2,1,0:T(8,128)S(1)} %broadcast_maximum_fusion), kind=kLoop, calls=%fused_computation.7 | loop fusion | flops 1044480 | bytes 2129920 | tf_op jit(solution)/shard_map/reduce_sum | solution.py:78
  23.3 2.0 %fusion.12 = f32[2,4,128,128,1]{2,3,4,1,0:T(8,128)} fusion(bf16[2,64,4,8,128]{4,3,2,1,0:T(8,128)(2,1)S(1)} %bitcast.87, f32[2,4,8,64,128]{4,3,2,1,0:T(8,128)S(1)} %get-tuple-element.37, f32[2,4,8,64]{3,2,1,0:T(8,128)S(1)} %log_add_fusion), kind=kOutput, calls=%fused_computation.23 | convolution fusion | flops 135266304 | bytes 3686400 | tf_op jit(solution)/shard_map/lkgtu,ltkgd->lukd/dot_general | solution.py:98
  25.4 2.0 %multiply_reduce_fusion = (f32[2,64,4,8]{1,3,2,0:T(8,128)S(1)}, bf16[2,64,4,8,128]{4,1,3,2,0:T(8,128)(2,1)}) fusion(bf16[2,64,4,8,128]{4,3,2,1,0:T(8,128)(2,1)S(1)} %bitcast.88, bf16[2,128,4,128,1]{1,3,4,2,0:T(8,128)(2,1)S(1)} %bitcast.96, f32[2,4,8,64,128]{4,3,2,1,0:T(8,128)S(1)} %get-tuple-element.37, f32[2,4,8,64]{3,2,1,0:T(8,128)S(1)} %log_add_fusion), kind=kOutput, calls=%fused_computation.5 | convolution fusion | flops 137883648 | bytes 4489216 | tf_op jit(solution)/shard_map/lkgtu,lukd->ltkgd/dot_general | solution.py:82
  27.6 1.3 %fusion.1 = bf16[2,4,8,64,128]{4,3,2,1,0:T(8,128)(2,1)S(1)} fusion(f32[2,4,8,64,128]{4,3,2,1,0:T(8,128)S(1)} %get-tuple-element.37, bf16[2,128,4,128,1]{1,3,4,2,0:T(8,128)(2,1)S(1)} %bitcast.97, f32[2,4,8,64]{3,2,1,0:T(8,128)S(1)} %bitcast.106, f32[2,4,8,64]{3,2,1,0:T(8,128)S(1)} %log_add_fusion, bf16[2,64,4,8,128]{4,3,2,1,0:T(8,128)(2,1)S(1)} %bitcast.89), kind=kOutput, calls=%fused_computation.2 | convolution fusion | flops 136314880 | bytes 4489216 | tf_op jit(solution)/shard_map/ltkgd,lukd->lkgtu/dot_general | solution.py:90
  28.9 1.0 %copy-done = bf16[2,4,8,64,128]{4,3,2,1,0:T(8,128)(2,1)} copy-done((bf16[2,4,8,64,128]{4,3,2,1,0:T(8,128)(2,1)}, bf16[2,4,8,64,128]{4,3,2,1,0:T(8,128)(2,1)S(1)}, u32[]{:S(2)}) %copy-start) | copy-done | bytes 1048600
  29.8 0.7 %fusion.5 = f32[2,4,128,128]{2,3,1,0:T(8,128)S(1)} fusion(bf16[2,4,8,64,128]{4,3,2,1,0:T(8,128)(2,1)S(1)} %fusion.1, bf16[2,64,4,8,128]{4,3,2,1,0:T(8,128)(2,1)S(1)} %bitcast.91), kind=kOutput, calls=%fused_computation.16 | convolution fusion | flops 134348800 | bytes 2621440 | tf_op jit(solution)/shard_map/lkgtu,ltkgd->lukd/dot_general | solution.py:95
  30.6 0.6 %broadcast_in_dim.16 = f32[32,1,32]{2,1,0:T(1,128)} broadcast(f32[32]{0:T(128)S(1)} %neg.11), dimensions={2} | broadcast | bytes 4224 | tf_op jit(solution)/shard_map/broadcast_in_dim | solution.py:29
  31.2 5.1 %all-to-all-start = ((f32[32,1,32]{2,1,0:T(1,128)}), f32[32,1,32]{2,1,0:T(1,128)S(1)}, u32[]{:S(2)}, u32[]{:S(2)}) async-start(f32[32,1,32]{2,1,0:T(1,128)} %broadcast_in_dim.16), calls=%async_computation | async-start | bytes 32768 | tf_op jit(solution)/shard_map/all_to_all | solution.py:30
  36.4 0.8 %slice_bitcast_fusion.3 = (bf16[64,1024]{0,1:T(8,128)(2,1)}, bf16[64,1024]{0,1:T(8,128)(2,1)}) fusion(bf16[2,128,1024]{1,2,0:T(8,128)(2,1)S(1)} %fusion.9), kind=kLoop, calls=%fused_computation.34 | loop fusion | bytes 524288 | tf_op jit(solution)/shard_map/squeeze | solution.py:113
  37.2 4.3 %collective-permute-start.2 = (bf16[64,1024]{0,1:T(8,128)(2,1)}, bf16[64,1024]{0,1:T(8,128)(2,1)}, u32[]{:S(2)}, u32[]{:S(2)}) collective-permute-start(bf16[64,1024]{0,1:T(8,128)(2,1)} %get-tuple-element.11), channel_id=1, source_target_pairs={{2,0},{4,2},{6,4},{8,6},{10,8},{12,10},{14,12},{16,14},{18,16},{20... | collective-permute-start | bytes 393224 | tf_op jit(solution)/shard_map/ppermute | solution.py:22
  41.5 0.4 fusion.4
  42.0 0.7 %copy.50 = bf16[2,64,4,8,128]{4,3,2,1,0:T(8,128)(2,1)S(1)} copy(bf16[2,64,4,8,128]{4,1,3,2,0:T(8,128)(2,1)S(1)} %copy-done.5) | data formatting | bytes 2097152 | tf_op jit(solution)/shard_map/convert_element_type | solution.py:84
  42.6 1.3 %reshape.161 = bf16[1,1,2,64,4096]{4,3,2,1,0:T(8,128)(2,1)} reshape(bf16[2,64,4,8,128]{4,3,2,1,0:T(8,128)(2,1)S(1)} %copy.50) | data formatting | bytes 2097152 | tf_op jit(solution)/shard_map/reshape | solution.py:119
  43.9 0.7 %copy.55 = bf16[2,64,4,8,128]{4,3,2,1,0:T(8,128)(2,1)S(1)} copy(bf16[2,64,4,8,128]{4,1,3,2,0:T(8,128)(2,1)S(1)} %fusion.4) | data formatting | bytes 2097152 | tf_op jit(solution)/shard_map/convert_element_type | solution.py:120
  44.6 1.3 %reshape.163 = bf16[1,1,2,64,4096]{4,3,2,1,0:T(8,128)(2,1)} reshape(bf16[2,64,4,8,128]{4,3,2,1,0:T(8,128)(2,1)S(1)} %copy.55) | data formatting | bytes 2097152 | tf_op jit(solution)/shard_map/reshape | solution.py:120
  45.9 1.9 %collective-permute-start.3 = (bf16[64,1024]{0,1:T(8,128)(2,1)S(1)}, bf16[64,1024]{0,1:T(8,128)(2,1)S(1)}, u32[]{:S(2)}, u32[]{:S(2)}) collective-permute-start(bf16[64,1024]{0,1:T(8,128)(2,1)S(1)} %copy-done.12), channel_id=1, source_target_pairs={{0,2},{2,4},{4,6},{6,8},{8,10},{10,12},{12,14},{14,16},{16,18},{18... | collective-permute-start | bytes 393224 | tf_op jit(solution)/shard_map/ppermute | solution.py:17
  47.8 0.5 reduce_sum.39
  48.4 1.0 %select_bitcast_fusion = bf16[1,64,1024]{1,2,0:T(8,128)(2,1)S(1)} fusion(bf16[64,1024]{0,1:T(8,128)(2,1)} %collective-permute-done.2, pred[]{:T(512)S(6)} %eq.3, bf16[2,128,1024]{1,2,0:T(8,128)(2,1)S(1)} %copy-done.7), kind=kLoop, calls=%fused_computation.37 | loop fusion | flops 65536 | bytes 393217 | tf_op jit(solution)/shard_map/stack | solution.py:115
  49.3 8.3 %collective-permute-done.3 = bf16[64,1024]{0,1:T(8,128)(2,1)S(1)} collective-permute-done((bf16[64,1024]{0,1:T(8,128)(2,1)S(1)}, bf16[64,1024]{0,1:T(8,128)(2,1)S(1)}, u32[]{:S(2)}, u32[]{:S(2)}) %collective-permute-start.3) | collective-permute-done | bytes 131104 | tf_op jit(solution)/shard_map/ppermute | solution.py:17
  57.7 0.3 fusion.8
  58.0 0.8 %copy.60 = bf16[1,1,2,64,512]{4,3,2,1,0:T(8,128)(2,1)} copy(bf16[1,1,2,64,512]{3,4,2,1,0:T(8,128)(2,1)S(1)} %get-tuple-element.28) | data formatting | bytes 262144
  58.8 0.8 %copy.59 = bf16[1,1,2,64,512]{4,3,2,1,0:T(8,128)(2,1)} copy(bf16[1,1,2,64,512]{3,4,2,1,0:T(8,128)(2,1)S(1)} %get-tuple-element.29) | data formatting | bytes 262144
  (43 shorter events, 1.8 us)
Async XLA Ops:
  0.6 11.7 %copy-start.10 = (bf16[1,1,2,64,4096]{4,3,2,1,0:T(8,128)(2,1)S(1)}, bf16[1,1,2,64,4096]{4,3,2,1,0:T(8,128)(2,1)}, u32[]{:S(2)}) copy-start(bf16[1,1,2,64,4096]{4,3,2,1,0:T(8,128)(2,1)} %param.6) | copy-start | bytes 3145732
  3.0 17.6 %collective-permute-start = (bf16[64,1024]{0,1:T(8,128)(2,1)S(1)}, bf16[64,1024]{0,1:T(8,128)(2,1)S(1)}, u32[]{:S(2)}, u32[]{:S(2)}) collective-permute-start(bf16[64,1024]{0,1:T(8,128)(2,1)S(1)} %get-tuple-element.9), channel_id=1, source_target_pairs={{0,2},{2,4},{4,6},{6,8},{8,10},{10,12},{12,14},{14,16},{16,18},{18... | collective-permute-start | bytes 393224 | tf_op jit(solution)/shard_map/ppermute | solution.py:17
  6.4 13.2 %collective-permute-start.1 = (bf16[64,1024]{0,1:T(8,128)(2,1)S(1)}, bf16[64,1024]{0,1:T(8,128)(2,1)}, u32[]{:S(2)}, u32[]{:S(2)}) collective-permute-start(bf16[64,1024]{0,1:T(8,128)(2,1)S(1)} %get-tuple-element.10), channel_id=1, source_target_pairs={{2,0},{4,2},{6,4},{8,6},{10,8},{12,10},{14,12},{16,14},{18,16},{20... | collective-permute-start | bytes 393224 | tf_op jit(solution)/shard_map/ppermute | solution.py:22
  12.3 1.3 %copy-start.11 = (bf16[1,1,2,64,4096]{4,3,2,1,0:T(8,128)(2,1)S(1)}, bf16[1,1,2,64,4096]{4,3,2,1,0:T(8,128)(2,1)}, u32[]{:S(2)}) copy-start(bf16[1,1,2,64,4096]{4,3,2,1,0:T(8,128)(2,1)} %param.11) | copy-start | bytes 3145732
  12.6 8.4 %copy-start.2 = (bf16[16,8,32,128]{3,2,1,0:T(8,128)(2,1)}, bf16[16,8,32,128]{3,2,1,0:T(8,128)(2,1)S(1)}, u32[]{:S(2)}) copy-start(bf16[16,8,32,128]{3,2,1,0:T(8,128)(2,1)S(1)} %copy.75) | copy-start | bytes 3145732
  21.0 2.3 %copy-start.8 = (bf16[2,128,512]{1,2,0:T(8,128)(2,1)}, bf16[2,128,512]{1,2,0:T(8,128)(2,1)S(1)}, u32[]{:S(2)}) copy-start(bf16[2,128,512]{1,2,0:T(8,128)(2,1)S(1)} %get-tuple-element.32) | copy-start | bytes 786436
  27.6 2.2 %copy-start.3 = (bf16[16,8,32,128]{3,2,1,0:T(8,128)(2,1)S(1)}, bf16[16,8,32,128]{3,2,1,0:T(8,128)(2,1)}, u32[]{:S(2)}) copy-start(bf16[16,8,32,128]{3,2,1,0:T(8,128)(2,1)} %copy-done.2) | copy-start | bytes 3145732
  28.8 1.0 %copy-start = (bf16[2,4,8,64,128]{4,3,2,1,0:T(8,128)(2,1)}, bf16[2,4,8,64,128]{4,3,2,1,0:T(8,128)(2,1)S(1)}, u32[]{:S(2)}) copy-start(bf16[2,4,8,64,128]{4,3,2,1,0:T(8,128)(2,1)S(1)} %fusion.1) | copy-start | bytes 3145732
  29.8 6.5 %copy-start.4 = (f32[2,4,128,128,1]{2,3,4,1,0:T(8,128)S(1)}, f32[2,4,128,128,1]{2,3,4,1,0:T(8,128)}, u32[]{:S(2)}) copy-start(f32[2,4,128,128,1]{2,3,4,1,0:T(8,128)} %fusion.12) | copy-start | bytes 1572868
  29.8 11.7 %copy-start.9 = (bf16[2,128,512]{1,2,0:T(8,128)(2,1)S(1)}, bf16[2,128,512]{1,2,0:T(8,128)(2,1)}, u32[]{:S(2)}) copy-start(bf16[2,128,512]{1,2,0:T(8,128)(2,1)} %copy-done.8) | copy-start | bytes 786436
  30.6 10.9 %copy-start.1 = (bf16[2,4,8,64,128]{4,3,2,1,0:T(8,128)(2,1)S(1)}, bf16[2,4,8,64,128]{4,3,2,1,0:T(8,128)(2,1)}, u32[]{:S(2)}) copy-start(bf16[2,4,8,64,128]{4,3,2,1,0:T(8,128)(2,1)} %copy-done) | copy-start | bytes 3145732
  31.2 16.6 %all-to-all-start = ((f32[32,1,32]{2,1,0:T(1,128)}), f32[32,1,32]{2,1,0:T(1,128)S(1)}, u32[]{:S(2)}, u32[]{:S(2)}) async-start(f32[32,1,32]{2,1,0:T(1,128)} %broadcast_in_dim.16), calls=%async_computation | async-start | bytes 32768 | tf_op jit(solution)/shard_map/all_to_all | solution.py:30
  36.4 5.6 %copy-start.6 = (bf16[2,128,1024]{1,2,0:T(8,128)(2,1)}, bf16[2,128,1024]{1,2,0:T(8,128)(2,1)S(1)}, u32[]{:S(2)}) copy-start(bf16[2,128,1024]{1,2,0:T(8,128)(2,1)S(1)} %fusion.9) | copy-start | bytes 1572868
  36.4 5.6 %copy-start.5 = (bf16[2,64,4,8,128]{4,1,3,2,0:T(8,128)(2,1)S(1)}, bf16[2,64,4,8,128]{4,1,3,2,0:T(8,128)(2,1)}, u32[]{:S(2)}) copy-start(bf16[2,64,4,8,128]{4,1,3,2,0:T(8,128)(2,1)} %get-tuple-element.39) | copy-start | bytes 3145732
  37.2 11.1 %collective-permute-start.2 = (bf16[64,1024]{0,1:T(8,128)(2,1)}, bf16[64,1024]{0,1:T(8,128)(2,1)}, u32[]{:S(2)}, u32[]{:S(2)}) collective-permute-start(bf16[64,1024]{0,1:T(8,128)(2,1)} %get-tuple-element.11), channel_id=1, source_target_pairs={{2,0},{4,2},{6,4},{8,6},{10,8},{12,10},{14,12},{16,14},{18,16},{20... | collective-permute-start | bytes 393224 | tf_op jit(solution)/shard_map/ppermute | solution.py:22
  43.9 2.0 %copy-start.12 = (bf16[64,1024]{0,1:T(8,128)(2,1)S(1)}, bf16[64,1024]{0,1:T(8,128)(2,1)}, u32[]{:S(2)}) copy-start(bf16[64,1024]{0,1:T(8,128)(2,1)} %get-tuple-element.12) | copy-start | bytes 393220
  44.6 3.8 %copy-start.7 = (bf16[2,128,1024]{1,2,0:T(8,128)(2,1)S(1)}, bf16[2,128,1024]{1,2,0:T(8,128)(2,1)}, u32[]{:S(2)}) copy-start(bf16[2,128,1024]{1,2,0:T(8,128)(2,1)} %copy-done.6) | copy-start | bytes 1572868
  45.9 11.8 %collective-permute-start.3 = (bf16[64,1024]{0,1:T(8,128)(2,1)S(1)}, bf16[64,1024]{0,1:T(8,128)(2,1)S(1)}, u32[]{:S(2)}, u32[]{:S(2)}) collective-permute-start(bf16[64,1024]{0,1:T(8,128)(2,1)S(1)} %copy-done.12), channel_id=1, source_target_pairs={{0,2},{2,4},{4,6},{6,8},{8,10},{10,12},{12,14},{14,16},{16,18},{18... | collective-permute-start | bytes 393224 | tf_op jit(solution)/shard_map/ppermute | solution.py:17

commit v3 on v2

--- a/solution.py
+++ b/solution.py
@@ -51,67 +51,89 @@
     prev1 = shift_down(send1, "ctx")
     prev1 = jnp.where(at_fold, own_pair[0], prev1)
     prev_pair = jnp.stack([prev0, prev1])
-    window = jnp.concatenate([prev_pair, own_pair], axis=1)
-    window_keys = window[:, :, :value_width].reshape(2, span, KV_HEADS, HEAD_DIM)
-    window_values = window[:, :, value_width:].reshape(2, span, KV_HEADS, HEAD_DIM)
+    own_keys = own_pair[:, :, :value_width].reshape(2, block_rows, KV_HEADS, HEAD_DIM)
+    own_values = own_pair[:, :, value_width:].reshape(2, block_rows, KV_HEADS, HEAD_DIM)
+    prev_keys = prev_pair[:, :, :value_width].reshape(2, block_rows, KV_HEADS, HEAD_DIM)
+    prev_values = prev_pair[:, :, value_width:].reshape(2, block_rows, KV_HEADS, HEAD_DIM)
 
     lane_block = jnp.stack([my_index, last_block - my_index]).astype(jnp.int32)
     row_offsets = jnp.arange(block_rows, dtype=jnp.int32)
-    window_offsets = jnp.arange(span, dtype=jnp.int32)
     query_pos = lane_block[:, None] * block_rows + row_offsets[None, :]
-    key_pos = (lane_block[:, None] - REACH) * block_rows + window_offsets[None, :]
+    prev_pos = query_pos - REACH * block_rows
     first_pos = doc_bounds.reshape(2, 2, block_rows)[:, 0]
-    allowed = (key_pos[:, None, :] <= query_pos[:, :, None]) & (
-        key_pos[:, None, :] >= first_pos[:, :, None]
+    allowed_own = (query_pos[:, None, :] <= query_pos[:, :, None]) & (
+        query_pos[:, None, :] >= first_pos[:, :, None]
     )
-    allowed = allowed[:, None, None]
+    allowed_prev = prev_pos[:, None, :] >= first_pos[:, :, None]
+    allowed_own = allowed_own[:, None, None]
+    allowed_prev = allowed_prev[:, None, None]
     sink_col = sink_logit.reshape(1, KV_HEADS, GROUP, 1)
 
-    scores = (
-        jnp.einsum(
-            "ltkgd,lukd->lkgtu", query_lanes, window_keys, preferred_element_type=jnp.float32
+    def block_scores(side_keys):
+        return (
+            jnp.einsum(
+                "ltkgd,lukd->lkgtu", query_lanes, side_keys, preferred_element_type=jnp.float32
+            )
+            * score_scale
         )
-        * score_scale
+
+    def grad_scores(side_values):
+        return jnp.einsum(
+            "ltkgd,lukd->lkgtu", grad_lanes, side_values, preferred_element_type=jnp.float32
+        )
+
+    def mix(side_weights, side_rows):
+        return jnp.einsum(
+            "lkgtu,lukd->ltkgd", side_weights, side_rows, preferred_element_type=jnp.float32
+        )
+
+    def key_side(side_weights, rows):
+        summed = jnp.einsum(
+            "lkgtu,ltkgd->lukd", side_weights, rows, preferred_element_type=jnp.float32
+        )
+        return summed.reshape(2, block_rows, value_width)
+
+    masked_own = jnp.where(allowed_own, block_scores(own_keys), -jnp.inf)
+    dprob_own = grad_scores(own_values)
+    masked_prev = jnp.where(allowed_prev, block_scores(prev_keys), -jnp.inf)
+
+    row_top = jnp.maximum(
+        sink_col, jnp.maximum(jnp.max(masked_own, axis=-1), jnp.max(masked_prev, axis=-1))
     )
-    masked = jnp.where(allowed, scores, -jnp.inf)
-    row_top = jnp.maximum(sink_col, jnp.max(masked, axis=-1))
-    row_total = jnp.exp(sink_col - row_top) + jnp.sum(jnp.exp(masked - row_top[..., None]), axis=-1)
+    row_total = (
+        jnp.exp(sink_col - row_top)
+        + jnp.sum(jnp.exp(masked_own - row_top[..., None]), axis=-1)
+        + jnp.sum(jnp.exp(masked_prev - row_top[..., None]), axis=-1)
+    )
     log_total = row_top + jnp.log(row_total)
-    probs = jnp.exp(masked - log_total[..., None])
-    weights = probs.astype(jnp.bfloat16)
-    attended = jnp.einsum(
-        "lkgtu,lukd->ltkgd", weights, window_values, preferred_element_type=jnp.float32
-    ).astype(jnp.bfloat16)
+    probs_own = jnp.exp(masked_own - log_total[..., None])
+    probs_prev = jnp.exp(masked_prev - log_total[..., None])
+    weights_own = probs_own.astype(jnp.bfloat16)
+    weights_prev = probs_prev.astype(jnp.bfloat16)
+    attended = (mix(weights_own, own_values) + mix(weights_prev, prev_values)).astype(jnp.bfloat16)
     row_delta = jnp.sum(grad_lanes.astype(jnp.float32) * attended.astype(jnp.float32), axis=-1)
     delta_cols = jnp.transpose(row_delta, (0, 2, 3, 1))
     sink_terms = -jnp.sum(jnp.exp(sink_col - log_total) * delta_cols, axis=(0, 3))
     sink_grad = all_sum(sink_terms.reshape(HEADS), ("ctx", "dp"))
 
-    dprob = jnp.einsum(
-        "ltkgd,lukd->lkgtu", grad_lanes, window_values, preferred_element_type=jnp.float32
+    dscore_prev = (probs_prev * (grad_scores(prev_values) - delta_cols[..., None])).astype(
+        jnp.bfloat16
     )
-    dscore = (probs * (dprob - delta_cols[..., None])).astype(jnp.bfloat16)
-    key_part = (
-        jnp.einsum("lkgtu,ltkgd->lukd", dscore, query_lanes, preferred_element_type=jnp.float32)
-        * score_scale
-    )
-    value_part = jnp.einsum(
-        "lkgtu,ltkgd->lukd", weights, grad_lanes, preferred_element_type=jnp.float32
-    )
-    partial = jnp.concatenate(
-        [key_part.reshape(2, span, value_width), value_part.reshape(2, span, value_width)], axis=2
-    )
-    dquery = (
-        jnp.einsum("lkgtu,lukd->ltkgd", dscore, window_keys, preferred_element_type=jnp.float32)
-        * score_scale
+    prev_part = jnp.concatenate(
+        [key_side(dscore_prev, query_lanes) * score_scale, key_side(weights_prev, grad_lanes)],
+        axis=2,
+    ).astype(jnp.bfloat16)
+    dscore_own = (probs_own * (dprob_own - delta_cols[..., None])).astype(jnp.bfloat16)
+    dquery = (mix(dscore_own, own_keys) + mix(dscore_prev, prev_keys)) * score_scale
+    own_part = jnp.concatenate(
+        [key_side(dscore_own, query_lanes) * score_scale, key_side(weights_own, grad_lanes)],
+        axis=2,
     )
 
-    prev_part = partial[:, :block_rows].astype(jnp.bfloat16)
     send0, send1 = lax.optimization_barrier((prev_part[0], prev_part[1]))
     into0 = shift_down(send0, "ctx")
     into1 = shift_up(send1, "ctx")
     into0 = jnp.where(at_fold, prev_part[1], into0)
-    own_part = partial[:, block_rows:]
     gathered = own_part + jnp.stack([into0, into1]).astype(jnp.float32)
 
     out_shape = (1, 1, 2, block_rows, query_width)

time: 60 us -> 62.4 us (1.040)
  the two profiles are of different devices: /device:TPU:8 before, /device:TPU:0 now
where the time goes in v3:
time: 62.4 us; the launch traced here: 61.9 us
  starting transfers between devices  21.6 us (35%)
  local copies, waits for them, and re-layouts  16.6 us (27%)
  matrix products  14.1 us (23%)
  other arithmetic  7.34 us (12%)
  waiting for transfers between devices  1.34 us (2%)
  between operations  0.9 us (1%)
    ppermute x2, starting transfers between devices, shift_up(): return lax.ppermute(x, axis, [(i, i + 1) for i in range(size - 1)])  11.6 us
    all_to_all x1, starting transfers between devices, all_sum(): return jnp.sum(lax.all_to_all(spread, axes, 0, 0, tiled=True), axis=0)  7.41 us
    dot_general x2, matrix products, block_scores(): jnp.einsum('ltkgd,lukd->lkgtu', query_lanes, side_keys, preferred_element...  4.14 us
    dot_general x4, matrix products, key_side(): jnp.einsum('lkgtu,ltkgd->lukd', side_weights, rows, preferred_element_typ...  4.1 us
    dot_general x4, matrix products, mix(): jnp.einsum('lkgtu,lukd->ltkgd', side_weights, side_rows, preferred_elemen...  3.55 us
    unnamed x25, local copies, waits for them, and re-layouts  3.07 us
    ppermute x2, starting transfers between devices, shift_down(): return lax.ppermute(x, axis, [(i + 1, i) for i in range(size - 1)])  2.56 us
    another operation x2, other arithmetic, per_device(): prev_pair = jnp.stack([prev0, prev1])  2.53 us
  transfers between devices with their start and end apart: 5, of which 1 were waited for; matrix products, arithmetic and copies ran while one was open for 26% of the time, Pallas kernels for 0%

profile of v3, /device:TPU:0, one launch (start us, length us, event | category | flops | bytes accessed | tf_op | source)
XLA Modules:
  0.0 61.9 jit_solution(10716417684010525709)
XLA Ops:
  0.6 1.7 %fusion.33 = (bf16[64,1024]{1,0:T(8,128)(2,1)}, bf16[64,1024]{1,0:T(8,128)(2,1)}) fusion(bf16[2,64,512]{2,1,0:T(8,128)(2,1)} %bitcast.157, bf16[2,64,512]{2,1,0:T(8,128)(2,1)} %bitcast.156), kind=kLoop, calls=%fused_computation.59 | loop fusion | flops 524288 | bytes 524288 | tf_op jit(solution)/shard_map/squeeze | solution.py:49
  2.3 1.3 %collective-permute-start.1 = (bf16[64,1024]{1,0:T(8,128)(2,1)}, bf16[64,1024]{1,0:T(8,128)(2,1)}, u32[]{:S(2)}, u32[]{:S(2)}) collective-permute-start(bf16[64,1024]{1,0:T(8,128)(2,1)} %get-tuple-element.10), channel_id=1, source_target_pairs={{2,0},{4,2},{6,4},{8,6},{10,8},{12,10},{14,12},{16,14},{18,16},{20... | collective-permute-start | bytes 393224 | tf_op jit(solution)/shard_map/ppermute | solution.py:22
  3.6 6.1 %collective-permute-start = (bf16[64,1024]{1,0:T(8,128)(2,1)}, bf16[64,1024]{1,0:T(8,128)(2,1)}, u32[]{:S(2)}, u32[]{:S(2)}) collective-permute-start(bf16[64,1024]{1,0:T(8,128)(2,1)} %get-tuple-element.9), channel_id=1, source_target_pairs={{0,2},{2,4},{4,6},{6,8},{8,10},{10,12},{12,14},{14,16},{16,18},{18... | collective-permute-start | bytes 393224 | tf_op jit(solution)/shard_map/ppermute | solution.py:17
  9.7 0.9 %reshape_reshape.6 = bf16[2,64,4,128]{3,2,1,0:T(4,128)(2,1)S(1)} reshape(bf16[1,1,2,64,512]{4,3,2,1,0:T(8,128)(2,1)} %param.7) | data formatting | bytes 262144 | tf_op jit(solution)/shard_map/reshape;reshape | solution.py:54
  10.8 0.7 %slice.40 = s32[2,1,64]{2,1,0:T(1,128)S(1)} slice(s32[2,2,64]{2,1,0:T(2,128)} %bitcast.160), slice={[0:2], [0:1], [0:64]} | slice | bytes 1024 | tf_op jit(solution)/shard_map/slice | solution.py:63
  11.5 1.4 %copy.141 = bf16[16,8,32,128]{3,2,1,0:T(8,128)(2,1)S(1)} copy(bf16[16,8,32,128]{3,1,2,0:T(8,128)(2,1)} %bitcast.152) | data formatting | bytes 2097152
  13.1 1.8 %fusion.43 = (f32[2,4,8,64]{3,2,1,0:T(8,128)}, f32[2,4,8,64,64]{3,4,2,1,0:T(8,128)S(1)}) fusion(bf16[2,64,4,8,128]{4,3,2,1,0:T(8,128)(2,1)S(1)} %bitcast.140, bf16[2,64,4,128,1]{3,2,1,0,4:T(4,128)(2,1)S(1)} %bitcast.144, pred[2,64,64]{1,2,0:T(8,128)(4,1)S(1)} %get-tuple-element.24), kind=kOutput, calls=%fused_computation.79 | convolution fusion | flops 67891200 | bytes 2252800 | tf_op jit(solution)/shard_map/ltkgd,lukd->lkgtu/dot_general | solution.py:74
  14.9 1.3 %max.27 = f32[4,8]{1,0:T(4,128)} reshape(f32[32]{0:T(128)} %param.10) | data formatting | bytes 256 | tf_op jit(solution)/shard_map/max | solution.py:100
  16.2 1.4 %copy.142 = bf16[16,8,32,128]{3,2,1,0:T(8,128)(2,1)S(1)} copy(bf16[16,8,32,128]{3,1,2,0:T(8,128)(2,1)} %bitcast.153) | data formatting | bytes 2097152
  17.7 0.9 %select_bitcast_fusion.1 = bf16[1,64,1024]{2,1,0:T(8,128)(2,1)S(1)} fusion(bf16[64,1024]{1,0:T(8,128)(2,1)} %get-tuple-element.9, bf16[64,1024]{1,0:T(8,128)(2,1)} %collective-permute-done.1, pred[]{:T(512)S(6)} %eq.3), kind=kLoop, calls=%fused_computation.61 | loop fusion | flops 65536 | bytes 393217 | tf_op jit(solution)/shard_map/stack | solution.py:53
  18.6 1.6 %pad_maximum_fusion = (bf16[2,64,512]{2,1,0:T(8,128)(2,1)}, bf16[2,64,512]{2,1,0:T(8,128)(2,1)}) fusion(bf16[1,64,1024]{2,1,0:T(8,128)(2,1)S(1)} %select_bitcast_fusion.1, bf16[1,64,1024]{2,1,0:T(8,128)(2,1)} %bitcast.10), kind=kLoop, calls=%fused_computation.57 | loop fusion | flops 524288 | bytes 524288 | tf_op jit(solution)/shard_map/stack | solution.py:53
  20.2 0.9 %reshape.172 = bf16[2,64,4,128]{3,2,1,0:T(4,128)(2,1)S(1)} reshape(bf16[2,64,512]{2,1,0:T(8,128)(2,1)} %get-tuple-element.20) | data formatting | bytes 262144 | tf_op jit(solution)/shard_map/reshape | solution.py:56
  21.2 1.6 %reshape.173 = bf16[2,64,4,128]{3,2,1,0:T(4,128)(2,1)} reshape(bf16[2,64,512]{2,1,0:T(8,128)(2,1)} %get-tuple-element.19) | data formatting | bytes 262144 | tf_op jit(solution)/shard_map/reshape | solution.py:57
  22.8 2.4 %fusion.44 = (f32[2,4,8,64]{3,2,1,0:T(8,128)S(1)}, f32[2,4,8,64,64]{3,4,2,1,0:T(8,128)S(1)}) fusion(bf16[2,64,4,8,128]{4,3,2,1,0:T(8,128)(2,1)} %bitcast.141, bf16[2,64,4,128,1]{3,2,1,0,4:T(4,128)(2,1)S(1)} %bitcast.146, pred[2,64,64]{1,2,0:T(8,128)(4,1)S(1)} %get-tuple-element.23), kind=kOutput, calls=%fused_computation.80 | convolution fusion | flops 67891200 | bytes 2252800 | tf_op jit(solution)/shard_map/ltkgd,lukd->lkgtu/dot_general | solution.py:74
  25.2 1.1 %exponential_reduce_fusion.1 = (f32[2,4,8,64]{3,2,1,0:T(8,128)S(1)}, f32[2,4,8,64]{3,2,1,0:T(8,128)S(1)}) fusion(f32[2,4,8,64,64]{3,4,2,1,0:T(8,128)S(1)} %get-tuple-element.28, f32[2,4,8,64]{3,2,1,0:T(8,128)S(1)} %maximum_maximum_fusion, f32[2,4,8,64,64]{3,4,2,1,0:T(8,128)S(1)} %get-tuple-element.30), kind=kLoop, calls=%fused_computation.17 | loop fusion | flops 1040384 | bytes 2146304 | tf_op jit(solution)/shard_map/reduce_sum | solution.py:105
  27.0 0.8 %fusion.15 = bf16[2,4,8,8,128]{4,3,2,1,0:T(8,128)(2,1)S(1)} fusion(bf16[2,64,4,8,128]{4,3,2,1,0:T(8,128)(2,1)S(1)} %bitcast.135, f32[2,4,8,64,64]{3,4,2,1,0:T(8,128)S(1)} %get-tuple-element.30, f32[2,4,8,64]{3,2,1,0:T(8,128)S(1)} %log_add_fusion), kind=kOutput, calls=%fused_computation.30 | convolution fusion | flops 67698688 | bytes 2244608 | tf_op jit(solution)/shard_map/lkgtu,ltkgd->lukd/dot_general | solution.py:91
  27.9 2.0 %multiply_reduce_fusion = (f32[2,64,4,8]{1,3,2,0:T(8,128)S(1)}, bf16[2,64,4,8,128]{4,1,3,2,0:T(8,128)(2,1)}) fusion(bf16[2,64,4,8,128]{4,3,2,1,0:T(8,128)(2,1)S(1)} %bitcast.136, f32[2,4,8,64,64]{3,4,2,1,0:T(8,128)S(1)} %get-tuple-element.30, f32[2,4,8,64]{3,2,1,0:T(8,128)S(1)} %log_add_fusion, bf16[2,64,4,128,1]{3,2,1,0,4:T(4,128)(2,1)S(1)} %bitcast.150, ...), kind=kOutput, calls=%fused_computation.13 | convolution fusion | flops 70774784 | bytes 5406720 | tf_op jit(solution)/shard_map/lkgtu,lukd->ltkgd/dot_general | solution.py:86
  29.8 1.2 %fusion.3 = bf16[2,4,8,64,64]{3,4,2,1,0:T(8,128)(2,1)S(1)} fusion(f32[2,4,8,64,64]{3,4,2,1,0:T(8,128)S(1)} %get-tuple-element.30, f32[2,4,8,64]{3,2,1,0:T(8,128)S(1)} %bitcast.154, f32[2,4,8,64]{3,2,1,0:T(8,128)S(1)} %log_add_fusion, bf16[2,64,4,8,128]{4,3,2,1,0:T(8,128)(2,1)S(1)} %bitcast.137, bf16[2,64,4,128,1]{3,2,1,0,4:T(4,128)(2,1)S(1)} %bitcast.151), kind=kOutput, calls=%fused_computation.5 | convolution fusion | flops 68157440 | bytes 2785280 | tf_op jit(solution)/shard_map/ltkgd,lukd->lkgtu/dot_general | solution.py:81
  31.0 1.2 %fusion.5 = bf16[2,4,8,64,64]{3,4,2,1,0:T(8,128)(2,1)S(1)} fusion(f32[2,4,8,64,64]{3,4,2,1,0:T(8,128)S(1)} %get-tuple-element.28, f32[2,4,8,64]{3,2,1,0:T(8,128)S(1)} %bitcast.155, f32[2,4,8,64]{3,2,1,0:T(8,128)S(1)} %log_add_fusion, bf16[2,64,4,8,128]{4,3,2,1,0:T(8,128)(2,1)S(1)} %bitcast.138, bf16[2,64,4,128,1]{3,2,1,0,4:T(4,128)(2,1)S(1)} %bitcast.149), kind=kOutput, calls=%fused_computation.8 | convolution fusion | flops 68157440 | bytes 2785280 | tf_op jit(solution)/shard_map/ltkgd,lukd->lkgtu/dot_general | solution.py:81
  32.2 1.4 %convolution_bitcast_fusion.2 = f32[2,4,8,8,128]{4,3,2,1,0:T(8,128)} fusion(bf16[2,64,4,8,128]{4,3,2,1,0:T(8,128)(2,1)S(1)} %bitcast.139, f32[2,4,8,64,64]{3,4,2,1,0:T(8,128)S(1)} %get-tuple-element.28, f32[2,4,8,64]{3,2,1,0:T(8,128)S(1)} %log_add_fusion), kind=kOutput, calls=%fused_computation.22 | convolution fusion | flops 67633152 | bytes 2375680 | tf_op jit(solution)/shard_map/lkgtu,ltkgd->lukd/dot_general | solution.py:91
  33.6 1.3 %fusion.10 = f32[2,4,8,8,128]{4,3,2,1,0:T(8,128)} fusion(bf16[2,4,8,64,64]{3,4,2,1,0:T(8,128)(2,1)S(1)} %fusion.5, bf16[2,64,4,8,128]{4,3,2,1,0:T(8,128)(2,1)S(1)} %bitcast.142), kind=kOutput, calls=%fused_computation.25 | convolution fusion | flops 67174400 | bytes 1835008 | tf_op jit(solution)/shard_map/lkgtu,ltkgd->lukd/dot_general | solution.py:91
  36.2 0.8 %slice_bitcast_fusion.3 = (bf16[64,1024]{1,0:T(8,128)(2,1)}, bf16[64,1024]{1,0:T(8,128)(2,1)}) fusion(bf16[2,64,1024]{2,1,0:T(8,128)(2,1)S(1)} %bitcast_dynamic-update-slice_fusion), kind=kLoop, calls=%fused_computation.56 | loop fusion | bytes 524288 | tf_op jit(solution)/shard_map/squeeze | solution.py:136
  37.0 1.3 %collective-permute-start.2 = (bf16[64,1024]{1,0:T(8,128)(2,1)}, bf16[64,1024]{1,0:T(8,128)(2,1)S(1)}, u32[]{:S(2)}, u32[]{:S(2)}) collective-permute-start(bf16[64,1024]{1,0:T(8,128)(2,1)} %get-tuple-element.11), channel_id=1, source_target_pairs={{2,0},{4,2},{6,4},{8,6},{10,8},{12,10},{14,12},{16,14},{18,16},{20... | collective-permute-start | bytes 393224 | tf_op jit(solution)/shard_map/ppermute | solution.py:22
  38.3 5.5 %collective-permute-start.3 = (bf16[64,1024]{1,0:T(8,128)(2,1)}, bf16[64,1024]{1,0:T(8,128)(2,1)}, u32[]{:S(2)}, u32[]{:S(2)}) collective-permute-start(bf16[64,1024]{1,0:T(8,128)(2,1)} %get-tuple-element.12), channel_id=1, source_target_pairs={{0,2},{2,4},{4,6},{6,8},{8,10},{10,12},{12,14},{14,16},{16,18},{18... | collective-permute-start | bytes 393224 | tf_op jit(solution)/shard_map/ppermute | solution.py:17
  45.0 7.4 %all-to-all-start = ((f32[32,1,32]{2,1,0:T(1,128)}), f32[32,1,32]{2,1,0:T(1,128)S(1)}, u32[]{:S(2)}, u32[]{:S(2)}) async-start(f32[32,1,32]{2,1,0:T(1,128)} %broadcast_in_dim.23), calls=%async_computation | async-start | bytes 32768 | tf_op jit(solution)/shard_map/all_to_all | solution.py:30
  52.4 1.9 %copy_bitcast_fusion = (f32[2,64,512]{2,1,0:T(8,128)}, f32[2,64,512]{2,1,0:T(8,128)}) fusion(f32[2,4,8,8,128]{4,3,2,1,0:T(8,128)} %convolution_bitcast_fusion.2, f32[2,4,8,8,128]{4,3,2,1,0:T(8,128)} %fusion.10), kind=kLoop, calls=%fused_computation.41 | loop fusion | bytes 1048576 | tf_op jit(solution)/shard_map/reshape | solution.py:94
  55.0 1.3 %reshape.176 = bf16[1,1,2,64,4096]{4,3,2,1,0:T(8,128)(2,1)} reshape(bf16[2,64,4,8,128]{4,3,2,1,0:T(8,128)(2,1)S(1)} %copy.95) | data formatting | bytes 2097152 | tf_op jit(solution)/shard_map/reshape | solution.py:142
  56.3 0.7 %copy.85 = bf16[2,64,4,8,128]{4,3,2,1,0:T(8,128)(2,1)S(1)} copy(bf16[2,64,4,8,128]{4,1,3,2,0:T(8,128)(2,1)S(1)} %copy-done.2) | data formatting | bytes 2097152 | tf_op jit(solution)/shard_map/convert_element_type | solution.py:113
  57.0 1.3 %reshape.174 = bf16[1,1,2,64,4096]{4,3,2,1,0:T(8,128)(2,1)} reshape(bf16[2,64,4,8,128]{4,3,2,1,0:T(8,128)(2,1)S(1)} %copy.85) | data formatting | bytes 2097152 | tf_op jit(solution)/shard_map/reshape | solution.py:141
  58.3 1.3 %all-to-all-done = f32[32,1,32]{2,1,0:T(1,128)S(1)} async-done(((f32[32,1,32]{2,1,0:T(1,128)}), f32[32,1,32]{2,1,0:T(1,128)S(1)}, u32[]{:S(2)}, u32[]{:S(2)}) %all-to-all-start) | async-done | bytes 4128 | tf_op jit(solution)/shard_map/all_to_all | solution.py:30
  60.2 1.0 %fusion.24 = bf16[2,64,1024]{2,1,0:T(8,128)(2,1)S(1)} fusion(f32[2,64,512]{2,1,0:T(8,128)S(1)} %copy-done.6, f32[2,64,512]{2,1,0:T(8,128)S(1)} %copy-done.7, bf16[1,64,1024]{2,1,0:T(8,128)(2,1)} %bitcast.42, bf16[1,64,1024]{2,1,0:T(8,128)(2,1)S(1)} %select_bitcast_fusion), kind=kLoop, calls=%fused_computation.40 | loop fusion | flops 655360 | bytes 1048576 | tf_op jit(solution)/shard_map/convert.1
  61.1 0.7 %slice_bitcast_fusion = (bf16[1,1,2,64,512]{4,3,2,1,0:T(8,128)(2,1)}, bf16[1,1,2,64,512]{4,3,2,1,0:T(8,128)(2,1)}) fusion(bf16[2,64,1024]{2,1,0:T(8,128)(2,1)S(1)} %fusion.24), kind=kLoop, calls=%fused_computation.53 | loop fusion | bytes 524288 | tf_op jit(solution)/shard_map/reshape | solution.py:144
  (45 shorter events, 4.9 us)
Async XLA Ops:
  2.3 15.4 %collective-permute-start.1 = (bf16[64,1024]{1,0:T(8,128)(2,1)}, bf16[64,1024]{1,0:T(8,128)(2,1)}, u32[]{:S(2)}, u32[]{:S(2)}) collective-permute-start(bf16[64,1024]{1,0:T(8,128)(2,1)} %get-tuple-element.10), channel_id=1, source_target_pairs={{2,0},{4,2},{6,4},{8,6},{10,8},{12,10},{14,12},{16,14},{18,16},{20... | collective-permute-start | bytes 393224 | tf_op jit(solution)/shard_map/ppermute | solution.py:22
  3.6 15.0 %collective-permute-start = (bf16[64,1024]{1,0:T(8,128)(2,1)}, bf16[64,1024]{1,0:T(8,128)(2,1)}, u32[]{:S(2)}, u32[]{:S(2)}) collective-permute-start(bf16[64,1024]{1,0:T(8,128)(2,1)} %get-tuple-element.9), channel_id=1, source_target_pairs={{0,2},{2,4},{4,6},{6,8},{8,10},{10,12},{12,14},{14,16},{16,18},{18... | collective-permute-start | bytes 393224 | tf_op jit(solution)/shard_map/ppermute | solution.py:17
  13.0 3.3 %copy-start = (bf16[16,8,32,128]{3,2,1,0:T(8,128)(2,1)}, bf16[16,8,32,128]{3,2,1,0:T(8,128)(2,1)S(1)}, u32[]{:S(2)}) copy-start(bf16[16,8,32,128]{3,2,1,0:T(8,128)(2,1)S(1)} %copy.141) | copy-start | bytes 3145732
  13.0 1.9 %copy-start.8 = (bf16[1,1,2,64,512]{4,3,2,1,0:T(8,128)(2,1)S(1)}, bf16[1,1,2,64,512]{4,3,2,1,0:T(8,128)(2,1)}, u32[]{:S(2)}) copy-start(bf16[1,1,2,64,512]{4,3,2,1,0:T(8,128)(2,1)} %param.8) | copy-start | bytes 393220
  22.8 2.4 %copy-start.9 = (f32[2,4,8,64]{3,2,1,0:T(8,128)S(1)}, f32[2,4,8,64]{3,2,1,0:T(8,128)}, u32[]{:S(2)}) copy-start(f32[2,4,8,64]{3,2,1,0:T(8,128)} %get-tuple-element.27) | copy-start | bytes 49156
  22.8 2.4 %copy-start.10 = (f32[4,8]{1,0:T(4,128)S(1)}, f32[4,8]{1,0:T(4,128)}, u32[]{:S(2)}) copy-start(f32[4,8]{1,0:T(4,128)} %max.27) | copy-start | bytes 388
  27.0 0.9 %copy-start.3 = (bf16[2,64,4,128]{3,2,1,0:T(4,128)(2,1)S(1)}, bf16[2,64,4,128]{3,2,1,0:T(4,128)(2,1)}, u32[]{:S(2)}) copy-start(bf16[2,64,4,128]{3,2,1,0:T(4,128)(2,1)} %reshape.173) | copy-start | bytes 393220
  32.2 1.4 %copy-start.1 = (bf16[16,8,32,128]{3,2,1,0:T(8,128)(2,1)S(1)}, bf16[16,8,32,128]{3,2,1,0:T(8,128)(2,1)}, u32[]{:S(2)}) copy-start(bf16[16,8,32,128]{3,2,1,0:T(8,128)(2,1)} %copy-done) | copy-start | bytes 3145732
  36.2 2.1 %copy-start.4 = (bf16[2,64,1024]{2,1,0:T(8,128)(2,1)}, bf16[2,64,1024]{2,1,0:T(8,128)(2,1)S(1)}, u32[]{:S(2)}) copy-start(bf16[2,64,1024]{2,1,0:T(8,128)(2,1)S(1)} %bitcast_dynamic-update-slice_fusion) | copy-start | bytes 786436
  37.0 23.1 %collective-permute-start.2 = (bf16[64,1024]{1,0:T(8,128)(2,1)}, bf16[64,1024]{1,0:T(8,128)(2,1)S(1)}, u32[]{:S(2)}, u32[]{:S(2)}) collective-permute-start(bf16[64,1024]{1,0:T(8,128)(2,1)} %get-tuple-element.11), channel_id=1, source_target_pairs={{2,0},{4,2},{6,4},{8,6},{10,8},{12,10},{14,12},{16,14},{18,16},{20... | collective-permute-start | bytes 393224 | tf_op jit(solution)/shard_map/ppermute | solution.py:22
  38.3 21.8 %collective-permute-start.3 = (bf16[64,1024]{1,0:T(8,128)(2,1)}, bf16[64,1024]{1,0:T(8,128)(2,1)}, u32[]{:S(2)}, u32[]{:S(2)}) collective-permute-start(bf16[64,1024]{1,0:T(8,128)(2,1)} %get-tuple-element.12), channel_id=1, source_target_pairs={{0,2},{2,4},{4,6},{6,8},{8,10},{10,12},{12,14},{14,16},{16,18},{18... | collective-permute-start | bytes 393224 | tf_op jit(solution)/shard_map/ppermute | solution.py:17
  45.0 14.6 %all-to-all-start = ((f32[32,1,32]{2,1,0:T(1,128)}), f32[32,1,32]{2,1,0:T(1,128)S(1)}, u32[]{:S(2)}, u32[]{:S(2)}) async-start(f32[32,1,32]{2,1,0:T(1,128)} %broadcast_in_dim.23), calls=%async_computation | async-start | bytes 32768 | tf_op jit(solution)/shard_map/all_to_all | solution.py:30
  54.3 2.0 %copy-start.2 = (bf16[2,64,4,8,128]{4,1,3,2,0:T(8,128)(2,1)S(1)}, bf16[2,64,4,8,128]{4,1,3,2,0:T(8,128)(2,1)}, u32[]{:S(2)}) copy-start(bf16[2,64,4,8,128]{4,1,3,2,0:T(8,128)(2,1)} %get-tuple-element.32) | copy-start | bytes 3145732
  56.3 3.8 %copy-start.5 = (bf16[2,64,1024]{2,1,0:T(8,128)(2,1)S(1)}, bf16[2,64,1024]{2,1,0:T(8,128)(2,1)}, u32[]{:S(2)}) copy-start(bf16[2,64,1024]{2,1,0:T(8,128)(2,1)} %copy-done.4) | copy-start | bytes 786436
  56.3 3.9 %copy-start.6 = (f32[2,64,512]{2,1,0:T(8,128)S(1)}, f32[2,64,512]{2,1,0:T(8,128)}, u32[]{:S(2)}) copy-start(f32[2,64,512]{2,1,0:T(8,128)} %get-tuple-element.33) | copy-start | bytes 786436
  56.3 3.9 %copy-start.7 = (f32[2,64,512]{2,1,0:T(8,128)S(1)}, f32[2,64,512]{2,1,0:T(8,128)}, u32[]{:S(2)}) copy-start(f32[2,64,512]{2,1,0:T(8,128)} %get-tuple-element.34) | copy-start | bytes 786436

commit v4 on v2

v4 whole, which is shorter than its diff:
```python
import math

import jax
import jax.numpy as jnp
from jax import lax
from jax.experimental import pallas as pl
from jax.experimental.pallas import tpu as pltpu
from jax.sharding import PartitionSpec as P

HEADS = 32
KV_HEADS = 4
HEAD_DIM = 128
GROUP = 8
REACH = 1


def shift_up(x, axis):
    size = lax.axis_size(axis)
    return lax.ppermute(x, axis, [(i, i + 1) for i in range(size - 1)])


def shift_down(x, axis):
    size = lax.axis_size(axis)
    return lax.ppermute(x, axis, [(i + 1, i) for i in range(size - 1)])


def all_sum(x, axes):
    count = 1
    for axis in axes:
        count *= lax.axis_size(axis)
    spread = jnp.broadcast_to(x[None], (count,) + x.shape)
    return jnp.sum(lax.all_to_all(spread, axes, 0, 0, tiled=True), axis=0)


def group_kernel(
    sink_ref, q_ref, g_ref, k_ref, v_ref, allow_ref, o_ref, dq_ref, dk_ref, dv_ref, st_ref
):
    group = pl.program_id(1)
    rows = q_ref.shape[1]
    score_scale = 1.0 / math.sqrt(HEAD_DIM)
    heads = [pl.ds(h * HEAD_DIM, HEAD_DIM) for h in range(GROUP)]
    query = jnp.concatenate([q_ref[0, :, cols] for cols in heads], axis=0)
    grad = jnp.concatenate([g_ref[0, :, cols] for cols in heads], axis=0)
    key = k_ref[0]
    value = v_ref[0]
    allowed = jnp.concatenate([allow_ref[0]] * GROUP, axis=0) > 0.5
    head_of_row = lax.broadcasted_iota(jnp.int32, (GROUP * rows, 1), 0) // rows
    sink = jnp.zeros((GROUP * rows, 1), jnp.float32)
    for h in range(GROUP):
        sink = jnp.where(head_of_row == h, sink_ref[group * GROUP + h], sink)
    contract_last = (((1,), (1,)), ((), ()))
    contract_first = (((0,), (0,)), ((), ()))
    scores = (
        lax.dot_general(query, key, contract_last, preferred_element_type=jnp.float32)
        * score_scale
    )
    masked = jnp.where(allowed, scores, -jnp.inf)
    row_top = jnp.maximum(sink, jnp.max(masked, axis=1, keepdims=True))
    row_total = jnp.exp(sink - row_top) + jnp.sum(
        jnp.exp(masked - row_top), axis=1, keepdims=True
    )
    log_total = row_top + jnp.log(row_total)
    probs = jnp.exp(masked - log_total)
    weights = probs.astype(jnp.bfloat16)
    attended = jnp.dot(weights, value, preferred_element_type=jnp.float32).astype(jnp.bfloat16)
    row_delta = jnp.sum(
        grad.astype(jnp.float32) * attended.astype(jnp.float32), axis=1, keepdims=True
    )
    dprob = lax.dot_general(grad, value, contract_last, preferred_element_type=jnp.float32)
    dscore = (probs * (dprob - row_delta)).astype(jnp.bfloat16)
    dquery = jnp.dot(dscore, key, preferred_element_type=jnp.float32) * score_scale
    dk_ref[0] = (
        lax.dot_general(dscore, query, contract_first, preferred_element_type=jnp.float32)
        * score_scale
    )
    dv_ref[0] = lax.dot_general(weights, grad, contract_first, preferred_element_type=jnp.float32)
    sink_share = jnp.exp(sink - log_total) * row_delta
    for h in range(GROUP):
        part = slice(h * rows, (h + 1) * rows)
        o_ref[0, :, heads[h]] = attended[part]
        dq_ref[0, :, heads[h]] = dquery[part].astype(jnp.bfloat16)
        total = -jnp.sum(sink_share[part], axis=0, keepdims=True)
        st_ref[0, 0, pl.ds(h, 1), :] = jnp.broadcast_to(total, (1, 128))


def attend_blocks(sink_logit, queries, out_grad, window, allowed):
    lanes, rows, query_width = queries.shape
    span = window.shape[1]
    group_width = GROUP * HEAD_DIM
    lane_rows = lambda lane, group: (lane, 0, group)
    flops = 2 * lanes * HEADS * rows * span * HEAD_DIM * 6
    moved = 2 * (4 * queries.size + 2 * window.size) + 4 * allowed.size + 8 * window.size
    return pl.pallas_call(
        group_kernel,
        grid=(lanes, KV_HEADS),
        in_specs=[
            pl.BlockSpec(memory_space=pltpu.SMEM),
            pl.BlockSpec((1, rows, group_width), lane_rows),
            pl.BlockSpec((1, rows, group_width), lane_rows),
            pl.BlockSpec((1, span, HEAD_DIM), lane_rows),
            pl.BlockSpec((1, span, HEAD_DIM), lambda lane, group: (lane, 0, KV_HEADS + group)),
            pl.BlockSpec((1, rows, span), lambda lane, group: (lane, 0, 0)),
        ],
        out_specs=[
            pl.BlockSpec((1, rows, group_width), lane_rows),
            pl.BlockSpec((1, rows, group_width), lane_rows),
            pl.BlockSpec((1, span, HEAD_DIM), lane_rows),
            pl.BlockSpec((1, span, HEAD_DIM), lane_rows),
            pl.BlockSpec((1, 1, GROUP, 128), lambda lane, group: (lane, group, 0, 0)),
        ],
        out_shape=[
            jax.ShapeDtypeStruct((lanes, rows, query_width), jnp.bfloat16),
            jax.ShapeDtypeStruct((lanes, rows, query_width), jnp.bfloat16),
            jax.ShapeDtypeStruct((lanes, span, KV_HEADS * HEAD_DIM), jnp.float32),
            jax.ShapeDtypeStruct((lanes, span, KV_HEADS * HEAD_DIM), jnp.float32),
            jax.ShapeDtypeStruct((lanes, KV_HEADS, GROUP, 128), jnp.float32),
        ],
        cost_estimate=pl.CostEstimate(
            flops=flops, transcendentals=2 * lanes * HEADS * rows * span, bytes_accessed=moved
        ),
    )(sink_logit, queries, out_grad, window, window, allowed)

def per_device(queries, keys, values, doc_bounds, sink_logit, out_grad):
    block_rows = queries.shape[3]
    query_width = queries.shape[4]
    value_width = keys.shape[4]
    pair_count = lax.axis_size("ctx")
    my_index = lax.axis_index("ctx")
    score_scale = 1.0 / math.sqrt(HEAD_DIM)
    at_fold = my_index == pair_count - 1
    last_block = 2 * pair_count - 1
    span = (REACH + 1) * block_rows

    own_pair = jnp.concatenate(
        [keys.reshape(2, block_rows, value_width), values.reshape(2, block_rows, value_width)], axis=2
    )
    send0, send1 = lax.optimization_barrier((own_pair[0], own_pair[1]))
    prev0 = shift_up(send0, "ctx")
    prev1 = shift_down(send1, "ctx")
    prev1 = jnp.where(at_fold, own_pair[0], prev1)
    prev_pair = jnp.stack([prev0, prev1])
    window = jnp.concatenate([prev_pair, own_pair], axis=1)

    lane_block = jnp.stack([my_index, last_block - my_index]).astype(jnp.int32)
    row_offsets = jnp.arange(block_rows, dtype=jnp.int32)
    window_offsets = jnp.arange(span, dtype=jnp.int32)
    query_pos = lane_block[:, None] * block_rows + row_offsets[None, :]
    key_pos = (lane_block[:, None] - REACH) * block_rows + window_offsets[None, :]
    first_pos = doc_bounds.reshape(2, 2, block_rows)[:, 0]
    allowed = (key_pos[:, None, :] <= query_pos[:, :, None]) & (
        key_pos[:, None, :] >= first_pos[:, :, None]
    )
    attended, dquery, key_part, value_part, sink_parts = attend_blocks(
        sink_logit,
        queries.reshape(2, block_rows, query_width),
        out_grad.reshape(2, block_rows, query_width),
        window,
        allowed.astype(jnp.float32),
    )
    sink_terms = jnp.sum(sink_parts[:, :, :, 0], axis=0)
    sink_grad = all_sum(sink_terms.reshape(HEADS), ("ctx", "dp"))
    partial = jnp.concatenate([key_part, value_part], axis=2)

    prev_part = partial[:, :block_rows].astype(jnp.bfloat16)
    send0, send1 = lax.optimization_barrier((prev_part[0], prev_part[1]))
    into0 = shift_down(send0, "ctx")
    into1 = shift_up(send1, "ctx")
    into0 = jnp.where(at_fold, prev_part[1], into0)
    own_part = partial[:, block_rows:]
    gathered = own_part + jnp.stack([into0, into1]).astype(jnp.float32)

    out_shape = (1, 1, 2, block_rows, query_width)
    pair_out = (1, 1, 2, block_rows, value_width)
    attn_out = attended.reshape(out_shape)
    query_grad = dquery.reshape(out_shape)
    key_grad = gathered[:, :, :value_width].astype(jnp.bfloat16).reshape(pair_out)
    value_grad = gathered[:, :, value_width:].astype(jnp.bfloat16).reshape(pair_out)
    return (attn_out, query_grad, key_grad, value_grad, sink_grad)


def solution(mesh):
    in_specs = (
        P("dp", "ctx", None, None, None),
        P("dp", "ctx", None, None, None),
        P("dp", "ctx", None, None, None),
        P("dp", "ctx", None, None, None),
        P(),
        P("dp", "ctx", None, None, None),
    )
    out_specs = (
        P("dp", "ctx", None, None, None),
        P("dp", "ctx", None, None, None),
        P("dp", "ctx", None, None, None),
        P("dp", "ctx", None, None, None),
        P(),
    )
    return jax.shard_map(
        per_device, mesh=mesh, in_specs=in_specs, out_specs=out_specs, check_vma=False
    )
```

time: 60 us -> 44.9 us (0.75)
  the two profiles are of different devices: /device:TPU:8 before, /device:TPU:0 now
where the time goes in v4:
time: 44.9 us; the launch traced here: 44.1 us
  starting transfers between devices  19.2 us (43%)
  Pallas kernels  9.22 us (21%)
  waiting for transfers between devices  8 us (18%)
  other arithmetic  3.55 us (8%)
  local copies, waits for them, and re-layouts  3.29 us (7%)
  between operations  0.8 us (2%)
    pallas_call x1, Pallas kernels, attend_blocks(): pl.pallas_call(group_kernel, grid=(lanes, KV_HEADS), in_specs=[pl.BlockSp...  9.22 us
    ppermute x2, starting transfers between devices, shift_up(): return lax.ppermute(x, axis, [(i, i + 1) for i in range(size - 1)])  8.53 us
    all_to_all x1, starting transfers between devices, all_sum(): return jnp.sum(lax.all_to_all(spread, axes, 0, 0, tiled=True), axis=0)  8.09 us
    ppermute x2, waiting for transfers between devices, shift_down(): return lax.ppermute(x, axis, [(i + 1, i) for i in range(size - 1)])  4.61 us
    all_to_all x1, waiting for transfers between devices, all_sum(): return jnp.sum(lax.all_to_all(spread, axes, 0, 0, tiled=True), axis=0)  3.39 us
    ppermute x2, starting transfers between devices, shift_down(): return lax.ppermute(x, axis, [(i + 1, i) for i in range(size - 1)])  2.58 us
    unnamed x11, local copies, waits for them, and re-layouts  1.81 us
    squeeze x1, other arithmetic, per_device(): send0, send1 = lax.optimization_barrier((own_pair[0], own_pair[1]))  0.96 us
  transfers between devices with their start and end apart: 5, of which 2 were waited for; matrix products, arithmetic and copies ran while one was open for 5% of the time, Pallas kernels for 0%

profile of v4, /device:TPU:0, one launch (start us, length us, event | category | flops | bytes accessed | tf_op | source)
XLA Modules:
  0.0 44.1 jit_solution(3897775634185695192)
XLA Ops:
  0.6 1.0 %fusion.3 = (bf16[64,1024]{1,0:T(8,128)(2,1)S(1)}, bf16[64,1024]{1,0:T(8,128)(2,1)S(1)}) fusion(bf16[2,64,512]{2,1,0:T(8,128)(2,1)} %bitcast.33, bf16[2,64,512]{2,1,0:T(8,128)(2,1)} %bitcast.35), kind=kLoop, calls=%fused_computation.12 | loop fusion | flops 524288 | bytes 524288 | tf_op jit(solution)/shard_map/squeeze | solution.py:137
  1.6 4.8 %collective-permute-start = (bf16[64,1024]{1,0:T(8,128)(2,1)S(1)}, bf16[64,1024]{1,0:T(8,128)(2,1)S(1)}, u32[]{:S(2)}, u32[]{:S(2)}) collective-permute-start(bf16[64,1024]{1,0:T(8,128)(2,1)S(1)} %get-tuple-element.14), channel_id=1, source_target_pairs={{0,2},{2,4},{4,6},{6,8},{8,10},{10,12},{12,14},{14,16},{16,18},{18... | collective-permute-start | bytes 393224 | tf_op jit(solution)/shard_map/ppermute | solution.py:19
  6.5 1.3 %collective-permute-start.1 = (bf16[64,1024]{1,0:T(8,128)(2,1)S(1)}, bf16[64,1024]{1,0:T(8,128)(2,1)S(1)}, u32[]{:S(2)}, u32[]{:S(2)}) collective-permute-start(bf16[64,1024]{1,0:T(8,128)(2,1)S(1)} %get-tuple-element.15), channel_id=1, source_target_pairs={{2,0},{4,2},{6,4},{8,6},{10,8},{12,10},{14,12},{16,14},{18,16},{20... | collective-permute-start | bytes 393224 | tf_op jit(solution)/shard_map/ppermute | solution.py:24
  7.8 0.1 add_multiply_fusion
  7.8 0.1 iota_add_fusion.1
  7.9 0.1 iota_add_fusion
  8.0 0.6 %copy-done.4 = s32[1,1,2,2,64]{4,3,2,1,0:T(2,128)S(1)} copy-done((s32[1,1,2,2,64]{4,3,2,1,0:T(2,128)S(1)}, s32[1,1,2,2,64]{4,3,2,1,0:T(2,128)}, u32[]{:S(2)}) %copy-start.4) | copy-done | bytes 1048
  8.6 0.7 %and_convert_fusion.allow_ref = f32[2,64,128]{2,1,0:T(8,128)} fusion(s32[2,64]{1,0:T(2,128)S(1)} %bitcast.40, s32[2,64]{1,0:T(2,128)S(1)} %iota_add_fusion, s32[2,128]{1,0:T(2,128)S(1)} %iota_add_fusion.1), kind=kLoop, calls=%fused_computation.15 | loop fusion | flops 65536 | bytes 67584 | tf_op jit(solution)/shard_map/convert_element_type | solution.py:158
  9.3 4.6 %collective-permute-done.1 = bf16[64,1024]{1,0:T(8,128)(2,1)S(1)} collective-permute-done((bf16[64,1024]{1,0:T(8,128)(2,1)S(1)}, bf16[64,1024]{1,0:T(8,128)(2,1)S(1)}, u32[]{:S(2)}, u32[]{:S(2)}) %collective-permute-start.1) | collective-permute-done | bytes 131104 | tf_op jit(solution)/shard_map/ppermute | solution.py:24
  14.0 0.0 collective-permute-done
  14.0 0.0 copy-done.1
  14.0 0.0 copy-done.2
  14.0 0.8 %maximum_maximum_fusion.k_ref.v_ref = bf16[2,128,1024]{2,1,0:T(8,128)(2,1)} fusion(bf16[2,64,512]{2,1,0:T(8,128)(2,1)S(1)} %bitcast.34, bf16[2,64,512]{2,1,0:T(8,128)(2,1)S(1)} %bitcast.36, bf16[1,64,1024]{2,1,0:T(8,128)(2,1)S(1)} %select_bitcast_fusion.1, bf16[1,64,1024]{2,1,0:T(8,128)(2,1)S(1)} %bitcast.37), kind=kLoop, calls=%fused_computation.2 | loop fusion | flops 2097152 | bytes 1048576 | tf_op jit(solution)/shard_map/concatenate | solution.py:142
  14.8 9.2 %shard_map.101 = (bf16[2,64,4096]{2,1,0:T(8,128)(2,1)}, bf16[2,64,4096]{2,1,0:T(8,128)(2,1)}, f32[2,128,512]{2,1,0:T(8,128)}, f32[2,128,512]{2,1,0:T(8,128)}, f32[2,4,8,128]{3,2,1,0:T(8,128)}) custom-call(f32[32]{0:T(128)} %sink_ref.1, bf16[2,64,4096]{2,1,0:T(8,128)(2,1)} %bitcast.31, bf16[2,64,4096]{2,1,0:T(8,128)(2,1)} %bitcast.32, ...), custom_call_target="tpu_custom_call" | custom-call | flops 805306368 | bytes 7405568 | tf_op jit(solution)/shard_map/pallas_call | solution.py:93
  24.1 0.0 copy-start
  24.1 1.1 %constant_dynamic-update-slice_fusion.1 = f32[2,128,1024]{2,1,0:T(8,128)S(1)} fusion(f32[2,128,512]{2,1,0:T(8,128)} %get-tuple-element.18), kind=kLoop, calls=%fused_computation.18 | loop fusion | bytes 1048576
  25.2 0.0 copy-done
  25.3 0.1 convert.7
  25.4 0.0 copy-start.3
  25.4 1.3 %collective-permute-start.2 = (bf16[64,1024]{1,0:T(8,128)(2,1)S(1)}, bf16[64,1024]{1,0:T(8,128)(2,1)S(1)}, u32[]{:S(2)}, u32[]{:S(2)}) collective-permute-start(bf16[64,1024]{1,0:T(8,128)(2,1)S(1)} %get-tuple-element.20), channel_id=1, source_target_pairs={{2,0},{4,2},{6,4},{8,6},{10,8},{12,10},{14,12},{16,14},{18,16},{20... | collective-permute-start | bytes 393224 | tf_op jit(solution)/shard_map/ppermute | solution.py:24
  26.7 0.0 copy-done.3
  26.7 0.1 slice_reduce_fusion
  26.8 0.1 broadcast_in_dim.4
  26.9 0.6 %broadcast_in_dim.5 = f32[32,1,32]{2,1,0:T(1,128)} broadcast(f32[32]{0:T(128)S(1)} %broadcast_in_dim.4), dimensions={2} | broadcast | bytes 4224 | tf_op jit(solution)/shard_map/broadcast_in_dim | solution.py:31
  27.5 8.1 %all-to-all-start = ((f32[32,1,32]{2,1,0:T(1,128)}), f32[32,1,32]{2,1,0:T(1,128)S(1)}, u32[]{:S(2)}, u32[]{:S(2)}) async-start(f32[32,1,32]{2,1,0:T(1,128)} %broadcast_in_dim.5), calls=%async_computation | async-start | bytes 32768 | tf_op jit(solution)/shard_map/all_to_all | solution.py:32
  35.6 3.7 %collective-permute-start.3 = (bf16[64,1024]{1,0:T(8,128)(2,1)S(1)}, bf16[64,1024]{1,0:T(8,128)(2,1)S(1)}, u32[]{:S(2)}, u32[]{:S(2)}) collective-permute-start(bf16[64,1024]{1,0:T(8,128)(2,1)S(1)} %get-tuple-element.21), channel_id=1, source_target_pairs={{0,2},{2,4},{4,6},{6,8},{8,10},{10,12},{12,14},{14,16},{16,18},{18... | collective-permute-start | bytes 393224 | tf_op jit(solution)/shard_map/ppermute | solution.py:19
  39.3 3.4 %all-to-all-done = f32[32,1,32]{2,1,0:T(1,128)S(1)} async-done(((f32[32,1,32]{2,1,0:T(1,128)}), f32[32,1,32]{2,1,0:T(1,128)S(1)}, u32[]{:S(2)}, u32[]{:S(2)}) %all-to-all-start) | async-done | bytes 4128 | tf_op jit(solution)/shard_map/all_to_all | solution.py:32
  42.7 0.5 %reduce_sum.19 = f32[32]{0:T(128)} reduce(f32[32,1,32]{2,0,1:T(8,128)S(1)} %bitcast.39, f32[]{:T(128)} %constant.16.clone.1), dimensions={0,1}, to_apply=%region_1.2 | reduce | flops 992 | bytes 4228 | tf_op jit(solution)/shard_map/reduce_sum | solution.py:32
  43.2 0.0 collective-permute-done.2
  43.3 0.0 collective-permute-done.3
  43.3 0.1 fusion
  43.3 0.7 %slice_bitcast_fusion = (bf16[1,1,2,64,512]{4,3,2,1,0:T(8,128)(2,1)}, bf16[1,1,2,64,512]{4,3,2,1,0:T(8,128)(2,1)}) fusion(bf16[2,64,1024]{2,1,0:T(8,128)(2,1)S(1)} %fusion), kind=kLoop, calls=%fused_computation.7 | loop fusion | bytes 524288 | tf_op jit(solution)/shard_map/reshape | solution.py:177
  (8 shorter events, 0.1 us)
Async XLA Ops:
  1.6 12.4 %collective-permute-start = (bf16[64,1024]{1,0:T(8,128)(2,1)S(1)}, bf16[64,1024]{1,0:T(8,128)(2,1)S(1)}, u32[]{:S(2)}, u32[]{:S(2)}) collective-permute-start(bf16[64,1024]{1,0:T(8,128)(2,1)S(1)} %get-tuple-element.14), channel_id=1, source_target_pairs={{0,2},{2,4},{4,6},{6,8},{8,10},{10,12},{12,14},{14,16},{16,18},{18... | collective-permute-start | bytes 393224 | tf_op jit(solution)/shard_map/ppermute | solution.py:19
  6.5 7.5 %collective-permute-start.1 = (bf16[64,1024]{1,0:T(8,128)(2,1)S(1)}, bf16[64,1024]{1,0:T(8,128)(2,1)S(1)}, u32[]{:S(2)}, u32[]{:S(2)}) collective-permute-start(bf16[64,1024]{1,0:T(8,128)(2,1)S(1)} %get-tuple-element.15), channel_id=1, source_target_pairs={{2,0},{4,2},{6,4},{8,6},{10,8},{12,10},{14,12},{16,14},{18,16},{20... | collective-permute-start | bytes 393224 | tf_op jit(solution)/shard_map/ppermute | solution.py:24
  7.9 0.7 %copy-start.4 = (s32[1,1,2,2,64]{4,3,2,1,0:T(2,128)S(1)}, s32[1,1,2,2,64]{4,3,2,1,0:T(2,128)}, u32[]{:S(2)}) copy-start(s32[1,1,2,2,64]{4,3,2,1,0:T(2,128)} %param.9) | copy-start | bytes 3076
  9.3 4.6 %copy-start.1 = (bf16[1,1,2,64,512]{4,3,2,1,0:T(8,128)(2,1)S(1)}, bf16[1,1,2,64,512]{4,3,2,1,0:T(8,128)(2,1)}, u32[]{:S(2)}) copy-start(bf16[1,1,2,64,512]{4,3,2,1,0:T(8,128)(2,1)} %param.8) | copy-start | bytes 393220
  9.3 4.6 %copy-start.2 = (bf16[1,1,2,64,512]{4,3,2,1,0:T(8,128)(2,1)S(1)}, bf16[1,1,2,64,512]{4,3,2,1,0:T(8,128)(2,1)}, u32[]{:S(2)}) copy-start(bf16[1,1,2,64,512]{4,3,2,1,0:T(8,128)(2,1)} %param.7) | copy-start | bytes 393220
  24.1 1.2 %copy-start = (f32[2,128,512]{2,1,0:T(8,128)S(1)}, f32[2,128,512]{2,1,0:T(8,128)}, u32[]{:S(2)}) copy-start(f32[2,128,512]{2,1,0:T(8,128)} %get-tuple-element.19) | copy-start | bytes 1572868
  25.4 1.3 %copy-start.3 = (f32[2,4,8,128]{3,2,1,0:T(8,128)S(1)}, f32[2,4,8,128]{3,2,1,0:T(8,128)}, u32[]{:S(2)}) copy-start(f32[2,4,8,128]{3,2,1,0:T(8,128)} %get-tuple-element.22) | copy-start | bytes 98308
  25.4 17.8 %collective-permute-start.2 = (bf16[64,1024]{1,0:T(8,128)(2,1)S(1)}, bf16[64,1024]{1,0:T(8,128)(2,1)S(1)}, u32[]{:S(2)}, u32[]{:S(2)}) collective-permute-start(bf16[64,1024]{1,0:T(8,128)(2,1)S(1)} %get-tuple-element.20), channel_id=1, source_target_pairs={{2,0},{4,2},{6,4},{8,6},{10,8},{12,10},{14,12},{16,14},{18,16},{20... | collective-permute-start | bytes 393224 | tf_op jit(solution)/shard_map/ppermute | solution.py:24
  27.5 15.2 %all-to-all-start = ((f32[32,1,32]{2,1,0:T(1,128)}), f32[32,1,32]{2,1,0:T(1,128)S(1)}, u32[]{:S(2)}, u32[]{:S(2)}) async-start(f32[32,1,32]{2,1,0:T(1,128)} %broadcast_in_dim.5), calls=%async_computation | async-start | bytes 32768 | tf_op jit(solution)/shard_map/all_to_all | solution.py:32
  35.6 7.6 %collective-permute-start.3 = (bf16[64,1024]{1,0:T(8,128)(2,1)S(1)}, bf16[64,1024]{1,0:T(8,128)(2,1)S(1)}, u32[]{:S(2)}, u32[]{:S(2)}) collective-permute-start(bf16[64,1024]{1,0:T(8,128)(2,1)S(1)} %get-tuple-element.21), channel_id=1, source_target_pairs={{0,2},{2,4},{4,6},{6,8},{8,10},{10,12},{12,14},{14,16},{16,18},{18... | collective-permute-start | bytes 393224 | tf_op jit(solution)/shard_map/ppermute | solution.py:19

commit v5 on v4

--- a/solution.py
+++ b/solution.py
@@ -33,7 +33,7 @@
 
 
 def group_kernel(
-    sink_ref, q_ref, g_ref, k_ref, v_ref, allow_ref, o_ref, dq_ref, dk_ref, dv_ref, st_ref
+    sink_ref, q_ref, g_ref, k_ref, v_ref, allow_ref, o_ref, dq_ref, msg_ref, own_ref, st_ref
 ):
     group = pl.program_id(1)
     rows = q_ref.shape[1]
@@ -69,18 +69,30 @@
     dprob = lax.dot_general(grad, value, contract_last, preferred_element_type=jnp.float32)
     dscore = (probs * (dprob - row_delta)).astype(jnp.bfloat16)
     dquery = jnp.dot(dscore, key, preferred_element_type=jnp.float32) * score_scale
-    dk_ref[0] = (
+    dkey = (
         lax.dot_general(dscore, query, contract_first, preferred_element_type=jnp.float32)
         * score_scale
     )
-    dv_ref[0] = lax.dot_general(weights, grad, contract_first, preferred_element_type=jnp.float32)
+    dvalue = lax.dot_general(weights, grad, contract_first, preferred_element_type=jnp.float32)
+    msg_ref[0, :, pl.ds(0, HEAD_DIM)] = dkey[:rows].astype(jnp.bfloat16)
+    msg_ref[0, :, pl.ds(HEAD_DIM, HEAD_DIM)] = dvalue[:rows].astype(jnp.bfloat16)
+    own_ref[0, :, pl.ds(0, HEAD_DIM)] = dkey[rows:]
+    own_ref[0, :, pl.ds(HEAD_DIM, HEAD_DIM)] = dvalue[rows:]
     sink_share = jnp.exp(sink - log_total) * row_delta
+    lane = lax.broadcasted_iota(jnp.int32, (1, 128), 1)
+    sink_row = jnp.zeros((1, 128), jnp.float32)
     for h in range(GROUP):
         part = slice(h * rows, (h + 1) * rows)
         o_ref[0, :, heads[h]] = attended[part]
         dq_ref[0, :, heads[h]] = dquery[part].astype(jnp.bfloat16)
         total = -jnp.sum(sink_share[part], axis=0, keepdims=True)
-        st_ref[0, 0, pl.ds(h, 1), :] = jnp.broadcast_to(total, (1, 128))
+        sink_row = jnp.where(lane == group * GROUP + h, total, sink_row)
+
+    @pl.when((pl.program_id(0) == 0) & (group == 0))
+    def _():
+        st_ref[...] = jnp.zeros_like(st_ref)
+
+    st_ref[pl.ds(0, 1), :] += sink_row
 
 
 def attend_blocks(sink_logit, queries, out_grad, window, allowed):
@@ -104,16 +116,16 @@
         out_specs=[
             pl.BlockSpec((1, rows, group_width), lane_rows),
             pl.BlockSpec((1, rows, group_width), lane_rows),
-            pl.BlockSpec((1, span, HEAD_DIM), lane_rows),
-            pl.BlockSpec((1, span, HEAD_DIM), lane_rows),
-            pl.BlockSpec((1, 1, GROUP, 128), lambda lane, group: (lane, group, 0, 0)),
+            pl.BlockSpec((1, rows, 2 * HEAD_DIM), lane_rows),
+            pl.BlockSpec((1, rows, 2 * HEAD_DIM), lane_rows),
+            pl.BlockSpec((8, 128), lambda lane, group: (0, 0)),
         ],
         out_shape=[
             jax.ShapeDtypeStruct((lanes, rows, query_width), jnp.bfloat16),
             jax.ShapeDtypeStruct((lanes, rows, query_width), jnp.bfloat16),
-            jax.ShapeDtypeStruct((lanes, span, KV_HEADS * HEAD_DIM), jnp.float32),
-            jax.ShapeDtypeStruct((lanes, span, KV_HEADS * HEAD_DIM), jnp.float32),
-            jax.ShapeDtypeStruct((lanes, KV_HEADS, GROUP, 128), jnp.float32),
+            jax.ShapeDtypeStruct((lanes, rows, 2 * KV_HEADS * HEAD_DIM), jnp.bfloat16),
+            jax.ShapeDtypeStruct((lanes, rows, 2 * KV_HEADS * HEAD_DIM), jnp.float32),
+            jax.ShapeDtypeStruct((8, 128), jnp.float32),
         ],
         cost_estimate=pl.CostEstimate(
             flops=flops, transcendentals=2 * lanes * HEADS * rows * span, bytes_accessed=moved
@@ -150,31 +162,28 @@
     allowed = (key_pos[:, None, :] <= query_pos[:, :, None]) & (
         key_pos[:, None, :] >= first_pos[:, :, None]
     )
-    attended, dquery, key_part, value_part, sink_parts = attend_blocks(
+    attended, dquery, message, own_part, sink_row = attend_blocks(
         sink_logit,
         queries.reshape(2, block_rows, query_width),
         out_grad.reshape(2, block_rows, query_width),
         window,
         allowed.astype(jnp.float32),
     )
-    sink_terms = jnp.sum(sink_parts[:, :, :, 0], axis=0)
-    sink_grad = all_sum(sink_terms.reshape(HEADS), ("ctx", "dp"))
-    partial = jnp.concatenate([key_part, value_part], axis=2)
-
-    prev_part = partial[:, :block_rows].astype(jnp.bfloat16)
-    send0, send1 = lax.optimization_barrier((prev_part[0], prev_part[1]))
+    sink_grad = all_sum(sink_row[0, :HEADS], ("ctx", "dp"))
+
+    send0, send1 = lax.optimization_barrier((message[0], message[1]))
     into0 = shift_down(send0, "ctx")
     into1 = shift_up(send1, "ctx")
-    into0 = jnp.where(at_fold, prev_part[1], into0)
-    own_part = partial[:, block_rows:]
+    into0 = jnp.where(at_fold, message[1], into0)
     gathered = own_part + jnp.stack([into0, into1]).astype(jnp.float32)
+    gathered = gathered.reshape(2, block_rows, KV_HEADS, 2, HEAD_DIM)
 
     out_shape = (1, 1, 2, block_rows, query_width)
     pair_out = (1, 1, 2, block_rows, value_width)
     attn_out = attended.reshape(out_shape)
     query_grad = dquery.reshape(out_shape)
-    key_grad = gathered[:, :, :value_width].astype(jnp.bfloat16).reshape(pair_out)
-    value_grad = gathered[:, :, value_width:].astype(jnp.bfloat16).reshape(pair_out)
+    key_grad = gathered[:, :, :, 0].astype(jnp.bfloat16).reshape(pair_out)
+    value_grad = gathered[:, :, :, 1].astype(jnp.bfloat16).reshape(pair_out)
     return (attn_out, query_grad, key_grad, value_grad, sink_grad)
 
 

time: 44.9 us -> 48 us (1.069)
  local copies, waits for them, and re-layouts: 3.29 us -> 6.06 us
  Pallas kernels: 9.22 us -> 9.72 us
    slice x0 -> x2, local copies, waits for them, and re-layouts: none -> 2.16 us  [the longest x1 1.47 us: per_device(): value_grad = gathered[:, :, :, 1].astype(jnp.bfloat16).reshape(pair_out)]
    convert_element_type x0 -> x2, local copies, waits for them, and re-layouts: none -> 1.42 us  [the longest x1 0.71 us: per_device(): value_grad = gathered[:, :, :, 1].astype(jnp.bfloat16).reshape(pair_out)]
    unnamed x11 -> x10, local copies, waits for them, and re-layouts: 1.81 us -> 0.63 us
    squeeze x1, local copies, waits for them, and re-layouts: 0.02 us -> 1.06 us  [per_device(): into0 = jnp.where(at_fold, message[1], into0)]
    reshape x1 -> x0, local copies, waits for them, and re-layouts: 0.72 us -> none  [per_device(): gathered[:, :, value_width:].astype(jnp.bfloat16).reshape(pair_out)]
    pallas_call x1, Pallas kernels: 9.22 us -> 9.72 us  [attend_blocks(): pl.pallas_call(group_kernel, grid=(lanes, KV_HEADS), in_specs=[pl.BlockSp...]
  transfers between devices with their start and end apart: 5 -> 5, of which waited for: 2 -> 2; matrix products, arithmetic and copies ran while one was open for 5% -> 6% of each run, Pallas kernels for 0% -> 0%
where the time goes in v5:
time: 48 us; the launch traced here: 47.1 us
  starting transfers between devices  19.2 us (40%)
  Pallas kernels  9.72 us (20%)
  waiting for transfers between devices  8 us (17%)
  local copies, waits for them, and re-layouts  6.06 us (13%)
  other arithmetic  3.38 us (7%)
  between operations  0.78 us (2%)
    pallas_call x1, Pallas kernels, attend_blocks(): pl.pallas_call(group_kernel, grid=(lanes, KV_HEADS), in_specs=[pl.BlockSp...  9.72 us
    ppermute x2, starting transfers between devices, shift_up(): return lax.ppermute(x, axis, [(i, i + 1) for i in range(size - 1)])  8.53 us
    all_to_all x1, starting transfers between devices, all_sum(): return jnp.sum(lax.all_to_all(spread, axes, 0, 0, tiled=True), axis=0)  8.09 us
    ppermute x2, waiting for transfers between devices, shift_down(): return lax.ppermute(x, axis, [(i + 1, i) for i in range(size - 1)])  4.61 us
    all_to_all x1, waiting for transfers between devices, all_sum(): return jnp.sum(lax.all_to_all(spread, axes, 0, 0, tiled=True), axis=0)  3.39 us
    ppermute x2, starting transfers between devices, shift_down(): return lax.ppermute(x, axis, [(i + 1, i) for i in range(size - 1)])  2.58 us
    slice x1, local copies, waits for them, and re-layouts, per_device(): value_grad = gathered[:, :, :, 1].astype(jnp.bfloat16).reshape(pair_out)  1.47 us
    squeeze x1, local copies, waits for them, and re-layouts, per_device(): into0 = jnp.where(at_fold, message[1], into0)  1.06 us
  transfers between devices with their start and end apart: 5, of which 2 were waited for; matrix products, arithmetic and copies ran while one was open for 6% of the time, Pallas kernels for 0%

profile of v5, /device:TPU:0, one launch (start us, length us, event | category | flops | bytes accessed | tf_op | source)
XLA Modules:
  0.0 47.1 jit_solution(223221265024727609)
XLA Ops:
  0.6 1.0 %fusion.2 = (bf16[64,1024]{1,0:T(8,128)(2,1)S(1)}, bf16[64,1024]{1,0:T(8,128)(2,1)S(1)}) fusion(bf16[2,64,512]{2,1,0:T(8,128)(2,1)} %bitcast.31, bf16[2,64,512]{2,1,0:T(8,128)(2,1)} %bitcast.33), kind=kLoop, calls=%fused_computation.9 | loop fusion | flops 524288 | bytes 524288 | tf_op jit(solution)/shard_map/squeeze | solution.py:149
  1.6 4.8 %collective-permute-start = (bf16[64,1024]{1,0:T(8,128)(2,1)S(1)}, bf16[64,1024]{1,0:T(8,128)(2,1)S(1)}, u32[]{:S(2)}, u32[]{:S(2)}) collective-permute-start(bf16[64,1024]{1,0:T(8,128)(2,1)S(1)} %get-tuple-element.14), channel_id=1, source_target_pairs={{0,2},{2,4},{4,6},{6,8},{8,10},{10,12},{12,14},{14,16},{16,18},{18... | collective-permute-start | bytes 393224 | tf_op jit(solution)/shard_map/ppermute | solution.py:19
  6.5 1.3 %collective-permute-start.1 = (bf16[64,1024]{1,0:T(8,128)(2,1)S(1)}, bf16[64,1024]{1,0:T(8,128)(2,1)S(1)}, u32[]{:S(2)}, u32[]{:S(2)}) collective-permute-start(bf16[64,1024]{1,0:T(8,128)(2,1)S(1)} %get-tuple-element.15), channel_id=1, source_target_pairs={{2,0},{4,2},{6,4},{8,6},{10,8},{12,10},{14,12},{16,14},{18,16},{20... | collective-permute-start | bytes 393224 | tf_op jit(solution)/shard_map/ppermute | solution.py:24
  7.8 0.1 add_multiply_fusion
  7.8 0.1 iota_add_fusion.1
  7.9 0.1 iota_add_fusion
  8.0 0.6 %copy-done.4 = s32[1,1,2,2,64]{4,3,2,1,0:T(2,128)S(1)} copy-done((s32[1,1,2,2,64]{4,3,2,1,0:T(2,128)S(1)}, s32[1,1,2,2,64]{4,3,2,1,0:T(2,128)}, u32[]{:S(2)}) %copy-start.4) | copy-done | bytes 1048
  8.6 0.7 %and_convert_fusion.allow_ref = f32[2,64,128]{2,1,0:T(8,128)} fusion(s32[2,64]{1,0:T(2,128)S(1)} %bitcast.38, s32[2,64]{1,0:T(2,128)S(1)} %iota_add_fusion, s32[2,128]{1,0:T(2,128)S(1)} %iota_add_fusion.1), kind=kLoop, calls=%fused_computation.14 | loop fusion | flops 65536 | bytes 67584 | tf_op jit(solution)/shard_map/convert_element_type | solution.py:170
  9.3 4.6 %collective-permute-done.1 = bf16[64,1024]{1,0:T(8,128)(2,1)S(1)} collective-permute-done((bf16[64,1024]{1,0:T(8,128)(2,1)S(1)}, bf16[64,1024]{1,0:T(8,128)(2,1)S(1)}, u32[]{:S(2)}, u32[]{:S(2)}) %collective-permute-start.1) | collective-permute-done | bytes 131104 | tf_op jit(solution)/shard_map/ppermute | solution.py:24
  14.0 0.0 collective-permute-done
  14.0 0.0 copy-done.2
  14.0 0.0 copy-done.3
  14.0 0.8 %maximum_maximum_fusion.k_ref.v_ref = bf16[2,128,1024]{2,1,0:T(8,128)(2,1)} fusion(bf16[2,64,512]{2,1,0:T(8,128)(2,1)S(1)} %bitcast.32, bf16[2,64,512]{2,1,0:T(8,128)(2,1)S(1)} %bitcast.34, bf16[1,64,1024]{2,1,0:T(8,128)(2,1)S(1)} %select_bitcast_fusion.1, bf16[1,64,1024]{2,1,0:T(8,128)(2,1)S(1)} %bitcast.35), kind=kLoop, calls=%fused_computation | loop fusion | flops 2097152 | bytes 1048576 | tf_op jit(solution)/shard_map/concatenate | solution.py:154
  14.8 9.7 %shard_map.101 = (bf16[2,64,4096]{2,1,0:T(8,128)(2,1)}, bf16[2,64,4096]{2,1,0:T(8,128)(2,1)}, bf16[2,64,1024]{2,1,0:T(8,128)(2,1)}, f32[2,64,1024]{2,1,0:T(8,128)}, f32[8,128]{1,0:T(8,128)}) custom-call(f32[32]{0:T(128)} %sink_ref.1, bf16[2,64,4096]{2,1,0:T(8,128)(2,1)} %bitcast.29, bf16[2,64,4096]{2,1,0:T(8,128)(2,1)} %bitcast.30, ...), custom_call_target="tpu_custom_call" | custom-call | flops 805306368 | bytes 7405568 | tf_op jit(solution)/shard_map/pallas_call | solution.py:105
  24.6 0.0 copy-start.1
  24.6 1.1 %slice_bitcast_fusion.1 = (bf16[64,1024]{1,0:T(8,128)(2,1)S(1)}, bf16[64,1024]{1,0:T(8,128)(2,1)S(1)}) fusion(bf16[2,64,1024]{2,1,0:T(8,128)(2,1)} %get-tuple-element.19), kind=kLoop, calls=%fused_computation.12 | loop fusion | bytes 524288 | tf_op jit(solution)/shard_map/squeeze | solution.py:177
  25.6 1.3 %collective-permute-start.2 = (bf16[64,1024]{1,0:T(8,128)(2,1)S(1)}, bf16[64,1024]{1,0:T(8,128)(2,1)S(1)}, u32[]{:S(2)}, u32[]{:S(2)}) collective-permute-start(bf16[64,1024]{1,0:T(8,128)(2,1)S(1)} %get-tuple-element.20), channel_id=1, source_target_pairs={{2,0},{4,2},{6,4},{8,6},{10,8},{12,10},{14,12},{16,14},{18,16},{20... | collective-permute-start | bytes 393224 | tf_op jit(solution)/shard_map/ppermute | solution.py:24
  26.9 0.7 %slice_bitcast_fusion.2 = f32[32]{0:T(128)S(1)} fusion(f32[8,128]{1,0:T(8,128)} %get-tuple-element.22), kind=kLoop, calls=%fused_computation.18 | loop fusion | bytes 256 | tf_op jit(solution)/shard_map/slice | solution.py:172
  27.6 0.6 %broadcast_in_dim.2 = f32[32,1,32]{2,1,0:T(1,128)} broadcast(f32[32]{0:T(128)S(1)} %slice_bitcast_fusion.2), dimensions={2} | broadcast | bytes 4224 | tf_op jit(solution)/shard_map/broadcast_in_dim | solution.py:31
  28.2 8.1 %all-to-all-start = ((f32[32,1,32]{2,1,0:T(1,128)}), f32[32,1,32]{2,1,0:T(1,128)S(1)}, u32[]{:S(2)}, u32[]{:S(2)}) async-start(f32[32,1,32]{2,1,0:T(1,128)} %broadcast_in_dim.2), calls=%async_computation | async-start | bytes 32768 | tf_op jit(solution)/shard_map/all_to_all | solution.py:32
  36.3 3.7 %collective-permute-start.3 = (bf16[64,1024]{1,0:T(8,128)(2,1)S(1)}, bf16[64,1024]{1,0:T(8,128)(2,1)S(1)}, u32[]{:S(2)}, u32[]{:S(2)}) collective-permute-start(bf16[64,1024]{1,0:T(8,128)(2,1)S(1)} %get-tuple-element.21), channel_id=1, source_target_pairs={{0,2},{2,4},{4,6},{6,8},{8,10},{10,12},{12,14},{14,16},{16,18},{18... | collective-permute-start | bytes 393224 | tf_op jit(solution)/shard_map/ppermute | solution.py:19
  40.0 3.4 %all-to-all-done = f32[32,1,32]{2,1,0:T(1,128)S(1)} async-done(((f32[32,1,32]{2,1,0:T(1,128)}), f32[32,1,32]{2,1,0:T(1,128)S(1)}, u32[]{:S(2)}, u32[]{:S(2)}) %all-to-all-start) | async-done | bytes 4128 | tf_op jit(solution)/shard_map/all_to_all | solution.py:32
  43.4 0.5 %reduce_sum.9 = f32[32]{0:T(128)} reduce(f32[32,1,32]{2,0,1:T(8,128)S(1)} %bitcast.37, f32[]{:T(128)} %constant.16.clone.1), dimensions={0,1}, to_apply=%region_0.1 | reduce | flops 992 | bytes 4228 | tf_op jit(solution)/shard_map/reduce_sum | solution.py:32
  43.9 0.0 collective-permute-done.2
  43.9 0.0 copy-done
  44.0 0.0 collective-permute-done.3
  44.0 0.0 copy-done.1
  44.0 0.1 add_convert_fusion
  44.1 0.2 reshape.148
  44.2 1.5 %slice_reduce_fusion = (bf16[2,64,4,128]{3,2,1,0:T(4,128)(2,1)S(1)}, bf16[2,64,4,128]{3,2,1,0:T(4,128)(2,1)S(1)}) fusion(bf16[2,64,4,2,128]{4,3,2,1,0:T(2,128)(2,1)S(1)} %reshape.148), kind=kLoop, calls=%fused_computation.2 | loop fusion | bytes 524288 | tf_op jit(solution)/shard_map/slice | solution.py:186
  45.7 0.7 %convert_element_type.31 = bf16[1,1,2,64,512]{4,3,2,1,0:T(8,128)(2,1)} reshape(bf16[2,64,4,128]{3,2,1,0:T(4,128)(2,1)S(1)} %get-tuple-element.23) | data formatting | bytes 262144 | tf_op jit(solution)/shard_map/convert_element_type | solution.py:186
  46.4 0.7 %convert_element_type.30 = bf16[1,1,2,64,512]{4,3,2,1,0:T(8,128)(2,1)} reshape(bf16[2,64,4,128]{3,2,1,0:T(4,128)(2,1)S(1)} %get-tuple-element.24) | data formatting | bytes 262144 | tf_op jit(solution)/shard_map/convert_element_type | solution.py:185
  (7 shorter events, 0.0 us)
Async XLA Ops:
  1.6 12.4 %collective-permute-start = (bf16[64,1024]{1,0:T(8,128)(2,1)S(1)}, bf16[64,1024]{1,0:T(8,128)(2,1)S(1)}, u32[]{:S(2)}, u32[]{:S(2)}) collective-permute-start(bf16[64,1024]{1,0:T(8,128)(2,1)S(1)} %get-tuple-element.14), channel_id=1, source_target_pairs={{0,2},{2,4},{4,6},{6,8},{8,10},{10,12},{12,14},{14,16},{16,18},{18... | collective-permute-start | bytes 393224 | tf_op jit(solution)/shard_map/ppermute | solution.py:19
  6.5 7.5 %collective-permute-start.1 = (bf16[64,1024]{1,0:T(8,128)(2,1)S(1)}, bf16[64,1024]{1,0:T(8,128)(2,1)S(1)}, u32[]{:S(2)}, u32[]{:S(2)}) collective-permute-start(bf16[64,1024]{1,0:T(8,128)(2,1)S(1)} %get-tuple-element.15), channel_id=1, source_target_pairs={{2,0},{4,2},{6,4},{8,6},{10,8},{12,10},{14,12},{16,14},{18,16},{20... | collective-permute-start | bytes 393224 | tf_op jit(solution)/shard_map/ppermute | solution.py:24
  7.9 0.7 %copy-start.4 = (s32[1,1,2,2,64]{4,3,2,1,0:T(2,128)S(1)}, s32[1,1,2,2,64]{4,3,2,1,0:T(2,128)}, u32[]{:S(2)}) copy-start(s32[1,1,2,2,64]{4,3,2,1,0:T(2,128)} %param.9) | copy-start | bytes 3076
  9.3 4.6 %copy-start.2 = (bf16[1,1,2,64,512]{4,3,2,1,0:T(8,128)(2,1)S(1)}, bf16[1,1,2,64,512]{4,3,2,1,0:T(8,128)(2,1)}, u32[]{:S(2)}) copy-start(bf16[1,1,2,64,512]{4,3,2,1,0:T(8,128)(2,1)} %param.8) | copy-start | bytes 393220
  9.3 4.6 %copy-start.3 = (bf16[1,1,2,64,512]{4,3,2,1,0:T(8,128)(2,1)S(1)}, bf16[1,1,2,64,512]{4,3,2,1,0:T(8,128)(2,1)}, u32[]{:S(2)}) copy-start(bf16[1,1,2,64,512]{4,3,2,1,0:T(8,128)(2,1)} %param.7) | copy-start | bytes 393220
  24.6 19.4 %copy-start = (bf16[2,64,1024]{2,1,0:T(8,128)(2,1)S(1)}, bf16[2,64,1024]{2,1,0:T(8,128)(2,1)}, u32[]{:S(2)}) copy-start(bf16[2,64,1024]{2,1,0:T(8,128)(2,1)} %get-tuple-element.19) | copy-start | bytes 786436
  24.6 19.4 %copy-start.1 = (f32[2,64,1024]{2,1,0:T(8,128)S(1)}, f32[2,64,1024]{2,1,0:T(8,128)}, u32[]{:S(2)}) copy-start(f32[2,64,1024]{2,1,0:T(8,128)} %get-tuple-element.18) | copy-start | bytes 1572868
  25.6 18.3 %collective-permute-start.2 = (bf16[64,1024]{1,0:T(8,128)(2,1)S(1)}, bf16[64,1024]{1,0:T(8,128)(2,1)S(1)}, u32[]{:S(2)}, u32[]{:S(2)}) collective-permute-start(bf16[64,1024]{1,0:T(8,128)(2,1)S(1)} %get-tuple-element.20), channel_id=1, source_target_pairs={{2,0},{4,2},{6,4},{8,6},{10,8},{12,10},{14,12},{16,14},{18,16},{20... | collective-permute-start | bytes 393224 | tf_op jit(solution)/shard_map/ppermute | solution.py:24
  28.2 15.2 %all-to-all-start = ((f32[32,1,32]{2,1,0:T(1,128)}), f32[32,1,32]{2,1,0:T(1,128)S(1)}, u32[]{:S(2)}, u32[]{:S(2)}) async-start(f32[32,1,32]{2,1,0:T(1,128)} %broadcast_in_dim.2), calls=%async_computation | async-start | bytes 32768 | tf_op jit(solution)/shard_map/all_to_all | solution.py:32
  36.3 7.6 %collective-permute-start.3 = (bf16[64,1024]{1,0:T(8,128)(2,1)S(1)}, bf16[64,1024]{1,0:T(8,128)(2,1)S(1)}, u32[]{:S(2)}, u32[]{:S(2)}) collective-permute-start(bf16[64,1024]{1,0:T(8,128)(2,1)S(1)} %get-tuple-element.21), channel_id=1, source_target_pairs={{0,2},{2,4},{4,6},{6,8},{8,10},{10,12},{12,14},{14,16},{16,18},{18... | collective-permute-start | bytes 393224 | tf_op jit(solution)/shard_map/ppermute | solution.py:19

commit v6 on v4

--- a/solution.py
+++ b/solution.py
@@ -22,6 +22,28 @@
 def shift_down(x, axis):
     size = lax.axis_size(axis)
     return lax.ppermute(x, axis, [(i + 1, i) for i in range(size - 1)])
+
+
+def swap_pairs(x, axis, offset):
+    size = lax.axis_size(axis)
+    pairs = []
+    for i in range(size):
+        partner = i + 1 if (i - offset) % 2 == 0 else i - 1
+        if 0 <= partner < size:
+            pairs.append((i, partner))
+    return lax.ppermute(x, axis, pairs)
+
+
+def neighbour_swap(to_next, to_prev, axis):
+    even = lax.axis_index(axis) % 2 == 0
+    first, second = lax.optimization_barrier(
+        (jnp.where(even, to_next, to_prev), jnp.where(even, to_prev, to_next))
+    )
+    got_first = swap_pairs(first, axis, 0)
+    got_second = swap_pairs(second, axis, 1)
+    from_prev = jnp.where(even, got_second, got_first)
+    from_next = jnp.where(even, got_first, got_second)
+    return from_prev, from_next
 
 
 def all_sum(x, axes):
@@ -134,9 +156,7 @@
     own_pair = jnp.concatenate(
         [keys.reshape(2, block_rows, value_width), values.reshape(2, block_rows, value_width)], axis=2
     )
-    send0, send1 = lax.optimization_barrier((own_pair[0], own_pair[1]))
-    prev0 = shift_up(send0, "ctx")
-    prev1 = shift_down(send1, "ctx")
+    prev0, prev1 = neighbour_swap(own_pair[0], own_pair[1], "ctx")
     prev1 = jnp.where(at_fold, own_pair[0], prev1)
     prev_pair = jnp.stack([prev0, prev1])
     window = jnp.concatenate([prev_pair, own_pair], axis=1)
@@ -162,9 +182,7 @@
     partial = jnp.concatenate([key_part, value_part], axis=2)
 
     prev_part = partial[:, :block_rows].astype(jnp.bfloat16)
-    send0, send1 = lax.optimization_barrier((prev_part[0], prev_part[1]))
-    into0 = shift_down(send0, "ctx")
-    into1 = shift_up(send1, "ctx")
+    into1, into0 = neighbour_swap(prev_part[1], prev_part[0], "ctx")
     into0 = jnp.where(at_fold, prev_part[1], into0)
     own_part = partial[:, block_rows:]
     gathered = own_part + jnp.stack([into0, into1]).astype(jnp.float32)

time: 44.9 us -> 43.7 us (0.973)
  blocking collectives: 0 us -> 13.5 us
  starting transfers between devices: 19.2 us -> 8.96 us
  waiting for transfers between devices: 8 us -> 4.37 us
  local copies, waits for them, and re-layouts: 3.29 us -> 2.66 us
    all_to_all x0 -> x1, blocking collectives: none -> 13.5 us  [all_sum(): return jnp.sum(lax.all_to_all(spread, axes, 0, 0, tiled=True), axis=0)]
    all_to_all x1 -> x0, starting transfers between devices: 8.09 us -> none  [all_sum(): return jnp.sum(lax.all_to_all(spread, axes, 0, 0, tiled=True), axis=0)]
    all_to_all x1 -> x0, waiting for transfers between devices: 3.39 us -> none  [all_sum(): return jnp.sum(lax.all_to_all(spread, axes, 0, 0, tiled=True), axis=0)]
    ppermute x4, starting transfers between devices: 11.1 us -> 8.96 us  [swap_pairs(): return lax.ppermute(x, axis, pairs)]
    select_n x0 -> x2, other arithmetic: none -> 1.12 us  [neighbour_swap(): jnp.where(even, to_prev, to_next)]
    squeeze x1 -> x0, other arithmetic: 0.96 us -> none  [per_device(): send0, send1 = lax.optimization_barrier((own_pair[0], own_pair[1]))]
    broadcast_in_dim x2, local copies, waits for them, and re-layouts: 0.71 us -> 0.1 us  [all_sum(): spread = jnp.broadcast_to(x[None], (count,) + x.shape)]
  transfers between devices with their start and end apart: 5 -> 4, of which waited for: 2 -> 1; matrix products, arithmetic and copies ran while one was open for 5% -> 4% of each run, Pallas kernels for 0% -> 0%
where the time goes in v6:
time: 43.7 us; the launch traced here: 43.3 us
  blocking collectives  13.5 us (31%)
  Pallas kernels  9.22 us (21%)
  starting transfers between devices  8.96 us (21%)
  waiting for transfers between devices  4.37 us (10%)
  other arithmetic  3.77 us (9%)
  local copies, waits for them, and re-layouts  2.66 us (6%)
  between operations  0.77 us (2%)
    all_to_all x1, blocking collectives, all_sum(): return jnp.sum(lax.all_to_all(spread, axes, 0, 0, tiled=True), axis=0)  13.5 us
    pallas_call x1, Pallas kernels, attend_blocks(): pl.pallas_call(group_kernel, grid=(lanes, KV_HEADS), in_specs=[pl.BlockSp...  9.22 us
    ppermute x4, starting transfers between devices, swap_pairs(): return lax.ppermute(x, axis, pairs)  8.96 us
    ppermute x4, waiting for transfers between devices, swap_pairs(): return lax.ppermute(x, axis, pairs)  4.37 us
    unnamed x11, local copies, waits for them, and re-layouts  1.81 us
    select_n x2, other arithmetic, neighbour_swap(): jnp.where(even, to_prev, to_next)  1.12 us
  transfers between devices with their start and end apart: 4, of which 1 were waited for; matrix products, arithmetic and copies ran while one was open for 4% of the time, Pallas kernels for 0%

profile of v6, /device:TPU:0, one launch (start us, length us, event | category | flops | bytes accessed | tf_op | source)
XLA Modules:
  0.0 43.3 jit_solution(14618385639886839085)
XLA Ops:
  0.6 0.0 copy-start
  0.7 0.0 copy-start.1
  0.7 1.1 %broadcast_select_fusion.2 = (bf16[64,1024]{1,0:T(8,128)(2,1)S(1)}, bf16[64,1024]{1,0:T(8,128)(2,1)S(1)}) fusion(pred[]{:T(512)S(6)} %eq.10, bf16[2,64,512]{2,1,0:T(8,128)(2,1)} %bitcast.51, bf16[2,64,512]{2,1,0:T(8,128)(2,1)} %bitcast.54), kind=kLoop, calls=%fused_computation.19 | loop fusion | flops 917504 | bytes 524289 | tf_op jit(solution)/shard_map/jit(_where)/select_n | solution.py:40
  1.8 0.7 %collective-permute-start = (bf16[64,1024]{1,0:T(8,128)(2,1)S(1)}, bf16[64,1024]{1,0:T(8,128)(2,1)S(1)}, u32[]{:S(2)}, u32[]{:S(2)}) collective-permute-start(bf16[64,1024]{1,0:T(8,128)(2,1)S(1)} %get-tuple-element.14), channel_id=1, source_target_pairs={{2,4},{4,2},{6,8},{8,6},{10,12},{12,10},{14,16},{16,14},{18,20},{2... | collective-permute-start | bytes 393224 | tf_op jit(solution)/shard_map/ppermute | solution.py:34
  2.4 5.7 %collective-permute-start.1 = (bf16[64,1024]{1,0:T(8,128)(2,1)S(1)}, bf16[64,1024]{1,0:T(8,128)(2,1)S(1)}, u32[]{:S(2)}, u32[]{:S(2)}) collective-permute-start(bf16[64,1024]{1,0:T(8,128)(2,1)S(1)} %get-tuple-element.15), channel_id=1, source_target_pairs={{0,2},{2,0},{4,6},{6,4},{8,10},{10,8},{12,14},{14,12},{16,18},{18,... | collective-permute-start | bytes 393224 | tf_op jit(solution)/shard_map/ppermute | solution.py:34
  8.2 0.1 add_multiply_fusion
  8.3 0.1 iota_add_fusion.1
  8.3 0.1 iota_add_fusion
  8.4 0.6 %copy-done.4 = s32[1,1,2,2,64]{4,3,2,1,0:T(2,128)S(1)} copy-done((s32[1,1,2,2,64]{4,3,2,1,0:T(2,128)S(1)}, s32[1,1,2,2,64]{4,3,2,1,0:T(2,128)}, u32[]{:S(2)}) %copy-start.4) | copy-done | bytes 1048
  9.0 0.7 %and_convert_fusion.allow_ref = f32[2,64,128]{2,1,0:T(8,128)} fusion(s32[2,64]{1,0:T(2,128)S(1)} %bitcast.60, s32[2,64]{1,0:T(2,128)S(1)} %iota_add_fusion, s32[2,128]{1,0:T(2,128)S(1)} %iota_add_fusion.1), kind=kLoop, calls=%fused_computation.21 | loop fusion | flops 65536 | bytes 67584 | tf_op jit(solution)/shard_map/convert_element_type | solution.py:178
  9.7 0.0 collective-permute-done
  9.8 4.4 %collective-permute-done.1 = bf16[64,1024]{1,0:T(8,128)(2,1)S(1)} collective-permute-done((bf16[64,1024]{1,0:T(8,128)(2,1)S(1)}, bf16[64,1024]{1,0:T(8,128)(2,1)S(1)}, u32[]{:S(2)}, u32[]{:S(2)}) %collective-permute-start.1) | collective-permute-done | bytes 131104 | tf_op jit(solution)/shard_map/ppermute | solution.py:34
  14.1 0.0 copy-done
  14.1 0.0 copy-done.1
  14.1 0.1 select_bitcast_fusion.3
  14.2 0.8 %maximum_maximum_fusion.k_ref.v_ref = bf16[2,128,1024]{2,1,0:T(8,128)(2,1)} fusion(bf16[2,64,512]{2,1,0:T(8,128)(2,1)S(1)} %bitcast.53, bf16[2,64,512]{2,1,0:T(8,128)(2,1)S(1)} %bitcast.56, bf16[1,64,1024]{2,1,0:T(8,128)(2,1)S(1)} %get-tuple-element.30, bf16[1,64,1024]{2,1,0:T(8,128)(2,1)S(1)} %get-tuple-element.29), kind=kLoop, calls=%fused_computation.2 | loop fusion | flops 2097152 | bytes 1048576 | tf_op jit(solution)/shard_map/concatenate | solution.py:162
  15.0 9.2 %shard_map.101 = (bf16[2,64,4096]{2,1,0:T(8,128)(2,1)}, bf16[2,64,4096]{2,1,0:T(8,128)(2,1)}, f32[2,128,512]{2,1,0:T(8,128)}, f32[2,128,512]{2,1,0:T(8,128)}, f32[2,4,8,128]{3,2,1,0:T(8,128)}) custom-call(f32[32]{0:T(128)} %sink_ref.1, bf16[2,64,4096]{2,1,0:T(8,128)(2,1)} %bitcast.57, bf16[2,64,4096]{2,1,0:T(8,128)(2,1)} %bitcast.58, ...), custom_call_target="tpu_custom_call" | custom-call | flops 805306368 | bytes 7405568 | tf_op jit(solution)/shard_map/pallas_call | solution.py:115
  24.3 0.0 copy-start.2
  24.3 1.1 %constant_dynamic-update-slice_fusion.1 = f32[2,128,1024]{2,1,0:T(8,128)S(1)} fusion(f32[2,128,512]{2,1,0:T(8,128)} %get-tuple-element.18), kind=kLoop, calls=%fused_computation.24 | loop fusion | bytes 1048576
  25.4 0.0 copy-done.2
  25.5 0.1 convert.7
  25.6 0.0 copy-start.3
  25.6 1.9 %collective-permute-start.2 = (bf16[64,1024]{1,0:T(8,128)(2,1)S(1)}, bf16[64,1024]{1,0:T(8,128)(2,1)S(1)}, u32[]{:S(2)}, u32[]{:S(2)}) collective-permute-start(bf16[64,1024]{1,0:T(8,128)(2,1)S(1)} %get-tuple-element.20), channel_id=1, source_target_pairs={{0,2},{2,0},{4,6},{6,4},{8,10},{10,8},{12,14},{14,12},{16,18},{18,... | collective-permute-start | bytes 393224 | tf_op jit(solution)/shard_map/ppermute | solution.py:34
  27.5 0.7 %collective-permute-start.3 = (bf16[64,1024]{1,0:T(8,128)(2,1)S(1)}, bf16[64,1024]{1,0:T(8,128)(2,1)S(1)}, u32[]{:S(2)}, u32[]{:S(2)}) collective-permute-start(bf16[64,1024]{1,0:T(8,128)(2,1)S(1)} %get-tuple-element.21), channel_id=1, source_target_pairs={{2,4},{4,2},{6,8},{8,6},{10,12},{12,10},{14,16},{16,14},{18,20},{2... | collective-permute-start | bytes 393224 | tf_op jit(solution)/shard_map/ppermute | solution.py:34
  28.2 0.1 slice_reduce_fusion
  28.3 0.1 broadcast_in_dim.4
  28.4 13.5 %all_to_all.6 = f32[32,1,32]{2,1,0:T(1,128)S(1)} all-to-all(f32[32,1,32]{2,1,0:T(1,128)S(1)} %broadcast_in_dim.5), channel_id=1, replica_groups=mesh['ctx'=16,'dp'=2] {'ctx','dp'}, dimensions={0} | all-to-all | bytes 8192 | tf_op jit(solution)/shard_map/all_to_all | solution.py:54
  41.9 0.5 %reduce_sum.19 = f32[32]{0:T(128)} reduce(f32[32,1,32]{2,0,1:T(8,128)S(1)} %bitcast.59, f32[]{:T(128)} %constant.32.clone.1), dimensions={0,1}, to_apply=%region_1.2 | reduce | flops 992 | bytes 4228 | tf_op jit(solution)/shard_map/reduce_sum | solution.py:54
  42.4 0.0 collective-permute-done.2
  42.4 0.0 collective-permute-done.3
  42.5 0.1 fusion
  42.5 0.7 %slice_bitcast_fusion = (bf16[1,1,2,64,512]{4,3,2,1,0:T(8,128)(2,1)}, bf16[1,1,2,64,512]{4,3,2,1,0:T(8,128)(2,1)}) fusion(bf16[2,64,1024]{2,1,0:T(8,128)(2,1)S(1)} %fusion), kind=kLoop, calls=%fused_computation.7 | loop fusion | bytes 524288 | tf_op jit(solution)/shard_map/reshape | solution.py:195
  (7 shorter events, 0.1 us)
Async XLA Ops:
  0.6 13.5 %copy-start = (bf16[1,1,2,64,512]{4,3,2,1,0:T(8,128)(2,1)S(1)}, bf16[1,1,2,64,512]{4,3,2,1,0:T(8,128)(2,1)}, u32[]{:S(2)}) copy-start(bf16[1,1,2,64,512]{4,3,2,1,0:T(8,128)(2,1)} %param.8) | copy-start | bytes 393220
  0.7 13.5 %copy-start.1 = (bf16[1,1,2,64,512]{4,3,2,1,0:T(8,128)(2,1)S(1)}, bf16[1,1,2,64,512]{4,3,2,1,0:T(8,128)(2,1)}, u32[]{:S(2)}) copy-start(bf16[1,1,2,64,512]{4,3,2,1,0:T(8,128)(2,1)} %param.7) | copy-start | bytes 393220
  1.8 8.0 %collective-permute-start = (bf16[64,1024]{1,0:T(8,128)(2,1)S(1)}, bf16[64,1024]{1,0:T(8,128)(2,1)S(1)}, u32[]{:S(2)}, u32[]{:S(2)}) collective-permute-start(bf16[64,1024]{1,0:T(8,128)(2,1)S(1)} %get-tuple-element.14), channel_id=1, source_target_pairs={{2,4},{4,2},{6,8},{8,6},{10,12},{12,10},{14,16},{16,14},{18,20},{2... | collective-permute-start | bytes 393224 | tf_op jit(solution)/shard_map/ppermute | solution.py:34
  2.4 11.7 %collective-permute-start.1 = (bf16[64,1024]{1,0:T(8,128)(2,1)S(1)}, bf16[64,1024]{1,0:T(8,128)(2,1)S(1)}, u32[]{:S(2)}, u32[]{:S(2)}) collective-permute-start(bf16[64,1024]{1,0:T(8,128)(2,1)S(1)} %get-tuple-element.15), channel_id=1, source_target_pairs={{0,2},{2,0},{4,6},{6,4},{8,10},{10,8},{12,14},{14,12},{16,18},{18,... | collective-permute-start | bytes 393224 | tf_op jit(solution)/shard_map/ppermute | solution.py:34
  8.3 0.7 %copy-start.4 = (s32[1,1,2,2,64]{4,3,2,1,0:T(2,128)S(1)}, s32[1,1,2,2,64]{4,3,2,1,0:T(2,128)}, u32[]{:S(2)}) copy-start(s32[1,1,2,2,64]{4,3,2,1,0:T(2,128)} %param.9) | copy-start | bytes 3076
  24.3 1.2 %copy-start.2 = (f32[2,128,512]{2,1,0:T(8,128)S(1)}, f32[2,128,512]{2,1,0:T(8,128)}, u32[]{:S(2)}) copy-start(f32[2,128,512]{2,1,0:T(8,128)} %get-tuple-element.19) | copy-start | bytes 1572868
  25.6 2.6 %copy-start.3 = (f32[2,4,8,128]{3,2,1,0:T(8,128)S(1)}, f32[2,4,8,128]{3,2,1,0:T(8,128)}, u32[]{:S(2)}) copy-start(f32[2,4,8,128]{3,2,1,0:T(8,128)} %get-tuple-element.22) | copy-start | bytes 98308
  25.6 16.8 %collective-permute-start.2 = (bf16[64,1024]{1,0:T(8,128)(2,1)S(1)}, bf16[64,1024]{1,0:T(8,128)(2,1)S(1)}, u32[]{:S(2)}, u32[]{:S(2)}) collective-permute-start(bf16[64,1024]{1,0:T(8,128)(2,1)S(1)} %get-tuple-element.20), channel_id=1, source_target_pairs={{0,2},{2,0},{4,6},{6,4},{8,10},{10,8},{12,14},{14,12},{16,18},{18,... | collective-permute-start | bytes 393224 | tf_op jit(solution)/shard_map/ppermute | solution.py:34
  27.5 14.9 %collective-permute-start.3 = (bf16[64,1024]{1,0:T(8,128)(2,1)S(1)}, bf16[64,1024]{1,0:T(8,128)(2,1)S(1)}, u32[]{:S(2)}, u32[]{:S(2)}) collective-permute-start(bf16[64,1024]{1,0:T(8,128)(2,1)S(1)} %get-tuple-element.21), channel_id=1, source_target_pairs={{2,4},{4,2},{6,8},{8,6},{10,12},{12,10},{14,16},{16,14},{18,20},{2... | collective-permute-start | bytes 393224 | tf_op jit(solution)/shard_map/ppermute | solution.py:34

commit v7 on v6

--- a/solution.py
+++ b/solution.py
@@ -57,90 +57,97 @@
 def group_kernel(
     sink_ref, q_ref, g_ref, k_ref, v_ref, allow_ref, o_ref, dq_ref, dk_ref, dv_ref, st_ref
 ):
-    group = pl.program_id(1)
     rows = q_ref.shape[1]
     score_scale = 1.0 / math.sqrt(HEAD_DIM)
-    heads = [pl.ds(h * HEAD_DIM, HEAD_DIM) for h in range(GROUP)]
-    query = jnp.concatenate([q_ref[0, :, cols] for cols in heads], axis=0)
-    grad = jnp.concatenate([g_ref[0, :, cols] for cols in heads], axis=0)
-    key = k_ref[0]
-    value = v_ref[0]
+    contract_last = (((1,), (1,)), ((), ()))
+    contract_first = (((0,), (0,)), ((), ()))
     allowed = jnp.concatenate([allow_ref[0]] * GROUP, axis=0) > 0.5
     head_of_row = lax.broadcasted_iota(jnp.int32, (GROUP * rows, 1), 0) // rows
-    sink = jnp.zeros((GROUP * rows, 1), jnp.float32)
-    for h in range(GROUP):
-        sink = jnp.where(head_of_row == h, sink_ref[group * GROUP + h], sink)
-    contract_last = (((1,), (1,)), ((), ()))
-    contract_first = (((0,), (0,)), ((), ()))
-    scores = (
-        lax.dot_general(query, key, contract_last, preferred_element_type=jnp.float32)
-        * score_scale
-    )
-    masked = jnp.where(allowed, scores, -jnp.inf)
-    row_top = jnp.maximum(sink, jnp.max(masked, axis=1, keepdims=True))
-    row_total = jnp.exp(sink - row_top) + jnp.sum(
-        jnp.exp(masked - row_top), axis=1, keepdims=True
-    )
-    log_total = row_top + jnp.log(row_total)
-    probs = jnp.exp(masked - log_total)
-    weights = probs.astype(jnp.bfloat16)
-    attended = jnp.dot(weights, value, preferred_element_type=jnp.float32).astype(jnp.bfloat16)
-    row_delta = jnp.sum(
-        grad.astype(jnp.float32) * attended.astype(jnp.float32), axis=1, keepdims=True
-    )
-    dprob = lax.dot_general(grad, value, contract_last, preferred_element_type=jnp.float32)
-    dscore = (probs * (dprob - row_delta)).astype(jnp.bfloat16)
-    dquery = jnp.dot(dscore, key, preferred_element_type=jnp.float32) * score_scale
-    dk_ref[0] = (
-        lax.dot_general(dscore, query, contract_first, preferred_element_type=jnp.float32)
-        * score_scale
-    )
-    dv_ref[0] = lax.dot_general(weights, grad, contract_first, preferred_element_type=jnp.float32)
-    sink_share = jnp.exp(sink - log_total) * row_delta
-    for h in range(GROUP):
-        part = slice(h * rows, (h + 1) * rows)
-        o_ref[0, :, heads[h]] = attended[part]
-        dq_ref[0, :, heads[h]] = dquery[part].astype(jnp.bfloat16)
-        total = -jnp.sum(sink_share[part], axis=0, keepdims=True)
-        st_ref[0, 0, pl.ds(h, 1), :] = jnp.broadcast_to(total, (1, 128))
+    for group in range(KV_HEADS):
+        heads = [pl.ds((group * GROUP + h) * HEAD_DIM, HEAD_DIM) for h in range(GROUP)]
+        side = pl.ds(group * HEAD_DIM, HEAD_DIM)
+        query = jnp.concatenate([q_ref[0, :, cols] for cols in heads], axis=0)
+        grad = jnp.concatenate([g_ref[0, :, cols] for cols in heads], axis=0)
+        key = k_ref[0, :, side]
+        value = v_ref[0, :, side]
+        sink = jnp.zeros((GROUP * rows, 1), jnp.float32)
+        for h in range(GROUP):
+            sink = jnp.where(head_of_row == h, sink_ref[group * GROUP + h], sink)
+        scores = (
+            lax.dot_general(query, key, contract_last, preferred_element_type=jnp.float32)
+            * score_scale
+        )
+        masked = jnp.where(allowed, scores, -jnp.inf)
+        row_top = jnp.maximum(sink, jnp.max(masked, axis=1, keepdims=True))
+        row_total = jnp.exp(sink - row_top) + jnp.sum(
+            jnp.exp(masked - row_top), axis=1, keepdims=True
+        )
+        log_total = row_top + jnp.log(row_total)
+        probs = jnp.exp(masked - log_total)
+        weights = probs.astype(jnp.bfloat16)
+        attended = jnp.dot(weights, value, preferred_element_type=jnp.float32).astype(
+            jnp.bfloat16
+        )
+        row_delta = jnp.sum(
+            grad.astype(jnp.float32) * attended.astype(jnp.float32), axis=1, keepdims=True
+        )
+        dprob = lax.dot_general(grad, value, contract_last, preferred_element_type=jnp.float32)
+        dscore = (probs * (dprob - row_delta)).astype(jnp.bfloat16)
+        dquery = jnp.dot(dscore, key, preferred_element_type=jnp.float32) * score_scale
+        dk_ref[0, :, side] = (
+            lax.dot_general(dscore, query, contract_first, preferred_element_type=jnp.float32)
+            * score_scale
+        )
+        dv_ref[0, :, side] = lax.dot_general(
+            weights, grad, contract_first, preferred_element_type=jnp.float32
+        )
+        sink_share = jnp.exp(sink - log_total) * row_delta
+        for h in range(GROUP):
+            part = slice(h * rows, (h + 1) * rows)
+            o_ref[0, :, heads[h]] = attended[part]
+            dq_ref[0, :, heads[h]] = dquery[part].astype(jnp.bfloat16)
+            total = -jnp.sum(sink_share[part], axis=0, keepdims=True)
+            st_ref[0, group, pl.ds(h, 1), :] = jnp.broadcast_to(total, (1, 128))
 
 
 def attend_blocks(sink_logit, queries, out_grad, window, allowed):
     lanes, rows, query_width = queries.shape
     span = window.shape[1]
-    group_width = GROUP * HEAD_DIM
-    lane_rows = lambda lane, group: (lane, 0, group)
+    side_width = KV_HEADS * HEAD_DIM
+    row_spec = pl.BlockSpec((1, rows, query_width), lambda lane: (lane, 0, 0))
+    side_spec = pl.BlockSpec((1, span, side_width), lambda lane: (lane, 0, 0))
     flops = 2 * lanes * HEADS * rows * span * HEAD_DIM * 6
     moved = 2 * (4 * queries.size + 2 * window.size) + 4 * allowed.size + 8 * window.size
     return pl.pallas_call(
         group_kernel,
-        grid=(lanes, KV_HEADS),
+        grid=(lanes,),
         in_specs=[
             pl.BlockSpec(memory_space=pltpu.SMEM),
-            pl.BlockSpec((1, rows, group_width), lane_rows),
-            pl.BlockSpec((1, rows, group_width), lane_rows),
-            pl.BlockSpec((1, span, HEAD_DIM), lane_rows),
-            pl.BlockSpec((1, span, HEAD_DIM), lambda lane, group: (lane, 0, KV_HEADS + group)),
-            pl.BlockSpec((1, rows, span), lambda lane, group: (lane, 0, 0)),
+            row_spec,
+            row_spec,
+            side_spec,
+            pl.BlockSpec((1, span, side_width), lambda lane: (lane, 0, 1)),
+            pl.BlockSpec((1, rows, span), lambda lane: (lane, 0, 0)),
         ],
         out_specs=[
-            pl.BlockSpec((1, rows, group_width), lane_rows),
-            pl.BlockSpec((1, rows, group_width), lane_rows),
-            pl.BlockSpec((1, span, HEAD_DIM), lane_rows),
-            pl.BlockSpec((1, span, HEAD_DIM), lane_rows),
-            pl.BlockSpec((1, 1, GROUP, 128), lambda lane, group: (lane, group, 0, 0)),
+            row_spec,
+            row_spec,
+            side_spec,
+            side_spec,
+            pl.BlockSpec((1, KV_HEADS, GROUP, 128), lambda lane: (lane, 0, 0, 0)),
         ],
         out_shape=[
             jax.ShapeDtypeStruct((lanes, rows, query_width), jnp.bfloat16),
             jax.ShapeDtypeStruct((lanes, rows, query_width), jnp.bfloat16),
-            jax.ShapeDtypeStruct((lanes, span, KV_HEADS * HEAD_DIM), jnp.float32),
-            jax.ShapeDtypeStruct((lanes, span, KV_HEADS * HEAD_DIM), jnp.float32),
+            jax.ShapeDtypeStruct((lanes, span, side_width), jnp.float32),
+            jax.ShapeDtypeStruct((lanes, span, side_width), jnp.float32),
             jax.ShapeDtypeStruct((lanes, KV_HEADS, GROUP, 128), jnp.float32),
         ],
         cost_estimate=pl.CostEstimate(
             flops=flops, transcendentals=2 * lanes * HEADS * rows * span, bytes_accessed=moved
         ),
     )(sink_logit, queries, out_grad, window, window, allowed)
+
 
 def per_device(queries, keys, values, doc_bounds, sink_logit, out_grad):
     block_rows = queries.shape[3]

time: 43.7 us -> 42.8 us (0.979)
  Pallas kernels: 9.22 us -> 8.42 us
    pallas_call x1, Pallas kernels: 9.22 us -> 8.42 us  [attend_blocks(): pl.pallas_call(group_kernel, grid=(lanes,), in_specs=[pl.BlockSpec(memory...]
where the time goes in v7:
time: 42.8 us; the launch traced here: 42.5 us
  blocking collectives  13.5 us (32%)
  starting transfers between devices  8.96 us (21%)
  Pallas kernels  8.42 us (20%)
  waiting for transfers between devices  4.37 us (10%)
  other arithmetic  3.77 us (9%)
  local copies, waits for them, and re-layouts  2.67 us (6%)
  between operations  0.77 us (2%)
    all_to_all x1, blocking collectives, all_sum(): return jnp.sum(lax.all_to_all(spread, axes, 0, 0, tiled=True), axis=0)  13.5 us
    ppermute x4, starting transfers between devices, swap_pairs(): return lax.ppermute(x, axis, pairs)  8.96 us
    pallas_call x1, Pallas kernels, attend_blocks(): pl.pallas_call(group_kernel, grid=(lanes,), in_specs=[pl.BlockSpec(memory...  8.42 us
    ppermute x4, waiting for transfers between devices, swap_pairs(): return lax.ppermute(x, axis, pairs)  4.37 us
    unnamed x11, local copies, waits for them, and re-layouts  1.81 us
    select_n x2, other arithmetic, neighbour_swap(): jnp.where(even, to_prev, to_next)  1.12 us
  transfers between devices with their start and end apart: 4, of which 1 were waited for; matrix products, arithmetic and copies ran while one was open for 4% of the time, Pallas kernels for 0%

profile of v7, /device:TPU:0, one launch (start us, length us, event | category | flops | bytes accessed | tf_op | source)
XLA Modules:
  0.0 42.5 jit_solution(2862375101090782356)
XLA Ops:
  0.6 0.0 copy-start
  0.7 0.0 copy-start.1
  0.7 1.1 %broadcast_select_fusion.2 = (bf16[64,1024]{1,0:T(8,128)(2,1)S(1)}, bf16[64,1024]{1,0:T(8,128)(2,1)S(1)}) fusion(pred[]{:T(512)S(6)} %eq.10, bf16[2,64,512]{2,1,0:T(8,128)(2,1)} %bitcast.51, bf16[2,64,512]{2,1,0:T(8,128)(2,1)} %bitcast.54), kind=kLoop, calls=%fused_computation.19 | loop fusion | flops 917504 | bytes 524289 | tf_op jit(solution)/shard_map/jit(_where)/select_n | solution.py:40
  1.8 0.7 %collective-permute-start = (bf16[64,1024]{1,0:T(8,128)(2,1)S(1)}, bf16[64,1024]{1,0:T(8,128)(2,1)S(1)}, u32[]{:S(2)}, u32[]{:S(2)}) collective-permute-start(bf16[64,1024]{1,0:T(8,128)(2,1)S(1)} %get-tuple-element.14), channel_id=1, source_target_pairs={{2,4},{4,2},{6,8},{8,6},{10,12},{12,10},{14,16},{16,14},{18,20},{2... | collective-permute-start | bytes 393224 | tf_op jit(solution)/shard_map/ppermute | solution.py:34
  2.4 5.7 %collective-permute-start.1 = (bf16[64,1024]{1,0:T(8,128)(2,1)S(1)}, bf16[64,1024]{1,0:T(8,128)(2,1)S(1)}, u32[]{:S(2)}, u32[]{:S(2)}) collective-permute-start(bf16[64,1024]{1,0:T(8,128)(2,1)S(1)} %get-tuple-element.15), channel_id=1, source_target_pairs={{0,2},{2,0},{4,6},{6,4},{8,10},{10,8},{12,14},{14,12},{16,18},{18,... | collective-permute-start | bytes 393224 | tf_op jit(solution)/shard_map/ppermute | solution.py:34
  8.2 0.1 add_multiply_fusion
  8.3 0.1 iota_add_fusion.1
  8.3 0.1 iota_add_fusion
  8.4 0.6 %copy-done.4 = s32[1,1,2,2,64]{4,3,2,1,0:T(2,128)S(1)} copy-done((s32[1,1,2,2,64]{4,3,2,1,0:T(2,128)S(1)}, s32[1,1,2,2,64]{4,3,2,1,0:T(2,128)}, u32[]{:S(2)}) %copy-start.4) | copy-done | bytes 1048
  9.0 0.7 %and_convert_fusion.allow_ref = f32[2,64,128]{2,1,0:T(8,128)} fusion(s32[2,64]{1,0:T(2,128)S(1)} %bitcast.60, s32[2,64]{1,0:T(2,128)S(1)} %iota_add_fusion, s32[2,128]{1,0:T(2,128)S(1)} %iota_add_fusion.1), kind=kLoop, calls=%fused_computation.21 | loop fusion | flops 65536 | bytes 67584 | tf_op jit(solution)/shard_map/convert_element_type | solution.py:185
  9.7 0.0 collective-permute-done
  9.8 4.4 %collective-permute-done.1 = bf16[64,1024]{1,0:T(8,128)(2,1)S(1)} collective-permute-done((bf16[64,1024]{1,0:T(8,128)(2,1)S(1)}, bf16[64,1024]{1,0:T(8,128)(2,1)S(1)}, u32[]{:S(2)}, u32[]{:S(2)}) %collective-permute-start.1) | collective-permute-done | bytes 131104 | tf_op jit(solution)/shard_map/ppermute | solution.py:34
  14.1 0.0 copy-done
  14.1 0.0 copy-done.1
  14.1 0.1 select_bitcast_fusion.3
  14.2 0.8 %maximum_maximum_fusion.k_ref.v_ref = bf16[2,128,1024]{2,1,0:T(8,128)(2,1)} fusion(bf16[2,64,512]{2,1,0:T(8,128)(2,1)S(1)} %bitcast.53, bf16[2,64,512]{2,1,0:T(8,128)(2,1)S(1)} %bitcast.56, bf16[1,64,1024]{2,1,0:T(8,128)(2,1)S(1)} %get-tuple-element.30, bf16[1,64,1024]{2,1,0:T(8,128)(2,1)S(1)} %get-tuple-element.29), kind=kLoop, calls=%fused_computation.2 | loop fusion | flops 2097152 | bytes 1048576 | tf_op jit(solution)/shard_map/concatenate | solution.py:169
  15.0 8.4 %shard_map.101 = (bf16[2,64,4096]{2,1,0:T(8,128)(2,1)}, bf16[2,64,4096]{2,1,0:T(8,128)(2,1)}, f32[2,128,512]{2,1,0:T(8,128)}, f32[2,128,512]{2,1,0:T(8,128)}, f32[2,4,8,128]{3,2,1,0:T(8,128)}) custom-call(f32[32]{0:T(128)} %sink_ref.1, bf16[2,64,4096]{2,1,0:T(8,128)(2,1)} %bitcast.57, bf16[2,64,4096]{2,1,0:T(8,128)(2,1)} %bitcast.58, ...), custom_call_target="tpu_custom_call" | custom-call | flops 805306368 | bytes 7405568 | tf_op jit(solution)/shard_map/pallas_call | solution.py:121
  23.5 1.1 %constant_dynamic-update-slice_fusion.1 = f32[2,128,1024]{2,1,0:T(8,128)S(1)} fusion(f32[2,128,512]{2,1,0:T(8,128)} %get-tuple-element.18), kind=kLoop, calls=%fused_computation.24 | loop fusion | bytes 1048576
  24.6 0.1 copy-done.2
  24.7 0.1 convert.7
  24.8 0.0 copy-start.3
  24.8 1.9 %collective-permute-start.2 = (bf16[64,1024]{1,0:T(8,128)(2,1)S(1)}, bf16[64,1024]{1,0:T(8,128)(2,1)S(1)}, u32[]{:S(2)}, u32[]{:S(2)}) collective-permute-start(bf16[64,1024]{1,0:T(8,128)(2,1)S(1)} %get-tuple-element.20), channel_id=1, source_target_pairs={{0,2},{2,0},{4,6},{6,4},{8,10},{10,8},{12,14},{14,12},{16,18},{18,... | collective-permute-start | bytes 393224 | tf_op jit(solution)/shard_map/ppermute | solution.py:34
  26.7 0.7 %collective-permute-start.3 = (bf16[64,1024]{1,0:T(8,128)(2,1)S(1)}, bf16[64,1024]{1,0:T(8,128)(2,1)S(1)}, u32[]{:S(2)}, u32[]{:S(2)}) collective-permute-start(bf16[64,1024]{1,0:T(8,128)(2,1)S(1)} %get-tuple-element.21), channel_id=1, source_target_pairs={{2,4},{4,2},{6,8},{8,6},{10,12},{12,10},{14,16},{16,14},{18,20},{2... | collective-permute-start | bytes 393224 | tf_op jit(solution)/shard_map/ppermute | solution.py:34
  27.4 0.0 copy-done.3
  27.4 0.1 slice_reduce_fusion
  27.5 0.1 broadcast_in_dim.4
  27.6 13.5 %all_to_all.6 = f32[32,1,32]{2,1,0:T(1,128)S(1)} all-to-all(f32[32,1,32]{2,1,0:T(1,128)S(1)} %broadcast_in_dim.5), channel_id=1, replica_groups=mesh['ctx'=16,'dp'=2] {'ctx','dp'}, dimensions={0} | all-to-all | bytes 8192 | tf_op jit(solution)/shard_map/all_to_all | solution.py:54
  41.1 0.5 %reduce_sum.19 = f32[32]{0:T(128)} reduce(f32[32,1,32]{2,0,1:T(8,128)S(1)} %bitcast.59, f32[]{:T(128)} %constant.32.clone.1), dimensions={0,1}, to_apply=%region_1.2 | reduce | flops 992 | bytes 4228 | tf_op jit(solution)/shard_map/reduce_sum | solution.py:54
  41.6 0.0 collective-permute-done.2
  41.6 0.0 collective-permute-done.3
  41.7 0.1 fusion
  41.7 0.7 %slice_bitcast_fusion = (bf16[1,1,2,64,512]{4,3,2,1,0:T(8,128)(2,1)}, bf16[1,1,2,64,512]{4,3,2,1,0:T(8,128)(2,1)}) fusion(bf16[2,64,1024]{2,1,0:T(8,128)(2,1)S(1)} %fusion), kind=kLoop, calls=%fused_computation.7 | loop fusion | bytes 524288 | tf_op jit(solution)/shard_map/reshape | solution.py:202
  (7 shorter events, 0.1 us)
Async XLA Ops:
  0.6 13.5 %copy-start = (bf16[1,1,2,64,512]{4,3,2,1,0:T(8,128)(2,1)S(1)}, bf16[1,1,2,64,512]{4,3,2,1,0:T(8,128)(2,1)}, u32[]{:S(2)}) copy-start(bf16[1,1,2,64,512]{4,3,2,1,0:T(8,128)(2,1)} %param.8) | copy-start | bytes 393220
  0.7 13.5 %copy-start.1 = (bf16[1,1,2,64,512]{4,3,2,1,0:T(8,128)(2,1)S(1)}, bf16[1,1,2,64,512]{4,3,2,1,0:T(8,128)(2,1)}, u32[]{:S(2)}) copy-start(bf16[1,1,2,64,512]{4,3,2,1,0:T(8,128)(2,1)} %param.7) | copy-start | bytes 393220
  1.8 8.0 %collective-permute-start = (bf16[64,1024]{1,0:T(8,128)(2,1)S(1)}, bf16[64,1024]{1,0:T(8,128)(2,1)S(1)}, u32[]{:S(2)}, u32[]{:S(2)}) collective-permute-start(bf16[64,1024]{1,0:T(8,128)(2,1)S(1)} %get-tuple-element.14), channel_id=1, source_target_pairs={{2,4},{4,2},{6,8},{8,6},{10,12},{12,10},{14,16},{16,14},{18,20},{2... | collective-permute-start | bytes 393224 | tf_op jit(solution)/shard_map/ppermute | solution.py:34
  2.4 11.7 %collective-permute-start.1 = (bf16[64,1024]{1,0:T(8,128)(2,1)S(1)}, bf16[64,1024]{1,0:T(8,128)(2,1)S(1)}, u32[]{:S(2)}, u32[]{:S(2)}) collective-permute-start(bf16[64,1024]{1,0:T(8,128)(2,1)S(1)} %get-tuple-element.15), channel_id=1, source_target_pairs={{0,2},{2,0},{4,6},{6,4},{8,10},{10,8},{12,14},{14,12},{16,18},{18,... | collective-permute-start | bytes 393224 | tf_op jit(solution)/shard_map/ppermute | solution.py:34
  8.3 0.7 %copy-start.4 = (s32[1,1,2,2,64]{4,3,2,1,0:T(2,128)S(1)}, s32[1,1,2,2,64]{4,3,2,1,0:T(2,128)}, u32[]{:S(2)}) copy-start(s32[1,1,2,2,64]{4,3,2,1,0:T(2,128)} %param.9) | copy-start | bytes 3076
  23.5 1.2 %copy-start.2 = (f32[2,128,512]{2,1,0:T(8,128)S(1)}, f32[2,128,512]{2,1,0:T(8,128)}, u32[]{:S(2)}) copy-start(f32[2,128,512]{2,1,0:T(8,128)} %get-tuple-element.19) | copy-start | bytes 1572868
  24.8 2.6 %copy-start.3 = (f32[2,4,8,128]{3,2,1,0:T(8,128)S(1)}, f32[2,4,8,128]{3,2,1,0:T(8,128)}, u32[]{:S(2)}) copy-start(f32[2,4,8,128]{3,2,1,0:T(8,128)} %get-tuple-element.22) | copy-start | bytes 98308
  24.8 16.8 %collective-permute-start.2 = (bf16[64,1024]{1,0:T(8,128)(2,1)S(1)}, bf16[64,1024]{1,0:T(8,128)(2,1)S(1)}, u32[]{:S(2)}, u32[]{:S(2)}) collective-permute-start(bf16[64,1024]{1,0:T(8,128)(2,1)S(1)} %get-tuple-element.20), channel_id=1, source_target_pairs={{0,2},{2,0},{4,6},{6,4},{8,10},{10,8},{12,14},{14,12},{16,18},{18,... | collective-permute-start | bytes 393224 | tf_op jit(solution)/shard_map/ppermute | solution.py:34
  26.7 14.9 %collective-permute-start.3 = (bf16[64,1024]{1,0:T(8,128)(2,1)S(1)}, bf16[64,1024]{1,0:T(8,128)(2,1)S(1)}, u32[]{:S(2)}, u32[]{:S(2)}) collective-permute-start(bf16[64,1024]{1,0:T(8,128)(2,1)S(1)} %get-tuple-element.21), channel_id=1, source_target_pairs={{2,4},{4,2},{6,8},{8,6},{10,12},{12,10},{14,16},{16,14},{18,20},{2... | collective-permute-start | bytes 393224 | tf_op jit(solution)/shard_map/ppermute | solution.py:34

commit v8 on v7

--- a/solution.py
+++ b/solution.py
@@ -55,7 +55,8 @@
 
 
 def group_kernel(
-    sink_ref, q_ref, g_ref, k_ref, v_ref, allow_ref, o_ref, dq_ref, dk_ref, dv_ref, st_ref
+    sink_ref, q_ref, g_ref, own_ref, prev_ref, allow_ref,
+    o_ref, dq_ref, msg_ref, dk_ref, dv_ref, st_ref,
 ):
     rows = q_ref.shape[1]
     score_scale = 1.0 / math.sqrt(HEAD_DIM)
@@ -66,10 +67,11 @@
     for group in range(KV_HEADS):
         heads = [pl.ds((group * GROUP + h) * HEAD_DIM, HEAD_DIM) for h in range(GROUP)]
         side = pl.ds(group * HEAD_DIM, HEAD_DIM)
+        value_side = pl.ds((KV_HEADS + group) * HEAD_DIM, HEAD_DIM)
         query = jnp.concatenate([q_ref[0, :, cols] for cols in heads], axis=0)
         grad = jnp.concatenate([g_ref[0, :, cols] for cols in heads], axis=0)
-        key = k_ref[0, :, side]
-        value = v_ref[0, :, side]
+        key = jnp.concatenate([prev_ref[0, :, side], own_ref[0, :, side]], axis=0)
+        value = jnp.concatenate([prev_ref[0, :, value_side], own_ref[0, :, value_side]], axis=0)
         sink = jnp.zeros((GROUP * rows, 1), jnp.float32)
         for h in range(GROUP):
             sink = jnp.where(head_of_row == h, sink_ref[group * GROUP + h], sink)
@@ -94,13 +96,15 @@
         dprob = lax.dot_general(grad, value, contract_last, preferred_element_type=jnp.float32)
         dscore = (probs * (dprob - row_delta)).astype(jnp.bfloat16)
         dquery = jnp.dot(dscore, key, preferred_element_type=jnp.float32) * score_scale
-        dk_ref[0, :, side] = (
+        dkey = (
             lax.dot_general(dscore, query, contract_first, preferred_element_type=jnp.float32)
             * score_scale
         )
-        dv_ref[0, :, side] = lax.dot_general(
-            weights, grad, contract_first, preferred_element_type=jnp.float32
-        )
+        dvalue = lax.dot_general(weights, grad, contract_first, preferred_element_type=jnp.float32)
+        msg_ref[0, :, side] = dkey[:rows].astype(jnp.bfloat16)
+        msg_ref[0, :, value_side] = dvalue[:rows].astype(jnp.bfloat16)
+        dk_ref[0, :, side] = dkey[rows:]
+        dv_ref[0, :, side] = dvalue[rows:]
         sink_share = jnp.exp(sink - log_total) * row_delta
         for h in range(GROUP):
             part = slice(h * rows, (h + 1) * rows)
@@ -110,43 +114,44 @@
             st_ref[0, group, pl.ds(h, 1), :] = jnp.broadcast_to(total, (1, 128))
 
 
-def attend_blocks(sink_logit, queries, out_grad, window, allowed):
+def attend_blocks(sink_logit, queries, out_grad, own_pair, prev_pair, allowed):
     lanes, rows, query_width = queries.shape
-    span = window.shape[1]
+    pair_width = own_pair.shape[2]
     side_width = KV_HEADS * HEAD_DIM
-    row_spec = pl.BlockSpec((1, rows, query_width), lambda lane: (lane, 0, 0))
-    side_spec = pl.BlockSpec((1, span, side_width), lambda lane: (lane, 0, 0))
-    flops = 2 * lanes * HEADS * rows * span * HEAD_DIM * 6
-    moved = 2 * (4 * queries.size + 2 * window.size) + 4 * allowed.size + 8 * window.size
+    lane_block = lambda width: pl.BlockSpec((1, rows, width), lambda lane: (lane, 0, 0))
+    flops = 2 * lanes * HEADS * rows * 2 * rows * HEAD_DIM * 6
+    moved = 8 * queries.size + 4 * own_pair.size + 6 * own_pair.size + 4 * allowed.size
     return pl.pallas_call(
         group_kernel,
         grid=(lanes,),
         in_specs=[
             pl.BlockSpec(memory_space=pltpu.SMEM),
-            row_spec,
-            row_spec,
-            side_spec,
-            pl.BlockSpec((1, span, side_width), lambda lane: (lane, 0, 1)),
-            pl.BlockSpec((1, rows, span), lambda lane: (lane, 0, 0)),
+            lane_block(query_width),
+            lane_block(query_width),
+            lane_block(pair_width),
+            lane_block(pair_width),
+            pl.BlockSpec((1, rows, 2 * rows), lambda lane: (lane, 0, 0)),
         ],
         out_specs=[
-            row_spec,
-            row_spec,
-            side_spec,
-            side_spec,
+            lane_block(query_width),
+            lane_block(query_width),
+            lane_block(pair_width),
+            lane_block(side_width),
+            lane_block(side_width),
             pl.BlockSpec((1, KV_HEADS, GROUP, 128), lambda lane: (lane, 0, 0, 0)),
         ],
         out_shape=[
             jax.ShapeDtypeStruct((lanes, rows, query_width), jnp.bfloat16),
             jax.ShapeDtypeStruct((lanes, rows, query_width), jnp.bfloat16),
-            jax.ShapeDtypeStruct((lanes, span, side_width), jnp.float32),
-            jax.ShapeDtypeStruct((lanes, span, side_width), jnp.float32),
+            jax.ShapeDtypeStruct((lanes, rows, pair_width), jnp.bfloat16),
+            jax.ShapeDtypeStruct((lanes, rows, side_width), jnp.float32),
+            jax.ShapeDtypeStruct((lanes, rows, side_width), jnp.float32),
             jax.ShapeDtypeStruct((lanes, KV_HEADS, GROUP, 128), jnp.float32),
         ],
         cost_estimate=pl.CostEstimate(
-            flops=flops, transcendentals=2 * lanes * HEADS * rows * span, bytes_accessed=moved
+            flops=flops, transcendentals=4 * lanes * HEADS * rows * rows, bytes_accessed=moved
         ),
-    )(sink_logit, queries, out_grad, window, window, allowed)
+    )(sink_logit, queries, out_grad, own_pair, prev_pair, allowed)
 
 
 def per_device(queries, keys, values, doc_bounds, sink_logit, out_grad):
@@ -166,7 +171,6 @@
     prev0, prev1 = neighbour_swap(own_pair[0], own_pair[1], "ctx")
     prev1 = jnp.where(at_fold, own_pair[0], prev1)
     prev_pair = jnp.stack([prev0, prev1])
-    window = jnp.concatenate([prev_pair, own_pair], axis=1)
 
     lane_block = jnp.stack([my_index, last_block - my_index]).astype(jnp.int32)
     row_offsets = jnp.arange(block_rows, dtype=jnp.int32)
@@ -177,29 +181,27 @@
     allowed = (key_pos[:, None, :] <= query_pos[:, :, None]) & (
         key_pos[:, None, :] >= first_pos[:, :, None]
     )
-    attended, dquery, key_part, value_part, sink_parts = attend_blocks(
+    attended, dquery, message, key_own, value_own, sink_parts = attend_blocks(
         sink_logit,
         queries.reshape(2, block_rows, query_width),
         out_grad.reshape(2, block_rows, query_width),
-        window,
+        own_pair,
+        prev_pair,
         allowed.astype(jnp.float32),
     )
     sink_terms = jnp.sum(sink_parts[:, :, :, 0], axis=0)
     sink_grad = all_sum(sink_terms.reshape(HEADS), ("ctx", "dp"))
-    partial = jnp.concatenate([key_part, value_part], axis=2)
-
-    prev_part = partial[:, :block_rows].astype(jnp.bfloat16)
-    into1, into0 = neighbour_swap(prev_part[1], prev_part[0], "ctx")
-    into0 = jnp.where(at_fold, prev_part[1], into0)
-    own_part = partial[:, block_rows:]
-    gathered = own_part + jnp.stack([into0, into1]).astype(jnp.float32)
+
+    into1, into0 = neighbour_swap(message[1], message[0], "ctx")
+    into0 = jnp.where(at_fold, message[1], into0)
+    arrived = jnp.stack([into0, into1]).astype(jnp.float32)
 
     out_shape = (1, 1, 2, block_rows, query_width)
     pair_out = (1, 1, 2, block_rows, value_width)
     attn_out = attended.reshape(out_shape)
     query_grad = dquery.reshape(out_shape)
-    key_grad = gathered[:, :, :value_width].astype(jnp.bfloat16).reshape(pair_out)
-    value_grad = gathered[:, :, value_width:].astype(jnp.bfloat16).reshape(pair_out)
+    key_grad = (key_own + arrived[:, :, :value_width]).astype(jnp.bfloat16).reshape(pair_out)
+    value_grad = (value_own + arrived[:, :, value_width:]).astype(jnp.bfloat16).reshape(pair_out)
     return (attn_out, query_grad, key_grad, value_grad, sink_grad)
 
 

time: 42.8 us -> 43.5 us (1.016)
  other arithmetic: 3.77 us -> 5.52 us
  local copies, waits for them, and re-layouts: 2.67 us -> 1.7 us
    select_n x2, other arithmetic: 1.12 us -> 2.2 us  [neighbour_swap(): jnp.where(even, to_prev, to_next)]
    reshape x0 -> x1, other arithmetic: none -> 0.77 us  [per_device(): (value_own + arrived[:, :, value_width:]).astype(jnp.bfloat16)]
    reshape x1 -> x0, local copies, waits for them, and re-layouts: 0.72 us -> none  [per_device(): gathered[:, :, value_width:].astype(jnp.bfloat16).reshape(pair_out)]
    unnamed x11 -> x14, local copies, waits for them, and re-layouts: 1.81 us -> 1.6 us
where the time goes in v8:
time: 43.5 us; the launch traced here: 43.2 us
  blocking collectives  13.5 us (31%)
  starting transfers between devices  8.95 us (21%)
  Pallas kernels  8.37 us (19%)
  other arithmetic  5.52 us (13%)
  waiting for transfers between devices  4.37 us (10%)
  local copies, waits for them, and re-layouts  1.7 us (4%)
  between operations  0.77 us (2%)
    all_to_all x1, blocking collectives, all_sum(): return jnp.sum(lax.all_to_all(spread, axes, 0, 0, tiled=True), axis=0)  13.5 us
    ppermute x4, starting transfers between devices, swap_pairs(): return lax.ppermute(x, axis, pairs)  8.95 us
    pallas_call x1, Pallas kernels, attend_blocks(): pl.pallas_call(group_kernel, grid=(lanes,), in_specs=[pl.BlockSpec(memory...  8.37 us
    ppermute x4, waiting for transfers between devices, swap_pairs(): return lax.ppermute(x, axis, pairs)  4.37 us
    select_n x2, other arithmetic, neighbour_swap(): jnp.where(even, to_prev, to_next)  2.2 us
    unnamed x14, local copies, waits for them, and re-layouts  1.6 us
  transfers between devices with their start and end apart: 4, of which 1 were waited for; matrix products, arithmetic and copies ran while one was open for 4% of the time, Pallas kernels for 0%

profile of v8, /device:TPU:0, one launch (start us, length us, event | category | flops | bytes accessed | tf_op | source)
XLA Modules:
  0.0 43.2 jit_solution(14596576617266026269)
XLA Ops:
  0.6 0.0 copy-start
  0.7 0.0 copy-start.1
  0.7 1.2 %broadcast_select_fusion = (bf16[64,1024]{1,0:T(8,128)(2,1)S(1)}, bf16[64,1024]{1,0:T(8,128)(2,1)S(1)}) fusion(pred[]{:T(512)S(6)} %eq.10, bf16[2,64,512]{2,1,0:T(8,128)(2,1)} %bitcast.46, bf16[2,64,512]{2,1,0:T(8,128)(2,1)} %bitcast.49), kind=kLoop, calls=%fused_computation.24 | loop fusion | flops 1179648 | bytes 524289 | tf_op jit(solution)/shard_map/jit(_where)/select_n | solution.py:40
  1.8 0.7 %collective-permute-start = (bf16[64,1024]{1,0:T(8,128)(2,1)S(1)}, bf16[64,1024]{1,0:T(8,128)(2,1)S(1)}, u32[]{:S(2)}, u32[]{:S(2)}) collective-permute-start(bf16[64,1024]{1,0:T(8,128)(2,1)S(1)} %get-tuple-element.15), channel_id=1, source_target_pairs={{2,4},{4,2},{6,8},{8,6},{10,12},{12,10},{14,16},{16,14},{18,20},{2... | collective-permute-start | bytes 393224 | tf_op jit(solution)/shard_map/ppermute | solution.py:34
  2.5 5.7 %collective-permute-start.1 = (bf16[64,1024]{1,0:T(8,128)(2,1)S(1)}, bf16[64,1024]{1,0:T(8,128)(2,1)S(1)}, u32[]{:S(2)}, u32[]{:S(2)}) collective-permute-start(bf16[64,1024]{1,0:T(8,128)(2,1)S(1)} %get-tuple-element.16), channel_id=1, source_target_pairs={{0,2},{2,0},{4,6},{6,4},{8,10},{10,8},{12,14},{14,12},{16,18},{18,... | collective-permute-start | bytes 393224 | tf_op jit(solution)/shard_map/ppermute | solution.py:34
  8.2 0.1 add_multiply_fusion
  8.3 0.1 iota_add_fusion.1
  8.4 0.1 iota_add_fusion
  8.5 0.6 %copy-done.6 = s32[1,1,2,2,64]{4,3,2,1,0:T(2,128)S(1)} copy-done((s32[1,1,2,2,64]{4,3,2,1,0:T(2,128)S(1)}, s32[1,1,2,2,64]{4,3,2,1,0:T(2,128)}, u32[]{:S(2)}) %copy-start.6) | copy-done | bytes 1048
  9.1 0.7 %and_convert_fusion.allow_ref = f32[2,64,128]{2,1,0:T(8,128)} fusion(s32[2,64]{1,0:T(2,128)S(1)} %bitcast.53, s32[2,64]{1,0:T(2,128)S(1)} %iota_add_fusion, s32[2,128]{1,0:T(2,128)S(1)} %iota_add_fusion.1), kind=kLoop, calls=%fused_computation.26 | loop fusion | flops 65536 | bytes 67584 | tf_op jit(solution)/shard_map/convert_element_type | solution.py:190
  9.8 0.0 collective-permute-done
  9.8 4.4 %collective-permute-done.1 = bf16[64,1024]{1,0:T(8,128)(2,1)S(1)} collective-permute-done((bf16[64,1024]{1,0:T(8,128)(2,1)S(1)}, bf16[64,1024]{1,0:T(8,128)(2,1)S(1)}, u32[]{:S(2)}, u32[]{:S(2)}) %collective-permute-start.1) | collective-permute-done | bytes 131104 | tf_op jit(solution)/shard_map/ppermute | solution.py:34
  14.2 0.0 copy-done
  14.2 0.1 select_bitcast_fusion.2
  14.3 0.8 %pad_maximum_fusion = (bf16[2,64,1024]{2,1,0:T(8,128)(2,1)}, bf16[2,64,1024]{2,1,0:T(8,128)(2,1)}) fusion(bf16[2,64,512]{2,1,0:T(8,128)(2,1)S(1)} %bitcast.48, bf16[2,64,512]{2,1,0:T(8,128)(2,1)S(1)} %bitcast.51, bf16[1,64,1024]{2,1,0:T(8,128)(2,1)S(1)} %get-tuple-element.32, bf16[1,64,1024]{2,1,0:T(8,128)(2,1)S(1)} %get-tuple-element.31), kind=kLoop, calls=%fused_computation.2 | loop fusion | flops 1048576 | bytes 1048576 | tf_op jit(solution)/shard_map/concatenate | solution.py:168
  15.1 8.4 %shard_map.101 = (bf16[2,64,4096]{2,1,0:T(8,128)(2,1)}, bf16[2,64,4096]{2,1,0:T(8,128)(2,1)}, bf16[2,64,1024]{2,1,0:T(8,128)(2,1)}, f32[2,64,512]{2,1,0:T(8,128)...) custom-call(f32[32]{0:T(128)} %sink_ref.1, bf16[2,64,4096]{2,1,0:T(8,128)(2,1)} %bitcast.55, ...), custom_call_target="tpu_custom_call" | custom-call | flops 805306368 | bytes 5570560 | tf_op jit(solution)/shard_map/pallas_call | solution.py:124
  23.5 0.0 copy-start.5
  23.5 1.0 %bitcast_select_fusion = (bf16[64,1024]{1,0:T(8,128)(2,1)S(1)}, bf16[64,1024]{1,0:T(8,128)(2,1)S(1)}) fusion(pred[]{:T(512)S(6)} %eq.10, bf16[2,64,1024]{2,1,0:T(8,128)(2,1)} %get-tuple-element.20), kind=kLoop, calls=%fused_computation.17 | loop fusion | flops 131072 | bytes 524289 | tf_op jit(solution)/shard_map/jit(_where)/select_n | solution.py:40
  24.5 1.9 %collective-permute-start.2 = (bf16[64,1024]{1,0:T(8,128)(2,1)S(1)}, bf16[64,1024]{1,0:T(8,128)(2,1)S(1)}, u32[]{:S(2)}, u32[]{:S(2)}) collective-permute-start(bf16[64,1024]{1,0:T(8,128)(2,1)S(1)} %get-tuple-element.21), channel_id=1, source_target_pairs={{0,2},{2,0},{4,6},{6,4},{8,10},{10,8},{12,14},{14,12},{16,18},{18,... | collective-permute-start | bytes 393224 | tf_op jit(solution)/shard_map/ppermute | solution.py:34
  26.4 0.7 %collective-permute-start.3 = (bf16[64,1024]{1,0:T(8,128)(2,1)S(1)}, bf16[64,1024]{1,0:T(8,128)(2,1)S(1)}, u32[]{:S(2)}, u32[]{:S(2)}) collective-permute-start(bf16[64,1024]{1,0:T(8,128)(2,1)S(1)} %get-tuple-element.22), channel_id=1, source_target_pairs={{2,4},{4,2},{6,8},{8,6},{10,12},{12,10},{14,16},{16,14},{18,20},{2... | collective-permute-start | bytes 393224 | tf_op jit(solution)/shard_map/ppermute | solution.py:34
  27.1 0.1 slice_reduce_fusion
  27.2 0.1 broadcast_in_dim.4
  27.3 13.5 %all_to_all.6 = f32[32,1,32]{2,1,0:T(1,128)S(1)} all-to-all(f32[32,1,32]{2,1,0:T(1,128)S(1)} %broadcast_in_dim.5), channel_id=1, replica_groups=mesh['ctx'=16,'dp'=2] {'ctx','dp'}, dimensions={0} | all-to-all | bytes 8192 | tf_op jit(solution)/shard_map/all_to_all | solution.py:54
  40.8 0.5 %reduce_sum.19 = f32[32]{0:T(128)} reduce(f32[32,1,32]{2,0,1:T(8,128)S(1)} %bitcast.52, f32[]{:T(128)} %constant.32.clone.1), dimensions={0,1}, to_apply=%region_1.2 | reduce | flops 992 | bytes 4228 | tf_op jit(solution)/shard_map/reduce_sum | solution.py:54
  41.3 0.0 collective-permute-done.2
  41.4 0.0 collective-permute-done.3
  41.4 0.0 copy-done.2
  41.4 0.0 copy-start.3
  41.4 0.0 copy-start.4
  41.5 0.9 %copy-done.3 = f32[2,64,512]{2,1,0:T(8,128)S(1)} copy-done((f32[2,64,512]{2,1,0:T(8,128)S(1)}, f32[2,64,512]{2,1,0:T(8,128)}, u32[]{:S(2)}) %copy-start.3) | copy-done | bytes 262168
  42.3 0.1 copy-done.4
  42.4 0.8 %fusion.3 = (bf16[1,1,2,64,512]{4,3,2,1,0:T(8,128)(2,1)}, bf16[1,1,2,64,512]{4,3,2,1,0:T(8,128)(2,1)}) fusion(f32[2,64,512]{2,1,0:T(8,128)S(1)} %copy-done.4, f32[2,64,1024]{2,1,0:T(8,128)S(1)} %maximum_convert_fusion, f32[2,64,512]{2,1,0:T(8,128)S(1)} %copy-done.3), kind=kLoop, calls=%fused_computation.12 | loop fusion | flops 262144 | bytes 1310720 | tf_op jit(solution)/shard_map/reshape | solution.py:204
  (8 shorter events, 0.1 us)
Async XLA Ops:
  0.6 13.5 %copy-start = (bf16[1,1,2,64,512]{4,3,2,1,0:T(8,128)(2,1)S(1)}, bf16[1,1,2,64,512]{4,3,2,1,0:T(8,128)(2,1)}, u32[]{:S(2)}) copy-start(bf16[1,1,2,64,512]{4,3,2,1,0:T(8,128)(2,1)} %param.8) | copy-start | bytes 393220
  0.7 13.5 %copy-start.1 = (bf16[1,1,2,64,512]{4,3,2,1,0:T(8,128)(2,1)S(1)}, bf16[1,1,2,64,512]{4,3,2,1,0:T(8,128)(2,1)}, u32[]{:S(2)}) copy-start(bf16[1,1,2,64,512]{4,3,2,1,0:T(8,128)(2,1)} %param.7) | copy-start | bytes 393220
  1.8 8.0 %collective-permute-start = (bf16[64,1024]{1,0:T(8,128)(2,1)S(1)}, bf16[64,1024]{1,0:T(8,128)(2,1)S(1)}, u32[]{:S(2)}, u32[]{:S(2)}) collective-permute-start(bf16[64,1024]{1,0:T(8,128)(2,1)S(1)} %get-tuple-element.15), channel_id=1, source_target_pairs={{2,4},{4,2},{6,8},{8,6},{10,12},{12,10},{14,16},{16,14},{18,20},{2... | collective-permute-start | bytes 393224 | tf_op jit(solution)/shard_map/ppermute | solution.py:34
  2.5 11.7 %collective-permute-start.1 = (bf16[64,1024]{1,0:T(8,128)(2,1)S(1)}, bf16[64,1024]{1,0:T(8,128)(2,1)S(1)}, u32[]{:S(2)}, u32[]{:S(2)}) collective-permute-start(bf16[64,1024]{1,0:T(8,128)(2,1)S(1)} %get-tuple-element.16), channel_id=1, source_target_pairs={{0,2},{2,0},{4,6},{6,4},{8,10},{10,8},{12,14},{14,12},{16,18},{18,... | collective-permute-start | bytes 393224 | tf_op jit(solution)/shard_map/ppermute | solution.py:34
  8.4 0.7 %copy-start.6 = (s32[1,1,2,2,64]{4,3,2,1,0:T(2,128)S(1)}, s32[1,1,2,2,64]{4,3,2,1,0:T(2,128)}, u32[]{:S(2)}) copy-start(s32[1,1,2,2,64]{4,3,2,1,0:T(2,128)} %param.9) | copy-start | bytes 3076
  23.5 3.6 %copy-start.5 = (f32[2,4,8,128]{3,2,1,0:T(8,128)S(1)}, f32[2,4,8,128]{3,2,1,0:T(8,128)}, u32[]{:S(2)}) copy-start(f32[2,4,8,128]{3,2,1,0:T(8,128)} %get-tuple-element.24) | copy-start | bytes 98308
  23.5 17.9 %copy-start.2 = (bf16[2,64,1024]{2,1,0:T(8,128)(2,1)S(1)}, bf16[2,64,1024]{2,1,0:T(8,128)(2,1)}, u32[]{:S(2)}) copy-start(bf16[2,64,1024]{2,1,0:T(8,128)(2,1)} %get-tuple-element.20) | copy-start | bytes 786436
  24.5 16.8 %collective-permute-start.2 = (bf16[64,1024]{1,0:T(8,128)(2,1)S(1)}, bf16[64,1024]{1,0:T(8,128)(2,1)S(1)}, u32[]{:S(2)}, u32[]{:S(2)}) collective-permute-start(bf16[64,1024]{1,0:T(8,128)(2,1)S(1)} %get-tuple-element.21), channel_id=1, source_target_pairs={{0,2},{2,0},{4,6},{6,4},{8,10},{10,8},{12,14},{14,12},{16,18},{18,... | collective-permute-start | bytes 393224 | tf_op jit(solution)/shard_map/ppermute | solution.py:34
  26.4 14.9 %collective-permute-start.3 = (bf16[64,1024]{1,0:T(8,128)(2,1)S(1)}, bf16[64,1024]{1,0:T(8,128)(2,1)S(1)}, u32[]{:S(2)}, u32[]{:S(2)}) collective-permute-start(bf16[64,1024]{1,0:T(8,128)(2,1)S(1)} %get-tuple-element.22), channel_id=1, source_target_pairs={{2,4},{4,2},{6,8},{8,6},{10,12},{12,10},{14,16},{16,14},{18,20},{2... | collective-permute-start | bytes 393224 | tf_op jit(solution)/shard_map/ppermute | solution.py:34
  41.4 1.0 %copy-start.3 = (f32[2,64,512]{2,1,0:T(8,128)S(1)}, f32[2,64,512]{2,1,0:T(8,128)}, u32[]{:S(2)}) copy-start(f32[2,64,512]{2,1,0:T(8,128)} %get-tuple-element.19) | copy-start | bytes 786436
  41.4 1.0 %copy-start.4 = (f32[2,64,512]{2,1,0:T(8,128)S(1)}, f32[2,64,512]{2,1,0:T(8,128)}, u32[]{:S(2)}) copy-start(f32[2,64,512]{2,1,0:T(8,128)} %get-tuple-element.23) | copy-start | bytes 786436

commit v9 on v8

--- a/solution.py
+++ b/solution.py
@@ -29,21 +29,11 @@
     pairs = []
     for i in range(size):
         partner = i + 1 if (i - offset) % 2 == 0 else i - 1
-        if 0 <= partner < size:
+        if partner == size:
+            partner = i
+        if partner >= 0:
             pairs.append((i, partner))
     return lax.ppermute(x, axis, pairs)
-
-
-def neighbour_swap(to_next, to_prev, axis):
-    even = lax.axis_index(axis) % 2 == 0
-    first, second = lax.optimization_barrier(
-        (jnp.where(even, to_next, to_prev), jnp.where(even, to_prev, to_next))
-    )
-    got_first = swap_pairs(first, axis, 0)
-    got_second = swap_pairs(second, axis, 1)
-    from_prev = jnp.where(even, got_second, got_first)
-    from_next = jnp.where(even, got_first, got_second)
-    return from_prev, from_next
 
 
 def all_sum(x, axes):
@@ -55,7 +45,7 @@
 
 
 def group_kernel(
-    sink_ref, q_ref, g_ref, own_ref, prev_ref, allow_ref,
+    flag_ref, sink_ref, q_ref, g_ref, k_ref, v_ref, first_ref, second_ref, allow_ref,
     o_ref, dq_ref, msg_ref, dk_ref, dv_ref, st_ref,
 ):
     rows = q_ref.shape[1]
@@ -64,14 +54,17 @@
     contract_first = (((0,), (0,)), ((), ()))
     allowed = jnp.concatenate([allow_ref[0]] * GROUP, axis=0) > 0.5
     head_of_row = lax.broadcasted_iota(jnp.int32, (GROUP * rows, 1), 0) // rows
+    use_second = (pl.program_id(0) + flag_ref[0]) % 2 == 1
     for group in range(KV_HEADS):
         heads = [pl.ds((group * GROUP + h) * HEAD_DIM, HEAD_DIM) for h in range(GROUP)]
         side = pl.ds(group * HEAD_DIM, HEAD_DIM)
         value_side = pl.ds((KV_HEADS + group) * HEAD_DIM, HEAD_DIM)
         query = jnp.concatenate([q_ref[0, :, cols] for cols in heads], axis=0)
         grad = jnp.concatenate([g_ref[0, :, cols] for cols in heads], axis=0)
-        key = jnp.concatenate([prev_ref[0, :, side], own_ref[0, :, side]], axis=0)
-        value = jnp.concatenate([prev_ref[0, :, value_side], own_ref[0, :, value_side]], axis=0)
+        prev_key = jnp.where(use_second, second_ref[:, side], first_ref[:, side])
+        prev_value = jnp.where(use_second, second_ref[:, value_side], first_ref[:, value_side])
+        key = jnp.concatenate([prev_key, k_ref[0, :, side]], axis=0)
+        value = jnp.concatenate([prev_value, v_ref[0, :, side]], axis=0)
         sink = jnp.zeros((GROUP * rows, 1), jnp.float32)
         for h in range(GROUP):
             sink = jnp.where(head_of_row == h, sink_ref[group * GROUP + h], sink)
@@ -114,32 +107,41 @@
             st_ref[0, group, pl.ds(h, 1), :] = jnp.broadcast_to(total, (1, 128))
 
 
-def attend_blocks(sink_logit, queries, out_grad, own_pair, prev_pair, allowed):
+def attend_blocks(flag, sink_logit, queries, out_grad, keys, values, first, second, allowed):
     lanes, rows, query_width = queries.shape
-    pair_width = own_pair.shape[2]
-    side_width = KV_HEADS * HEAD_DIM
-    lane_block = lambda width: pl.BlockSpec((1, rows, width), lambda lane: (lane, 0, 0))
+    side_width = keys.shape[2]
+    pair_width = first.shape[1]
+    lane_block = lambda width: pl.BlockSpec((1, rows, width), lambda lane, flag_ref: (lane, 0, 0))
+    whole = pl.BlockSpec((rows, pair_width), lambda lane, flag_ref: (0, 0))
     flops = 2 * lanes * HEADS * rows * 2 * rows * HEAD_DIM * 6
-    moved = 8 * queries.size + 4 * own_pair.size + 6 * own_pair.size + 4 * allowed.size
-    return pl.pallas_call(
-        group_kernel,
+    moved = 8 * queries.size + 4 * keys.size + 10 * keys.size + 4 * allowed.size
+    grid_spec = pltpu.PrefetchScalarGridSpec(
+        num_scalar_prefetch=1,
         grid=(lanes,),
         in_specs=[
             pl.BlockSpec(memory_space=pltpu.SMEM),
             lane_block(query_width),
             lane_block(query_width),
-            lane_block(pair_width),
-            lane_block(pair_width),
-            pl.BlockSpec((1, rows, 2 * rows), lambda lane: (lane, 0, 0)),
+            lane_block(side_width),
+            lane_block(side_width),
+            whole,
+            whole,
+            pl.BlockSpec((1, rows, 2 * rows), lambda lane, flag_ref: (lane, 0, 0)),
         ],
         out_specs=[
             lane_block(query_width),
             lane_block(query_width),
-            lane_block(pair_width),
-            lane_block(side_width),
-            lane_block(side_width),
-            pl.BlockSpec((1, KV_HEADS, GROUP, 128), lambda lane: (lane, 0, 0, 0)),
+            pl.BlockSpec(
+                (1, rows, pair_width), lambda lane, flag_ref: ((lane + flag_ref[0]) % 2, 0, 0)
+            ),
+            lane_block(side_width),
+            lane_block(side_width),
+            pl.BlockSpec((1, KV_HEADS, GROUP, 128), lambda lane, flag_ref: (lane, 0, 0, 0)),
         ],
+    )
+    return pl.pallas_call(
+        group_kernel,
+        grid_spec=grid_spec,
         out_shape=[
             jax.ShapeDtypeStruct((lanes, rows, query_width), jnp.bfloat16),
             jax.ShapeDtypeStruct((lanes, rows, query_width), jnp.bfloat16),
@@ -151,7 +153,7 @@
         cost_estimate=pl.CostEstimate(
             flops=flops, transcendentals=4 * lanes * HEADS * rows * rows, bytes_accessed=moved
         ),
-    )(sink_logit, queries, out_grad, own_pair, prev_pair, allowed)
+    )(flag, sink_logit, queries, out_grad, keys, values, first, second, allowed)
 
 
 def per_device(queries, keys, values, doc_bounds, sink_logit, out_grad):
@@ -161,16 +163,25 @@
     pair_count = lax.axis_size("ctx")
     my_index = lax.axis_index("ctx")
     score_scale = 1.0 / math.sqrt(HEAD_DIM)
-    at_fold = my_index == pair_count - 1
     last_block = 2 * pair_count - 1
     span = (REACH + 1) * block_rows
 
-    own_pair = jnp.concatenate(
-        [keys.reshape(2, block_rows, value_width), values.reshape(2, block_rows, value_width)], axis=2
-    )
-    prev0, prev1 = neighbour_swap(own_pair[0], own_pair[1], "ctx")
-    prev1 = jnp.where(at_fold, own_pair[0], prev1)
-    prev_pair = jnp.stack([prev0, prev1])
+    key_lanes = keys.reshape(2, block_rows, value_width)
+    value_lanes = values.reshape(2, block_rows, value_width)
+    even = (my_index % 2 == 0).astype(jnp.int32)
+
+    def lane_pair(lane):
+        return jnp.concatenate(
+            [
+                lax.dynamic_index_in_dim(key_lanes, lane, keepdims=False),
+                lax.dynamic_index_in_dim(value_lanes, lane, keepdims=False),
+            ],
+            axis=1,
+        )
+
+    first_send, second_send = lax.optimization_barrier((lane_pair(1 - even), lane_pair(even)))
+    first = swap_pairs(first_send, "ctx", 0)
+    second = swap_pairs(second_send, "ctx", 1)
 
     lane_block = jnp.stack([my_index, last_block - my_index]).astype(jnp.int32)
     row_offsets = jnp.arange(block_rows, dtype=jnp.int32)
@@ -182,19 +193,26 @@
         key_pos[:, None, :] >= first_pos[:, :, None]
     )
     attended, dquery, message, key_own, value_own, sink_parts = attend_blocks(
+        even.reshape(1),
         sink_logit,
         queries.reshape(2, block_rows, query_width),
         out_grad.reshape(2, block_rows, query_width),
-        own_pair,
-        prev_pair,
+        key_lanes,
+        value_lanes,
+        first,
+        second,
         allowed.astype(jnp.float32),
     )
     sink_terms = jnp.sum(sink_parts[:, :, :, 0], axis=0)
     sink_grad = all_sum(sink_terms.reshape(HEADS), ("ctx", "dp"))
 
-    into1, into0 = neighbour_swap(message[1], message[0], "ctx")
-    into0 = jnp.where(at_fold, message[1], into0)
-    arrived = jnp.stack([into0, into1]).astype(jnp.float32)
+    sent_first, sent_second = lax.optimization_barrier((message[0], message[1]))
+    got_first = swap_pairs(sent_first, "ctx", 0)
+    got_second = swap_pairs(sent_second, "ctx", 1)
+    is_even = even == 1
+    arrived = jnp.stack(
+        [jnp.where(is_even, got_first, got_second), jnp.where(is_even, got_second, got_first)]
+    ).astype(jnp.float32)
 
     out_shape = (1, 1, 2, block_rows, query_width)
     pair_out = (1, 1, 2, block_rows, value_width)

time: 43.5 us -> 43.2 us (level)
  blocking collectives: 13.5 us -> 0 us
  starting transfers between devices: 8.95 us -> 17.6 us
  waiting for transfers between devices: 4.37 us -> 8.33 us
  local copies, waits for them, and re-layouts: 1.7 us -> 4.93 us
  other arithmetic: 5.52 us -> 2.43 us
  Pallas kernels: 8.37 us -> 8.81 us
    all_to_all x1 -> x0, blocking collectives: 13.5 us -> none  [all_sum(): return jnp.sum(lax.all_to_all(spread, axes, 0, 0, tiled=True), axis=0)]
    all_to_all x0 -> x1, starting transfers between devices: none -> 7.78 us  [all_sum(): return jnp.sum(lax.all_to_all(spread, axes, 0, 0, tiled=True), axis=0)]
    all_to_all x0 -> x1, waiting for transfers between devices: none -> 7.07 us  [all_sum(): return jnp.sum(lax.all_to_all(spread, axes, 0, 0, tiled=True), axis=0)]
    ppermute x4, waiting for transfers between devices: 4.37 us -> 1.26 us  [swap_pairs(): return lax.ppermute(x, axis, pairs)]
    select_n x2 -> x0, other arithmetic: 2.2 us -> none  [neighbour_swap(): jnp.where(even, to_prev, to_next)]
    squeeze x0 -> x2, local copies, waits for them, and re-layouts: none -> 1.95 us  [the longest x1 0.99 us: per_device(): sent_first, sent_second = lax.optimization_barrier((message[0], message[1]))]
    ppermute x4, starting transfers between devices: 8.95 us -> 9.85 us  [swap_pairs(): return lax.ppermute(x, axis, pairs)]
    concatenate x1 -> x2, other arithmetic: 0.85 us -> 0.02 us  [lane_pair(): jnp.concatenate([lax.dynamic_index_in_dim(key_lanes, lane, keepdims=False...]
  transfers between devices with their start and end apart: 4 -> 5, of which waited for: 1 -> 2; matrix products, arithmetic and copies ran while one was open for 4% -> 5% of each run, Pallas kernels for 0% -> 0%
where the time goes in v9:
time: 43.2 us; the launch traced here: 42.9 us
  starting transfers between devices  17.6 us (41%)
  Pallas kernels  8.81 us (20%)
  waiting for transfers between devices  8.33 us (19%)
  local copies, waits for them, and re-layouts  4.93 us (11%)
  other arithmetic  2.43 us (6%)
  between operations  0.76 us (2%)
    ppermute x4, starting transfers between devices, swap_pairs(): return lax.ppermute(x, axis, pairs)  9.85 us
    pallas_call x1, Pallas kernels, attend_blocks(): pl.pallas_call(group_kernel, grid_spec=grid_spec, out_shape=[jax.ShapeDty...  8.81 us
    all_to_all x1, starting transfers between devices, all_sum(): return jnp.sum(lax.all_to_all(spread, axes, 0, 0, tiled=True), axis=0)  7.78 us
    all_to_all x1, waiting for transfers between devices, all_sum(): return jnp.sum(lax.all_to_all(spread, axes, 0, 0, tiled=True), axis=0)  7.07 us
    unnamed x12, local copies, waits for them, and re-layouts  2.28 us
    ppermute x4, waiting for transfers between devices, swap_pairs(): return lax.ppermute(x, axis, pairs)  1.26 us
    squeeze x1, local copies, waits for them, and re-layouts, per_device(): sent_first, sent_second = lax.optimization_barrier((message[0], message[1]))  0.99 us
    squeeze x1, local copies, waits for them, and re-layouts, lane_pair(): lax.dynamic_index_in_dim(value_lanes, lane, keepdims=False)  0.96 us
  transfers between devices with their start and end apart: 5, of which 2 were waited for; matrix products, arithmetic and copies ran while one was open for 5% of the time, Pallas kernels for 0%

profile of v9, /device:TPU:0, one launch (start us, length us, event | category | flops | bytes accessed | tf_op | source)
XLA Modules:
  0.0 42.9 jit_solution(2734001443390641811)
XLA Ops:
  0.6 1.0 %dynamic-slice_bitcast_fusion = (bf16[64,512]{1,0:T(8,128)(2,1)S(1)}, bf16[64,512]{1,0:T(8,128)(2,1)S(1)}, bf16[64,512]{1,0:T(8,128)(2,1)S(1)}, bf16[64,512]{1,0:T(8,128)(2,1)S(1)}) fusion(bf16[1,1,2,64,512]{4,3,2,1,0:T(8,128)(2,1)} %param.8, s32[]{:T(128)S(6)} %select_n.30, s32[]{:T(128)S(6)} %select_n.29, bf16[1,1,2,64,512]{4,3,2,1,0:T(8,128)(2,1)} %param.7), kind=kLoop, calls=%fused_computation.13 | loop fusion | bytes 524296 | tf_op jit(solution)/shard_map/jit(dynamic_index_in_dim)/squeeze | solution.py:177
  1.6 3.0 %collective-permute-start = (bf16[64,1024]{1,0:T(8,128)(2,1)S(1)}, bf16[64,1024]{1,0:T(8,128)(2,1)S(1)}, u32[]{:S(2)}, u32[]{:S(2)}) collective-permute-start(bf16[64,1024]{1,0:T(8,128)(2,1)S(1)} %pad_maximum_fusion), channel_id=1, source_target_pairs={{0,2},{2,0},{4,6},{6,4},{8,10},{10,8},{12,14},{14,12},{16,18},{18,... | collective-permute-start | bytes 393224 | tf_op jit(solution)/shard_map/ppermute | solution.py:36
  4.6 0.7 %collective-permute-start.1 = (bf16[64,1024]{1,0:T(8,128)(2,1)S(1)}, bf16[64,1024]{1,0:T(8,128)(2,1)S(1)}, u32[]{:S(2)}, u32[]{:S(2)}) collective-permute-start(bf16[64,1024]{1,0:T(8,128)(2,1)S(1)} %pad_maximum_fusion.1), channel_id=1, source_target_pairs={{2,4},{4,2},{6,8},{8,6},{10,12},{12,10},{14,16},{16,14},{18,20},{2... | collective-permute-start | bytes 393224 | tf_op jit(solution)/shard_map/ppermute | solution.py:36
  5.3 0.1 add_multiply_fusion
  5.4 0.1 iota_add_fusion.1
  5.5 0.1 iota_add_fusion
  5.5 0.6 %copy-done.3 = s32[1,1,2,2,64]{4,3,2,1,0:T(2,128)S(1)} copy-done((s32[1,1,2,2,64]{4,3,2,1,0:T(2,128)S(1)}, s32[1,1,2,2,64]{4,3,2,1,0:T(2,128)}, u32[]{:S(2)}) %copy-start.3) | copy-done | bytes 1048
  6.2 0.7 %and_convert_fusion.allow_ref = f32[2,64,128]{2,1,0:T(8,128)} fusion(s32[2,64]{1,0:T(2,128)S(1)} %bitcast.35, s32[2,64]{1,0:T(2,128)S(1)} %iota_add_fusion, s32[2,128]{1,0:T(2,128)S(1)} %iota_add_fusion.1), kind=kLoop, calls=%fused_computation.17 | loop fusion | flops 65536 | bytes 67584 | tf_op jit(solution)/shard_map/convert_element_type | solution.py:204
  6.9 1.3 %collective-permute-done.first_ref = bf16[64,1024]{1,0:T(8,128)(2,1)S(1)} collective-permute-done((bf16[64,1024]{1,0:T(8,128)(2,1)S(1)}, bf16[64,1024]{1,0:T(8,128)(2,1)S(1)}, u32[]{:S(2)}, u32[]{:S(2)}) %collective-permute-start) | collective-permute-done | bytes 131104 | tf_op jit(solution)/shard_map/ppermute | solution.py:36
  8.1 0.0 copy-start.4
  8.1 0.0 collective-permute-done.1.second_ref
  8.2 0.6 %copy-done.4 = bf16[64,1024]{1,0:T(8,128)(2,1)} copy-done((bf16[64,1024]{1,0:T(8,128)(2,1)}, bf16[64,1024]{1,0:T(8,128)(2,1)S(1)}, u32[]{:S(2)}) %copy-start.4) | copy-done | bytes 131096
  8.8 0.0 copy-done.5
  8.8 8.8 %shard_map.101 = (bf16[2,64,4096]{2,1,0:T(8,128)(2,1)}, bf16[2,64,4096]{2,1,0:T(8,128)(2,1)}, bf16[2,64,1024]{2,1,0:T(8,128)(2,1)}, f32[2,64,512]{2,1,0:T(8,128)...) custom-call(s32[1]{0:T(128)} %bitcast.flag_ref, f32[32]{0:T(128)} %sink_ref.1, bf16[2,64,4096]{2,1,0:T(8,128)(2,1)} %bitcast.37, ...), custom_call_target="tpu_custom_call" | custom-call | flops 805306368 | bytes 5177344 | tf_op jit(solution)/shard_map/pallas_call | solution.py:142
  17.7 0.0 copy-start.2
  17.7 1.0 %slice_bitcast_fusion = (bf16[64,1024]{1,0:T(8,128)(2,1)S(1)}, bf16[64,1024]{1,0:T(8,128)(2,1)S(1)}) fusion(bf16[2,64,1024]{2,1,0:T(8,128)(2,1)} %get-tuple-element.20), kind=kLoop, calls=%fused_computation.11 | loop fusion | bytes 524288 | tf_op jit(solution)/shard_map/squeeze | solution.py:209
  18.7 5.5 %collective-permute-start.2 = (bf16[64,1024]{1,0:T(8,128)(2,1)S(1)}, bf16[64,1024]{1,0:T(8,128)(2,1)S(1)}, u32[]{:S(2)}, u32[]{:S(2)}) collective-permute-start(bf16[64,1024]{1,0:T(8,128)(2,1)S(1)} %get-tuple-element.21), channel_id=1, source_target_pairs={{0,2},{2,0},{4,6},{6,4},{8,10},{10,8},{12,14},{14,12},{16,18},{18,... | collective-permute-start | bytes 393224 | tf_op jit(solution)/shard_map/ppermute | solution.py:36
  24.2 0.7 %collective-permute-start.3 = (bf16[64,1024]{1,0:T(8,128)(2,1)S(1)}, bf16[64,1024]{1,0:T(8,128)(2,1)S(1)}, u32[]{:S(2)}, u32[]{:S(2)}) collective-permute-start(bf16[64,1024]{1,0:T(8,128)(2,1)S(1)} %get-tuple-element.22), channel_id=1, source_target_pairs={{2,4},{4,2},{6,8},{8,6},{10,12},{12,10},{14,16},{16,14},{18,20},{2... | collective-permute-start | bytes 393224 | tf_op jit(solution)/shard_map/ppermute | solution.py:36
  24.9 0.0 copy-done.2
  24.9 0.1 slice_reduce_fusion
  25.0 0.1 broadcast_in_dim.4
  25.0 0.6 %broadcast_in_dim.5 = f32[32,1,32]{2,1,0:T(1,128)} broadcast(f32[32]{0:T(128)S(1)} %broadcast_in_dim.4), dimensions={2} | broadcast | bytes 4224 | tf_op jit(solution)/shard_map/broadcast_in_dim | solution.py:43
  25.7 7.8 %all-to-all-start = ((f32[32,1,32]{2,1,0:T(1,128)}), f32[32,1,32]{2,1,0:T(1,128)S(1)}, u32[]{:S(2)}, u32[]{:S(2)}) async-start(f32[32,1,32]{2,1,0:T(1,128)} %broadcast_in_dim.5), calls=%async_computation | async-start | bytes 32768 | tf_op jit(solution)/shard_map/all_to_all | solution.py:44
  33.5 7.1 %all-to-all-done = f32[32,1,32]{2,1,0:T(1,128)S(1)} async-done(((f32[32,1,32]{2,1,0:T(1,128)}), f32[32,1,32]{2,1,0:T(1,128)S(1)}, u32[]{:S(2)}, u32[]{:S(2)}) %all-to-all-start) | async-done | bytes 4128 | tf_op jit(solution)/shard_map/all_to_all | solution.py:44
  40.5 0.5 %reduce_sum.19 = f32[32]{0:T(128)} reduce(f32[32,1,32]{2,0,1:T(8,128)S(1)} %bitcast.34, f32[]{:T(128)} %constant.45.clone.1), dimensions={0,1}, to_apply=%region_1.2 | reduce | flops 992 | bytes 4228 | tf_op jit(solution)/shard_map/reduce_sum | solution.py:44
  41.1 0.0 collective-permute-done.2
  41.1 0.0 collective-permute-done.3
  41.1 0.0 copy-start
  41.1 0.0 copy-start.1
  41.2 0.9 %copy-done = f32[2,64,512]{2,1,0:T(8,128)S(1)} copy-done((f32[2,64,512]{2,1,0:T(8,128)S(1)}, f32[2,64,512]{2,1,0:T(8,128)}, u32[]{:S(2)}) %copy-start) | copy-done | bytes 262168
  42.0 0.1 copy-done.1
  42.1 0.8 %fusion.3 = (bf16[1,1,2,64,512]{4,3,2,1,0:T(8,128)(2,1)}, bf16[1,1,2,64,512]{4,3,2,1,0:T(8,128)(2,1)}) fusion(f32[2,64,512]{2,1,0:T(8,128)S(1)} %copy-done.1, f32[2,64,1024]{2,1,0:T(8,128)S(1)} %maximum_convert_fusion, f32[2,64,512]{2,1,0:T(8,128)S(1)} %copy-done), kind=kLoop, calls=%fused_computation.6 | loop fusion | flops 262144 | bytes 1310720 | tf_op jit(solution)/shard_map/reshape | solution.py:222
  (7 shorter events, 0.1 us)
Async XLA Ops:
  1.6 6.5 %collective-permute-start = (bf16[64,1024]{1,0:T(8,128)(2,1)S(1)}, bf16[64,1024]{1,0:T(8,128)(2,1)S(1)}, u32[]{:S(2)}, u32[]{:S(2)}) collective-permute-start(bf16[64,1024]{1,0:T(8,128)(2,1)S(1)} %pad_maximum_fusion), channel_id=1, source_target_pairs={{0,2},{2,0},{4,6},{6,4},{8,10},{10,8},{12,14},{14,12},{16,18},{18,... | collective-permute-start | bytes 393224 | tf_op jit(solution)/shard_map/ppermute | solution.py:36
  4.6 3.5 %collective-permute-start.1 = (bf16[64,1024]{1,0:T(8,128)(2,1)S(1)}, bf16[64,1024]{1,0:T(8,128)(2,1)S(1)}, u32[]{:S(2)}, u32[]{:S(2)}) collective-permute-start(bf16[64,1024]{1,0:T(8,128)(2,1)S(1)} %pad_maximum_fusion.1), channel_id=1, source_target_pairs={{2,4},{4,2},{6,8},{8,6},{10,12},{12,10},{14,16},{16,14},{18,20},{2... | collective-permute-start | bytes 393224 | tf_op jit(solution)/shard_map/ppermute | solution.py:36
  5.5 0.7 %copy-start.3 = (s32[1,1,2,2,64]{4,3,2,1,0:T(2,128)S(1)}, s32[1,1,2,2,64]{4,3,2,1,0:T(2,128)}, u32[]{:S(2)}) copy-start(s32[1,1,2,2,64]{4,3,2,1,0:T(2,128)} %param.9) | copy-start | bytes 3076
  8.1 0.7 %copy-start.4 = (bf16[64,1024]{1,0:T(8,128)(2,1)}, bf16[64,1024]{1,0:T(8,128)(2,1)S(1)}, u32[]{:S(2)}) copy-start(bf16[64,1024]{1,0:T(8,128)(2,1)S(1)} %collective-permute-done.first_ref) | copy-start | bytes 393220
  8.2 0.7 %copy-start.5 = (bf16[64,1024]{1,0:T(8,128)(2,1)}, bf16[64,1024]{1,0:T(8,128)(2,1)S(1)}, u32[]{:S(2)}) copy-start(bf16[64,1024]{1,0:T(8,128)(2,1)S(1)} %collective-permute-done.1.second_ref) | copy-start | bytes 393220
  17.7 7.2 %copy-start.2 = (f32[2,4,8,128]{3,2,1,0:T(8,128)S(1)}, f32[2,4,8,128]{3,2,1,0:T(8,128)}, u32[]{:S(2)}) copy-start(f32[2,4,8,128]{3,2,1,0:T(8,128)} %get-tuple-element.24) | copy-start | bytes 98308
  18.7 22.4 %collective-permute-start.2 = (bf16[64,1024]{1,0:T(8,128)(2,1)S(1)}, bf16[64,1024]{1,0:T(8,128)(2,1)S(1)}, u32[]{:S(2)}, u32[]{:S(2)}) collective-permute-start(bf16[64,1024]{1,0:T(8,128)(2,1)S(1)} %get-tuple-element.21), channel_id=1, source_target_pairs={{0,2},{2,0},{4,6},{6,4},{8,10},{10,8},{12,14},{14,12},{16,18},{18,... | collective-permute-start | bytes 393224 | tf_op jit(solution)/shard_map/ppermute | solution.py:36
  24.2 16.9 %collective-permute-start.3 = (bf16[64,1024]{1,0:T(8,128)(2,1)S(1)}, bf16[64,1024]{1,0:T(8,128)(2,1)S(1)}, u32[]{:S(2)}, u32[]{:S(2)}) collective-permute-start(bf16[64,1024]{1,0:T(8,128)(2,1)S(1)} %get-tuple-element.22), channel_id=1, source_target_pairs={{2,4},{4,2},{6,8},{8,6},{10,12},{12,10},{14,16},{16,14},{18,20},{2... | collective-permute-start | bytes 393224 | tf_op jit(solution)/shard_map/ppermute | solution.py:36
  25.7 14.9 %all-to-all-start = ((f32[32,1,32]{2,1,0:T(1,128)}), f32[32,1,32]{2,1,0:T(1,128)S(1)}, u32[]{:S(2)}, u32[]{:S(2)}) async-start(f32[32,1,32]{2,1,0:T(1,128)} %broadcast_in_dim.5), calls=%async_computation | async-start | bytes 32768 | tf_op jit(solution)/shard_map/all_to_all | solution.py:44
  41.1 1.0 %copy-start = (f32[2,64,512]{2,1,0:T(8,128)S(1)}, f32[2,64,512]{2,1,0:T(8,128)}, u32[]{:S(2)}) copy-start(f32[2,64,512]{2,1,0:T(8,128)} %get-tuple-element.19) | copy-start | bytes 786436
  41.1 1.0 %copy-start.1 = (f32[2,64,512]{2,1,0:T(8,128)S(1)}, f32[2,64,512]{2,1,0:T(8,128)}, u32[]{:S(2)}) copy-start(f32[2,64,512]{2,1,0:T(8,128)} %get-tuple-element.23) | copy-start | bytes 786436

commit v10 on v9

--- a/solution.py
+++ b/solution.py
@@ -36,17 +36,13 @@
     return lax.ppermute(x, axis, pairs)
 
 
-def all_sum(x, axes):
-    count = 1
-    for axis in axes:
-        count *= lax.axis_size(axis)
-    spread = jnp.broadcast_to(x[None], (count,) + x.shape)
+def all_sum(spread, axes):
     return jnp.sum(lax.all_to_all(spread, axes, 0, 0, tiled=True), axis=0)
 
 
 def group_kernel(
     flag_ref, sink_ref, q_ref, g_ref, k_ref, v_ref, first_ref, second_ref, allow_ref,
-    o_ref, dq_ref, msg_ref, dk_ref, dv_ref, st_ref,
+    o_ref, dq_ref, first_msg_ref, second_msg_ref, dk_ref, dv_ref, st_ref,
 ):
     rows = q_ref.shape[1]
     score_scale = 1.0 / math.sqrt(HEAD_DIM)
@@ -55,6 +51,8 @@
     allowed = jnp.concatenate([allow_ref[0]] * GROUP, axis=0) > 0.5
     head_of_row = lax.broadcasted_iota(jnp.int32, (GROUP * rows, 1), 0) // rows
     use_second = (pl.program_id(0) + flag_ref[0]) % 2 == 1
+    head_lane = lax.broadcasted_iota(jnp.int32, (1, HEADS), 1)
+    sink_row = jnp.zeros((1, HEADS), jnp.float32)
     for group in range(KV_HEADS):
         heads = [pl.ds((group * GROUP + h) * HEAD_DIM, HEAD_DIM) for h in range(GROUP)]
         side = pl.ds(group * HEAD_DIM, HEAD_DIM)
@@ -94,8 +92,13 @@
             * score_scale
         )
         dvalue = lax.dot_general(weights, grad, contract_first, preferred_element_type=jnp.float32)
-        msg_ref[0, :, side] = dkey[:rows].astype(jnp.bfloat16)
-        msg_ref[0, :, value_side] = dvalue[:rows].astype(jnp.bfloat16)
+        for msg_ref, slot in ((first_msg_ref, 0), (second_msg_ref, 1)):
+
+            @pl.when((pl.program_id(0) + flag_ref[0]) % 2 == slot)
+            def _():
+                msg_ref[:, side] = dkey[:rows].astype(jnp.bfloat16)
+                msg_ref[:, value_side] = dvalue[:rows].astype(jnp.bfloat16)
+
         dk_ref[0, :, side] = dkey[rows:]
         dv_ref[0, :, side] = dvalue[rows:]
         sink_share = jnp.exp(sink - log_total) * row_delta
@@ -104,10 +107,18 @@
             o_ref[0, :, heads[h]] = attended[part]
             dq_ref[0, :, heads[h]] = dquery[part].astype(jnp.bfloat16)
             total = -jnp.sum(sink_share[part], axis=0, keepdims=True)
-            st_ref[0, group, pl.ds(h, 1), :] = jnp.broadcast_to(total, (1, 128))
-
-
-def attend_blocks(flag, sink_logit, queries, out_grad, keys, values, first, second, allowed):
+            sink_row = jnp.where(head_lane == group * GROUP + h, total, sink_row)
+
+    @pl.when(pl.program_id(0) == 0)
+    def _():
+        st_ref[...] = jnp.zeros_like(st_ref)
+
+    st_ref[...] += jnp.broadcast_to(sink_row, st_ref.shape)
+
+
+def attend_blocks(
+    flag, sink_logit, queries, out_grad, keys, values, first, second, allowed, devices
+):
     lanes, rows, query_width = queries.shape
     side_width = keys.shape[2]
     pair_width = first.shape[1]
@@ -131,12 +142,11 @@
         out_specs=[
             lane_block(query_width),
             lane_block(query_width),
-            pl.BlockSpec(
-                (1, rows, pair_width), lambda lane, flag_ref: ((lane + flag_ref[0]) % 2, 0, 0)
-            ),
-            lane_block(side_width),
-            lane_block(side_width),
-            pl.BlockSpec((1, KV_HEADS, GROUP, 128), lambda lane, flag_ref: (lane, 0, 0, 0)),
+            whole,
+            whole,
+            lane_block(side_width),
+            lane_block(side_width),
+            pl.BlockSpec((devices, HEADS), lambda lane, flag_ref: (0, 0)),
         ],
     )
     return pl.pallas_call(
@@ -145,10 +155,11 @@
         out_shape=[
             jax.ShapeDtypeStruct((lanes, rows, query_width), jnp.bfloat16),
             jax.ShapeDtypeStruct((lanes, rows, query_width), jnp.bfloat16),
-            jax.ShapeDtypeStruct((lanes, rows, pair_width), jnp.bfloat16),
+            jax.ShapeDtypeStruct((rows, pair_width), jnp.bfloat16),
+            jax.ShapeDtypeStruct((rows, pair_width), jnp.bfloat16),
             jax.ShapeDtypeStruct((lanes, rows, side_width), jnp.float32),
             jax.ShapeDtypeStruct((lanes, rows, side_width), jnp.float32),
-            jax.ShapeDtypeStruct((lanes, KV_HEADS, GROUP, 128), jnp.float32),
+            jax.ShapeDtypeStruct((devices, HEADS), jnp.float32),
         ],
         cost_estimate=pl.CostEstimate(
             flops=flops, transcendentals=4 * lanes * HEADS * rows * rows, bytes_accessed=moved
@@ -192,7 +203,8 @@
     allowed = (key_pos[:, None, :] <= query_pos[:, :, None]) & (
         key_pos[:, None, :] >= first_pos[:, :, None]
     )
-    attended, dquery, message, key_own, value_own, sink_parts = attend_blocks(
+    devices = lax.axis_size("ctx") * lax.axis_size("dp")
+    attended, dquery, sent_first, sent_second, key_own, value_own, sink_spread = attend_blocks(
         even.reshape(1),
         sink_logit,
         queries.reshape(2, block_rows, query_width),
@@ -202,11 +214,10 @@
         first,
         second,
         allowed.astype(jnp.float32),
-    )
-    sink_terms = jnp.sum(sink_parts[:, :, :, 0], axis=0)
-    sink_grad = all_sum(sink_terms.reshape(HEADS), ("ctx", "dp"))
-
-    sent_first, sent_second = lax.optimization_barrier((message[0], message[1]))
+        devices,
+    )
+    sink_grad = all_sum(sink_spread, ("ctx", "dp"))
+
     got_first = swap_pairs(sent_first, "ctx", 0)
     got_second = swap_pairs(sent_second, "ctx", 1)
     is_even = even == 1

time: 43.2 us -> 43.4 us (level)
  Pallas kernels: 8.81 us -> 10.7 us
  local copies, waits for them, and re-layouts: 4.93 us -> 3.23 us
    pallas_call x1, Pallas kernels: 8.81 us -> 10.7 us  [attend_blocks(): pl.pallas_call(group_kernel, grid_spec=grid_spec, out_shape=[jax.ShapeDty...]
    squeeze x1 -> x0, local copies, waits for them, and re-layouts: 0.99 us -> none  [per_device(): sent_first, sent_second = lax.optimization_barrier((message[0], message[1]))]
    broadcast_in_dim x2 -> x0, local copies, waits for them, and re-layouts: 0.71 us -> none  [all_sum(): spread = jnp.broadcast_to(x[None], (count,) + x.shape)]
    unnamed x12 -> x10, local copies, waits for them, and re-layouts: 2.28 us -> 2.27 us
  transfers between devices with their start and end apart: 5 -> 5, of which waited for: 2 -> 2; matrix products, arithmetic and copies ran while one was open for 5% -> 3% of each run, Pallas kernels for 0% -> 0%
where the time goes in v10:
time: 43.4 us; the launch traced here: 43.1 us
  starting transfers between devices  17.6 us (41%)
  Pallas kernels  10.7 us (25%)
  waiting for transfers between devices  8.43 us (19%)
  local copies, waits for them, and re-layouts  3.23 us (7%)
  other arithmetic  2.35 us (5%)
  between operations  0.74 us (2%)
    pallas_call x1, Pallas kernels, attend_blocks(): pl.pallas_call(group_kernel, grid_spec=grid_spec, out_shape=[jax.ShapeDty...  10.7 us
    ppermute x4, starting transfers between devices, swap_pairs(): return lax.ppermute(x, axis, pairs)  9.85 us
    all_to_all x1, starting transfers between devices, all_sum(): return jnp.sum(lax.all_to_all(spread, axes, 0, 0, tiled=True), axis=0)  7.79 us
    all_to_all x1, waiting for transfers between devices, all_sum(): return jnp.sum(lax.all_to_all(spread, axes, 0, 0, tiled=True), axis=0)  7.14 us
    unnamed x10, local copies, waits for them, and re-layouts  2.27 us
    ppermute x4, waiting for transfers between devices, swap_pairs(): return lax.ppermute(x, axis, pairs)  1.28 us
    squeeze x1, local copies, waits for them, and re-layouts, lane_pair(): lax.dynamic_index_in_dim(value_lanes, lane, keepdims=False)  0.96 us
  transfers between devices with their start and end apart: 5, of which 2 were waited for; matrix products, arithmetic and copies ran while one was open for 3% of the time, Pallas kernels for 0%

profile of v10, /device:TPU:0, one launch (start us, length us, event | category | flops | bytes accessed | tf_op | source)
XLA Modules:
  0.0 43.1 jit_solution(7338850467095646564)
XLA Ops:
  0.6 1.0 %dynamic-slice_bitcast_fusion = (bf16[64,512]{1,0:T(8,128)(2,1)S(1)}, bf16[64,512]{1,0:T(8,128)(2,1)S(1)}, bf16[64,512]{1,0:T(8,128)(2,1)S(1)}, bf16[64,512]{1,0:T(8,128)(2,1)S(1)}) fusion(bf16[1,1,2,64,512]{4,3,2,1,0:T(8,128)(2,1)} %param.8, s32[]{:T(128)S(6)} %select_n.30, s32[]{:T(128)S(6)} %select_n.29, bf16[1,1,2,64,512]{4,3,2,1,0:T(8,128)(2,1)} %param.7), kind=kLoop, calls=%fused_computation.11 | loop fusion | bytes 524296 | tf_op jit(solution)/shard_map/jit(dynamic_index_in_dim)/squeeze | solution.py:188
  1.6 3.0 %collective-permute-start = (bf16[64,1024]{1,0:T(8,128)(2,1)S(1)}, bf16[64,1024]{1,0:T(8,128)(2,1)S(1)}, u32[]{:S(2)}, u32[]{:S(2)}) collective-permute-start(bf16[64,1024]{1,0:T(8,128)(2,1)S(1)} %pad_maximum_fusion), channel_id=1, source_target_pairs={{0,2},{2,0},{4,6},{6,4},{8,10},{10,8},{12,14},{14,12},{16,18},{18,... | collective-permute-start | bytes 393224 | tf_op jit(solution)/shard_map/ppermute | solution.py:36
  4.6 0.7 %collective-permute-start.1 = (bf16[64,1024]{1,0:T(8,128)(2,1)S(1)}, bf16[64,1024]{1,0:T(8,128)(2,1)S(1)}, u32[]{:S(2)}, u32[]{:S(2)}) collective-permute-start(bf16[64,1024]{1,0:T(8,128)(2,1)S(1)} %pad_maximum_fusion.1), channel_id=1, source_target_pairs={{2,4},{4,2},{6,8},{8,6},{10,12},{12,10},{14,16},{16,14},{18,20},{2... | collective-permute-start | bytes 393224 | tf_op jit(solution)/shard_map/ppermute | solution.py:36
  5.3 0.1 add_multiply_fusion
  5.4 0.1 iota_add_fusion.1
  5.5 0.0 copy-start.2
  5.5 0.1 iota_add_fusion
  5.5 0.6 %copy-done.2 = s32[1,1,2,2,64]{4,3,2,1,0:T(2,128)S(1)} copy-done((s32[1,1,2,2,64]{4,3,2,1,0:T(2,128)S(1)}, s32[1,1,2,2,64]{4,3,2,1,0:T(2,128)}, u32[]{:S(2)}) %copy-start.2) | copy-done | bytes 1048
  6.2 0.7 %and_convert_fusion.allow_ref = f32[2,64,128]{2,1,0:T(8,128)} fusion(s32[2,64]{1,0:T(2,128)S(1)} %bitcast.33, s32[2,64]{1,0:T(2,128)S(1)} %iota_add_fusion, s32[2,128]{1,0:T(2,128)S(1)} %iota_add_fusion.1), kind=kLoop, calls=%fused_computation.15 | loop fusion | flops 65536 | bytes 67584 | tf_op jit(solution)/shard_map/convert_element_type | solution.py:216
  6.9 1.3 %collective-permute-done.first_ref = bf16[64,1024]{1,0:T(8,128)(2,1)S(1)} collective-permute-done((bf16[64,1024]{1,0:T(8,128)(2,1)S(1)}, bf16[64,1024]{1,0:T(8,128)(2,1)S(1)}, u32[]{:S(2)}, u32[]{:S(2)}) %collective-permute-start) | collective-permute-done | bytes 131104 | tf_op jit(solution)/shard_map/ppermute | solution.py:36
  8.1 0.0 copy-start.3
  8.1 0.0 collective-permute-done.1.second_ref
  8.2 0.0 copy-start.4
  8.2 0.6 %copy-done.3 = bf16[64,1024]{1,0:T(8,128)(2,1)} copy-done((bf16[64,1024]{1,0:T(8,128)(2,1)}, bf16[64,1024]{1,0:T(8,128)(2,1)S(1)}, u32[]{:S(2)}) %copy-start.3) | copy-done | bytes 131096
  8.8 0.0 copy-done.4
  8.8 10.7 %shard_map.101 = (bf16[2,64,4096]{2,1,0:T(8,128)(2,1)}, bf16[2,64,4096]{2,1,0:T(8,128)(2,1)}, bf16[64,1024]{1,0:T(8,128)(2,1)}, bf16[64,1024]{1,0:T(8,128)(2,1)}...) custom-call(s32[1]{0:T(128)} %bitcast.flag_ref, f32[32]{0:T(128)} %sink_ref.1, ...), custom_call_target="tpu_custom_call" | custom-call | flops 805306368 | bytes 5177344 | tf_op jit(solution)/shard_map/pallas_call | solution.py:152
  19.6 5.5 %collective-permute-start.2 = (bf16[64,1024]{1,0:T(8,128)(2,1)}, bf16[64,1024]{1,0:T(8,128)(2,1)S(1)}, u32[]{:S(2)}, u32[]{:S(2)}) collective-permute-start(bf16[64,1024]{1,0:T(8,128)(2,1)} %get-tuple-element.19), channel_id=1, source_target_pairs={{0,2},{2,0},{4,6},{6,4},{8,10},{10,8},{12,14},{14,12},{16,18},{18,... | collective-permute-start | bytes 393224 | tf_op jit(solution)/shard_map/ppermute | solution.py:36
  25.1 0.7 %collective-permute-start.3 = (bf16[64,1024]{1,0:T(8,128)(2,1)}, bf16[64,1024]{1,0:T(8,128)(2,1)S(1)}, u32[]{:S(2)}, u32[]{:S(2)}) collective-permute-start(bf16[64,1024]{1,0:T(8,128)(2,1)} %get-tuple-element.20), channel_id=1, source_target_pairs={{2,4},{4,2},{6,8},{8,6},{10,12},{12,10},{14,16},{16,14},{18,20},{2... | collective-permute-start | bytes 393224 | tf_op jit(solution)/shard_map/ppermute | solution.py:36
  25.8 7.8 %all-to-all-start = ((f32[32,1,32]{2,1,0:T(1,128)}), f32[32,1,32]{2,1,0:T(1,128)S(1)}, u32[]{:S(2)}, u32[]{:S(2)}) async-start(f32[32,1,32]{2,1,0:T(1,128)} %bitcast.32), calls=%async_computation | async-start | bytes 32768 | tf_op jit(solution)/shard_map/all_to_all | solution.py:40
  33.6 7.1 %all-to-all-done = f32[32,1,32]{2,1,0:T(1,128)S(1)} async-done(((f32[32,1,32]{2,1,0:T(1,128)}), f32[32,1,32]{2,1,0:T(1,128)S(1)}, u32[]{:S(2)}, u32[]{:S(2)}) %all-to-all-start) | async-done | bytes 4128 | tf_op jit(solution)/shard_map/all_to_all | solution.py:40
  40.7 0.6 %reduce_sum.9 = f32[32]{0:T(128)} reduce(f32[32,1,32]{2,1,0:T(1,128)S(1)} %all-to-all-done, f32[]{:T(128)} %constant.45.clone.1), dimensions={0,1}, to_apply=%region_0.1 | reduce | flops 992 | bytes 4228 | tf_op jit(solution)/shard_map/reduce_sum | solution.py:40
  41.3 0.0 collective-permute-done.2
  41.3 0.0 collective-permute-done.3
  41.3 0.0 copy-start
  41.3 0.0 copy-start.1
  41.4 0.9 %copy-done = f32[2,64,512]{2,1,0:T(8,128)S(1)} copy-done((f32[2,64,512]{2,1,0:T(8,128)S(1)}, f32[2,64,512]{2,1,0:T(8,128)}, u32[]{:S(2)}) %copy-start) | copy-done | bytes 262168
  42.3 0.1 copy-done.1
  42.3 0.8 %fusion.3 = (bf16[1,1,2,64,512]{4,3,2,1,0:T(8,128)(2,1)}, bf16[1,1,2,64,512]{4,3,2,1,0:T(8,128)(2,1)}) fusion(f32[2,64,512]{2,1,0:T(8,128)S(1)} %copy-done.1, f32[2,64,1024]{2,1,0:T(8,128)S(1)} %maximum_convert_fusion, f32[2,64,512]{2,1,0:T(8,128)S(1)} %copy-done), kind=kLoop, calls=%fused_computation.6 | loop fusion | flops 262144 | bytes 1310720 | tf_op jit(solution)/shard_map/reshape | solution.py:233
  (5 shorter events, 0.1 us)
Async XLA Ops:
  1.6 6.5 %collective-permute-start = (bf16[64,1024]{1,0:T(8,128)(2,1)S(1)}, bf16[64,1024]{1,0:T(8,128)(2,1)S(1)}, u32[]{:S(2)}, u32[]{:S(2)}) collective-permute-start(bf16[64,1024]{1,0:T(8,128)(2,1)S(1)} %pad_maximum_fusion), channel_id=1, source_target_pairs={{0,2},{2,0},{4,6},{6,4},{8,10},{10,8},{12,14},{14,12},{16,18},{18,... | collective-permute-start | bytes 393224 | tf_op jit(solution)/shard_map/ppermute | solution.py:36
  4.6 3.5 %collective-permute-start.1 = (bf16[64,1024]{1,0:T(8,128)(2,1)S(1)}, bf16[64,1024]{1,0:T(8,128)(2,1)S(1)}, u32[]{:S(2)}, u32[]{:S(2)}) collective-permute-start(bf16[64,1024]{1,0:T(8,128)(2,1)S(1)} %pad_maximum_fusion.1), channel_id=1, source_target_pairs={{2,4},{4,2},{6,8},{8,6},{10,12},{12,10},{14,16},{16,14},{18,20},{2... | collective-permute-start | bytes 393224 | tf_op jit(solution)/shard_map/ppermute | solution.py:36
  5.5 0.7 %copy-start.2 = (s32[1,1,2,2,64]{4,3,2,1,0:T(2,128)S(1)}, s32[1,1,2,2,64]{4,3,2,1,0:T(2,128)}, u32[]{:S(2)}) copy-start(s32[1,1,2,2,64]{4,3,2,1,0:T(2,128)} %param.9) | copy-start | bytes 3076
  8.1 0.7 %copy-start.3 = (bf16[64,1024]{1,0:T(8,128)(2,1)}, bf16[64,1024]{1,0:T(8,128)(2,1)S(1)}, u32[]{:S(2)}) copy-start(bf16[64,1024]{1,0:T(8,128)(2,1)S(1)} %collective-permute-done.first_ref) | copy-start | bytes 393220
  8.2 0.7 %copy-start.4 = (bf16[64,1024]{1,0:T(8,128)(2,1)}, bf16[64,1024]{1,0:T(8,128)(2,1)S(1)}, u32[]{:S(2)}) copy-start(bf16[64,1024]{1,0:T(8,128)(2,1)S(1)} %collective-permute-done.1.second_ref) | copy-start | bytes 393220
  19.6 21.7 %collective-permute-start.2 = (bf16[64,1024]{1,0:T(8,128)(2,1)}, bf16[64,1024]{1,0:T(8,128)(2,1)S(1)}, u32[]{:S(2)}, u32[]{:S(2)}) collective-permute-start(bf16[64,1024]{1,0:T(8,128)(2,1)} %get-tuple-element.19), channel_id=1, source_target_pairs={{0,2},{2,0},{4,6},{6,4},{8,10},{10,8},{12,14},{14,12},{16,18},{18,... | collective-permute-start | bytes 393224 | tf_op jit(solution)/shard_map/ppermute | solution.py:36
  25.1 16.2 %collective-permute-start.3 = (bf16[64,1024]{1,0:T(8,128)(2,1)}, bf16[64,1024]{1,0:T(8,128)(2,1)S(1)}, u32[]{:S(2)}, u32[]{:S(2)}) collective-permute-start(bf16[64,1024]{1,0:T(8,128)(2,1)} %get-tuple-element.20), channel_id=1, source_target_pairs={{2,4},{4,2},{6,8},{8,6},{10,12},{12,10},{14,16},{16,14},{18,20},{2... | collective-permute-start | bytes 393224 | tf_op jit(solution)/shard_map/ppermute | solution.py:36
  25.8 14.9 %all-to-all-start = ((f32[32,1,32]{2,1,0:T(1,128)}), f32[32,1,32]{2,1,0:T(1,128)S(1)}, u32[]{:S(2)}, u32[]{:S(2)}) async-start(f32[32,1,32]{2,1,0:T(1,128)} %bitcast.32), calls=%async_computation | async-start | bytes 32768 | tf_op jit(solution)/shard_map/all_to_all | solution.py:40
  41.3 1.0 %copy-start = (f32[2,64,512]{2,1,0:T(8,128)S(1)}, f32[2,64,512]{2,1,0:T(8,128)}, u32[]{:S(2)}) copy-start(f32[2,64,512]{2,1,0:T(8,128)} %get-tuple-element.18) | copy-start | bytes 786436
  41.3 1.0 %copy-start.1 = (f32[2,64,512]{2,1,0:T(8,128)S(1)}, f32[2,64,512]{2,1,0:T(8,128)}, u32[]{:S(2)}) copy-start(f32[2,64,512]{2,1,0:T(8,128)} %get-tuple-element.21) | copy-start | bytes 786436

commit v11 on v10

--- a/solution.py
+++ b/solution.py
@@ -218,6 +218,9 @@
     )
     sink_grad = all_sum(sink_spread, ("ctx", "dp"))
 
+    sent_first, sent_second, sink_grad = lax.optimization_barrier(
+        (sent_first, sent_second, sink_grad)
+    )
     got_first = swap_pairs(sent_first, "ctx", 0)
     got_second = swap_pairs(sent_second, "ctx", 1)
     is_even = even == 1

time: 43.4 us -> 45.6 us (1.051)
  the two profiles are of different devices: /device:TPU:0 before, /device:TPU:2 now
where the time goes in v11:
time: 45.6 us; the launch traced here: 45.3 us
  blocking collectives  11.4 us (25%)
  Pallas kernels  10.7 us (23%)
  starting transfers between devices  8.93 us (20%)
  waiting for transfers between devices  8 us (18%)
  local copies, waits for them, and re-layouts  3.2 us (7%)
  other arithmetic  2.37 us (5%)
  between operations  0.74 us (2%)
    all_to_all x1, blocking collectives, all_sum(): return jnp.sum(lax.all_to_all(spread, axes, 0, 0, tiled=True), axis=0)  11.4 us
    pallas_call x1, Pallas kernels, attend_blocks(): pl.pallas_call(group_kernel, grid_spec=grid_spec, out_shape=[jax.ShapeDty...  10.7 us
    ppermute x4, starting transfers between devices, swap_pairs(): return lax.ppermute(x, axis, pairs)  8.93 us
    ppermute x4, waiting for transfers between devices, swap_pairs(): return lax.ppermute(x, axis, pairs)  8 us
    unnamed x10, local copies, waits for them, and re-layouts  2.24 us
    squeeze x1, local copies, waits for them, and re-layouts, lane_pair(): lax.dynamic_index_in_dim(value_lanes, lane, keepdims=False)  0.96 us
  transfers between devices with their start and end apart: 4, of which 3 were waited for; matrix products, arithmetic and copies ran while one was open for 2% of the time, Pallas kernels for 0%

profile of v11, /device:TPU:2, one launch (start us, length us, event | category | flops | bytes accessed | tf_op | source)
XLA Modules:
  0.0 45.3 jit_solution(6256774154714710083)
XLA Ops:
  0.6 1.0 %dynamic-slice_bitcast_fusion = (bf16[64,512]{1,0:T(8,128)(2,1)S(1)}, bf16[64,512]{1,0:T(8,128)(2,1)S(1)}, bf16[64,512]{1,0:T(8,128)(2,1)S(1)}, bf16[64,512]{1,0:T(8,128)(2,1)S(1)}) fusion(bf16[1,1,2,64,512]{4,3,2,1,0:T(8,128)(2,1)} %param.8, s32[]{:T(128)S(6)} %select_n.30, s32[]{:T(128)S(6)} %select_n.29, bf16[1,1,2,64,512]{4,3,2,1,0:T(8,128)(2,1)} %param.7), kind=kLoop, calls=%fused_computation.11 | loop fusion | bytes 524296 | tf_op jit(solution)/shard_map/jit(dynamic_index_in_dim)/squeeze | solution.py:188
  1.6 0.1 collective-permute-start
  1.7 4.9 %collective-permute-start.1 = (bf16[64,1024]{1,0:T(8,128)(2,1)S(1)}, bf16[64,1024]{1,0:T(8,128)(2,1)S(1)}, u32[]{:S(2)}, u32[]{:S(2)}) collective-permute-start(bf16[64,1024]{1,0:T(8,128)(2,1)S(1)} %pad_maximum_fusion.1), channel_id=1, source_target_pairs={{2,4},{4,2},{6,8},{8,6},{10,12},{12,10},{14,16},{16,14},{18,20},{2... | collective-permute-start | bytes 393224 | tf_op jit(solution)/shard_map/ppermute | solution.py:36
  6.6 0.1 add_multiply_fusion
  6.7 0.1 iota_add_fusion.1
  6.8 0.0 copy-start.2
  6.8 0.1 iota_add_fusion
  6.8 0.6 %copy-done.2 = s32[1,1,2,2,64]{4,3,2,1,0:T(2,128)S(1)} copy-done((s32[1,1,2,2,64]{4,3,2,1,0:T(2,128)S(1)}, s32[1,1,2,2,64]{4,3,2,1,0:T(2,128)}, u32[]{:S(2)}) %copy-start.2) | copy-done | bytes 1048
  7.4 0.7 %and_convert_fusion.allow_ref = f32[2,64,128]{2,1,0:T(8,128)} fusion(s32[2,64]{1,0:T(2,128)S(1)} %bitcast.33, s32[2,64]{1,0:T(2,128)S(1)} %iota_add_fusion, s32[2,128]{1,0:T(2,128)S(1)} %iota_add_fusion.1), kind=kLoop, calls=%fused_computation.15 | loop fusion | flops 65536 | bytes 67584 | tf_op jit(solution)/shard_map/convert_element_type | solution.py:216
  8.2 0.0 collective-permute-done.first_ref
  8.2 0.0 copy-start.3
  8.2 2.5 %collective-permute-done.1.second_ref = bf16[64,1024]{1,0:T(8,128)(2,1)S(1)} collective-permute-done((bf16[64,1024]{1,0:T(8,128)(2,1)S(1)}, bf16[64,1024]{1,0:T(8,128)(2,1)S(1)}, u32[]{:S(2)}, u32[]{:S(2)}) %collective-permute-start.1) | collective-permute-done | bytes 131104 | tf_op jit(solution)/shard_map/ppermute | solution.py:36
  10.7 0.0 copy-start.4
  10.7 0.0 copy-done.3
  10.7 0.7 %copy-done.4 = bf16[64,1024]{1,0:T(8,128)(2,1)} copy-done((bf16[64,1024]{1,0:T(8,128)(2,1)}, bf16[64,1024]{1,0:T(8,128)(2,1)S(1)}, u32[]{:S(2)}) %copy-start.4) | copy-done | bytes 131096
  11.4 10.7 %shard_map.101 = (bf16[2,64,4096]{2,1,0:T(8,128)(2,1)}, bf16[2,64,4096]{2,1,0:T(8,128)(2,1)}, bf16[64,1024]{1,0:T(8,128)(2,1)}, bf16[64,1024]{1,0:T(8,128)(2,1)}...) custom-call(s32[1]{0:T(128)} %bitcast.flag_ref, f32[32]{0:T(128)} %sink_ref.1, ...), custom_call_target="tpu_custom_call" | custom-call | flops 805306368 | bytes 5177344 | tf_op jit(solution)/shard_map/pallas_call | solution.py:152
  22.1 11.4 %all_to_all.9 = f32[32,1,32]{2,1,0:T(1,128)S(1)} all-to-all(f32[32,1,32]{2,1,0:T(1,128)} %bitcast.32), channel_id=1, replica_groups=mesh['ctx'=16,'dp'=2] {'ctx','dp'}, dimensions={0} | all-to-all | bytes 8192 | tf_op jit(solution)/shard_map/all_to_all | solution.py:40
  33.5 0.6 %reduce_sum.9 = f32[32]{0:T(128)} reduce(f32[32,1,32]{2,1,0:T(1,128)S(1)} %all_to_all.9, f32[]{:T(128)} %constant.45.clone.1), dimensions={0,1}, to_apply=%region_0.1 | reduce | flops 992 | bytes 4228 | tf_op jit(solution)/shard_map/reduce_sum | solution.py:40
  34.0 1.5 %collective-permute-start.2 = (bf16[64,1024]{1,0:T(8,128)(2,1)}, bf16[64,1024]{1,0:T(8,128)(2,1)S(1)}, u32[]{:S(2)}, u32[]{:S(2)}) collective-permute-start(bf16[64,1024]{1,0:T(8,128)(2,1)} %get-tuple-element.25), channel_id=1, source_target_pairs={{0,2},{2,0},{4,6},{6,4},{8,10},{10,8},{12,14},{14,12},{16,18},{18,... | collective-permute-start | bytes 393224 | tf_op jit(solution)/shard_map/ppermute | solution.py:36
  35.5 2.5 %collective-permute-start.3 = (bf16[64,1024]{1,0:T(8,128)(2,1)}, bf16[64,1024]{1,0:T(8,128)(2,1)S(1)}, u32[]{:S(2)}, u32[]{:S(2)}) collective-permute-start(bf16[64,1024]{1,0:T(8,128)(2,1)} %get-tuple-element.26), channel_id=1, source_target_pairs={{2,4},{4,2},{6,8},{8,6},{10,12},{12,10},{14,16},{16,14},{18,20},{2... | collective-permute-start | bytes 393224 | tf_op jit(solution)/shard_map/ppermute | solution.py:36
  38.0 1.5 %collective-permute-done.2 = bf16[64,1024]{1,0:T(8,128)(2,1)S(1)} collective-permute-done((bf16[64,1024]{1,0:T(8,128)(2,1)}, bf16[64,1024]{1,0:T(8,128)(2,1)S(1)}, u32[]{:S(2)}, u32[]{:S(2)}) %collective-permute-start.2) | collective-permute-done | bytes 131104 | tf_op jit(solution)/shard_map/ppermute | solution.py:36
  39.5 4.0 %collective-permute-done.3 = bf16[64,1024]{1,0:T(8,128)(2,1)S(1)} collective-permute-done((bf16[64,1024]{1,0:T(8,128)(2,1)}, bf16[64,1024]{1,0:T(8,128)(2,1)S(1)}, u32[]{:S(2)}, u32[]{:S(2)}) %collective-permute-start.3) | collective-permute-done | bytes 131104 | tf_op jit(solution)/shard_map/ppermute | solution.py:36
  43.5 0.0 copy-start
  43.5 0.0 copy-start.1
  43.6 0.9 %copy-done = f32[2,64,512]{2,1,0:T(8,128)S(1)} copy-done((f32[2,64,512]{2,1,0:T(8,128)S(1)}, f32[2,64,512]{2,1,0:T(8,128)}, u32[]{:S(2)}) %copy-start) | copy-done | bytes 262168
  44.5 0.1 copy-done.1
  44.6 0.8 %fusion.3 = (bf16[1,1,2,64,512]{4,3,2,1,0:T(8,128)(2,1)}, bf16[1,1,2,64,512]{4,3,2,1,0:T(8,128)(2,1)}) fusion(f32[2,64,512]{2,1,0:T(8,128)S(1)} %copy-done.1, f32[2,64,1024]{2,1,0:T(8,128)S(1)} %maximum_convert_fusion, f32[2,64,512]{2,1,0:T(8,128)S(1)} %copy-done), kind=kLoop, calls=%fused_computation.6 | loop fusion | flops 262144 | bytes 1310720 | tf_op jit(solution)/shard_map/reshape | solution.py:236
  (5 shorter events, 0.1 us)
Async XLA Ops:
  1.6 6.5 %collective-permute-start = (bf16[64,1024]{1,0:T(8,128)(2,1)S(1)}, bf16[64,1024]{1,0:T(8,128)(2,1)S(1)}, u32[]{:S(2)}, u32[]{:S(2)}) collective-permute-start(bf16[64,1024]{1,0:T(8,128)(2,1)S(1)} %pad_maximum_fusion), channel_id=1, source_target_pairs={{0,2},{2,0},{4,6},{6,4},{8,10},{10,8},{12,14},{14,12},{16,18},{18,... | collective-permute-start | bytes 393224 | tf_op jit(solution)/shard_map/ppermute | solution.py:36
  1.7 9.0 %collective-permute-start.1 = (bf16[64,1024]{1,0:T(8,128)(2,1)S(1)}, bf16[64,1024]{1,0:T(8,128)(2,1)S(1)}, u32[]{:S(2)}, u32[]{:S(2)}) collective-permute-start(bf16[64,1024]{1,0:T(8,128)(2,1)S(1)} %pad_maximum_fusion.1), channel_id=1, source_target_pairs={{2,4},{4,2},{6,8},{8,6},{10,12},{12,10},{14,16},{16,14},{18,20},{2... | collective-permute-start | bytes 393224 | tf_op jit(solution)/shard_map/ppermute | solution.py:36
  6.8 0.7 %copy-start.2 = (s32[1,1,2,2,64]{4,3,2,1,0:T(2,128)S(1)}, s32[1,1,2,2,64]{4,3,2,1,0:T(2,128)}, u32[]{:S(2)}) copy-start(s32[1,1,2,2,64]{4,3,2,1,0:T(2,128)} %param.9) | copy-start | bytes 3076
  8.2 2.5 %copy-start.3 = (bf16[64,1024]{1,0:T(8,128)(2,1)}, bf16[64,1024]{1,0:T(8,128)(2,1)S(1)}, u32[]{:S(2)}) copy-start(bf16[64,1024]{1,0:T(8,128)(2,1)S(1)} %collective-permute-done.first_ref) | copy-start | bytes 393220
  10.7 0.7 %copy-start.4 = (bf16[64,1024]{1,0:T(8,128)(2,1)}, bf16[64,1024]{1,0:T(8,128)(2,1)S(1)}, u32[]{:S(2)}) copy-start(bf16[64,1024]{1,0:T(8,128)(2,1)S(1)} %collective-permute-done.1.second_ref) | copy-start | bytes 393220
  34.0 5.5 %collective-permute-start.2 = (bf16[64,1024]{1,0:T(8,128)(2,1)}, bf16[64,1024]{1,0:T(8,128)(2,1)S(1)}, u32[]{:S(2)}, u32[]{:S(2)}) collective-permute-start(bf16[64,1024]{1,0:T(8,128)(2,1)} %get-tuple-element.25), channel_id=1, source_target_pairs={{0,2},{2,0},{4,6},{6,4},{8,10},{10,8},{12,14},{14,12},{16,18},{18,... | collective-permute-start | bytes 393224 | tf_op jit(solution)/shard_map/ppermute | solution.py:36
  35.5 8.0 %collective-permute-start.3 = (bf16[64,1024]{1,0:T(8,128)(2,1)}, bf16[64,1024]{1,0:T(8,128)(2,1)S(1)}, u32[]{:S(2)}, u32[]{:S(2)}) collective-permute-start(bf16[64,1024]{1,0:T(8,128)(2,1)} %get-tuple-element.26), channel_id=1, source_target_pairs={{2,4},{4,2},{6,8},{8,6},{10,12},{12,10},{14,16},{16,14},{18,20},{2... | collective-permute-start | bytes 393224 | tf_op jit(solution)/shard_map/ppermute | solution.py:36
  43.5 1.0 %copy-start = (f32[2,64,512]{2,1,0:T(8,128)S(1)}, f32[2,64,512]{2,1,0:T(8,128)}, u32[]{:S(2)}) copy-start(f32[2,64,512]{2,1,0:T(8,128)} %get-tuple-element.21) | copy-start | bytes 786436
  43.5 1.0 %copy-start.1 = (f32[2,64,512]{2,1,0:T(8,128)S(1)}, f32[2,64,512]{2,1,0:T(8,128)}, u32[]{:S(2)}) copy-start(f32[2,64,512]{2,1,0:T(8,128)} %get-tuple-element.27) | copy-start | bytes 786436

commit v12 on v9

--- a/solution.py
+++ b/solution.py
@@ -1,3 +1,4 @@
+import functools
 import math
 
 import jax
@@ -44,10 +45,12 @@
     return jnp.sum(lax.all_to_all(spread, axes, 0, 0, tiled=True), axis=0)
 
 
-def group_kernel(
-    flag_ref, sink_ref, q_ref, g_ref, k_ref, v_ref, first_ref, second_ref, allow_ref,
-    o_ref, dq_ref, msg_ref, dk_ref, dv_ref, st_ref,
-):
+def group_kernel(forward, flag_ref, sink_ref, q_ref, g_ref, k_ref, v_ref, first_ref, second_ref,
+                 allow_ref, *refs):
+    if forward:
+        o_ref, st_ref = refs
+    else:
+        o_ref, dq_ref, msg_ref, dk_ref, dv_ref = refs
     rows = q_ref.shape[1]
     score_scale = 1.0 / math.sqrt(HEAD_DIM)
     contract_last = (((1,), (1,)), ((), ()))
@@ -80,12 +83,23 @@
         log_total = row_top + jnp.log(row_total)
         probs = jnp.exp(masked - log_total)
         weights = probs.astype(jnp.bfloat16)
-        attended = jnp.dot(weights, value, preferred_element_type=jnp.float32).astype(
-            jnp.bfloat16
-        )
+        if forward:
+            attended = jnp.dot(weights, value, preferred_element_type=jnp.float32).astype(
+                jnp.bfloat16
+            )
+        else:
+            attended = jnp.concatenate([o_ref[0, :, cols] for cols in heads], axis=0)
         row_delta = jnp.sum(
             grad.astype(jnp.float32) * attended.astype(jnp.float32), axis=1, keepdims=True
         )
+        if forward:
+            sink_share = jnp.exp(sink - log_total) * row_delta
+            for h in range(GROUP):
+                part = slice(h * rows, (h + 1) * rows)
+                o_ref[0, :, heads[h]] = attended[part]
+                total = -jnp.sum(sink_share[part], axis=0, keepdims=True)
+                st_ref[0, group, pl.ds(h, 1), :] = jnp.broadcast_to(total, (1, 128))
+            continue
         dprob = lax.dot_general(grad, value, contract_last, preferred_element_type=jnp.float32)
         dscore = (probs * (dprob - row_delta)).astype(jnp.bfloat16)
         dquery = jnp.dot(dscore, key, preferred_element_type=jnp.float32) * score_scale
@@ -98,62 +112,70 @@
         msg_ref[0, :, value_side] = dvalue[:rows].astype(jnp.bfloat16)
         dk_ref[0, :, side] = dkey[rows:]
         dv_ref[0, :, side] = dvalue[rows:]
-        sink_share = jnp.exp(sink - log_total) * row_delta
         for h in range(GROUP):
             part = slice(h * rows, (h + 1) * rows)
-            o_ref[0, :, heads[h]] = attended[part]
             dq_ref[0, :, heads[h]] = dquery[part].astype(jnp.bfloat16)
-            total = -jnp.sum(sink_share[part], axis=0, keepdims=True)
-            st_ref[0, group, pl.ds(h, 1), :] = jnp.broadcast_to(total, (1, 128))
-
-
-def attend_blocks(flag, sink_logit, queries, out_grad, keys, values, first, second, allowed):
+
+
+def attend_blocks(flag, sink_logit, queries, out_grad, keys, values, first, second, allowed,
+                  attended=None):
+    forward = attended is None
     lanes, rows, query_width = queries.shape
     side_width = keys.shape[2]
     pair_width = first.shape[1]
     lane_block = lambda width: pl.BlockSpec((1, rows, width), lambda lane, flag_ref: (lane, 0, 0))
     whole = pl.BlockSpec((rows, pair_width), lambda lane, flag_ref: (0, 0))
-    flops = 2 * lanes * HEADS * rows * 2 * rows * HEAD_DIM * 6
-    moved = 8 * queries.size + 4 * keys.size + 10 * keys.size + 4 * allowed.size
-    grid_spec = pltpu.PrefetchScalarGridSpec(
-        num_scalar_prefetch=1,
-        grid=(lanes,),
-        in_specs=[
-            pl.BlockSpec(memory_space=pltpu.SMEM),
+    pass_flops = 2 * lanes * HEADS * rows * 2 * rows * HEAD_DIM
+    in_specs = [
+        pl.BlockSpec(memory_space=pltpu.SMEM),
+        lane_block(query_width),
+        lane_block(query_width),
+        lane_block(side_width),
+        lane_block(side_width),
+        whole,
+        whole,
+        pl.BlockSpec((1, rows, 2 * rows), lambda lane, flag_ref: (lane, 0, 0)),
+    ]
+    operands = [flag, sink_logit, queries, out_grad, keys, values, first, second, allowed]
+    if forward:
+        out_specs = [
             lane_block(query_width),
-            lane_block(query_width),
-            lane_block(side_width),
-            lane_block(side_width),
-            whole,
-            whole,
-            pl.BlockSpec((1, rows, 2 * rows), lambda lane, flag_ref: (lane, 0, 0)),
-        ],
-        out_specs=[
-            lane_block(query_width),
+            pl.BlockSpec((1, KV_HEADS, GROUP, 128), lambda lane, flag_ref: (lane, 0, 0, 0)),
+        ]
+        out_shape = [
+            jax.ShapeDtypeStruct((lanes, rows, query_width), jnp.bfloat16),
+            jax.ShapeDtypeStruct((lanes, KV_HEADS, GROUP, 128), jnp.float32),
+        ]
+        flops, moved = 2 * pass_flops, 6 * queries.size + 4 * keys.size + 4 * allowed.size
+    else:
+        in_specs.append(lane_block(query_width))
+        operands.append(attended)
+        out_specs = [
             lane_block(query_width),
             pl.BlockSpec(
                 (1, rows, pair_width), lambda lane, flag_ref: ((lane + flag_ref[0]) % 2, 0, 0)
             ),
             lane_block(side_width),
             lane_block(side_width),
-            pl.BlockSpec((1, KV_HEADS, GROUP, 128), lambda lane, flag_ref: (lane, 0, 0, 0)),
-        ],
-    )
-    return pl.pallas_call(
-        group_kernel,
-        grid_spec=grid_spec,
-        out_shape=[
-            jax.ShapeDtypeStruct((lanes, rows, query_width), jnp.bfloat16),
+        ]
+        out_shape = [
             jax.ShapeDtypeStruct((lanes, rows, query_width), jnp.bfloat16),
             jax.ShapeDtypeStruct((lanes, rows, pair_width), jnp.bfloat16),
             jax.ShapeDtypeStruct((lanes, rows, side_width), jnp.float32),
             jax.ShapeDtypeStruct((lanes, rows, side_width), jnp.float32),
-            jax.ShapeDtypeStruct((lanes, KV_HEADS, GROUP, 128), jnp.float32),
-        ],
+        ]
+        flops, moved = 5 * pass_flops, 8 * queries.size + 12 * keys.size + 4 * allowed.size
+    grid_spec = pltpu.PrefetchScalarGridSpec(
+        num_scalar_prefetch=1, grid=(lanes,), in_specs=in_specs, out_specs=out_specs
+    )
+    return pl.pallas_call(
+        functools.partial(group_kernel, forward),
+        grid_spec=grid_spec,
+        out_shape=out_shape,
         cost_estimate=pl.CostEstimate(
             flops=flops, transcendentals=4 * lanes * HEADS * rows * rows, bytes_accessed=moved
         ),
-    )(flag, sink_logit, queries, out_grad, keys, values, first, second, allowed)
+    )(*operands)
 
 
 def per_device(queries, keys, values, doc_bounds, sink_logit, out_grad):
@@ -192,7 +214,7 @@
     allowed = (key_pos[:, None, :] <= query_pos[:, :, None]) & (
         key_pos[:, None, :] >= first_pos[:, :, None]
     )
-    attended, dquery, message, key_own, value_own, sink_parts = attend_blocks(
+    operands = (
         even.reshape(1),
         sink_logit,
         queries.reshape(2, block_rows, query_width),
@@ -203,10 +225,14 @@
         second,
         allowed.astype(jnp.float32),
     )
+    attended, sink_parts = attend_blocks(*operands)
     sink_terms = jnp.sum(sink_parts[:, :, :, 0], axis=0)
     sink_grad = all_sum(sink_terms.reshape(HEADS), ("ctx", "dp"))
-
-    sent_first, sent_second = lax.optimization_barrier((message[0], message[1]))
+    dquery, message, key_own, value_own = attend_blocks(*operands, attended)
+
+    sent_first, sent_second, sink_grad = lax.optimization_barrier(
+        (message[0], message[1], sink_grad)
+    )
     got_first = swap_pairs(sent_first, "ctx", 0)
     got_second = swap_pairs(sent_second, "ctx", 1)
     is_even = even == 1

time: 43.2 us -> 44.1 us (1.021)
  the two profiles are of different devices: /device:TPU:0 before, /device:TPU:8 now
where the time goes in v12:
time: 44.1 us; the launch traced here: 43.7 us
  starting transfers between devices  13.9 us (32%)
  Pallas kernels  11.6 us (26%)
  waiting for transfers between devices  9.37 us (21%)
  local copies, waits for them, and re-layouts  4.88 us (11%)
  other arithmetic  3.19 us (7%)
  between operations  0.75 us (2%)
    pallas_call x2, Pallas kernels, attend_blocks(): pl.pallas_call(functools.partial(group_kernel, forward), grid_spec=grid_s...  11.6 us
    ppermute x4, starting transfers between devices, swap_pairs(): return lax.ppermute(x, axis, pairs)  9.65 us
    ppermute x4, waiting for transfers between devices, swap_pairs(): return lax.ppermute(x, axis, pairs)  9.37 us
    all_to_all x1, starting transfers between devices, all_sum(): return jnp.sum(lax.all_to_all(spread, axes, 0, 0, tiled=True), axis=0)  4.22 us
    unnamed x10, local copies, waits for them, and re-layouts  2.24 us
    squeeze x1, local copies, waits for them, and re-layouts, per_device(): message[1]  0.99 us
    squeeze x1, local copies, waits for them, and re-layouts, lane_pair(): lax.dynamic_index_in_dim(value_lanes, lane, keepdims=False)  0.96 us
  transfers between devices with their start and end apart: 5, of which 3 were waited for; matrix products, arithmetic and copies ran while one was open for 4% of the time, Pallas kernels for 15%

profile of v12, /device:TPU:8, one launch (start us, length us, event | category | flops | bytes accessed | tf_op | source)
XLA Modules:
  0.0 43.7 jit_solution(12953931120440334964)
XLA Ops:
  0.6 1.0 %dynamic-slice_bitcast_fusion = (bf16[64,512]{1,0:T(8,128)(2,1)S(1)}, bf16[64,512]{1,0:T(8,128)(2,1)S(1)}, bf16[64,512]{1,0:T(8,128)(2,1)S(1)}, bf16[64,512]{1,0:T(8,128)(2,1)S(1)}) fusion(bf16[1,1,2,64,512]{4,3,2,1,0:T(8,128)(2,1)} %param.8, s32[]{:T(128)S(6)} %select_n.30, s32[]{:T(128)S(6)} %select_n.29, bf16[1,1,2,64,512]{4,3,2,1,0:T(8,128)(2,1)} %param.7), kind=kLoop, calls=%fused_computation.13 | loop fusion | bytes 524296 | tf_op jit(solution)/shard_map/jit(dynamic_index_in_dim)/squeeze | solution.py:199
  1.6 1.6 %collective-permute-start = (bf16[64,1024]{1,0:T(8,128)(2,1)S(1)}, bf16[64,1024]{1,0:T(8,128)(2,1)S(1)}, u32[]{:S(2)}, u32[]{:S(2)}) collective-permute-start(bf16[64,1024]{1,0:T(8,128)(2,1)S(1)} %pad_maximum_fusion), channel_id=1, source_target_pairs={{0,2},{2,0},{4,6},{6,4},{8,10},{10,8},{12,14},{14,12},{16,18},{18,... | collective-permute-start | bytes 393224 | tf_op jit(solution)/shard_map/ppermute | solution.py:37
  3.2 3.3 %collective-permute-start.1 = (bf16[64,1024]{1,0:T(8,128)(2,1)S(1)}, bf16[64,1024]{1,0:T(8,128)(2,1)S(1)}, u32[]{:S(2)}, u32[]{:S(2)}) collective-permute-start(bf16[64,1024]{1,0:T(8,128)(2,1)S(1)} %pad_maximum_fusion.1), channel_id=1, source_target_pairs={{2,4},{4,2},{6,8},{8,6},{10,12},{12,10},{14,16},{16,14},{18,20},{2... | collective-permute-start | bytes 393224 | tf_op jit(solution)/shard_map/ppermute | solution.py:37
  6.5 0.1 add_multiply_fusion
  6.6 0.1 iota_add_fusion.1
  6.6 0.0 copy-start.4
  6.6 0.1 iota_add_fusion
  6.7 0.6 %copy-done.4 = s32[1,1,2,2,64]{4,3,2,1,0:T(2,128)S(1)} copy-done((s32[1,1,2,2,64]{4,3,2,1,0:T(2,128)S(1)}, s32[1,1,2,2,64]{4,3,2,1,0:T(2,128)}, u32[]{:S(2)}) %copy-start.4) | copy-done | bytes 1048
  7.3 0.7 %and_convert_fusion.allow_ref = f32[2,64,128]{2,1,0:T(8,128)} fusion(s32[2,64]{1,0:T(2,128)S(1)} %bitcast.42, s32[2,64]{1,0:T(2,128)S(1)} %iota_add_fusion, s32[2,128]{1,0:T(2,128)S(1)} %iota_add_fusion.1), kind=kLoop, calls=%fused_computation.17 | loop fusion | flops 65536 | bytes 67584 | tf_op jit(solution)/shard_map/convert_element_type | solution.py:226
  8.1 0.0 collective-permute-done.first_ref
  8.1 0.0 copy-start
  8.1 3.8 %collective-permute-done.1.second_ref = bf16[64,1024]{1,0:T(8,128)(2,1)S(1)} collective-permute-done((bf16[64,1024]{1,0:T(8,128)(2,1)S(1)}, bf16[64,1024]{1,0:T(8,128)(2,1)S(1)}, u32[]{:S(2)}, u32[]{:S(2)}) %collective-permute-start.1) | collective-permute-done | bytes 131104 | tf_op jit(solution)/shard_map/ppermute | solution.py:37
  11.9 0.0 copy-done
  11.9 0.7 %copy-done.1 = bf16[64,1024]{1,0:T(8,128)(2,1)} copy-done((bf16[64,1024]{1,0:T(8,128)(2,1)}, bf16[64,1024]{1,0:T(8,128)(2,1)S(1)}, u32[]{:S(2)}) %copy-start.1) | copy-done | bytes 131096
  12.5 5.1 %shard_map.101 = (bf16[2,64,4096]{2,1,0:T(8,128)(2,1)}, f32[2,4,8,128]{3,2,1,0:T(8,128)}) custom-call(s32[1]{0:T(128)} %bitcast.flag_ref, f32[32]{0:T(128)} %sink_ref.3, bf16[2,64,4096]{2,1,0:T(8,128)(2,1)} %bitcast.32, bf16[2,64,4096]{2,1,0:T(8,128)(2,1)} %bitcast.34, bf16[2,64,512]{2,1,0:T(8,128)(2,1)} %bitcast.36, bf16[2,64,512]{2,1,0:T(8,128)(2,1)} %bitcast.38, ...), custom_call_target="tpu_custom_call" | custom-call | flops 268435456 | bytes 3473408 | tf_op jit(solution)/shard_map/pallas_call | solution.py:171
  17.6 0.8 %slice_reduce_fusion = f32[4,8]{1,0:T(4,128)S(1)} fusion(f32[2,4,8,128]{3,2,1,0:T(8,128)} %get-tuple-element.22), kind=kLoop, calls=%fused_computation.18 | loop fusion | flops 32 | bytes 384 | tf_op jit(solution)/shard_map/reduce_sum | solution.py:229
  18.5 0.1 broadcast_in_dim.4
  18.6 0.6 %broadcast_in_dim.5 = f32[32,1,32]{2,1,0:T(1,128)} broadcast(f32[32]{0:T(128)S(1)} %broadcast_in_dim.4), dimensions={2} | broadcast | bytes 4224 | tf_op jit(solution)/shard_map/broadcast_in_dim | solution.py:44
  19.2 4.2 %all-to-all-start = ((f32[32,1,32]{2,1,0:T(1,128)}), f32[32,1,32]{2,1,0:T(1,128)S(1)}, u32[]{:S(2)}, u32[]{:S(2)}) async-start(f32[32,1,32]{2,1,0:T(1,128)} %broadcast_in_dim.5), calls=%async_computation | async-start | bytes 32768 | tf_op jit(solution)/shard_map/all_to_all | solution.py:45
  23.4 6.5 %shard_map.102 = (bf16[2,64,4096]{2,1,0:T(8,128)(2,1)}, bf16[2,64,1024]{2,1,0:T(8,128)(2,1)}, f32[2,64,512]{2,1,0:T(8,128)}, f32[2,64,512]{2,1,0:T(8,128)}) custom-call(s32[1]{0:T(128)} %bitcast.flag_ref, f32[32]{0:T(128)} %sink_ref.3, bf16[2,64,4096]{2,1,0:T(8,128)(2,1)} %bitcast.33, bf16[2,64,4096]{2,1,0:T(8,128)(2,1)} %bitcast.35, ...), custom_call_target="tpu_custom_call" | custom-call | flops 671088640 | bytes 5046272 | tf_op jit(solution)/shard_map/pallas_call | solution.py:171
  29.9 1.0 %slice_bitcast_fusion = (bf16[64,1024]{1,0:T(8,128)(2,1)S(1)}, bf16[64,1024]{1,0:T(8,128)(2,1)S(1)}) fusion(bf16[2,64,1024]{2,1,0:T(8,128)(2,1)} %get-tuple-element.21), kind=kLoop, calls=%fused_computation.11 | loop fusion | bytes 524288 | tf_op jit(solution)/shard_map/squeeze | solution.py:234
  30.9 0.0 all-to-all-done
  30.9 0.5 %reduce_sum.19 = f32[32]{0:T(128)} reduce(f32[32,1,32]{2,0,1:T(8,128)S(1)} %bitcast.41, f32[]{:T(128)} %constant.45.clone.1), dimensions={0,1}, to_apply=%region_1.2 | reduce | flops 992 | bytes 4228 | tf_op jit(solution)/shard_map/reduce_sum | solution.py:45
  31.4 1.5 %collective-permute-start.2 = (bf16[64,1024]{1,0:T(8,128)(2,1)S(1)}, bf16[64,1024]{1,0:T(8,128)(2,1)S(1)}, u32[]{:S(2)}, u32[]{:S(2)}) collective-permute-start(bf16[64,1024]{1,0:T(8,128)(2,1)S(1)} %get-tuple-element.23), channel_id=1, source_target_pairs={{0,2},{2,0},{4,6},{6,4},{8,10},{10,8},{12,14},{14,12},{16,18},{18,... | collective-permute-start | bytes 393224 | tf_op jit(solution)/shard_map/ppermute | solution.py:37
  32.9 3.4 %collective-permute-start.3 = (bf16[64,1024]{1,0:T(8,128)(2,1)S(1)}, bf16[64,1024]{1,0:T(8,128)(2,1)S(1)}, u32[]{:S(2)}, u32[]{:S(2)}) collective-permute-start(bf16[64,1024]{1,0:T(8,128)(2,1)S(1)} %get-tuple-element.24), channel_id=1, source_target_pairs={{2,4},{4,2},{6,8},{8,6},{10,12},{12,10},{14,16},{16,14},{18,20},{2... | collective-permute-start | bytes 393224 | tf_op jit(solution)/shard_map/ppermute | solution.py:37
  36.3 0.7 %collective-permute-done.2 = bf16[64,1024]{1,0:T(8,128)(2,1)S(1)} collective-permute-done((bf16[64,1024]{1,0:T(8,128)(2,1)S(1)}, bf16[64,1024]{1,0:T(8,128)(2,1)S(1)}, u32[]{:S(2)}, u32[]{:S(2)}) %collective-permute-start.2) | collective-permute-done | bytes 131104 | tf_op jit(solution)/shard_map/ppermute | solution.py:37
  37.0 4.9 %collective-permute-done.3 = bf16[64,1024]{1,0:T(8,128)(2,1)S(1)} collective-permute-done((bf16[64,1024]{1,0:T(8,128)(2,1)S(1)}, bf16[64,1024]{1,0:T(8,128)(2,1)S(1)}, u32[]{:S(2)}, u32[]{:S(2)}) %collective-permute-start.3) | collective-permute-done | bytes 131104 | tf_op jit(solution)/shard_map/ppermute | solution.py:37
  41.9 0.0 copy-start.2
  41.9 0.0 copy-start.3
  41.9 0.9 %copy-done.2 = f32[2,64,512]{2,1,0:T(8,128)S(1)} copy-done((f32[2,64,512]{2,1,0:T(8,128)S(1)}, f32[2,64,512]{2,1,0:T(8,128)}, u32[]{:S(2)}) %copy-start.2) | copy-done | bytes 262168
  42.8 0.1 copy-done.3
  42.9 0.8 %fusion.3 = (bf16[1,1,2,64,512]{4,3,2,1,0:T(8,128)(2,1)}, bf16[1,1,2,64,512]{4,3,2,1,0:T(8,128)(2,1)}) fusion(f32[2,64,512]{2,1,0:T(8,128)S(1)} %copy-done.3, f32[2,64,1024]{2,1,0:T(8,128)S(1)} %maximum_convert_fusion, f32[2,64,512]{2,1,0:T(8,128)S(1)} %copy-done.2), kind=kLoop, calls=%fused_computation.6 | loop fusion | flops 262144 | bytes 1310720 | tf_op jit(solution)/shard_map/reshape | solution.py:248
  (6 shorter events, 0.1 us)
Async XLA Ops:
  1.6 6.4 %collective-permute-start = (bf16[64,1024]{1,0:T(8,128)(2,1)S(1)}, bf16[64,1024]{1,0:T(8,128)(2,1)S(1)}, u32[]{:S(2)}, u32[]{:S(2)}) collective-permute-start(bf16[64,1024]{1,0:T(8,128)(2,1)S(1)} %pad_maximum_fusion), channel_id=1, source_target_pairs={{0,2},{2,0},{4,6},{6,4},{8,10},{10,8},{12,14},{14,12},{16,18},{18,... | collective-permute-start | bytes 393224 | tf_op jit(solution)/shard_map/ppermute | solution.py:37
  3.2 8.6 %collective-permute-start.1 = (bf16[64,1024]{1,0:T(8,128)(2,1)S(1)}, bf16[64,1024]{1,0:T(8,128)(2,1)S(1)}, u32[]{:S(2)}, u32[]{:S(2)}) collective-permute-start(bf16[64,1024]{1,0:T(8,128)(2,1)S(1)} %pad_maximum_fusion.1), channel_id=1, source_target_pairs={{2,4},{4,2},{6,8},{8,6},{10,12},{12,10},{14,16},{16,14},{18,20},{2... | collective-permute-start | bytes 393224 | tf_op jit(solution)/shard_map/ppermute | solution.py:37
  6.6 0.7 %copy-start.4 = (s32[1,1,2,2,64]{4,3,2,1,0:T(2,128)S(1)}, s32[1,1,2,2,64]{4,3,2,1,0:T(2,128)}, u32[]{:S(2)}) copy-start(s32[1,1,2,2,64]{4,3,2,1,0:T(2,128)} %param.9) | copy-start | bytes 3076
  8.1 3.8 %copy-start = (bf16[64,1024]{1,0:T(8,128)(2,1)}, bf16[64,1024]{1,0:T(8,128)(2,1)S(1)}, u32[]{:S(2)}) copy-start(bf16[64,1024]{1,0:T(8,128)(2,1)S(1)} %collective-permute-done.first_ref) | copy-start | bytes 393220
  11.8 0.7 %copy-start.1 = (bf16[64,1024]{1,0:T(8,128)(2,1)}, bf16[64,1024]{1,0:T(8,128)(2,1)S(1)}, u32[]{:S(2)}) copy-start(bf16[64,1024]{1,0:T(8,128)(2,1)S(1)} %collective-permute-done.1.second_ref) | copy-start | bytes 393220
  19.2 11.7 %all-to-all-start = ((f32[32,1,32]{2,1,0:T(1,128)}), f32[32,1,32]{2,1,0:T(1,128)S(1)}, u32[]{:S(2)}, u32[]{:S(2)}) async-start(f32[32,1,32]{2,1,0:T(1,128)} %broadcast_in_dim.5), calls=%async_computation | async-start | bytes 32768 | tf_op jit(solution)/shard_map/all_to_all | solution.py:45
  31.4 5.5 %collective-permute-start.2 = (bf16[64,1024]{1,0:T(8,128)(2,1)S(1)}, bf16[64,1024]{1,0:T(8,128)(2,1)S(1)}, u32[]{:S(2)}, u32[]{:S(2)}) collective-permute-start(bf16[64,1024]{1,0:T(8,128)(2,1)S(1)} %get-tuple-element.23), channel_id=1, source_target_pairs={{0,2},{2,0},{4,6},{6,4},{8,10},{10,8},{12,14},{14,12},{16,18},{18,... | collective-permute-start | bytes 393224 | tf_op jit(solution)/shard_map/ppermute | solution.py:37
  32.9 8.9 %collective-permute-start.3 = (bf16[64,1024]{1,0:T(8,128)(2,1)S(1)}, bf16[64,1024]{1,0:T(8,128)(2,1)S(1)}, u32[]{:S(2)}, u32[]{:S(2)}) collective-permute-start(bf16[64,1024]{1,0:T(8,128)(2,1)S(1)} %get-tuple-element.24), channel_id=1, source_target_pairs={{2,4},{4,2},{6,8},{8,6},{10,12},{12,10},{14,16},{16,14},{18,20},{2... | collective-permute-start | bytes 393224 | tf_op jit(solution)/shard_map/ppermute | solution.py:37
  41.9 1.0 %copy-start.2 = (f32[2,64,512]{2,1,0:T(8,128)S(1)}, f32[2,64,512]{2,1,0:T(8,128)}, u32[]{:S(2)}) copy-start(f32[2,64,512]{2,1,0:T(8,128)} %get-tuple-element.20) | copy-start | bytes 786436
  41.9 1.0 %copy-start.3 = (f32[2,64,512]{2,1,0:T(8,128)S(1)}, f32[2,64,512]{2,1,0:T(8,128)}, u32[]{:S(2)}) copy-start(f32[2,64,512]{2,1,0:T(8,128)} %get-tuple-element.25) | copy-start | bytes 786436

commit v13 on v7

--- a/solution.py
+++ b/solution.py
@@ -79,11 +79,10 @@
         )
         masked = jnp.where(allowed, scores, -jnp.inf)
         row_top = jnp.maximum(sink, jnp.max(masked, axis=1, keepdims=True))
-        row_total = jnp.exp(sink - row_top) + jnp.sum(
-            jnp.exp(masked - row_top), axis=1, keepdims=True
-        )
-        log_total = row_top + jnp.log(row_total)
-        probs = jnp.exp(masked - log_total)
+        shifted = jnp.exp(masked - row_top)
+        sink_weight = jnp.exp(sink - row_top)
+        inverse_total = 1.0 / (sink_weight + jnp.sum(shifted, axis=1, keepdims=True))
+        probs = shifted * inverse_total
         weights = probs.astype(jnp.bfloat16)
         attended = jnp.dot(weights, value, preferred_element_type=jnp.float32).astype(
             jnp.bfloat16
@@ -101,7 +100,7 @@
         dv_ref[0, :, side] = lax.dot_general(
             weights, grad, contract_first, preferred_element_type=jnp.float32
         )
-        sink_share = jnp.exp(sink - log_total) * row_delta
+        sink_share = sink_weight * inverse_total * row_delta
         for h in range(GROUP):
             part = slice(h * rows, (h + 1) * rows)
             o_ref[0, :, heads[h]] = attended[part]

time: 42.8 us -> 42.5 us (level)
  no operation moved by 1% of the time
where the time goes in v13:
time: 42.5 us; the launch traced here: 42.2 us
  blocking collectives  13.5 us (32%)
  starting transfers between devices  8.96 us (21%)
  Pallas kernels  8.19 us (19%)
  waiting for transfers between devices  4.37 us (10%)
  other arithmetic  3.77 us (9%)
  local copies, waits for them, and re-layouts  2.67 us (6%)
  between operations  0.77 us (2%)
    all_to_all x1, blocking collectives, all_sum(): return jnp.sum(lax.all_to_all(spread, axes, 0, 0, tiled=True), axis=0)  13.5 us
    ppermute x4, starting transfers between devices, swap_pairs(): return lax.ppermute(x, axis, pairs)  8.96 us
    pallas_call x1, Pallas kernels, attend_blocks(): pl.pallas_call(group_kernel, grid=(lanes,), in_specs=[pl.BlockSpec(memory...  8.19 us
    ppermute x4, waiting for transfers between devices, swap_pairs(): return lax.ppermute(x, axis, pairs)  4.37 us
    unnamed x11, local copies, waits for them, and re-layouts  1.81 us
    select_n x2, other arithmetic, neighbour_swap(): jnp.where(even, to_prev, to_next)  1.12 us
    concatenate x1, other arithmetic, per_device(): window = jnp.concatenate([prev_pair, own_pair], axis=1)  0.85 us
  transfers between devices with their start and end apart: 4, of which 1 were waited for; matrix products, arithmetic and copies ran while one was open for 4% of the time, Pallas kernels for 0%

profile of v13, /device:TPU:0, one launch (start us, length us, event | category | flops | bytes accessed | tf_op | source)
XLA Modules:
  0.0 42.2 jit_solution(8983173198351358277)
XLA Ops:
  0.6 0.0 copy-start
  0.7 0.0 copy-start.1
  0.7 1.1 %broadcast_select_fusion.2 = (bf16[64,1024]{1,0:T(8,128)(2,1)S(1)}, bf16[64,1024]{1,0:T(8,128)(2,1)S(1)}) fusion(pred[]{:T(512)S(6)} %eq.10, bf16[2,64,512]{2,1,0:T(8,128)(2,1)} %bitcast.51, bf16[2,64,512]{2,1,0:T(8,128)(2,1)} %bitcast.54), kind=kLoop, calls=%fused_computation.19 | loop fusion | flops 917504 | bytes 524289 | tf_op jit(solution)/shard_map/jit(_where)/select_n | solution.py:40
  1.8 0.7 %collective-permute-start = (bf16[64,1024]{1,0:T(8,128)(2,1)S(1)}, bf16[64,1024]{1,0:T(8,128)(2,1)S(1)}, u32[]{:S(2)}, u32[]{:S(2)}) collective-permute-start(bf16[64,1024]{1,0:T(8,128)(2,1)S(1)} %get-tuple-element.14), channel_id=1, source_target_pairs={{2,4},{4,2},{6,8},{8,6},{10,12},{12,10},{14,16},{16,14},{18,20},{2... | collective-permute-start | bytes 393224 | tf_op jit(solution)/shard_map/ppermute | solution.py:34
  2.4 5.7 %collective-permute-start.1 = (bf16[64,1024]{1,0:T(8,128)(2,1)S(1)}, bf16[64,1024]{1,0:T(8,128)(2,1)S(1)}, u32[]{:S(2)}, u32[]{:S(2)}) collective-permute-start(bf16[64,1024]{1,0:T(8,128)(2,1)S(1)} %get-tuple-element.15), channel_id=1, source_target_pairs={{0,2},{2,0},{4,6},{6,4},{8,10},{10,8},{12,14},{14,12},{16,18},{18,... | collective-permute-start | bytes 393224 | tf_op jit(solution)/shard_map/ppermute | solution.py:34
  8.2 0.1 add_multiply_fusion
  8.3 0.1 iota_add_fusion.1
  8.3 0.1 iota_add_fusion
  8.4 0.6 %copy-done.4 = s32[1,1,2,2,64]{4,3,2,1,0:T(2,128)S(1)} copy-done((s32[1,1,2,2,64]{4,3,2,1,0:T(2,128)S(1)}, s32[1,1,2,2,64]{4,3,2,1,0:T(2,128)}, u32[]{:S(2)}) %copy-start.4) | copy-done | bytes 1048
  9.0 0.7 %and_convert_fusion.allow_ref = f32[2,64,128]{2,1,0:T(8,128)} fusion(s32[2,64]{1,0:T(2,128)S(1)} %bitcast.60, s32[2,64]{1,0:T(2,128)S(1)} %iota_add_fusion, s32[2,128]{1,0:T(2,128)S(1)} %iota_add_fusion.1), kind=kLoop, calls=%fused_computation.21 | loop fusion | flops 65536 | bytes 67584 | tf_op jit(solution)/shard_map/convert_element_type | solution.py:184
  9.7 0.0 collective-permute-done
  9.8 4.4 %collective-permute-done.1 = bf16[64,1024]{1,0:T(8,128)(2,1)S(1)} collective-permute-done((bf16[64,1024]{1,0:T(8,128)(2,1)S(1)}, bf16[64,1024]{1,0:T(8,128)(2,1)S(1)}, u32[]{:S(2)}, u32[]{:S(2)}) %collective-permute-start.1) | collective-permute-done | bytes 131104 | tf_op jit(solution)/shard_map/ppermute | solution.py:34
  14.1 0.0 copy-done
  14.1 0.0 copy-done.1
  14.1 0.1 select_bitcast_fusion.3
  14.2 0.8 %maximum_maximum_fusion.k_ref.v_ref = bf16[2,128,1024]{2,1,0:T(8,128)(2,1)} fusion(bf16[2,64,512]{2,1,0:T(8,128)(2,1)S(1)} %bitcast.53, bf16[2,64,512]{2,1,0:T(8,128)(2,1)S(1)} %bitcast.56, bf16[1,64,1024]{2,1,0:T(8,128)(2,1)S(1)} %get-tuple-element.30, bf16[1,64,1024]{2,1,0:T(8,128)(2,1)S(1)} %get-tuple-element.29), kind=kLoop, calls=%fused_computation.2 | loop fusion | flops 2097152 | bytes 1048576 | tf_op jit(solution)/shard_map/concatenate | solution.py:168
  15.0 8.2 %shard_map.101 = (bf16[2,64,4096]{2,1,0:T(8,128)(2,1)}, bf16[2,64,4096]{2,1,0:T(8,128)(2,1)}, f32[2,128,512]{2,1,0:T(8,128)}, f32[2,128,512]{2,1,0:T(8,128)}, f32[2,4,8,128]{3,2,1,0:T(8,128)}) custom-call(f32[32]{0:T(128)} %sink_ref.1, bf16[2,64,4096]{2,1,0:T(8,128)(2,1)} %bitcast.57, bf16[2,64,4096]{2,1,0:T(8,128)(2,1)} %bitcast.58, ...), custom_call_target="tpu_custom_call" | custom-call | flops 805306368 | bytes 7405568 | tf_op jit(solution)/shard_map/pallas_call | solution.py:120
  23.2 1.1 %constant_dynamic-update-slice_fusion.1 = f32[2,128,1024]{2,1,0:T(8,128)S(1)} fusion(f32[2,128,512]{2,1,0:T(8,128)} %get-tuple-element.18), kind=kLoop, calls=%fused_computation.24 | loop fusion | bytes 1048576
  24.4 0.1 copy-done.2
  24.5 0.1 convert.7
  24.6 0.0 copy-start.3
  24.6 1.9 %collective-permute-start.2 = (bf16[64,1024]{1,0:T(8,128)(2,1)S(1)}, bf16[64,1024]{1,0:T(8,128)(2,1)S(1)}, u32[]{:S(2)}, u32[]{:S(2)}) collective-permute-start(bf16[64,1024]{1,0:T(8,128)(2,1)S(1)} %get-tuple-element.20), channel_id=1, source_target_pairs={{0,2},{2,0},{4,6},{6,4},{8,10},{10,8},{12,14},{14,12},{16,18},{18,... | collective-permute-start | bytes 393224 | tf_op jit(solution)/shard_map/ppermute | solution.py:34
  26.5 0.7 %collective-permute-start.3 = (bf16[64,1024]{1,0:T(8,128)(2,1)S(1)}, bf16[64,1024]{1,0:T(8,128)(2,1)S(1)}, u32[]{:S(2)}, u32[]{:S(2)}) collective-permute-start(bf16[64,1024]{1,0:T(8,128)(2,1)S(1)} %get-tuple-element.21), channel_id=1, source_target_pairs={{2,4},{4,2},{6,8},{8,6},{10,12},{12,10},{14,16},{16,14},{18,20},{2... | collective-permute-start | bytes 393224 | tf_op jit(solution)/shard_map/ppermute | solution.py:34
  27.2 0.0 copy-done.3
  27.2 0.1 slice_reduce_fusion
  27.3 0.1 broadcast_in_dim.4
  27.4 13.5 %all_to_all.6 = f32[32,1,32]{2,1,0:T(1,128)S(1)} all-to-all(f32[32,1,32]{2,1,0:T(1,128)S(1)} %broadcast_in_dim.5), channel_id=1, replica_groups=mesh['ctx'=16,'dp'=2] {'ctx','dp'}, dimensions={0} | all-to-all | bytes 8192 | tf_op jit(solution)/shard_map/all_to_all | solution.py:54
  40.9 0.5 %reduce_sum.19 = f32[32]{0:T(128)} reduce(f32[32,1,32]{2,0,1:T(8,128)S(1)} %bitcast.59, f32[]{:T(128)} %constant.32.clone.1), dimensions={0,1}, to_apply=%region_1.2 | reduce | flops 992 | bytes 4228 | tf_op jit(solution)/shard_map/reduce_sum | solution.py:54
  41.4 0.0 collective-permute-done.2
  41.4 0.0 collective-permute-done.3
  41.4 0.1 fusion
  41.5 0.7 %slice_bitcast_fusion = (bf16[1,1,2,64,512]{4,3,2,1,0:T(8,128)(2,1)}, bf16[1,1,2,64,512]{4,3,2,1,0:T(8,128)(2,1)}) fusion(bf16[2,64,1024]{2,1,0:T(8,128)(2,1)S(1)} %fusion), kind=kLoop, calls=%fused_computation.7 | loop fusion | bytes 524288 | tf_op jit(solution)/shard_map/reshape | solution.py:201
  (7 shorter events, 0.1 us)
Async XLA Ops:
  0.6 13.5 %copy-start = (bf16[1,1,2,64,512]{4,3,2,1,0:T(8,128)(2,1)S(1)}, bf16[1,1,2,64,512]{4,3,2,1,0:T(8,128)(2,1)}, u32[]{:S(2)}) copy-start(bf16[1,1,2,64,512]{4,3,2,1,0:T(8,128)(2,1)} %param.8) | copy-start | bytes 393220
  0.7 13.5 %copy-start.1 = (bf16[1,1,2,64,512]{4,3,2,1,0:T(8,128)(2,1)S(1)}, bf16[1,1,2,64,512]{4,3,2,1,0:T(8,128)(2,1)}, u32[]{:S(2)}) copy-start(bf16[1,1,2,64,512]{4,3,2,1,0:T(8,128)(2,1)} %param.7) | copy-start | bytes 393220
  1.8 8.0 %collective-permute-start = (bf16[64,1024]{1,0:T(8,128)(2,1)S(1)}, bf16[64,1024]{1,0:T(8,128)(2,1)S(1)}, u32[]{:S(2)}, u32[]{:S(2)}) collective-permute-start(bf16[64,1024]{1,0:T(8,128)(2,1)S(1)} %get-tuple-element.14), channel_id=1, source_target_pairs={{2,4},{4,2},{6,8},{8,6},{10,12},{12,10},{14,16},{16,14},{18,20},{2... | collective-permute-start | bytes 393224 | tf_op jit(solution)/shard_map/ppermute | solution.py:34
  2.4 11.7 %collective-permute-start.1 = (bf16[64,1024]{1,0:T(8,128)(2,1)S(1)}, bf16[64,1024]{1,0:T(8,128)(2,1)S(1)}, u32[]{:S(2)}, u32[]{:S(2)}) collective-permute-start(bf16[64,1024]{1,0:T(8,128)(2,1)S(1)} %get-tuple-element.15), channel_id=1, source_target_pairs={{0,2},{2,0},{4,6},{6,4},{8,10},{10,8},{12,14},{14,12},{16,18},{18,... | collective-permute-start | bytes 393224 | tf_op jit(solution)/shard_map/ppermute | solution.py:34
  8.3 0.7 %copy-start.4 = (s32[1,1,2,2,64]{4,3,2,1,0:T(2,128)S(1)}, s32[1,1,2,2,64]{4,3,2,1,0:T(2,128)}, u32[]{:S(2)}) copy-start(s32[1,1,2,2,64]{4,3,2,1,0:T(2,128)} %param.9) | copy-start | bytes 3076
  23.2 1.2 %copy-start.2 = (f32[2,128,512]{2,1,0:T(8,128)S(1)}, f32[2,128,512]{2,1,0:T(8,128)}, u32[]{:S(2)}) copy-start(f32[2,128,512]{2,1,0:T(8,128)} %get-tuple-element.19) | copy-start | bytes 1572868
  24.6 2.6 %copy-start.3 = (f32[2,4,8,128]{3,2,1,0:T(8,128)S(1)}, f32[2,4,8,128]{3,2,1,0:T(8,128)}, u32[]{:S(2)}) copy-start(f32[2,4,8,128]{3,2,1,0:T(8,128)} %get-tuple-element.22) | copy-start | bytes 98308
  24.6 16.8 %collective-permute-start.2 = (bf16[64,1024]{1,0:T(8,128)(2,1)S(1)}, bf16[64,1024]{1,0:T(8,128)(2,1)S(1)}, u32[]{:S(2)}, u32[]{:S(2)}) collective-permute-start(bf16[64,1024]{1,0:T(8,128)(2,1)S(1)} %get-tuple-element.20), channel_id=1, source_target_pairs={{0,2},{2,0},{4,6},{6,4},{8,10},{10,8},{12,14},{14,12},{16,18},{18,... | collective-permute-start | bytes 393224 | tf_op jit(solution)/shard_map/ppermute | solution.py:34
  26.5 14.9 %collective-permute-start.3 = (bf16[64,1024]{1,0:T(8,128)(2,1)S(1)}, bf16[64,1024]{1,0:T(8,128)(2,1)S(1)}, u32[]{:S(2)}, u32[]{:S(2)}) collective-permute-start(bf16[64,1024]{1,0:T(8,128)(2,1)S(1)} %get-tuple-element.21), channel_id=1, source_target_pairs={{2,4},{4,2},{6,8},{8,6},{10,12},{12,10},{14,16},{16,14},{18,20},{2... | collective-permute-start | bytes 393224 | tf_op jit(solution)/shard_map/ppermute | solution.py:34

commit v14 on v13

--- a/solution.py
+++ b/solution.py
@@ -39,8 +39,8 @@
     first, second = lax.optimization_barrier(
         (jnp.where(even, to_next, to_prev), jnp.where(even, to_prev, to_next))
     )
+    got_second = swap_pairs(second, axis, 1)
     got_first = swap_pairs(first, axis, 0)
-    got_second = swap_pairs(second, axis, 1)
     from_prev = jnp.where(even, got_second, got_first)
     from_next = jnp.where(even, got_first, got_second)
     return from_prev, from_next

time: 42.5 us -> 42.5 us (level)
  no operation moved by 1% of the time
where the time goes in v14:
time: 42.5 us; the launch traced here: 42.2 us
  blocking collectives  13.5 us (32%)
  starting transfers between devices  8.96 us (21%)
  Pallas kernels  8.19 us (19%)
  waiting for transfers between devices  4.37 us (10%)
  other arithmetic  3.77 us (9%)
  local copies, waits for them, and re-layouts  2.67 us (6%)
  between operations  0.77 us (2%)
    all_to_all x1, blocking collectives, all_sum(): return jnp.sum(lax.all_to_all(spread, axes, 0, 0, tiled=True), axis=0)  13.5 us
    ppermute x4, starting transfers between devices, swap_pairs(): return lax.ppermute(x, axis, pairs)  8.96 us
    pallas_call x1, Pallas kernels, attend_blocks(): pl.pallas_call(group_kernel, grid=(lanes,), in_specs=[pl.BlockSpec(memory...  8.19 us
    ppermute x4, waiting for transfers between devices, swap_pairs(): return lax.ppermute(x, axis, pairs)  4.37 us
    unnamed x11, local copies, waits for them, and re-layouts  1.81 us
    select_n x2, other arithmetic, neighbour_swap(): jnp.where(even, to_prev, to_next)  1.12 us
    concatenate x1, other arithmetic, per_device(): window = jnp.concatenate([prev_pair, own_pair], axis=1)  0.85 us
  transfers between devices with their start and end apart: 4, of which 1 were waited for; matrix products, arithmetic and copies ran while one was open for 4% of the time, Pallas kernels for 0%

profile of v14, /device:TPU:0, one launch (start us, length us, event | category | flops | bytes accessed | tf_op | source)
XLA Modules:
  0.0 42.2 jit_solution(8983173198351358277)
XLA Ops:
  0.6 0.0 copy-start
  0.7 0.0 copy-start.1
  0.7 1.1 %broadcast_select_fusion.2 = (bf16[64,1024]{1,0:T(8,128)(2,1)S(1)}, bf16[64,1024]{1,0:T(8,128)(2,1)S(1)}) fusion(pred[]{:T(512)S(6)} %eq.10, bf16[2,64,512]{2,1,0:T(8,128)(2,1)} %bitcast.51, bf16[2,64,512]{2,1,0:T(8,128)(2,1)} %bitcast.54), kind=kLoop, calls=%fused_computation.19 | loop fusion | flops 917504 | bytes 524289 | tf_op jit(solution)/shard_map/jit(_where)/select_n | solution.py:40
  1.8 0.7 %collective-permute-start = (bf16[64,1024]{1,0:T(8,128)(2,1)S(1)}, bf16[64,1024]{1,0:T(8,128)(2,1)S(1)}, u32[]{:S(2)}, u32[]{:S(2)}) collective-permute-start(bf16[64,1024]{1,0:T(8,128)(2,1)S(1)} %get-tuple-element.14), channel_id=1, source_target_pairs={{2,4},{4,2},{6,8},{8,6},{10,12},{12,10},{14,16},{16,14},{18,20},{2... | collective-permute-start | bytes 393224 | tf_op jit(solution)/shard_map/ppermute | solution.py:34
  2.4 5.7 %collective-permute-start.1 = (bf16[64,1024]{1,0:T(8,128)(2,1)S(1)}, bf16[64,1024]{1,0:T(8,128)(2,1)S(1)}, u32[]{:S(2)}, u32[]{:S(2)}) collective-permute-start(bf16[64,1024]{1,0:T(8,128)(2,1)S(1)} %get-tuple-element.15), channel_id=1, source_target_pairs={{0,2},{2,0},{4,6},{6,4},{8,10},{10,8},{12,14},{14,12},{16,18},{18,... | collective-permute-start | bytes 393224 | tf_op jit(solution)/shard_map/ppermute | solution.py:34
  8.2 0.1 add_multiply_fusion
  8.3 0.1 iota_add_fusion.1
  8.3 0.1 iota_add_fusion
  8.4 0.6 %copy-done.4 = s32[1,1,2,2,64]{4,3,2,1,0:T(2,128)S(1)} copy-done((s32[1,1,2,2,64]{4,3,2,1,0:T(2,128)S(1)}, s32[1,1,2,2,64]{4,3,2,1,0:T(2,128)}, u32[]{:S(2)}) %copy-start.4) | copy-done | bytes 1048
  9.0 0.7 %and_convert_fusion.allow_ref = f32[2,64,128]{2,1,0:T(8,128)} fusion(s32[2,64]{1,0:T(2,128)S(1)} %bitcast.60, s32[2,64]{1,0:T(2,128)S(1)} %iota_add_fusion, s32[2,128]{1,0:T(2,128)S(1)} %iota_add_fusion.1), kind=kLoop, calls=%fused_computation.21 | loop fusion | flops 65536 | bytes 67584 | tf_op jit(solution)/shard_map/convert_element_type | solution.py:184
  9.7 0.0 collective-permute-done
  9.8 4.4 %collective-permute-done.1 = bf16[64,1024]{1,0:T(8,128)(2,1)S(1)} collective-permute-done((bf16[64,1024]{1,0:T(8,128)(2,1)S(1)}, bf16[64,1024]{1,0:T(8,128)(2,1)S(1)}, u32[]{:S(2)}, u32[]{:S(2)}) %collective-permute-start.1) | collective-permute-done | bytes 131104 | tf_op jit(solution)/shard_map/ppermute | solution.py:34
  14.1 0.0 copy-done
  14.1 0.0 copy-done.1
  14.1 0.1 select_bitcast_fusion.3
  14.2 0.8 %maximum_maximum_fusion.k_ref.v_ref = bf16[2,128,1024]{2,1,0:T(8,128)(2,1)} fusion(bf16[2,64,512]{2,1,0:T(8,128)(2,1)S(1)} %bitcast.53, bf16[2,64,512]{2,1,0:T(8,128)(2,1)S(1)} %bitcast.56, bf16[1,64,1024]{2,1,0:T(8,128)(2,1)S(1)} %get-tuple-element.30, bf16[1,64,1024]{2,1,0:T(8,128)(2,1)S(1)} %get-tuple-element.29), kind=kLoop, calls=%fused_computation.2 | loop fusion | flops 2097152 | bytes 1048576 | tf_op jit(solution)/shard_map/concatenate | solution.py:168
  15.0 8.2 %shard_map.101 = (bf16[2,64,4096]{2,1,0:T(8,128)(2,1)}, bf16[2,64,4096]{2,1,0:T(8,128)(2,1)}, f32[2,128,512]{2,1,0:T(8,128)}, f32[2,128,512]{2,1,0:T(8,128)}, f32[2,4,8,128]{3,2,1,0:T(8,128)}) custom-call(f32[32]{0:T(128)} %sink_ref.1, bf16[2,64,4096]{2,1,0:T(8,128)(2,1)} %bitcast.57, bf16[2,64,4096]{2,1,0:T(8,128)(2,1)} %bitcast.58, ...), custom_call_target="tpu_custom_call" | custom-call | flops 805306368 | bytes 7405568 | tf_op jit(solution)/shard_map/pallas_call | solution.py:120
  23.2 1.1 %constant_dynamic-update-slice_fusion.1 = f32[2,128,1024]{2,1,0:T(8,128)S(1)} fusion(f32[2,128,512]{2,1,0:T(8,128)} %get-tuple-element.18), kind=kLoop, calls=%fused_computation.24 | loop fusion | bytes 1048576
  24.4 0.1 copy-done.2
  24.5 0.1 convert.7
  24.6 0.0 copy-start.3
  24.6 1.9 %collective-permute-start.2 = (bf16[64,1024]{1,0:T(8,128)(2,1)S(1)}, bf16[64,1024]{1,0:T(8,128)(2,1)S(1)}, u32[]{:S(2)}, u32[]{:S(2)}) collective-permute-start(bf16[64,1024]{1,0:T(8,128)(2,1)S(1)} %get-tuple-element.20), channel_id=1, source_target_pairs={{0,2},{2,0},{4,6},{6,4},{8,10},{10,8},{12,14},{14,12},{16,18},{18,... | collective-permute-start | bytes 393224 | tf_op jit(solution)/shard_map/ppermute | solution.py:34
  26.5 0.7 %collective-permute-start.3 = (bf16[64,1024]{1,0:T(8,128)(2,1)S(1)}, bf16[64,1024]{1,0:T(8,128)(2,1)S(1)}, u32[]{:S(2)}, u32[]{:S(2)}) collective-permute-start(bf16[64,1024]{1,0:T(8,128)(2,1)S(1)} %get-tuple-element.21), channel_id=1, source_target_pairs={{2,4},{4,2},{6,8},{8,6},{10,12},{12,10},{14,16},{16,14},{18,20},{2... | collective-permute-start | bytes 393224 | tf_op jit(solution)/shard_map/ppermute | solution.py:34
  27.2 0.0 copy-done.3
  27.2 0.1 slice_reduce_fusion
  27.3 0.1 broadcast_in_dim.4
  27.4 13.5 %all_to_all.6 = f32[32,1,32]{2,1,0:T(1,128)S(1)} all-to-all(f32[32,1,32]{2,1,0:T(1,128)S(1)} %broadcast_in_dim.5), channel_id=1, replica_groups=mesh['ctx'=16,'dp'=2] {'ctx','dp'}, dimensions={0} | all-to-all | bytes 8192 | tf_op jit(solution)/shard_map/all_to_all | solution.py:54
  40.9 0.5 %reduce_sum.19 = f32[32]{0:T(128)} reduce(f32[32,1,32]{2,0,1:T(8,128)S(1)} %bitcast.59, f32[]{:T(128)} %constant.32.clone.1), dimensions={0,1}, to_apply=%region_1.2 | reduce | flops 992 | bytes 4228 | tf_op jit(solution)/shard_map/reduce_sum | solution.py:54
  41.4 0.0 collective-permute-done.2
  41.4 0.0 collective-permute-done.3
  41.4 0.1 fusion
  41.5 0.7 %slice_bitcast_fusion = (bf16[1,1,2,64,512]{4,3,2,1,0:T(8,128)(2,1)}, bf16[1,1,2,64,512]{4,3,2,1,0:T(8,128)(2,1)}) fusion(bf16[2,64,1024]{2,1,0:T(8,128)(2,1)S(1)} %fusion), kind=kLoop, calls=%fused_computation.7 | loop fusion | bytes 524288 | tf_op jit(solution)/shard_map/reshape | solution.py:201
  (7 shorter events, 0.1 us)
Async XLA Ops:
  0.6 13.5 %copy-start = (bf16[1,1,2,64,512]{4,3,2,1,0:T(8,128)(2,1)S(1)}, bf16[1,1,2,64,512]{4,3,2,1,0:T(8,128)(2,1)}, u32[]{:S(2)}) copy-start(bf16[1,1,2,64,512]{4,3,2,1,0:T(8,128)(2,1)} %param.8) | copy-start | bytes 393220
  0.7 13.5 %copy-start.1 = (bf16[1,1,2,64,512]{4,3,2,1,0:T(8,128)(2,1)S(1)}, bf16[1,1,2,64,512]{4,3,2,1,0:T(8,128)(2,1)}, u32[]{:S(2)}) copy-start(bf16[1,1,2,64,512]{4,3,2,1,0:T(8,128)(2,1)} %param.7) | copy-start | bytes 393220
  1.8 8.0 %collective-permute-start = (bf16[64,1024]{1,0:T(8,128)(2,1)S(1)}, bf16[64,1024]{1,0:T(8,128)(2,1)S(1)}, u32[]{:S(2)}, u32[]{:S(2)}) collective-permute-start(bf16[64,1024]{1,0:T(8,128)(2,1)S(1)} %get-tuple-element.14), channel_id=1, source_target_pairs={{2,4},{4,2},{6,8},{8,6},{10,12},{12,10},{14,16},{16,14},{18,20},{2... | collective-permute-start | bytes 393224 | tf_op jit(solution)/shard_map/ppermute | solution.py:34
  2.4 11.7 %collective-permute-start.1 = (bf16[64,1024]{1,0:T(8,128)(2,1)S(1)}, bf16[64,1024]{1,0:T(8,128)(2,1)S(1)}, u32[]{:S(2)}, u32[]{:S(2)}) collective-permute-start(bf16[64,1024]{1,0:T(8,128)(2,1)S(1)} %get-tuple-element.15), channel_id=1, source_target_pairs={{0,2},{2,0},{4,6},{6,4},{8,10},{10,8},{12,14},{14,12},{16,18},{18,... | collective-permute-start | bytes 393224 | tf_op jit(solution)/shard_map/ppermute | solution.py:34
  8.3 0.7 %copy-start.4 = (s32[1,1,2,2,64]{4,3,2,1,0:T(2,128)S(1)}, s32[1,1,2,2,64]{4,3,2,1,0:T(2,128)}, u32[]{:S(2)}) copy-start(s32[1,1,2,2,64]{4,3,2,1,0:T(2,128)} %param.9) | copy-start | bytes 3076
  23.2 1.2 %copy-start.2 = (f32[2,128,512]{2,1,0:T(8,128)S(1)}, f32[2,128,512]{2,1,0:T(8,128)}, u32[]{:S(2)}) copy-start(f32[2,128,512]{2,1,0:T(8,128)} %get-tuple-element.19) | copy-start | bytes 1572868
  24.6 2.6 %copy-start.3 = (f32[2,4,8,128]{3,2,1,0:T(8,128)S(1)}, f32[2,4,8,128]{3,2,1,0:T(8,128)}, u32[]{:S(2)}) copy-start(f32[2,4,8,128]{3,2,1,0:T(8,128)} %get-tuple-element.22) | copy-start | bytes 98308
  24.6 16.8 %collective-permute-start.2 = (bf16[64,1024]{1,0:T(8,128)(2,1)S(1)}, bf16[64,1024]{1,0:T(8,128)(2,1)S(1)}, u32[]{:S(2)}, u32[]{:S(2)}) collective-permute-start(bf16[64,1024]{1,0:T(8,128)(2,1)S(1)} %get-tuple-element.20), channel_id=1, source_target_pairs={{0,2},{2,0},{4,6},{6,4},{8,10},{10,8},{12,14},{14,12},{16,18},{18,... | collective-permute-start | bytes 393224 | tf_op jit(solution)/shard_map/ppermute | solution.py:34
  26.5 14.9 %collective-permute-start.3 = (bf16[64,1024]{1,0:T(8,128)(2,1)S(1)}, bf16[64,1024]{1,0:T(8,128)(2,1)S(1)}, u32[]{:S(2)}, u32[]{:S(2)}) collective-permute-start(bf16[64,1024]{1,0:T(8,128)(2,1)S(1)} %get-tuple-element.21), channel_id=1, source_target_pairs={{2,4},{4,2},{6,8},{8,6},{10,12},{12,10},{14,16},{16,14},{18,20},{2... | collective-permute-start | bytes 393224 | tf_op jit(solution)/shard_map/ppermute | solution.py:34

commit v15 on v9

--- a/solution.py
+++ b/solution.py
@@ -44,27 +44,22 @@
     return jnp.sum(lax.all_to_all(spread, axes, 0, 0, tiled=True), axis=0)
 
 
-def group_kernel(
-    flag_ref, sink_ref, q_ref, g_ref, k_ref, v_ref, first_ref, second_ref, allow_ref,
-    o_ref, dq_ref, msg_ref, dk_ref, dv_ref, st_ref,
-):
+def group_kernel(lane_ref, sink_ref, q_ref, g_ref, k_ref, v_ref, prev_ref, allow_ref, *refs):
+    o_ref, dq_ref, msg_ref, dk_ref, dv_ref, st_ref = refs[-6:]
     rows = q_ref.shape[1]
     score_scale = 1.0 / math.sqrt(HEAD_DIM)
     contract_last = (((1,), (1,)), ((), ()))
     contract_first = (((0,), (0,)), ((), ()))
     allowed = jnp.concatenate([allow_ref[0]] * GROUP, axis=0) > 0.5
     head_of_row = lax.broadcasted_iota(jnp.int32, (GROUP * rows, 1), 0) // rows
-    use_second = (pl.program_id(0) + flag_ref[0]) % 2 == 1
     for group in range(KV_HEADS):
         heads = [pl.ds((group * GROUP + h) * HEAD_DIM, HEAD_DIM) for h in range(GROUP)]
         side = pl.ds(group * HEAD_DIM, HEAD_DIM)
-        value_side = pl.ds((KV_HEADS + group) * HEAD_DIM, HEAD_DIM)
         query = jnp.concatenate([q_ref[0, :, cols] for cols in heads], axis=0)
         grad = jnp.concatenate([g_ref[0, :, cols] for cols in heads], axis=0)
-        prev_key = jnp.where(use_second, second_ref[:, side], first_ref[:, side])
-        prev_value = jnp.where(use_second, second_ref[:, value_side], first_ref[:, value_side])
-        key = jnp.concatenate([prev_key, k_ref[0, :, side]], axis=0)
-        value = jnp.concatenate([prev_value, v_ref[0, :, side]], axis=0)
+        value_side = pl.ds((KV_HEADS + group) * HEAD_DIM, HEAD_DIM)
+        key = jnp.concatenate([prev_ref[:, side], k_ref[0, :, side]], axis=0)
+        value = jnp.concatenate([prev_ref[:, value_side], v_ref[0, :, side]], axis=0)
         sink = jnp.zeros((GROUP * rows, 1), jnp.float32)
         for h in range(GROUP):
             sink = jnp.where(head_of_row == h, sink_ref[group * GROUP + h], sink)
@@ -74,11 +69,10 @@
         )
         masked = jnp.where(allowed, scores, -jnp.inf)
         row_top = jnp.maximum(sink, jnp.max(masked, axis=1, keepdims=True))
-        row_total = jnp.exp(sink - row_top) + jnp.sum(
-            jnp.exp(masked - row_top), axis=1, keepdims=True
-        )
-        log_total = row_top + jnp.log(row_total)
-        probs = jnp.exp(masked - log_total)
+        shifted = jnp.exp(masked - row_top)
+        sink_weight = jnp.exp(sink - row_top)
+        inverse_total = 1.0 / (sink_weight + jnp.sum(shifted, axis=1, keepdims=True))
+        probs = shifted * inverse_total
         weights = probs.astype(jnp.bfloat16)
         attended = jnp.dot(weights, value, preferred_element_type=jnp.float32).astype(
             jnp.bfloat16
@@ -94,49 +88,53 @@
             * score_scale
         )
         dvalue = lax.dot_general(weights, grad, contract_first, preferred_element_type=jnp.float32)
-        msg_ref[0, :, side] = dkey[:rows].astype(jnp.bfloat16)
-        msg_ref[0, :, value_side] = dvalue[:rows].astype(jnp.bfloat16)
+        msg_ref[:, side] = dkey[:rows].astype(jnp.bfloat16)
+        msg_ref[:, value_side] = dvalue[:rows].astype(jnp.bfloat16)
         dk_ref[0, :, side] = dkey[rows:]
         dv_ref[0, :, side] = dvalue[rows:]
-        sink_share = jnp.exp(sink - log_total) * row_delta
+        sink_share = sink_weight * inverse_total * row_delta
         for h in range(GROUP):
             part = slice(h * rows, (h + 1) * rows)
             o_ref[0, :, heads[h]] = attended[part]
             dq_ref[0, :, heads[h]] = dquery[part].astype(jnp.bfloat16)
             total = -jnp.sum(sink_share[part], axis=0, keepdims=True)
-            st_ref[0, group, pl.ds(h, 1), :] = jnp.broadcast_to(total, (1, 128))
-
-
-def attend_blocks(flag, sink_logit, queries, out_grad, keys, values, first, second, allowed):
+            st_ref[group, pl.ds(h, 1), :] = jnp.broadcast_to(total, (1, 128))
+
+
+def attend_lane(lane, sink_logit, queries, out_grad, keys, values, prev, allowed, earlier=None):
     lanes, rows, query_width = queries.shape
     side_width = keys.shape[2]
-    pair_width = first.shape[1]
-    lane_block = lambda width: pl.BlockSpec((1, rows, width), lambda lane, flag_ref: (lane, 0, 0))
-    whole = pl.BlockSpec((rows, pair_width), lambda lane, flag_ref: (0, 0))
-    flops = 2 * lanes * HEADS * rows * 2 * rows * HEAD_DIM * 6
-    moved = 8 * queries.size + 4 * keys.size + 10 * keys.size + 4 * allowed.size
+    pair_width = prev.shape[1]
+    lane_block = lambda width: pl.BlockSpec((1, rows, width), lambda i, lane_ref: (lane_ref[0], 0, 0))
+    flops = 2 * HEADS * rows * 2 * rows * HEAD_DIM * 6
+    moved = 4 * queries.size + 3 * keys.size + 8 * prev.size + 2 * allowed.size
+    in_specs = [
+        pl.BlockSpec(memory_space=pltpu.SMEM),
+        lane_block(query_width),
+        lane_block(query_width),
+        lane_block(side_width),
+        lane_block(side_width),
+        pl.BlockSpec((rows, pair_width), lambda i, lane_ref: (0, 0)),
+        pl.BlockSpec((1, rows, 2 * rows), lambda i, lane_ref: (lane_ref[0], 0, 0)),
+    ]
+    operands = [lane, sink_logit, queries, out_grad, keys, values, prev, allowed]
+    aliases = {}
+    if earlier is not None:
+        for out_index, array in zip((0, 1, 3, 4), earlier):
+            aliases[len(operands)] = out_index
+            in_specs.append(pl.BlockSpec(memory_space=pl.ANY))
+            operands.append(array)
     grid_spec = pltpu.PrefetchScalarGridSpec(
         num_scalar_prefetch=1,
-        grid=(lanes,),
-        in_specs=[
-            pl.BlockSpec(memory_space=pltpu.SMEM),
-            lane_block(query_width),
-            lane_block(query_width),
-            lane_block(side_width),
-            lane_block(side_width),
-            whole,
-            whole,
-            pl.BlockSpec((1, rows, 2 * rows), lambda lane, flag_ref: (lane, 0, 0)),
-        ],
+        grid=(1,),
+        in_specs=in_specs,
         out_specs=[
             lane_block(query_width),
             lane_block(query_width),
-            pl.BlockSpec(
-                (1, rows, pair_width), lambda lane, flag_ref: ((lane + flag_ref[0]) % 2, 0, 0)
-            ),
+            pl.BlockSpec((rows, pair_width), lambda i, lane_ref: (0, 0)),
             lane_block(side_width),
             lane_block(side_width),
-            pl.BlockSpec((1, KV_HEADS, GROUP, 128), lambda lane, flag_ref: (lane, 0, 0, 0)),
+            pl.BlockSpec((KV_HEADS, GROUP, 128), lambda i, lane_ref: (0, 0, 0)),
         ],
     )
     return pl.pallas_call(
@@ -145,15 +143,16 @@
         out_shape=[
             jax.ShapeDtypeStruct((lanes, rows, query_width), jnp.bfloat16),
             jax.ShapeDtypeStruct((lanes, rows, query_width), jnp.bfloat16),
-            jax.ShapeDtypeStruct((lanes, rows, pair_width), jnp.bfloat16),
+            jax.ShapeDtypeStruct((rows, pair_width), jnp.bfloat16),
             jax.ShapeDtypeStruct((lanes, rows, side_width), jnp.float32),
             jax.ShapeDtypeStruct((lanes, rows, side_width), jnp.float32),
-            jax.ShapeDtypeStruct((lanes, KV_HEADS, GROUP, 128), jnp.float32),
+            jax.ShapeDtypeStruct((KV_HEADS, GROUP, 128), jnp.float32),
         ],
+        input_output_aliases=aliases,
         cost_estimate=pl.CostEstimate(
-            flops=flops, transcendentals=4 * lanes * HEADS * rows * rows, bytes_accessed=moved
+            flops=flops, transcendentals=2 * HEADS * rows * 2 * rows, bytes_accessed=moved
         ),
-    )(flag, sink_logit, queries, out_grad, keys, values, first, second, allowed)
+    )(*operands)
 
 
 def per_device(queries, keys, values, doc_bounds, sink_logit, out_grad):
@@ -179,9 +178,9 @@
             axis=1,
         )
 
-    first_send, second_send = lax.optimization_barrier((lane_pair(1 - even), lane_pair(even)))
-    first = swap_pairs(first_send, "ctx", 0)
-    second = swap_pairs(second_send, "ctx", 1)
+    near_send, far_send = lax.optimization_barrier((lane_pair(1 - even), lane_pair(even)))
+    far_prev = swap_pairs(far_send, "ctx", 1)
+    near_prev = swap_pairs(near_send, "ctx", 0)
 
     lane_block = jnp.stack([my_index, last_block - my_index]).astype(jnp.int32)
     row_offsets = jnp.arange(block_rows, dtype=jnp.int32)
@@ -192,26 +191,26 @@
     allowed = (key_pos[:, None, :] <= query_pos[:, :, None]) & (
         key_pos[:, None, :] >= first_pos[:, :, None]
     )
-    attended, dquery, message, key_own, value_own, sink_parts = attend_blocks(
-        even.reshape(1),
+    common = (
         sink_logit,
         queries.reshape(2, block_rows, query_width),
         out_grad.reshape(2, block_rows, query_width),
         key_lanes,
         value_lanes,
-        first,
-        second,
-        allowed.astype(jnp.float32),
-    )
-    sink_terms = jnp.sum(sink_parts[:, :, :, 0], axis=0)
+    )
+    mask = allowed.astype(jnp.float32)
+    near = attend_lane(even.reshape(1), *common, near_prev, mask)
+    got_far = swap_pairs(near[2], "ctx", 0)
+    far = attend_lane(
+        (1 - even).reshape(1), *common, far_prev, mask, (near[0], near[1], near[3], near[4])
+    )
+    attended, dquery, _, key_own, value_own, _ = far
+    sink_terms = (near[5] + far[5])[:, :, 0]
     sink_grad = all_sum(sink_terms.reshape(HEADS), ("ctx", "dp"))
-
-    sent_first, sent_second = lax.optimization_barrier((message[0], message[1]))
-    got_first = swap_pairs(sent_first, "ctx", 0)
-    got_second = swap_pairs(sent_second, "ctx", 1)
+    got_near = swap_pairs(far[2], "ctx", 1)
     is_even = even == 1
     arrived = jnp.stack(
-        [jnp.where(is_even, got_first, got_second), jnp.where(is_even, got_second, got_first)]
+        [jnp.where(is_even, got_far, got_near), jnp.where(is_even, got_near, got_far)]
     ).astype(jnp.float32)
 
     out_shape = (1, 1, 2, block_rows, query_width)

time: 43.2 us -> 45.9 us (1.062)
  waiting for transfers between devices: 8.33 us -> 11.4 us
  starting transfers between devices: 17.6 us -> 15.5 us
  Pallas kernels: 8.81 us -> 10.2 us
  other arithmetic: 2.43 us -> 3.13 us
    ppermute x4, waiting for transfers between devices: 1.26 us -> 4.38 us  [swap_pairs(): return lax.ppermute(x, axis, pairs)]
    all_to_all x1, starting transfers between devices: 7.78 us -> 5.3 us  [all_sum(): return jnp.sum(lax.all_to_all(spread, axes, 0, 0, tiled=True), axis=0)]
    pallas_call x1 -> x2, Pallas kernels: 8.81 us -> 10.2 us  [attend_lane(): pl.pallas_call(group_kernel, grid_spec=grid_spec, out_shape=[jax.ShapeDty...]
    squeeze x1 -> x0, local copies, waits for them, and re-layouts: 0.99 us -> none  [per_device(): sent_first, sent_second = lax.optimization_barrier((message[0], message[1]))]
    slice x0 -> x1, other arithmetic: none -> 0.8 us  [per_device(): sink_terms = (near[5] + far[5])[:, :, 0]]
    unnamed x12 -> x14, local copies, waits for them, and re-layouts: 2.28 us -> 2.89 us
  transfers between devices with their start and end apart: 5 -> 5, of which waited for: 2 -> 2; matrix products, arithmetic and copies ran while one was open for 5% -> 7% of each run, Pallas kernels for 0% -> 11%
where the time goes in v15:
time: 45.9 us; the launch traced here: 45.6 us
  starting transfers between devices  15.5 us (34%)
  waiting for transfers between devices  11.4 us (25%)
  Pallas kernels  10.2 us (22%)
  local copies, waits for them, and re-layouts  4.56 us (10%)
  other arithmetic  3.13 us (7%)
  between operations  0.76 us (2%)
    ppermute x4, starting transfers between devices, swap_pairs(): return lax.ppermute(x, axis, pairs)  10.2 us
    pallas_call x2, Pallas kernels, attend_lane(): pl.pallas_call(group_kernel, grid_spec=grid_spec, out_shape=[jax.ShapeDty...  10.2 us
    all_to_all x1, waiting for transfers between devices, all_sum(): return jnp.sum(lax.all_to_all(spread, axes, 0, 0, tiled=True), axis=0)  7.07 us
    all_to_all x1, starting transfers between devices, all_sum(): return jnp.sum(lax.all_to_all(spread, axes, 0, 0, tiled=True), axis=0)  5.3 us
    ppermute x4, waiting for transfers between devices, swap_pairs(): return lax.ppermute(x, axis, pairs)  4.38 us
    unnamed x14, local copies, waits for them, and re-layouts  2.89 us
    squeeze x1, local copies, waits for them, and re-layouts, lane_pair(): lax.dynamic_index_in_dim(value_lanes, lane, keepdims=False)  0.96 us
  transfers between devices with their start and end apart: 5, of which 2 were waited for; matrix products, arithmetic and copies ran while one was open for 7% of the time, Pallas kernels for 11%

profile of v15, /device:TPU:0, one launch (start us, length us, event | category | flops | bytes accessed | tf_op | source)
XLA Modules:
  0.0 45.6 jit_solution(783108192766414583)
XLA Ops:
  0.6 1.0 %dynamic-slice_bitcast_fusion = (bf16[64,512]{1,0:T(8,128)(2,1)S(1)}, bf16[64,512]{1,0:T(8,128)(2,1)S(1)}, bf16[64,512]{1,0:T(8,128)(2,1)S(1)}, bf16[64,512]{1,0:T(8,128)(2,1)S(1)}) fusion(bf16[1,1,2,64,512]{4,3,2,1,0:T(8,128)(2,1)} %param.8, s32[]{:T(128)S(6)} %select_n.30, s32[]{:T(128)S(6)} %select_n.29, bf16[1,1,2,64,512]{4,3,2,1,0:T(8,128)(2,1)} %param.7), kind=kLoop, calls=%fused_computation.11 | loop fusion | bytes 524296 | tf_op jit(solution)/shard_map/jit(dynamic_index_in_dim)/squeeze | solution.py:176
  1.6 0.7 %collective-permute-start = (bf16[64,1024]{1,0:T(8,128)(2,1)S(1)}, bf16[64,1024]{1,0:T(8,128)(2,1)S(1)}, u32[]{:S(2)}, u32[]{:S(2)}) collective-permute-start(bf16[64,1024]{1,0:T(8,128)(2,1)S(1)} %pad_maximum_fusion.1), channel_id=1, source_target_pairs={{2,4},{4,2},{6,8},{8,6},{10,12},{12,10},{14,16},{16,14},{18,20},{2... | collective-permute-start | bytes 393224 | tf_op jit(solution)/shard_map/ppermute | solution.py:36
  2.3 5.7 %collective-permute-start.1 = (bf16[64,1024]{1,0:T(8,128)(2,1)S(1)}, bf16[64,1024]{1,0:T(8,128)(2,1)S(1)}, u32[]{:S(2)}, u32[]{:S(2)}) collective-permute-start(bf16[64,1024]{1,0:T(8,128)(2,1)S(1)} %pad_maximum_fusion), channel_id=1, source_target_pairs={{0,2},{2,0},{4,6},{6,4},{8,10},{10,8},{12,14},{14,12},{16,18},{18,... | collective-permute-start | bytes 393224 | tf_op jit(solution)/shard_map/ppermute | solution.py:36
  8.1 0.1 add_multiply_fusion
  8.1 0.1 iota_add_fusion.1
  8.2 0.1 iota_add_fusion
  8.3 0.6 %copy-done.5 = s32[1,1,2,2,64]{4,3,2,1,0:T(2,128)S(1)} copy-done((s32[1,1,2,2,64]{4,3,2,1,0:T(2,128)S(1)}, s32[1,1,2,2,64]{4,3,2,1,0:T(2,128)}, u32[]{:S(2)}) %copy-start.5) | copy-done | bytes 1048
  8.9 0.7 %and_convert_fusion.allow_ref = f32[2,64,128]{2,1,0:T(8,128)} fusion(s32[2,64]{1,0:T(2,128)S(1)} %bitcast.40, s32[2,64]{1,0:T(2,128)S(1)} %iota_add_fusion, s32[2,128]{1,0:T(2,128)S(1)} %iota_add_fusion.1), kind=kLoop, calls=%fused_computation.15 | loop fusion | flops 65536 | bytes 67584 | tf_op jit(solution)/shard_map/convert_element_type | solution.py:201
  9.6 4.4 %collective-permute-done.1.prev_ref = bf16[64,1024]{1,0:T(8,128)(2,1)S(1)} collective-permute-done((bf16[64,1024]{1,0:T(8,128)(2,1)S(1)}, bf16[64,1024]{1,0:T(8,128)(2,1)S(1)}, u32[]{:S(2)}, u32[]{:S(2)}) %collective-permute-start.1) | collective-permute-done | bytes 131104 | tf_op jit(solution)/shard_map/ppermute | solution.py:36
  14.0 0.7 %copy-done.3 = bf16[64,1024]{1,0:T(8,128)(2,1)} copy-done((bf16[64,1024]{1,0:T(8,128)(2,1)}, bf16[64,1024]{1,0:T(8,128)(2,1)S(1)}, u32[]{:S(2)}) %copy-start.3) | copy-done | bytes 131096
  14.6 5.1 %shard_map.101 = (bf16[2,64,4096]{2,1,0:T(8,128)(2,1)}, bf16[2,64,4096]{2,1,0:T(8,128)(2,1)}, bf16[64,1024]{1,0:T(8,128)(2,1)}, f32[2,64,512]{2,1,0:T(8,128)}, f...) custom-call(s32[1]{0:T(128)} %bitcast.13.lane_ref, f32[32]{0:T(128)} %sink_ref.3, bf16[2,64,4096]{2,1,0:T(8,128)(2,1)} %bitcast.29, ...), custom_call_target="tpu_custom_call" | custom-call | flops 402653184 | bytes 2850816 | tf_op jit(solution)/shard_map/pallas_call | solution.py:140
  19.7 0.0 collective-permute-done.prev_ref
  19.7 0.0 copy-start.2
  19.7 0.6 %copy-done.2 = bf16[64,1024]{1,0:T(8,128)(2,1)} copy-done((bf16[64,1024]{1,0:T(8,128)(2,1)}, bf16[64,1024]{1,0:T(8,128)(2,1)S(1)}, u32[]{:S(2)}) %copy-start.2) | copy-done | bytes 131096
  20.4 5.1 %shard_map.102 = (bf16[2,64,4096]{2,1,0:T(8,128)(2,1)}, bf16[2,64,4096]{2,1,0:T(8,128)(2,1)}, bf16[64,1024]{1,0:T(8,128)(2,1)}, f32[2,64,512]{2,1,0:T(8,128)}, f...) custom-call(s32[1]{0:T(128)} %bitcast.lane_ref, ...), custom_call_target="tpu_custom_call", output_to_operand_aliasing={{0}: (8, {}), {1}: (9, {}), {3}: (10, {}), {4}: (11, {})} | custom-call | flops 402653184 | bytes 2850816 | tf_op jit(solution)/shard_map/pallas_call | solution.py:140
  25.5 0.7 %collective-permute-start.3 = (bf16[64,1024]{1,0:T(8,128)(2,1)}, bf16[64,1024]{1,0:T(8,128)(2,1)S(1)}, u32[]{:S(2)}, u32[]{:S(2)}) collective-permute-start(bf16[64,1024]{1,0:T(8,128)(2,1)} %get-tuple-element.29), channel_id=1, source_target_pairs={{2,4},{4,2},{6,8},{8,6},{10,12},{12,10},{14,16},{16,14},{18,20},{2... | collective-permute-start | bytes 393224 | tf_op jit(solution)/shard_map/ppermute | solution.py:36
  26.2 0.0 copy-done.6
  26.2 3.1 %collective-permute-start.2 = (bf16[64,1024]{1,0:T(8,128)(2,1)S(1)}, bf16[64,1024]{1,0:T(8,128)(2,1)S(1)}, u32[]{:S(2)}, u32[]{:S(2)}) collective-permute-start(bf16[64,1024]{1,0:T(8,128)(2,1)S(1)} %copy-done.6), channel_id=1, source_target_pairs={{0,2},{2,0},{4,6},{6,4},{8,10},{10,8},{12,14},{14,12},{16,18},{18,... | collective-permute-start | bytes 393224 | tf_op jit(solution)/shard_map/ppermute | solution.py:36
  29.3 0.0 copy-done.4
  29.3 0.8 %fusion.4 = f32[4,8]{1,0:T(4,128)S(1)} fusion(f32[4,8,128]{2,1,0:T(8,128)} %get-tuple-element.32, f32[4,8,128]{2,1,0:T(8,128)S(1)} %copy-done.4), kind=kLoop, calls=%fused_computation.17 | loop fusion | flops 32 | bytes 384 | tf_op jit(solution)/shard_map/slice | solution.py:208
  30.1 0.1 broadcast_in_dim.4
  30.2 0.6 %broadcast_in_dim.5 = f32[32,1,32]{2,1,0:T(1,128)} broadcast(f32[32]{0:T(128)S(1)} %broadcast_in_dim.4), dimensions={2} | broadcast | bytes 4224 | tf_op jit(solution)/shard_map/broadcast_in_dim | solution.py:43
  30.8 5.3 %all-to-all-start = ((f32[32,1,32]{2,1,0:T(1,128)}), f32[32,1,32]{2,1,0:T(1,128)S(1)}, u32[]{:S(2)}, u32[]{:S(2)}) async-start(f32[32,1,32]{2,1,0:T(1,128)} %broadcast_in_dim.5), calls=%async_computation | async-start | bytes 32768 | tf_op jit(solution)/shard_map/all_to_all | solution.py:44
  36.2 7.1 %all-to-all-done = f32[32,1,32]{2,1,0:T(1,128)S(1)} async-done(((f32[32,1,32]{2,1,0:T(1,128)}), f32[32,1,32]{2,1,0:T(1,128)S(1)}, u32[]{:S(2)}, u32[]{:S(2)}) %all-to-all-start) | async-done | bytes 4128 | tf_op jit(solution)/shard_map/all_to_all | solution.py:44
  43.2 0.5 %reduce_sum.9 = f32[32]{0:T(128)} reduce(f32[32,1,32]{2,0,1:T(8,128)S(1)} %bitcast.39, f32[]{:T(128)} %constant.45.clone.1), dimensions={0,1}, to_apply=%region_0.1 | reduce | flops 992 | bytes 4228 | tf_op jit(solution)/shard_map/reduce_sum | solution.py:44
  43.8 0.0 collective-permute-done.3
  43.8 0.0 collective-permute-done.2
  43.8 0.0 copy-start
  43.8 0.0 copy-start.1
  43.9 0.9 %copy-done = f32[2,64,512]{2,1,0:T(8,128)S(1)} copy-done((f32[2,64,512]{2,1,0:T(8,128)S(1)}, f32[2,64,512]{2,1,0:T(8,128)}, u32[]{:S(2)}) %copy-start) | copy-done | bytes 262168
  44.7 0.1 copy-done.1
  44.8 0.8 %fusion.3 = (bf16[1,1,2,64,512]{4,3,2,1,0:T(8,128)(2,1)}, bf16[1,1,2,64,512]{4,3,2,1,0:T(8,128)(2,1)}) fusion(f32[2,64,512]{2,1,0:T(8,128)S(1)} %copy-done.1, f32[2,64,1024]{2,1,0:T(8,128)S(1)} %maximum_convert_fusion, f32[2,64,512]{2,1,0:T(8,128)S(1)} %copy-done), kind=kLoop, calls=%fused_computation.6 | loop fusion | flops 262144 | bytes 1310720 | tf_op jit(solution)/shard_map/reshape | solution.py:221
  (9 shorter events, 0.1 us)
Async XLA Ops:
  1.6 18.1 %collective-permute-start = (bf16[64,1024]{1,0:T(8,128)(2,1)S(1)}, bf16[64,1024]{1,0:T(8,128)(2,1)S(1)}, u32[]{:S(2)}, u32[]{:S(2)}) collective-permute-start(bf16[64,1024]{1,0:T(8,128)(2,1)S(1)} %pad_maximum_fusion.1), channel_id=1, source_target_pairs={{2,4},{4,2},{6,8},{8,6},{10,12},{12,10},{14,16},{16,14},{18,20},{2... | collective-permute-start | bytes 393224 | tf_op jit(solution)/shard_map/ppermute | solution.py:36
  2.3 11.7 %collective-permute-start.1 = (bf16[64,1024]{1,0:T(8,128)(2,1)S(1)}, bf16[64,1024]{1,0:T(8,128)(2,1)S(1)}, u32[]{:S(2)}, u32[]{:S(2)}) collective-permute-start(bf16[64,1024]{1,0:T(8,128)(2,1)S(1)} %pad_maximum_fusion), channel_id=1, source_target_pairs={{0,2},{2,0},{4,6},{6,4},{8,10},{10,8},{12,14},{14,12},{16,18},{18,... | collective-permute-start | bytes 393224 | tf_op jit(solution)/shard_map/ppermute | solution.py:36
  8.2 0.7 %copy-start.5 = (s32[1,1,2,2,64]{4,3,2,1,0:T(2,128)S(1)}, s32[1,1,2,2,64]{4,3,2,1,0:T(2,128)}, u32[]{:S(2)}) copy-start(s32[1,1,2,2,64]{4,3,2,1,0:T(2,128)} %param.9) | copy-start | bytes 3076
  14.0 0.7 %copy-start.3 = (bf16[64,1024]{1,0:T(8,128)(2,1)}, bf16[64,1024]{1,0:T(8,128)(2,1)S(1)}, u32[]{:S(2)}) copy-start(bf16[64,1024]{1,0:T(8,128)(2,1)S(1)} %collective-permute-done.1.prev_ref) | copy-start | bytes 393220
  19.7 0.7 %copy-start.2 = (bf16[64,1024]{1,0:T(8,128)(2,1)}, bf16[64,1024]{1,0:T(8,128)(2,1)S(1)}, u32[]{:S(2)}) copy-start(bf16[64,1024]{1,0:T(8,128)(2,1)S(1)} %collective-permute-done.prev_ref) | copy-start | bytes 393220
  20.4 5.8 %copy-start.6 = (bf16[64,1024]{1,0:T(8,128)(2,1)S(1)}, bf16[64,1024]{1,0:T(8,128)(2,1)}, u32[]{:S(2)}) copy-start(bf16[64,1024]{1,0:T(8,128)(2,1)} %get-tuple-element.28) | copy-start | bytes 393220
  20.4 8.9 %copy-start.4 = (f32[4,8,128]{2,1,0:T(8,128)S(1)}, f32[4,8,128]{2,1,0:T(8,128)}, u32[]{:S(2)}) copy-start(f32[4,8,128]{2,1,0:T(8,128)} %get-tuple-element.31) | copy-start | bytes 49156
  25.5 18.3 %collective-permute-start.3 = (bf16[64,1024]{1,0:T(8,128)(2,1)}, bf16[64,1024]{1,0:T(8,128)(2,1)S(1)}, u32[]{:S(2)}, u32[]{:S(2)}) collective-permute-start(bf16[64,1024]{1,0:T(8,128)(2,1)} %get-tuple-element.29), channel_id=1, source_target_pairs={{2,4},{4,2},{6,8},{8,6},{10,12},{12,10},{14,16},{16,14},{18,20},{2... | collective-permute-start | bytes 393224 | tf_op jit(solution)/shard_map/ppermute | solution.py:36
  26.2 17.6 %collective-permute-start.2 = (bf16[64,1024]{1,0:T(8,128)(2,1)S(1)}, bf16[64,1024]{1,0:T(8,128)(2,1)S(1)}, u32[]{:S(2)}, u32[]{:S(2)}) collective-permute-start(bf16[64,1024]{1,0:T(8,128)(2,1)S(1)} %copy-done.6), channel_id=1, source_target_pairs={{0,2},{2,0},{4,6},{6,4},{8,10},{10,8},{12,14},{14,12},{16,18},{18,... | collective-permute-start | bytes 393224 | tf_op jit(solution)/shard_map/ppermute | solution.py:36
  30.8 12.4 %all-to-all-start = ((f32[32,1,32]{2,1,0:T(1,128)}), f32[32,1,32]{2,1,0:T(1,128)S(1)}, u32[]{:S(2)}, u32[]{:S(2)}) async-start(f32[32,1,32]{2,1,0:T(1,128)} %broadcast_in_dim.5), calls=%async_computation | async-start | bytes 32768 | tf_op jit(solution)/shard_map/all_to_all | solution.py:44
  43.8 1.0 %copy-start = (f32[2,64,512]{2,1,0:T(8,128)S(1)}, f32[2,64,512]{2,1,0:T(8,128)}, u32[]{:S(2)}) copy-start(f32[2,64,512]{2,1,0:T(8,128)} %get-tuple-element.27) | copy-start | bytes 786436
  43.8 1.0 %copy-start.1 = (f32[2,64,512]{2,1,0:T(8,128)S(1)}, f32[2,64,512]{2,1,0:T(8,128)}, u32[]{:S(2)}) copy-start(f32[2,64,512]{2,1,0:T(8,128)} %get-tuple-element.30) | copy-start | bytes 786436

commit v16 on v13

--- a/solution.py
+++ b/solution.py
@@ -63,7 +63,9 @@
     contract_first = (((0,), (0,)), ((), ()))
     allowed = jnp.concatenate([allow_ref[0]] * GROUP, axis=0) > 0.5
     head_of_row = lax.broadcasted_iota(jnp.int32, (GROUP * rows, 1), 0) // rows
-    for group in range(KV_HEADS):
+    groups = k_ref.shape[2] // HEAD_DIM
+    for group in range(groups):
+        first_head = (pl.program_id(1) * groups + group) * GROUP
         heads = [pl.ds((group * GROUP + h) * HEAD_DIM, HEAD_DIM) for h in range(GROUP)]
         side = pl.ds(group * HEAD_DIM, HEAD_DIM)
         query = jnp.concatenate([q_ref[0, :, cols] for cols in heads], axis=0)
@@ -72,7 +74,7 @@
         value = v_ref[0, :, side]
         sink = jnp.zeros((GROUP * rows, 1), jnp.float32)
         for h in range(GROUP):
-            sink = jnp.where(head_of_row == h, sink_ref[group * GROUP + h], sink)
+            sink = jnp.where(head_of_row == h, sink_ref[first_head + h], sink)
         scores = (
             lax.dot_general(query, key, contract_last, preferred_element_type=jnp.float32)
             * score_scale
@@ -112,34 +114,36 @@
 def attend_blocks(sink_logit, queries, out_grad, window, allowed):
     lanes, rows, query_width = queries.shape
     span = window.shape[1]
-    side_width = KV_HEADS * HEAD_DIM
-    row_spec = pl.BlockSpec((1, rows, query_width), lambda lane: (lane, 0, 0))
-    side_spec = pl.BlockSpec((1, span, side_width), lambda lane: (lane, 0, 0))
+    halves = 2
+    groups = KV_HEADS // halves
+    lane_half = lambda lane, half: (lane, 0, half)
+    row_spec = pl.BlockSpec((1, rows, groups * GROUP * HEAD_DIM), lane_half)
+    side_spec = pl.BlockSpec((1, span, groups * HEAD_DIM), lane_half)
     flops = 2 * lanes * HEADS * rows * span * HEAD_DIM * 6
     moved = 2 * (4 * queries.size + 2 * window.size) + 4 * allowed.size + 8 * window.size
     return pl.pallas_call(
         group_kernel,
-        grid=(lanes,),
+        grid=(lanes, halves),
         in_specs=[
             pl.BlockSpec(memory_space=pltpu.SMEM),
             row_spec,
             row_spec,
             side_spec,
-            pl.BlockSpec((1, span, side_width), lambda lane: (lane, 0, 1)),
-            pl.BlockSpec((1, rows, span), lambda lane: (lane, 0, 0)),
+            pl.BlockSpec((1, span, groups * HEAD_DIM), lambda lane, half: (lane, 0, halves + half)),
+            pl.BlockSpec((1, rows, span), lambda lane, half: (lane, 0, 0)),
         ],
         out_specs=[
             row_spec,
             row_spec,
             side_spec,
             side_spec,
-            pl.BlockSpec((1, KV_HEADS, GROUP, 128), lambda lane: (lane, 0, 0, 0)),
+            pl.BlockSpec((1, groups, GROUP, 128), lambda lane, half: (lane, half, 0, 0)),
         ],
         out_shape=[
             jax.ShapeDtypeStruct((lanes, rows, query_width), jnp.bfloat16),
             jax.ShapeDtypeStruct((lanes, rows, query_width), jnp.bfloat16),
-            jax.ShapeDtypeStruct((lanes, span, side_width), jnp.float32),
-            jax.ShapeDtypeStruct((lanes, span, side_width), jnp.float32),
+            jax.ShapeDtypeStruct((lanes, span, KV_HEADS * HEAD_DIM), jnp.float32),
+            jax.ShapeDtypeStruct((lanes, span, KV_HEADS * HEAD_DIM), jnp.float32),
             jax.ShapeDtypeStruct((lanes, KV_HEADS, GROUP, 128), jnp.float32),
         ],
         cost_estimate=pl.CostEstimate(

time: 42.5 us -> 42.5 us (level)
  no operation moved by 1% of the time
where the time goes in v16:
time: 42.5 us; the launch traced here: 42.2 us
  blocking collectives  13.5 us (32%)
  starting transfers between devices  8.96 us (21%)
  Pallas kernels  8.13 us (19%)
  waiting for transfers between devices  4.37 us (10%)
  other arithmetic  3.77 us (9%)
  local copies, waits for them, and re-layouts  2.67 us (6%)
  between operations  0.77 us (2%)
    all_to_all x1, blocking collectives, all_sum(): return jnp.sum(lax.all_to_all(spread, axes, 0, 0, tiled=True), axis=0)  13.5 us
    ppermute x4, starting transfers between devices, swap_pairs(): return lax.ppermute(x, axis, pairs)  8.96 us
    pallas_call x1, Pallas kernels, attend_blocks(): pl.pallas_call(group_kernel, grid=(lanes, halves), in_specs=[pl.BlockSpec...  8.13 us
    ppermute x4, waiting for transfers between devices, swap_pairs(): return lax.ppermute(x, axis, pairs)  4.37 us
    unnamed x11, local copies, waits for them, and re-layouts  1.81 us
    select_n x2, other arithmetic, neighbour_swap(): jnp.where(even, to_prev, to_next)  1.12 us
    concatenate x1, other arithmetic, per_device(): window = jnp.concatenate([prev_pair, own_pair], axis=1)  0.85 us
  transfers between devices with their start and end apart: 4, of which 1 were waited for; matrix products, arithmetic and copies ran while one was open for 4% of the time, Pallas kernels for 0%

profile of v16, /device:TPU:0, one launch (start us, length us, event | category | flops | bytes accessed | tf_op | source)
XLA Modules:
  0.0 42.2 jit_solution(5333140095757733609)
XLA Ops:
  0.6 0.0 copy-start
  0.7 0.0 copy-start.1
  0.7 1.1 %broadcast_select_fusion.2 = (bf16[64,1024]{1,0:T(8,128)(2,1)S(1)}, bf16[64,1024]{1,0:T(8,128)(2,1)S(1)}) fusion(pred[]{:T(512)S(6)} %eq.10, bf16[2,64,512]{2,1,0:T(8,128)(2,1)} %bitcast.51, bf16[2,64,512]{2,1,0:T(8,128)(2,1)} %bitcast.54), kind=kLoop, calls=%fused_computation.19 | loop fusion | flops 917504 | bytes 524289 | tf_op jit(solution)/shard_map/jit(_where)/select_n | solution.py:40
  1.8 0.7 %collective-permute-start = (bf16[64,1024]{1,0:T(8,128)(2,1)S(1)}, bf16[64,1024]{1,0:T(8,128)(2,1)S(1)}, u32[]{:S(2)}, u32[]{:S(2)}) collective-permute-start(bf16[64,1024]{1,0:T(8,128)(2,1)S(1)} %get-tuple-element.14), channel_id=1, source_target_pairs={{2,4},{4,2},{6,8},{8,6},{10,12},{12,10},{14,16},{16,14},{18,20},{2... | collective-permute-start | bytes 393224 | tf_op jit(solution)/shard_map/ppermute | solution.py:34
  2.4 5.7 %collective-permute-start.1 = (bf16[64,1024]{1,0:T(8,128)(2,1)S(1)}, bf16[64,1024]{1,0:T(8,128)(2,1)S(1)}, u32[]{:S(2)}, u32[]{:S(2)}) collective-permute-start(bf16[64,1024]{1,0:T(8,128)(2,1)S(1)} %get-tuple-element.15), channel_id=1, source_target_pairs={{0,2},{2,0},{4,6},{6,4},{8,10},{10,8},{12,14},{14,12},{16,18},{18,... | collective-permute-start | bytes 393224 | tf_op jit(solution)/shard_map/ppermute | solution.py:34
  8.2 0.1 add_multiply_fusion
  8.3 0.1 iota_add_fusion.1
  8.3 0.1 iota_add_fusion
  8.4 0.6 %copy-done.4 = s32[1,1,2,2,64]{4,3,2,1,0:T(2,128)S(1)} copy-done((s32[1,1,2,2,64]{4,3,2,1,0:T(2,128)S(1)}, s32[1,1,2,2,64]{4,3,2,1,0:T(2,128)}, u32[]{:S(2)}) %copy-start.4) | copy-done | bytes 1048
  9.0 0.7 %and_convert_fusion.allow_ref = f32[2,64,128]{2,1,0:T(8,128)} fusion(s32[2,64]{1,0:T(2,128)S(1)} %bitcast.60, s32[2,64]{1,0:T(2,128)S(1)} %iota_add_fusion, s32[2,128]{1,0:T(2,128)S(1)} %iota_add_fusion.1), kind=kLoop, calls=%fused_computation.21 | loop fusion | flops 65536 | bytes 67584 | tf_op jit(solution)/shard_map/convert_element_type | solution.py:188
  9.7 0.0 collective-permute-done
  9.8 4.4 %collective-permute-done.1 = bf16[64,1024]{1,0:T(8,128)(2,1)S(1)} collective-permute-done((bf16[64,1024]{1,0:T(8,128)(2,1)S(1)}, bf16[64,1024]{1,0:T(8,128)(2,1)S(1)}, u32[]{:S(2)}, u32[]{:S(2)}) %collective-permute-start.1) | collective-permute-done | bytes 131104 | tf_op jit(solution)/shard_map/ppermute | solution.py:34
  14.1 0.0 copy-done
  14.1 0.0 copy-done.1
  14.1 0.1 select_bitcast_fusion.3
  14.2 0.8 %maximum_maximum_fusion.k_ref.v_ref = bf16[2,128,1024]{2,1,0:T(8,128)(2,1)} fusion(bf16[2,64,512]{2,1,0:T(8,128)(2,1)S(1)} %bitcast.53, bf16[2,64,512]{2,1,0:T(8,128)(2,1)S(1)} %bitcast.56, bf16[1,64,1024]{2,1,0:T(8,128)(2,1)S(1)} %get-tuple-element.30, bf16[1,64,1024]{2,1,0:T(8,128)(2,1)S(1)} %get-tuple-element.29), kind=kLoop, calls=%fused_computation.2 | loop fusion | flops 2097152 | bytes 1048576 | tf_op jit(solution)/shard_map/concatenate | solution.py:172
  15.0 8.1 %shard_map.101 = (bf16[2,64,4096]{2,1,0:T(8,128)(2,1)}, bf16[2,64,4096]{2,1,0:T(8,128)(2,1)}, f32[2,128,512]{2,1,0:T(8,128)}, f32[2,128,512]{2,1,0:T(8,128)}, f32[2,4,8,128]{3,2,1,0:T(8,128)}) custom-call(f32[32]{0:T(128)} %sink_ref.1, bf16[2,64,4096]{2,1,0:T(8,128)(2,1)} %bitcast.57, bf16[2,64,4096]{2,1,0:T(8,128)(2,1)} %bitcast.58, ...), custom_call_target="tpu_custom_call" | custom-call | flops 805306368 | bytes 7405568 | tf_op jit(solution)/shard_map/pallas_call | solution.py:124
  23.2 1.1 %constant_dynamic-update-slice_fusion.1 = f32[2,128,1024]{2,1,0:T(8,128)S(1)} fusion(f32[2,128,512]{2,1,0:T(8,128)} %get-tuple-element.18), kind=kLoop, calls=%fused_computation.24 | loop fusion | bytes 1048576
  24.3 0.1 copy-done.2
  24.4 0.1 convert.7
  24.5 0.0 copy-start.3
  24.5 1.9 %collective-permute-start.2 = (bf16[64,1024]{1,0:T(8,128)(2,1)S(1)}, bf16[64,1024]{1,0:T(8,128)(2,1)S(1)}, u32[]{:S(2)}, u32[]{:S(2)}) collective-permute-start(bf16[64,1024]{1,0:T(8,128)(2,1)S(1)} %get-tuple-element.20), channel_id=1, source_target_pairs={{0,2},{2,0},{4,6},{6,4},{8,10},{10,8},{12,14},{14,12},{16,18},{18,... | collective-permute-start | bytes 393224 | tf_op jit(solution)/shard_map/ppermute | solution.py:34
  26.4 0.7 %collective-permute-start.3 = (bf16[64,1024]{1,0:T(8,128)(2,1)S(1)}, bf16[64,1024]{1,0:T(8,128)(2,1)S(1)}, u32[]{:S(2)}, u32[]{:S(2)}) collective-permute-start(bf16[64,1024]{1,0:T(8,128)(2,1)S(1)} %get-tuple-element.21), channel_id=1, source_target_pairs={{2,4},{4,2},{6,8},{8,6},{10,12},{12,10},{14,16},{16,14},{18,20},{2... | collective-permute-start | bytes 393224 | tf_op jit(solution)/shard_map/ppermute | solution.py:34
  27.1 0.0 copy-done.3
  27.1 0.1 slice_reduce_fusion
  27.2 0.1 broadcast_in_dim.4
  27.3 13.5 %all_to_all.6 = f32[32,1,32]{2,1,0:T(1,128)S(1)} all-to-all(f32[32,1,32]{2,1,0:T(1,128)S(1)} %broadcast_in_dim.5), channel_id=1, replica_groups=mesh['ctx'=16,'dp'=2] {'ctx','dp'}, dimensions={0} | all-to-all | bytes 8192 | tf_op jit(solution)/shard_map/all_to_all | solution.py:54
  40.8 0.5 %reduce_sum.19 = f32[32]{0:T(128)} reduce(f32[32,1,32]{2,0,1:T(8,128)S(1)} %bitcast.59, f32[]{:T(128)} %constant.32.clone.1), dimensions={0,1}, to_apply=%region_1.2 | reduce | flops 992 | bytes 4228 | tf_op jit(solution)/shard_map/reduce_sum | solution.py:54
  41.4 0.0 collective-permute-done.2
  41.4 0.0 collective-permute-done.3
  41.4 0.1 fusion
  41.5 0.7 %slice_bitcast_fusion = (bf16[1,1,2,64,512]{4,3,2,1,0:T(8,128)(2,1)}, bf16[1,1,2,64,512]{4,3,2,1,0:T(8,128)(2,1)}) fusion(bf16[2,64,1024]{2,1,0:T(8,128)(2,1)S(1)} %fusion), kind=kLoop, calls=%fused_computation.7 | loop fusion | bytes 524288 | tf_op jit(solution)/shard_map/reshape | solution.py:205
  (7 shorter events, 0.1 us)
Async XLA Ops:
  0.6 13.5 %copy-start = (bf16[1,1,2,64,512]{4,3,2,1,0:T(8,128)(2,1)S(1)}, bf16[1,1,2,64,512]{4,3,2,1,0:T(8,128)(2,1)}, u32[]{:S(2)}) copy-start(bf16[1,1,2,64,512]{4,3,2,1,0:T(8,128)(2,1)} %param.8) | copy-start | bytes 393220
  0.7 13.5 %copy-start.1 = (bf16[1,1,2,64,512]{4,3,2,1,0:T(8,128)(2,1)S(1)}, bf16[1,1,2,64,512]{4,3,2,1,0:T(8,128)(2,1)}, u32[]{:S(2)}) copy-start(bf16[1,1,2,64,512]{4,3,2,1,0:T(8,128)(2,1)} %param.7) | copy-start | bytes 393220
  1.8 8.0 %collective-permute-start = (bf16[64,1024]{1,0:T(8,128)(2,1)S(1)}, bf16[64,1024]{1,0:T(8,128)(2,1)S(1)}, u32[]{:S(2)}, u32[]{:S(2)}) collective-permute-start(bf16[64,1024]{1,0:T(8,128)(2,1)S(1)} %get-tuple-element.14), channel_id=1, source_target_pairs={{2,4},{4,2},{6,8},{8,6},{10,12},{12,10},{14,16},{16,14},{18,20},{2... | collective-permute-start | bytes 393224 | tf_op jit(solution)/shard_map/ppermute | solution.py:34
  2.4 11.7 %collective-permute-start.1 = (bf16[64,1024]{1,0:T(8,128)(2,1)S(1)}, bf16[64,1024]{1,0:T(8,128)(2,1)S(1)}, u32[]{:S(2)}, u32[]{:S(2)}) collective-permute-start(bf16[64,1024]{1,0:T(8,128)(2,1)S(1)} %get-tuple-element.15), channel_id=1, source_target_pairs={{0,2},{2,0},{4,6},{6,4},{8,10},{10,8},{12,14},{14,12},{16,18},{18,... | collective-permute-start | bytes 393224 | tf_op jit(solution)/shard_map/ppermute | solution.py:34
  8.3 0.7 %copy-start.4 = (s32[1,1,2,2,64]{4,3,2,1,0:T(2,128)S(1)}, s32[1,1,2,2,64]{4,3,2,1,0:T(2,128)}, u32[]{:S(2)}) copy-start(s32[1,1,2,2,64]{4,3,2,1,0:T(2,128)} %param.9) | copy-start | bytes 3076
  23.2 1.2 %copy-start.2 = (f32[2,128,512]{2,1,0:T(8,128)S(1)}, f32[2,128,512]{2,1,0:T(8,128)}, u32[]{:S(2)}) copy-start(f32[2,128,512]{2,1,0:T(8,128)} %get-tuple-element.19) | copy-start | bytes 1572868
  24.5 2.6 %copy-start.3 = (f32[2,4,8,128]{3,2,1,0:T(8,128)S(1)}, f32[2,4,8,128]{3,2,1,0:T(8,128)}, u32[]{:S(2)}) copy-start(f32[2,4,8,128]{3,2,1,0:T(8,128)} %get-tuple-element.22) | copy-start | bytes 98308
  24.5 16.8 %collective-permute-start.2 = (bf16[64,1024]{1,0:T(8,128)(2,1)S(1)}, bf16[64,1024]{1,0:T(8,128)(2,1)S(1)}, u32[]{:S(2)}, u32[]{:S(2)}) collective-permute-start(bf16[64,1024]{1,0:T(8,128)(2,1)S(1)} %get-tuple-element.20), channel_id=1, source_target_pairs={{0,2},{2,0},{4,6},{6,4},{8,10},{10,8},{12,14},{14,12},{16,18},{18,... | collective-permute-start | bytes 393224 | tf_op jit(solution)/shard_map/ppermute | solution.py:34
  26.4 14.9 %collective-permute-start.3 = (bf16[64,1024]{1,0:T(8,128)(2,1)S(1)}, bf16[64,1024]{1,0:T(8,128)(2,1)S(1)}, u32[]{:S(2)}, u32[]{:S(2)}) collective-permute-start(bf16[64,1024]{1,0:T(8,128)(2,1)S(1)} %get-tuple-element.21), channel_id=1, source_target_pairs={{2,4},{4,2},{6,8},{8,6},{10,12},{12,10},{14,16},{16,14},{18,20},{2... | collective-permute-start | bytes 393224 | tf_op jit(solution)/shard_map/ppermute | solution.py:34

commit v17 on v13

--- a/solution.py
+++ b/solution.py
@@ -55,7 +55,8 @@
 
 
 def group_kernel(
-    sink_ref, q_ref, g_ref, k_ref, v_ref, allow_ref, o_ref, dq_ref, dk_ref, dv_ref, st_ref
+    flag_ref, sink_ref, q_ref, g_ref, k_ref, v_ref, allow_ref,
+    o_ref, dq_ref, msg_ref, dk_ref, dv_ref, st_ref,
 ):
     rows = q_ref.shape[1]
     score_scale = 1.0 / math.sqrt(HEAD_DIM)
@@ -93,13 +94,17 @@
         dprob = lax.dot_general(grad, value, contract_last, preferred_element_type=jnp.float32)
         dscore = (probs * (dprob - row_delta)).astype(jnp.bfloat16)
         dquery = jnp.dot(dscore, key, preferred_element_type=jnp.float32) * score_scale
-        dk_ref[0, :, side] = (
+        dkey = (
             lax.dot_general(dscore, query, contract_first, preferred_element_type=jnp.float32)
             * score_scale
         )
-        dv_ref[0, :, side] = lax.dot_general(
-            weights, grad, contract_first, preferred_element_type=jnp.float32
-        )
+        dvalue = lax.dot_general(weights, grad, contract_first, preferred_element_type=jnp.float32)
+        msg_ref[0, :, side] = dkey[:rows].astype(jnp.bfloat16)
+        msg_ref[0, :, pl.ds((KV_HEADS + group) * HEAD_DIM, HEAD_DIM)] = dvalue[:rows].astype(
+            jnp.bfloat16
+        )
+        dk_ref[0, :, side] = dkey[rows:]
+        dv_ref[0, :, side] = dvalue[rows:]
         sink_share = sink_weight * inverse_total * row_delta
         for h in range(GROUP):
             part = slice(h * rows, (h + 1) * rows)
@@ -109,43 +114,52 @@
             st_ref[0, group, pl.ds(h, 1), :] = jnp.broadcast_to(total, (1, 128))
 
 
-def attend_blocks(sink_logit, queries, out_grad, window, allowed):
+def attend_blocks(flag, sink_logit, queries, out_grad, window, allowed):
     lanes, rows, query_width = queries.shape
     span = window.shape[1]
     side_width = KV_HEADS * HEAD_DIM
-    row_spec = pl.BlockSpec((1, rows, query_width), lambda lane: (lane, 0, 0))
-    side_spec = pl.BlockSpec((1, span, side_width), lambda lane: (lane, 0, 0))
+    row_spec = pl.BlockSpec((1, rows, query_width), lambda lane, flag_ref: (lane, 0, 0))
+    side_spec = pl.BlockSpec((1, span, side_width), lambda lane, flag_ref: (lane, 0, 0))
+    own_spec = pl.BlockSpec((1, rows, side_width), lambda lane, flag_ref: (lane, 0, 0))
     flops = 2 * lanes * HEADS * rows * span * HEAD_DIM * 6
-    moved = 2 * (4 * queries.size + 2 * window.size) + 4 * allowed.size + 8 * window.size
-    return pl.pallas_call(
-        group_kernel,
+    moved = 2 * (4 * queries.size + 2 * window.size) + 4 * allowed.size + 6 * window.size
+    grid_spec = pltpu.PrefetchScalarGridSpec(
+        num_scalar_prefetch=1,
         grid=(lanes,),
         in_specs=[
             pl.BlockSpec(memory_space=pltpu.SMEM),
             row_spec,
             row_spec,
             side_spec,
-            pl.BlockSpec((1, span, side_width), lambda lane: (lane, 0, 1)),
-            pl.BlockSpec((1, rows, span), lambda lane: (lane, 0, 0)),
+            pl.BlockSpec((1, span, side_width), lambda lane, flag_ref: (lane, 0, 1)),
+            pl.BlockSpec((1, rows, span), lambda lane, flag_ref: (lane, 0, 0)),
         ],
         out_specs=[
             row_spec,
             row_spec,
-            side_spec,
-            side_spec,
-            pl.BlockSpec((1, KV_HEADS, GROUP, 128), lambda lane: (lane, 0, 0, 0)),
+            pl.BlockSpec(
+                (1, rows, 2 * side_width), lambda lane, flag_ref: ((lane + flag_ref[0]) % 2, 0, 0)
+            ),
+            own_spec,
+            own_spec,
+            pl.BlockSpec((1, KV_HEADS, GROUP, 128), lambda lane, flag_ref: (lane, 0, 0, 0)),
         ],
+    )
+    return pl.pallas_call(
+        group_kernel,
+        grid_spec=grid_spec,
         out_shape=[
             jax.ShapeDtypeStruct((lanes, rows, query_width), jnp.bfloat16),
             jax.ShapeDtypeStruct((lanes, rows, query_width), jnp.bfloat16),
-            jax.ShapeDtypeStruct((lanes, span, side_width), jnp.float32),
-            jax.ShapeDtypeStruct((lanes, span, side_width), jnp.float32),
+            jax.ShapeDtypeStruct((lanes, rows, 2 * side_width), jnp.bfloat16),
+            jax.ShapeDtypeStruct((lanes, rows, side_width), jnp.float32),
+            jax.ShapeDtypeStruct((lanes, rows, side_width), jnp.float32),
             jax.ShapeDtypeStruct((lanes, KV_HEADS, GROUP, 128), jnp.float32),
         ],
         cost_estimate=pl.CostEstimate(
             flops=flops, transcendentals=2 * lanes * HEADS * rows * span, bytes_accessed=moved
         ),
-    )(sink_logit, queries, out_grad, window, window, allowed)
+    )(flag, sink_logit, queries, out_grad, window, window, allowed)
 
 
 def per_device(queries, keys, values, doc_bounds, sink_logit, out_grad):
@@ -176,7 +190,9 @@
     allowed = (key_pos[:, None, :] <= query_pos[:, :, None]) & (
         key_pos[:, None, :] >= first_pos[:, :, None]
     )
-    attended, dquery, key_part, value_part, sink_parts = attend_blocks(
+    even_flag = (my_index % 2 == 0).astype(jnp.int32)
+    attended, dquery, message, key_own, value_own, sink_parts = attend_blocks(
+        even_flag.reshape(1),
         sink_logit,
         queries.reshape(2, block_rows, query_width),
         out_grad.reshape(2, block_rows, query_width),
@@ -185,20 +201,21 @@
     )
     sink_terms = jnp.sum(sink_parts[:, :, :, 0], axis=0)
     sink_grad = all_sum(sink_terms.reshape(HEADS), ("ctx", "dp"))
-    partial = jnp.concatenate([key_part, value_part], axis=2)
-
-    prev_part = partial[:, :block_rows].astype(jnp.bfloat16)
-    into1, into0 = neighbour_swap(prev_part[1], prev_part[0], "ctx")
-    into0 = jnp.where(at_fold, prev_part[1], into0)
-    own_part = partial[:, block_rows:]
-    gathered = own_part + jnp.stack([into0, into1]).astype(jnp.float32)
+
+    is_even = even_flag == 1
+    got_first = swap_pairs(message[0], "ctx", 0)
+    got_second = swap_pairs(message[1], "ctx", 1)
+    into1 = jnp.where(is_even, got_second, got_first)
+    into0 = jnp.where(is_even, got_first, got_second)
+    into0 = jnp.where(at_fold, message[1], into0)
+    arrived = jnp.stack([into0, into1]).astype(jnp.float32)
 
     out_shape = (1, 1, 2, block_rows, query_width)
     pair_out = (1, 1, 2, block_rows, value_width)
     attn_out = attended.reshape(out_shape)
     query_grad = dquery.reshape(out_shape)
-    key_grad = gathered[:, :, :value_width].astype(jnp.bfloat16).reshape(pair_out)
-    value_grad = gathered[:, :, value_width:].astype(jnp.bfloat16).reshape(pair_out)
+    key_grad = (key_own + arrived[:, :, :value_width]).astype(jnp.bfloat16).reshape(pair_out)
+    value_grad = (value_own + arrived[:, :, value_width:]).astype(jnp.bfloat16).reshape(pair_out)
     return (attn_out, query_grad, key_grad, value_grad, sink_grad)
 
 

time: 42.5 us -> 43.9 us (1.033)
  blocking collectives: 13.5 us -> 0 us
  waiting for transfers between devices: 4.37 us -> 11.4 us
  starting transfers between devices: 8.96 us -> 15.5 us
  local copies, waits for them, and re-layouts: 2.67 us -> 3.33 us
  other arithmetic: 3.77 us -> 4.42 us
    all_to_all x1 -> x0, blocking collectives: 13.5 us -> none  [all_sum(): return jnp.sum(lax.all_to_all(spread, axes, 0, 0, tiled=True), axis=0)]
    all_to_all x0 -> x1, waiting for transfers between devices: none -> 7.07 us  [all_sum(): return jnp.sum(lax.all_to_all(spread, axes, 0, 0, tiled=True), axis=0)]
    all_to_all x0 -> x1, starting transfers between devices: none -> 6.56 us  [all_sum(): return jnp.sum(lax.all_to_all(spread, axes, 0, 0, tiled=True), axis=0)]
    squeeze x0 -> x1, local copies, waits for them, and re-layouts: none -> 1.03 us  [per_device(): got_first = swap_pairs(message[0], 'ctx', 0)]
    reshape x0 -> x1, other arithmetic: none -> 0.77 us  [per_device(): (value_own + arrived[:, :, value_width:]).astype(jnp.bfloat16)]
    reshape x1 -> x0, local copies, waits for them, and re-layouts: 0.72 us -> none  [per_device(): gathered[:, :, value_width:].astype(jnp.bfloat16).reshape(pair_out)]
    broadcast_in_dim x2, local copies, waits for them, and re-layouts: 0.1 us -> 0.71 us  [all_sum(): spread = jnp.broadcast_to(x[None], (count,) + x.shape)]
    unnamed x11 -> x14, local copies, waits for them, and re-layouts: 1.81 us -> 1.6 us
  transfers between devices with their start and end apart: 4 -> 5, of which waited for: 1 -> 2; matrix products, arithmetic and copies ran while one was open for 4% -> 5% of each run, Pallas kernels for 0% -> 0%
where the time goes in v17:
time: 43.9 us; the launch traced here: 43.7 us
  starting transfers between devices  15.5 us (35%)
  waiting for transfers between devices  11.4 us (26%)
  Pallas kernels  8.17 us (19%)
  other arithmetic  4.42 us (10%)
  local copies, waits for them, and re-layouts  3.33 us (8%)
  between operations  0.78 us (2%)
    ppermute x4, starting transfers between devices, swap_pairs(): return lax.ppermute(x, axis, pairs)  8.96 us
    pallas_call x1, Pallas kernels, attend_blocks(): pl.pallas_call(group_kernel, grid_spec=grid_spec, out_shape=[jax.ShapeDty...  8.17 us
    all_to_all x1, waiting for transfers between devices, all_sum(): return jnp.sum(lax.all_to_all(spread, axes, 0, 0, tiled=True), axis=0)  7.07 us
    all_to_all x1, starting transfers between devices, all_sum(): return jnp.sum(lax.all_to_all(spread, axes, 0, 0, tiled=True), axis=0)  6.56 us
    ppermute x4, waiting for transfers between devices, swap_pairs(): return lax.ppermute(x, axis, pairs)  4.37 us
    unnamed x14, local copies, waits for them, and re-layouts  1.6 us
    select_n x1, other arithmetic, neighbour_swap(): jnp.where(even, to_prev, to_next)  1.1 us
    squeeze x1, local copies, waits for them, and re-layouts, per_device(): got_first = swap_pairs(message[0], 'ctx', 0)  1.03 us
  transfers between devices with their start and end apart: 5, of which 2 were waited for; matrix products, arithmetic and copies ran while one was open for 5% of the time, Pallas kernels for 0%

profile of v17, /device:TPU:0, one launch (start us, length us, event | category | flops | bytes accessed | tf_op | source)
XLA Modules:
  0.0 43.7 jit_solution(10969436261040823764)
XLA Ops:
  0.6 0.0 copy-start
  0.7 0.0 copy-start.1
  0.7 1.1 %broadcast_select_fusion = (bf16[64,1024]{1,0:T(8,128)(2,1)S(1)}, bf16[64,1024]{1,0:T(8,128)(2,1)S(1)}) fusion(pred[]{:T(512)S(6)} %eq.13, bf16[2,64,512]{2,1,0:T(8,128)(2,1)} %bitcast.44, bf16[2,64,512]{2,1,0:T(8,128)(2,1)} %bitcast.47), kind=kLoop, calls=%fused_computation.20 | loop fusion | flops 917504 | bytes 524289 | tf_op jit(solution)/shard_map/jit(_where)/select_n | solution.py:40
  1.8 0.7 %collective-permute-start = (bf16[64,1024]{1,0:T(8,128)(2,1)S(1)}, bf16[64,1024]{1,0:T(8,128)(2,1)S(1)}, u32[]{:S(2)}, u32[]{:S(2)}) collective-permute-start(bf16[64,1024]{1,0:T(8,128)(2,1)S(1)} %get-tuple-element.13), channel_id=1, source_target_pairs={{2,4},{4,2},{6,8},{8,6},{10,12},{12,10},{14,16},{16,14},{18,20},{2... | collective-permute-start | bytes 393224 | tf_op jit(solution)/shard_map/ppermute | solution.py:34
  2.4 5.7 %collective-permute-start.1 = (bf16[64,1024]{1,0:T(8,128)(2,1)S(1)}, bf16[64,1024]{1,0:T(8,128)(2,1)S(1)}, u32[]{:S(2)}, u32[]{:S(2)}) collective-permute-start(bf16[64,1024]{1,0:T(8,128)(2,1)S(1)} %get-tuple-element.14), channel_id=1, source_target_pairs={{0,2},{2,0},{4,6},{6,4},{8,10},{10,8},{12,14},{14,12},{16,18},{18,... | collective-permute-start | bytes 393224 | tf_op jit(solution)/shard_map/ppermute | solution.py:34
  8.2 0.1 add_multiply_fusion
  8.3 0.1 iota_add_fusion
  8.3 0.1 iota_add_fusion.1
  8.4 0.6 %copy-done.6 = s32[1,1,2,2,64]{4,3,2,1,0:T(2,128)S(1)} copy-done((s32[1,1,2,2,64]{4,3,2,1,0:T(2,128)S(1)}, s32[1,1,2,2,64]{4,3,2,1,0:T(2,128)}, u32[]{:S(2)}) %copy-start.6) | copy-done | bytes 1048
  9.0 0.7 %and_convert_fusion.allow_ref = f32[2,64,128]{2,1,0:T(8,128)} fusion(s32[2,64]{1,0:T(2,128)S(1)} %bitcast.53, s32[2,64]{1,0:T(2,128)S(1)} %iota_add_fusion, s32[2,128]{1,0:T(2,128)S(1)} %iota_add_fusion.1), kind=kLoop, calls=%fused_computation.22 | loop fusion | flops 65536 | bytes 67584 | tf_op jit(solution)/shard_map/convert_element_type | solution.py:200
  9.7 0.0 collective-permute-done
  9.8 4.4 %collective-permute-done.1 = bf16[64,1024]{1,0:T(8,128)(2,1)S(1)} collective-permute-done((bf16[64,1024]{1,0:T(8,128)(2,1)S(1)}, bf16[64,1024]{1,0:T(8,128)(2,1)S(1)}, u32[]{:S(2)}, u32[]{:S(2)}) %collective-permute-start.1) | collective-permute-done | bytes 131104 | tf_op jit(solution)/shard_map/ppermute | solution.py:34
  14.1 0.0 copy-done
  14.1 0.1 select_bitcast_fusion.3
  14.2 0.8 %maximum_maximum_fusion.k_ref.v_ref = bf16[2,128,1024]{2,1,0:T(8,128)(2,1)} fusion(bf16[2,64,512]{2,1,0:T(8,128)(2,1)S(1)} %bitcast.46, bf16[2,64,512]{2,1,0:T(8,128)(2,1)S(1)} %bitcast.49, bf16[1,64,1024]{2,1,0:T(8,128)(2,1)S(1)} %get-tuple-element.28, bf16[1,64,1024]{2,1,0:T(8,128)(2,1)S(1)} %get-tuple-element.27), kind=kLoop, calls=%fused_computation | loop fusion | flops 2097152 | bytes 1048576 | tf_op jit(solution)/shard_map/concatenate | solution.py:182
  15.0 8.2 %shard_map.101 = (bf16[2,64,4096]{2,1,0:T(8,128)(2,1)}, bf16[2,64,4096]{2,1,0:T(8,128)(2,1)}, bf16[2,64,1024]{2,1,0:T(8,128)(2,1)}, f32[2,64,512]{2,1,0:T(8,128)...) custom-call(s32[1]{0:T(128)} %bitcast.flag_ref, f32[32]{0:T(128)} %sink_ref.1, bf16[2,64,4096]{2,1,0:T(8,128)(2,1)} %bitcast.50, ...), custom_call_target="tpu_custom_call" | custom-call | flops 805306368 | bytes 6881280 | tf_op jit(solution)/shard_map/pallas_call | solution.py:148
  23.2 0.0 copy-start.5
  23.2 0.0 copy-start.2
  23.2 1.0 %slice_bitcast_fusion = (bf16[64,1024]{1,0:T(8,128)(2,1)S(1)}, bf16[64,1024]{1,0:T(8,128)(2,1)S(1)}) fusion(bf16[2,64,1024]{2,1,0:T(8,128)(2,1)} %get-tuple-element.18), kind=kLoop, calls=%fused_computation.16 | loop fusion | bytes 524288 | tf_op jit(solution)/shard_map/squeeze | solution.py:206
  24.3 1.9 %collective-permute-start.2 = (bf16[64,1024]{1,0:T(8,128)(2,1)S(1)}, bf16[64,1024]{1,0:T(8,128)(2,1)S(1)}, u32[]{:S(2)}, u32[]{:S(2)}) collective-permute-start(bf16[64,1024]{1,0:T(8,128)(2,1)S(1)} %get-tuple-element.25), channel_id=1, source_target_pairs={{0,2},{2,0},{4,6},{6,4},{8,10},{10,8},{12,14},{14,12},{16,18},{18,... | collective-permute-start | bytes 393224 | tf_op jit(solution)/shard_map/ppermute | solution.py:34
  26.2 0.7 %collective-permute-start.3 = (bf16[64,1024]{1,0:T(8,128)(2,1)S(1)}, bf16[64,1024]{1,0:T(8,128)(2,1)S(1)}, u32[]{:S(2)}, u32[]{:S(2)}) collective-permute-start(bf16[64,1024]{1,0:T(8,128)(2,1)S(1)} %get-tuple-element.26), channel_id=1, source_target_pairs={{2,4},{4,2},{6,8},{8,6},{10,12},{12,10},{14,16},{16,14},{18,20},{2... | collective-permute-start | bytes 393224 | tf_op jit(solution)/shard_map/ppermute | solution.py:34
  26.8 0.1 slice_reduce_fusion
  26.9 0.1 broadcast_in_dim.4
  27.0 0.6 %broadcast_in_dim.5 = f32[32,1,32]{2,1,0:T(1,128)} broadcast(f32[32]{0:T(128)S(1)} %broadcast_in_dim.4), dimensions={2} | broadcast | bytes 4224 | tf_op jit(solution)/shard_map/broadcast_in_dim | solution.py:53
  27.6 6.6 %all-to-all-start = ((f32[32,1,32]{2,1,0:T(1,128)}), f32[32,1,32]{2,1,0:T(1,128)S(1)}, u32[]{:S(2)}, u32[]{:S(2)}) async-start(f32[32,1,32]{2,1,0:T(1,128)} %broadcast_in_dim.5), calls=%async_computation | async-start | bytes 32768 | tf_op jit(solution)/shard_map/all_to_all | solution.py:54
  34.2 7.1 %all-to-all-done = f32[32,1,32]{2,1,0:T(1,128)S(1)} async-done(((f32[32,1,32]{2,1,0:T(1,128)}), f32[32,1,32]{2,1,0:T(1,128)S(1)}, u32[]{:S(2)}, u32[]{:S(2)}) %all-to-all-start) | async-done | bytes 4128 | tf_op jit(solution)/shard_map/all_to_all | solution.py:54
  41.3 0.5 %reduce_sum.19 = f32[32]{0:T(128)} reduce(f32[32,1,32]{2,0,1:T(8,128)S(1)} %bitcast.52, f32[]{:T(128)} %constant.33.clone.1), dimensions={0,1}, to_apply=%region_1.2 | reduce | flops 992 | bytes 4228 | tf_op jit(solution)/shard_map/reduce_sum | solution.py:54
  41.8 0.0 collective-permute-done.2
  41.8 0.0 collective-permute-done.3
  41.9 0.9 %copy-done.3 = f32[2,64,512]{2,1,0:T(8,128)S(1)} copy-done((f32[2,64,512]{2,1,0:T(8,128)S(1)}, f32[2,64,512]{2,1,0:T(8,128)}, u32[]{:S(2)}) %copy-start.3) | copy-done | bytes 262168
  42.8 0.1 copy-done.4
  42.9 0.8 %fusion.5 = (bf16[1,1,2,64,512]{4,3,2,1,0:T(8,128)(2,1)}, bf16[1,1,2,64,512]{4,3,2,1,0:T(8,128)(2,1)}) fusion(f32[2,64,512]{2,1,0:T(8,128)S(1)} %copy-done.4, f32[2,64,1024]{2,1,0:T(8,128)S(1)} %maximum_convert_fusion, f32[2,64,512]{2,1,0:T(8,128)S(1)} %copy-done.3), kind=kLoop, calls=%fused_computation.11 | loop fusion | flops 262144 | bytes 1310720 | tf_op jit(solution)/shard_map/reshape | solution.py:218
  (9 shorter events, 0.1 us)
Async XLA Ops:
  0.6 13.5 %copy-start = (bf16[1,1,2,64,512]{4,3,2,1,0:T(8,128)(2,1)S(1)}, bf16[1,1,2,64,512]{4,3,2,1,0:T(8,128)(2,1)}, u32[]{:S(2)}) copy-start(bf16[1,1,2,64,512]{4,3,2,1,0:T(8,128)(2,1)} %param.8) | copy-start | bytes 393220
  0.7 13.5 %copy-start.1 = (bf16[1,1,2,64,512]{4,3,2,1,0:T(8,128)(2,1)S(1)}, bf16[1,1,2,64,512]{4,3,2,1,0:T(8,128)(2,1)}, u32[]{:S(2)}) copy-start(bf16[1,1,2,64,512]{4,3,2,1,0:T(8,128)(2,1)} %param.7) | copy-start | bytes 393220
  1.8 8.0 %collective-permute-start = (bf16[64,1024]{1,0:T(8,128)(2,1)S(1)}, bf16[64,1024]{1,0:T(8,128)(2,1)S(1)}, u32[]{:S(2)}, u32[]{:S(2)}) collective-permute-start(bf16[64,1024]{1,0:T(8,128)(2,1)S(1)} %get-tuple-element.13), channel_id=1, source_target_pairs={{2,4},{4,2},{6,8},{8,6},{10,12},{12,10},{14,16},{16,14},{18,20},{2... | collective-permute-start | bytes 393224 | tf_op jit(solution)/shard_map/ppermute | solution.py:34
  2.4 11.7 %collective-permute-start.1 = (bf16[64,1024]{1,0:T(8,128)(2,1)S(1)}, bf16[64,1024]{1,0:T(8,128)(2,1)S(1)}, u32[]{:S(2)}, u32[]{:S(2)}) collective-permute-start(bf16[64,1024]{1,0:T(8,128)(2,1)S(1)} %get-tuple-element.14), channel_id=1, source_target_pairs={{0,2},{2,0},{4,6},{6,4},{8,10},{10,8},{12,14},{14,12},{16,18},{18,... | collective-permute-start | bytes 393224 | tf_op jit(solution)/shard_map/ppermute | solution.py:34
  8.3 0.7 %copy-start.6 = (s32[1,1,2,2,64]{4,3,2,1,0:T(2,128)S(1)}, s32[1,1,2,2,64]{4,3,2,1,0:T(2,128)}, u32[]{:S(2)}) copy-start(s32[1,1,2,2,64]{4,3,2,1,0:T(2,128)} %param.9) | copy-start | bytes 3076
  23.2 3.6 %copy-start.5 = (f32[2,4,8,128]{3,2,1,0:T(8,128)S(1)}, f32[2,4,8,128]{3,2,1,0:T(8,128)}, u32[]{:S(2)}) copy-start(f32[2,4,8,128]{3,2,1,0:T(8,128)} %get-tuple-element.20) | copy-start | bytes 98308
  23.2 18.6 %copy-start.2 = (bf16[2,64,1024]{2,1,0:T(8,128)(2,1)S(1)}, bf16[2,64,1024]{2,1,0:T(8,128)(2,1)}, u32[]{:S(2)}) copy-start(bf16[2,64,1024]{2,1,0:T(8,128)(2,1)} %get-tuple-element.18) | copy-start | bytes 786436
  24.3 17.5 %collective-permute-start.2 = (bf16[64,1024]{1,0:T(8,128)(2,1)S(1)}, bf16[64,1024]{1,0:T(8,128)(2,1)S(1)}, u32[]{:S(2)}, u32[]{:S(2)}) collective-permute-start(bf16[64,1024]{1,0:T(8,128)(2,1)S(1)} %get-tuple-element.25), channel_id=1, source_target_pairs={{0,2},{2,0},{4,6},{6,4},{8,10},{10,8},{12,14},{14,12},{16,18},{18,... | collective-permute-start | bytes 393224 | tf_op jit(solution)/shard_map/ppermute | solution.py:34
  26.2 15.6 %collective-permute-start.3 = (bf16[64,1024]{1,0:T(8,128)(2,1)S(1)}, bf16[64,1024]{1,0:T(8,128)(2,1)S(1)}, u32[]{:S(2)}, u32[]{:S(2)}) collective-permute-start(bf16[64,1024]{1,0:T(8,128)(2,1)S(1)} %get-tuple-element.26), channel_id=1, source_target_pairs={{2,4},{4,2},{6,8},{8,6},{10,12},{12,10},{14,16},{16,14},{18,20},{2... | collective-permute-start | bytes 393224 | tf_op jit(solution)/shard_map/ppermute | solution.py:34
  27.6 13.6 %all-to-all-start = ((f32[32,1,32]{2,1,0:T(1,128)}), f32[32,1,32]{2,1,0:T(1,128)S(1)}, u32[]{:S(2)}, u32[]{:S(2)}) async-start(f32[32,1,32]{2,1,0:T(1,128)} %broadcast_in_dim.5), calls=%async_computation | async-start | bytes 32768 | tf_op jit(solution)/shard_map/all_to_all | solution.py:54
  41.9 1.0 %copy-start.3 = (f32[2,64,512]{2,1,0:T(8,128)S(1)}, f32[2,64,512]{2,1,0:T(8,128)}, u32[]{:S(2)}) copy-start(f32[2,64,512]{2,1,0:T(8,128)} %get-tuple-element.17) | copy-start | bytes 786436
  41.9 1.0 %copy-start.4 = (f32[2,64,512]{2,1,0:T(8,128)S(1)}, f32[2,64,512]{2,1,0:T(8,128)}, u32[]{:S(2)}) copy-start(f32[2,64,512]{2,1,0:T(8,128)} %get-tuple-element.19) | copy-start | bytes 786436

commit v18 on v13

--- a/solution.py
+++ b/solution.py
@@ -55,7 +55,8 @@
 
 
 def group_kernel(
-    sink_ref, q_ref, g_ref, k_ref, v_ref, allow_ref, o_ref, dq_ref, dk_ref, dv_ref, st_ref
+    sink_ref, q_ref, g_ref, k_ref, v_ref, prev0_ref, prev1_ref, allow_ref,
+    o_ref, dq_ref, dk_ref, dv_ref, st_ref,
 ):
     rows = q_ref.shape[1]
     score_scale = 1.0 / math.sqrt(HEAD_DIM)
@@ -68,8 +69,12 @@
         side = pl.ds(group * HEAD_DIM, HEAD_DIM)
         query = jnp.concatenate([q_ref[0, :, cols] for cols in heads], axis=0)
         grad = jnp.concatenate([g_ref[0, :, cols] for cols in heads], axis=0)
-        key = k_ref[0, :, side]
-        value = v_ref[0, :, side]
+        value_side = pl.ds((KV_HEADS + group) * HEAD_DIM, HEAD_DIM)
+        lane_zero = pl.program_id(0) == 0
+        prev_key = jnp.where(lane_zero, prev0_ref[:, side], prev1_ref[:, side])
+        prev_value = jnp.where(lane_zero, prev0_ref[:, value_side], prev1_ref[:, value_side])
+        key = jnp.concatenate([prev_key, k_ref[0, :, side]], axis=0)
+        value = jnp.concatenate([prev_value, v_ref[0, :, side]], axis=0)
         sink = jnp.zeros((GROUP * rows, 1), jnp.float32)
         for h in range(GROUP):
             sink = jnp.where(head_of_row == h, sink_ref[group * GROUP + h], sink)
@@ -109,14 +114,16 @@
             st_ref[0, group, pl.ds(h, 1), :] = jnp.broadcast_to(total, (1, 128))
 
 
-def attend_blocks(sink_logit, queries, out_grad, window, allowed):
+def attend_blocks(sink_logit, queries, out_grad, keys, values, prev0, prev1, allowed):
     lanes, rows, query_width = queries.shape
-    span = window.shape[1]
-    side_width = KV_HEADS * HEAD_DIM
+    span = 2 * rows
+    side_width = keys.shape[2]
     row_spec = pl.BlockSpec((1, rows, query_width), lambda lane: (lane, 0, 0))
+    own_spec = pl.BlockSpec((1, rows, side_width), lambda lane: (lane, 0, 0))
+    whole = pl.BlockSpec(prev0.shape, lambda lane: (0, 0))
     side_spec = pl.BlockSpec((1, span, side_width), lambda lane: (lane, 0, 0))
     flops = 2 * lanes * HEADS * rows * span * HEAD_DIM * 6
-    moved = 2 * (4 * queries.size + 2 * window.size) + 4 * allowed.size + 8 * window.size
+    moved = 8 * queries.size + 4 * keys.size + 4 * prev0.size + 4 * allowed.size + 16 * keys.size
     return pl.pallas_call(
         group_kernel,
         grid=(lanes,),
@@ -124,8 +131,10 @@
             pl.BlockSpec(memory_space=pltpu.SMEM),
             row_spec,
             row_spec,
-            side_spec,
-            pl.BlockSpec((1, span, side_width), lambda lane: (lane, 0, 1)),
+            own_spec,
+            own_spec,
+            whole,
+            whole,
             pl.BlockSpec((1, rows, span), lambda lane: (lane, 0, 0)),
         ],
         out_specs=[
@@ -145,7 +154,7 @@
         cost_estimate=pl.CostEstimate(
             flops=flops, transcendentals=2 * lanes * HEADS * rows * span, bytes_accessed=moved
         ),
-    )(sink_logit, queries, out_grad, window, window, allowed)
+    )(sink_logit, queries, out_grad, keys, values, prev0, prev1, allowed)
 
 
 def per_device(queries, keys, values, doc_bounds, sink_logit, out_grad):
@@ -164,8 +173,6 @@
     )
     prev0, prev1 = neighbour_swap(own_pair[0], own_pair[1], "ctx")
     prev1 = jnp.where(at_fold, own_pair[0], prev1)
-    prev_pair = jnp.stack([prev0, prev1])
-    window = jnp.concatenate([prev_pair, own_pair], axis=1)
 
     lane_block = jnp.stack([my_index, last_block - my_index]).astype(jnp.int32)
     row_offsets = jnp.arange(block_rows, dtype=jnp.int32)
@@ -180,7 +187,10 @@
         sink_logit,
         queries.reshape(2, block_rows, query_width),
         out_grad.reshape(2, block_rows, query_width),
-        window,
+        keys.reshape(2, block_rows, value_width),
+        values.reshape(2, block_rows, value_width),
+        prev0,
+        prev1,
         allowed.astype(jnp.float32),
     )
     sink_terms = jnp.sum(sink_parts[:, :, :, 0], axis=0)

time: 42.5 us -> 42.6 us (level)
    concatenate x1 -> x0, other arithmetic: 0.85 us -> none  [per_device(): window = jnp.concatenate([prev_pair, own_pair], axis=1)]
    select_n x0 -> x1, other arithmetic: none -> 0.77 us  [per_device(): prev1 = jnp.where(at_fold, own_pair[0], prev1)]
where the time goes in v18:
time: 42.6 us; the launch traced here: 42.3 us
  blocking collectives  13.5 us (32%)
  starting transfers between devices  8.96 us (21%)
  Pallas kernels  8.45 us (20%)
  waiting for transfers between devices  4.36 us (10%)
  other arithmetic  3.63 us (9%)
  local copies, waits for them, and re-layouts  2.67 us (6%)
  between operations  0.77 us (2%)
    all_to_all x1, blocking collectives, all_sum(): return jnp.sum(lax.all_to_all(spread, axes, 0, 0, tiled=True), axis=0)  13.5 us
    ppermute x4, starting transfers between devices, swap_pairs(): return lax.ppermute(x, axis, pairs)  8.96 us
    pallas_call x1, Pallas kernels, attend_blocks(): pl.pallas_call(group_kernel, grid=(lanes,), in_specs=[pl.BlockSpec(memory...  8.45 us
    ppermute x4, waiting for transfers between devices, swap_pairs(): return lax.ppermute(x, axis, pairs)  4.36 us
    unnamed x11, local copies, waits for them, and re-layouts  1.81 us
    select_n x2, other arithmetic, neighbour_swap(): jnp.where(even, to_prev, to_next)  1.12 us
  transfers between devices with their start and end apart: 4, of which 1 were waited for; matrix products, arithmetic and copies ran while one was open for 4% of the time, Pallas kernels for 0%

profile of v18, /device:TPU:0, one launch (start us, length us, event | category | flops | bytes accessed | tf_op | source)
XLA Modules:
  0.0 42.3 jit_solution(8409772465376472072)
XLA Ops:
  0.6 0.0 copy-start.1
  0.7 0.0 copy-start.2
  0.7 1.1 %broadcast_select_fusion.3 = (bf16[64,1024]{1,0:T(8,128)(2,1)S(1)}, bf16[64,1024]{1,0:T(8,128)(2,1)S(1)}) fusion(pred[]{:T(512)S(6)} %eq.10, bf16[2,64,512]{2,1,0:T(8,128)(2,1)} %bitcast.50, bf16[2,64,512]{2,1,0:T(8,128)(2,1)} %bitcast.47), kind=kLoop, calls=%fused_computation.18 | loop fusion | flops 917504 | bytes 524289 | tf_op jit(solution)/shard_map/jit(_where)/select_n | solution.py:40
  1.8 0.7 %collective-permute-start = (bf16[64,1024]{1,0:T(8,128)(2,1)S(1)}, bf16[64,1024]{1,0:T(8,128)(2,1)S(1)}, u32[]{:S(2)}, u32[]{:S(2)}) collective-permute-start(bf16[64,1024]{1,0:T(8,128)(2,1)S(1)} %get-tuple-element.14), channel_id=1, source_target_pairs={{2,4},{4,2},{6,8},{8,6},{10,12},{12,10},{14,16},{16,14},{18,20},{2... | collective-permute-start | bytes 393224 | tf_op jit(solution)/shard_map/ppermute | solution.py:34
  2.4 5.7 %collective-permute-start.1 = (bf16[64,1024]{1,0:T(8,128)(2,1)S(1)}, bf16[64,1024]{1,0:T(8,128)(2,1)S(1)}, u32[]{:S(2)}, u32[]{:S(2)}) collective-permute-start(bf16[64,1024]{1,0:T(8,128)(2,1)S(1)} %get-tuple-element.15), channel_id=1, source_target_pairs={{0,2},{2,0},{4,6},{6,4},{8,10},{10,8},{12,14},{14,12},{16,18},{18,... | collective-permute-start | bytes 393224 | tf_op jit(solution)/shard_map/ppermute | solution.py:34
  8.2 0.1 add_multiply_fusion
  8.3 0.1 iota_add_fusion.1
  8.3 0.1 iota_add_fusion
  8.4 0.6 %copy-done.4 = s32[1,1,2,2,64]{4,3,2,1,0:T(2,128)S(1)} copy-done((s32[1,1,2,2,64]{4,3,2,1,0:T(2,128)S(1)}, s32[1,1,2,2,64]{4,3,2,1,0:T(2,128)}, u32[]{:S(2)}) %copy-start.4) | copy-done | bytes 1048
  9.0 0.7 %and_convert_fusion.allow_ref = f32[2,64,128]{2,1,0:T(8,128)} fusion(s32[2,64]{1,0:T(2,128)S(1)} %bitcast.54, s32[2,64]{1,0:T(2,128)S(1)} %iota_add_fusion, s32[2,128]{1,0:T(2,128)S(1)} %iota_add_fusion.1), kind=kLoop, calls=%fused_computation.20 | loop fusion | flops 65536 | bytes 67584 | tf_op jit(solution)/shard_map/convert_element_type | solution.py:194
  9.8 0.0 collective-permute-done
  9.8 4.4 %collective-permute-done.1 = bf16[64,1024]{1,0:T(8,128)(2,1)S(1)} collective-permute-done((bf16[64,1024]{1,0:T(8,128)(2,1)S(1)}, bf16[64,1024]{1,0:T(8,128)(2,1)S(1)}, u32[]{:S(2)}, u32[]{:S(2)}) %collective-permute-start.1) | collective-permute-done | bytes 131104 | tf_op jit(solution)/shard_map/ppermute | solution.py:34
  14.1 0.0 copy-done.1
  14.1 0.0 copy-done.2
  14.1 0.8 %select_select_fusion = (bf16[64,1024]{1,0:T(8,128)(2,1)}, bf16[64,1024]{1,0:T(8,128)(2,1)}) fusion(bf16[64,1024]{1,0:T(8,128)(2,1)S(1)} %collective-permute-done.1, bf16[64,1024]{1,0:T(8,128)(2,1)S(1)} %collective-permute-done, pred[]{:T(512)S(6)} %eq.11, pred[]{:T(512)S(6)} %eq.10, bf16[2,64,512]{2,1,0:T(8,128)(2,1)S(1)} %bitcast.52, ...), kind=kLoop, calls=%fused_computation.14 | loop fusion | flops 458752 | bytes 786434 | tf_op jit(solution)/shard_map/jit(_where)/select_n | solution.py:175
  14.9 8.4 %shard_map.101 = (bf16[2,64,4096]{2,1,0:T(8,128)(2,1)}, bf16[2,64,4096]{2,1,0:T(8,128)(2,1)}, f32[2,128,512]{2,1,0:T(8,128)}, f32[2,128,512]{2,1,0:T(8,128)}, f32[2,4,8,128]{3,2,1,0:T(8,128)}) custom-call(f32[32]{0:T(128)} %sink_ref.1, bf16[2,64,4096]{2,1,0:T(8,128)(2,1)} %bitcast.56, bf16[2,64,4096]{2,1,0:T(8,128)(2,1)} %bitcast.57, ...), custom_call_target="tpu_custom_call" | custom-call | flops 805306368 | bytes 5832704 | tf_op jit(solution)/shard_map/pallas_call | solution.py:127
  23.3 0.0 copy-start
  23.3 1.1 %constant_dynamic-update-slice_fusion.1 = f32[2,128,1024]{2,1,0:T(8,128)S(1)} fusion(f32[2,128,512]{2,1,0:T(8,128)} %get-tuple-element.18), kind=kLoop, calls=%fused_computation.23 | loop fusion | bytes 1048576
  24.5 0.0 copy-done
  24.6 0.1 convert.7
  24.7 0.0 copy-start.3
  24.7 1.9 %collective-permute-start.2 = (bf16[64,1024]{1,0:T(8,128)(2,1)S(1)}, bf16[64,1024]{1,0:T(8,128)(2,1)S(1)}, u32[]{:S(2)}, u32[]{:S(2)}) collective-permute-start(bf16[64,1024]{1,0:T(8,128)(2,1)S(1)} %get-tuple-element.20), channel_id=1, source_target_pairs={{0,2},{2,0},{4,6},{6,4},{8,10},{10,8},{12,14},{14,12},{16,18},{18,... | collective-permute-start | bytes 393224 | tf_op jit(solution)/shard_map/ppermute | solution.py:34
  26.6 0.7 %collective-permute-start.3 = (bf16[64,1024]{1,0:T(8,128)(2,1)S(1)}, bf16[64,1024]{1,0:T(8,128)(2,1)S(1)}, u32[]{:S(2)}, u32[]{:S(2)}) collective-permute-start(bf16[64,1024]{1,0:T(8,128)(2,1)S(1)} %get-tuple-element.21), channel_id=1, source_target_pairs={{2,4},{4,2},{6,8},{8,6},{10,12},{12,10},{14,16},{16,14},{18,20},{2... | collective-permute-start | bytes 393224 | tf_op jit(solution)/shard_map/ppermute | solution.py:34
  27.3 0.0 copy-done.3
  27.3 0.1 slice_reduce_fusion
  27.4 0.1 broadcast_in_dim.4
  27.5 13.5 %all_to_all.6 = f32[32,1,32]{2,1,0:T(1,128)S(1)} all-to-all(f32[32,1,32]{2,1,0:T(1,128)S(1)} %broadcast_in_dim.5), channel_id=1, replica_groups=mesh['ctx'=16,'dp'=2] {'ctx','dp'}, dimensions={0} | all-to-all | bytes 8192 | tf_op jit(solution)/shard_map/all_to_all | solution.py:54
  41.0 0.5 %reduce_sum.19 = f32[32]{0:T(128)} reduce(f32[32,1,32]{2,0,1:T(8,128)S(1)} %bitcast.53, f32[]{:T(128)} %constant.32.clone.1), dimensions={0,1}, to_apply=%region_1.2 | reduce | flops 992 | bytes 4228 | tf_op jit(solution)/shard_map/reduce_sum | solution.py:54
  41.5 0.0 collective-permute-done.2
  41.5 0.0 collective-permute-done.3
  41.5 0.1 fusion
  41.6 0.7 %slice_bitcast_fusion = (bf16[1,1,2,64,512]{4,3,2,1,0:T(8,128)(2,1)}, bf16[1,1,2,64,512]{4,3,2,1,0:T(8,128)(2,1)}) fusion(bf16[2,64,1024]{2,1,0:T(8,128)(2,1)S(1)} %fusion), kind=kLoop, calls=%fused_computation.6 | loop fusion | bytes 524288 | tf_op jit(solution)/shard_map/reshape | solution.py:211
  (6 shorter events, 0.1 us)
Async XLA Ops:
  0.6 13.5 %copy-start.1 = (bf16[1,1,2,64,512]{4,3,2,1,0:T(8,128)(2,1)S(1)}, bf16[1,1,2,64,512]{4,3,2,1,0:T(8,128)(2,1)}, u32[]{:S(2)}) copy-start(bf16[1,1,2,64,512]{4,3,2,1,0:T(8,128)(2,1)} %param.7) | copy-start | bytes 393220
  0.7 13.5 %copy-start.2 = (bf16[1,1,2,64,512]{4,3,2,1,0:T(8,128)(2,1)S(1)}, bf16[1,1,2,64,512]{4,3,2,1,0:T(8,128)(2,1)}, u32[]{:S(2)}) copy-start(bf16[1,1,2,64,512]{4,3,2,1,0:T(8,128)(2,1)} %param.8) | copy-start | bytes 393220
  1.8 8.0 %collective-permute-start = (bf16[64,1024]{1,0:T(8,128)(2,1)S(1)}, bf16[64,1024]{1,0:T(8,128)(2,1)S(1)}, u32[]{:S(2)}, u32[]{:S(2)}) collective-permute-start(bf16[64,1024]{1,0:T(8,128)(2,1)S(1)} %get-tuple-element.14), channel_id=1, source_target_pairs={{2,4},{4,2},{6,8},{8,6},{10,12},{12,10},{14,16},{16,14},{18,20},{2... | collective-permute-start | bytes 393224 | tf_op jit(solution)/shard_map/ppermute | solution.py:34
  2.4 11.7 %collective-permute-start.1 = (bf16[64,1024]{1,0:T(8,128)(2,1)S(1)}, bf16[64,1024]{1,0:T(8,128)(2,1)S(1)}, u32[]{:S(2)}, u32[]{:S(2)}) collective-permute-start(bf16[64,1024]{1,0:T(8,128)(2,1)S(1)} %get-tuple-element.15), channel_id=1, source_target_pairs={{0,2},{2,0},{4,6},{6,4},{8,10},{10,8},{12,14},{14,12},{16,18},{18,... | collective-permute-start | bytes 393224 | tf_op jit(solution)/shard_map/ppermute | solution.py:34
  8.3 0.7 %copy-start.4 = (s32[1,1,2,2,64]{4,3,2,1,0:T(2,128)S(1)}, s32[1,1,2,2,64]{4,3,2,1,0:T(2,128)}, u32[]{:S(2)}) copy-start(s32[1,1,2,2,64]{4,3,2,1,0:T(2,128)} %param.9) | copy-start | bytes 3076
  23.3 1.2 %copy-start = (f32[2,128,512]{2,1,0:T(8,128)S(1)}, f32[2,128,512]{2,1,0:T(8,128)}, u32[]{:S(2)}) copy-start(f32[2,128,512]{2,1,0:T(8,128)} %get-tuple-element.19) | copy-start | bytes 1572868
  24.7 2.6 %copy-start.3 = (f32[2,4,8,128]{3,2,1,0:T(8,128)S(1)}, f32[2,4,8,128]{3,2,1,0:T(8,128)}, u32[]{:S(2)}) copy-start(f32[2,4,8,128]{3,2,1,0:T(8,128)} %get-tuple-element.22) | copy-start | bytes 98308
  24.7 16.8 %collective-permute-start.2 = (bf16[64,1024]{1,0:T(8,128)(2,1)S(1)}, bf16[64,1024]{1,0:T(8,128)(2,1)S(1)}, u32[]{:S(2)}, u32[]{:S(2)}) collective-permute-start(bf16[64,1024]{1,0:T(8,128)(2,1)S(1)} %get-tuple-element.20), channel_id=1, source_target_pairs={{0,2},{2,0},{4,6},{6,4},{8,10},{10,8},{12,14},{14,12},{16,18},{18,... | collective-permute-start | bytes 393224 | tf_op jit(solution)/shard_map/ppermute | solution.py:34
  26.6 14.9 %collective-permute-start.3 = (bf16[64,1024]{1,0:T(8,128)(2,1)S(1)}, bf16[64,1024]{1,0:T(8,128)(2,1)S(1)}, u32[]{:S(2)}, u32[]{:S(2)}) collective-permute-start(bf16[64,1024]{1,0:T(8,128)(2,1)S(1)} %get-tuple-element.21), channel_id=1, source_target_pairs={{2,4},{4,2},{6,8},{8,6},{10,12},{12,10},{14,16},{16,14},{18,20},{2... | collective-permute-start | bytes 393224 | tf_op jit(solution)/shard_map/ppermute | solution.py:34
